TPU v7x, 32 devices: a whole 2x2x4 slice. The times are simulated.
32 devices in a mesh: seq: 8 (over z, x), ch: 4 (over y, core).
Axes of the slice: x: 2, y: 2, z: 4, core: 2. Of those that a mesh axis runs over, the one named last changes fastest.
Arguments:
- tokens: int32 [2, 4096], P(None, 'seq'), may hold values from 0 to 3
- masked: int32 [2, 4096], P(None, 'seq'), may hold values 0 or 1
- hidden_forward: bfloat16 [2, 4096, 1024], P(None, 'seq', 'ch'), may hold values from -16 to 16
- hidden_reverse: bfloat16 [2, 4096, 1024], P(None, 'seq', 'ch'), may hold values from -16 to 16
- embed_table: bfloat16 [5, 1024], P(None, 'ch'), may hold values from -3 to 3
- conv_kernel: float32 [7, 1024], P(None, 'ch'), may hold values from -2.4 to 2.4
- conv_bias: float32 [1024], P('ch'), may hold values from -3 to 3
- norm_gain: float32 [1024], P('ch'), may hold values from 0.25 to 1.75
- w_gate: bfloat16 [1024, 4096], P(None, 'ch'), may hold values from -0.1875 to 0.1875
- w_value: bfloat16 [1024, 4096], P(None, 'ch'), may hold values from -0.1875 to 0.1875
- w_out: bfloat16 [4096, 1024], P('ch'), may hold values from -0.09375 to 0.09375
Outputs:
- out_forward: bfloat16 [2, 4096, 1024], P(None, 'seq', 'ch')
- out_reverse: bfloat16 [2, 4096, 1024], P(None, 'seq', 'ch')
Inputs may be any that keep to these rules, and one draw needn't show every extreme that they name: `tokens`: base ids A, C, G, T are 0, 1, 2, 3 and the complement of b is 3 - b.
All inputs are finite; a program needn't handle non-finite values. No bound on the sum of `masked` on one device may be relied on, other than what follows from the above.
Results may differ from a plain program's by a relative error of at most 0.0067.
Values may be sent and summed in bfloat16 or wider, within the bound.
No kernel may reach another device: no remote copies, remote signals or barrier semaphores. Data moves between devices by JAX's collectives and lax.ppermute only.
A program may use at most 128 MiB of HBM per device.

v0:
```python
import jax
import jax.numpy as jnp
from jax import lax
from jax.sharding import PartitionSpec as P


def mirror(value, axes, count):
    return lax.ppermute(value, axes, [(k, count - 1 - k) for k in range(count)])


def partner(value, axis, bit):
    mask = 1 << bit
    return lax.ppermute(value, axis, [(k, k ^ mask) for k in range(lax.axis_size(axis))])


def padded_2(cells, axis, dim, width):
    count = lax.axis_size(axis)
    ends = count - 1
    head = lax.slice_in_dim(cells, 0, width, axis=dim)
    tail = lax.slice_in_dim(cells, cells.shape[dim] - width, cells.shape[dim], axis=dim)
    return jnp.concatenate(
        [
            lax.ppermute(tail, axis, [(i, (i + 1) % count) for i in range(ends)]),
            cells,
            lax.ppermute(head, axis, [((i + 1) % count, i) for i in range(ends)]),
        ],
        axis=dim,
    )


def embedded(bases, table):
    out = jnp.zeros(bases.shape + (table.shape[1],), jnp.float32)
    for v in range(table.shape[0]):
        out = out + jnp.where(bases[..., None] == v, table[v], 0.0)
    return out


def gather_blocks(block, bits, me):
    cur = block[None]
    for bit in reversed(range(bits)):
        other = partner(cur, "ch", bit)
        low = ((me >> bit) & 1) == 0
        first = jnp.where(low, cur, other)
        second = jnp.where(low, other, cur)
        cur = jnp.stack([first, second], axis=1).reshape((-1,) + block.shape)
    return cur


def scatter_blocks(part, bits, me):
    cur = part
    for bit in range(bits):
        cur = cur.reshape((-1, 2) + part.shape[1:])
        low = ((me >> bit) & 1) == 0
        keep = jnp.where(low, cur[:, 0], cur[:, 1])
        give = jnp.where(low, cur[:, 1], cur[:, 0])
        if bit > 0:
            give = give.astype(jnp.bfloat16)
        cur = keep + partner(give, "ch", bit).astype(jnp.float32)
    return cur[0]


def local(
    tokens,
    masked,
    hidden_forward,
    hidden_reverse,
    embed_table,
    conv_kernel,
    conv_bias,
    norm_gain,
    w_gate,
    w_value,
    w_out,
):
    seq_count = lax.axis_size("seq")
    ch_count = lax.axis_size("ch")
    ch_bits = ch_count.bit_length() - 1
    me = lax.axis_index("ch")
    table = embed_table.astype(jnp.float32)
    base_in = jnp.where(masked == 1, 4, tokens)
    comp = jnp.where(masked == 1, 4, 3 - tokens)
    rev_here = jnp.flip(mirror(hidden_reverse, "seq", seq_count), axis=1)
    comp_back = jnp.flip(mirror(comp, "seq", seq_count), axis=1)

    local_width = hidden_forward.shape[-1]
    width = local_width * ch_count
    taps = conv_kernel.shape[0]
    half_width = taps // 2

    def conv_rows(hidden, bases, kernel):
        x = hidden.astype(jnp.float32) + embedded(bases, table)
        square = lax.psum(jnp.sum(x * x, axis=-1), "ch")
        normed = (x * lax.rsqrt(square[..., None] / width + 1e-05) * norm_gain).astype(jnp.bfloat16)
        length = normed.shape[1]
        padded = padded_2(normed, "seq", 1, half_width).astype(jnp.float32)
        conv = jnp.zeros(normed.shape, jnp.float32) + conv_bias
        for offset in range(taps):
            conv = conv + kernel[offset] * padded[:, offset : offset + length]
        return x, conv.astype(jnp.bfloat16).reshape(-1, local_width)

    def activation(rows):
        pieces = gather_blocks(rows, ch_bits, me)
        dims = (((0, 2), (0, 1)), ((), ()))
        gate = lax.dot_general(
            pieces, w_gate.reshape(ch_count, local_width, -1), dims, preferred_element_type=jnp.float32
        )
        value = lax.dot_general(
            pieces, w_value.reshape(ch_count, local_width, -1), dims, preferred_element_type=jnp.float32
        )
        return (jax.nn.silu(gate) * value).astype(jnp.bfloat16)

    x_fwd, rows_fwd = conv_rows(hidden_forward, base_in, conv_kernel)
    _, rows_rev = conv_rows(rev_here, comp, conv_kernel[::-1])
    act_fwd = activation(rows_fwd)
    act_rev = activation(rows_rev)
    contract = (((0,), (1,)), ((), ()))
    part = lax.dot_general(w_out, act_fwd, contract, preferred_element_type=jnp.float32) + jnp.flip(
        lax.dot_general(w_out, act_rev, contract, preferred_element_type=jnp.float32), axis=0
    )
    share = scatter_blocks(part.reshape(ch_count, local_width, -1), ch_bits, me)
    out_forward = x_fwd + share.T.reshape(x_fwd.shape)
    sent = mirror(
        jnp.flip(share, axis=0).T.astype(jnp.bfloat16).reshape(x_fwd.shape), ("seq", "ch"), seq_count * ch_count
    )
    x_rev = hidden_reverse.astype(jnp.float32) + embedded(comp_back, table)
    out_reverse = x_rev + jnp.flip(sent, axis=1).astype(jnp.float32)
    return (out_forward.astype(jnp.bfloat16), out_reverse.astype(jnp.bfloat16))


def solution(mesh):
    placed = (
        P(None, "seq"),
        P(None, "seq"),
        P(None, "seq", "ch"),
        P(None, "seq", "ch"),
        P(None, "ch"),
        P(None, "ch"),
        P("ch"),
        P("ch"),
        P(None, "ch"),
        P(None, "ch"),
        P("ch", None),
    )
    return jax.shard_map(
        local,
        mesh=mesh,
        in_specs=placed,
        out_specs=(P(None, "seq", "ch"), P(None, "seq", "ch")),
        check_vma=False,
    )
```

profile of v0, /device:TPU:17, one launch (start us, length us, event | category | flops | bytes accessed | tf_op | source)
XLA Modules:
  0.0 223.8 jit_solution(16020101666498695574)
XLA Ops:
  4.4 21.5 %collective-permute-done.4 = bf16[2,512,256]{2,1,0:T(8,128)(2,1)S(1)} collective-permute-done((bf16[2,512,256]{2,1,0:T(8,128)(2,1)}, bf16[2,512,256]{2,1,0:T(8,128)(2,1)S(1)}, u32[]{:S(2)}, u32[]{:S(2)}) %collective-permute-start.4) | collective-permute-done | bytes 524320 | tf_op jit(solution)/shard_map/ppermute | solution.py:8
  26.5 5.0 %multiply_reduce_fusion.1 = (f32[2,512]{1,0:T(2,128)S(1)}, f32[2,512]{1,0:T(2,128)S(1)}) fusion(f32[256]{0:T(256)S(1)} %bitcast.182, pred[2,512]{1,0:T(4,128)(4,1)S(1)} %get-tuple-element.51, f32[256]{0:T(256)S(1)} %bitcast.178, pred[2,512]{1,0:T(4,128)(4,1)S(1)} %get-tuple-element.53, f32[256]{0:T(256)S(1)} %bitcast.174, ...), kind=kLoop, calls=%fused_computation.67 | loop fusion | flops 6813696 | bytes 1072128 | tf_op jit(solution)/shard_map/reduce_sum | solution.py:92
  31.5 6.6 %all-reduce = (f32[2,512]{1,0:T(2,128)S(1)}, f32[2,512]{1,0:T(2,128)S(1)}) all-reduce(f32[2,512]{1,0:T(2,128)S(1)} %get-tuple-element.3, f32[2,512]{1,0:T(2,128)S(1)} %get-tuple-element.2), channel_id=1, replica_groups=mesh['seq'=8,'ch'=4] {'ch'}, use_global_device_ids=true, to_apply=%region_3.4 | all-reduce | flops 2048 | bytes 16384 | tf_op jit(solution)/shard_map/psum | solution.py:92
  39.3 3.0 %collective-permute-start.6 = (bf16[2,3,256]{2,1,0:T(4,128)(2,1)S(1)}, bf16[2,3,256]{2,1,0:T(4,128)(2,1)S(1)}, u32[]{:S(2)}, u32[]{:S(2)}) collective-permute-start(bf16[2,3,256]{2,1,0:T(4,128)(2,1)S(1)} %get-tuple-element.21), channel_id=1, source_target_pairs={{4,0},{8,4},{12,8},{16,12},{20,16},{24,20},{28,24},{5,1},{9,5},{13... | collective-permute-start | bytes 9224 | tf_op jit(solution)/shard_map/ppermute | solution.py:25
  42.4 2.3 %collective-permute-start.5 = (bf16[2,3,256]{2,1,0:T(4,128)(2,1)S(1)}, bf16[2,3,256]{2,1,0:T(4,128)(2,1)S(1)}, u32[]{:S(2)}, u32[]{:S(2)}) collective-permute-start(bf16[2,3,256]{2,1,0:T(4,128)(2,1)S(1)} %get-tuple-element.20), channel_id=1, source_target_pairs={{0,4},{4,8},{8,12},{12,16},{16,20},{20,24},{24,28},{1,5},{5,9},{9,... | collective-permute-start | bytes 9224 | tf_op jit(solution)/shard_map/ppermute | solution.py:23
  44.7 2.9 %collective-permute-done.5 = bf16[2,3,256]{2,1,0:T(4,128)(2,1)S(1)} collective-permute-done((bf16[2,3,256]{2,1,0:T(4,128)(2,1)S(1)}, bf16[2,3,256]{2,1,0:T(4,128)(2,1)S(1)}, u32[]{:S(2)}, u32[]{:S(2)}) %collective-permute-start.5) | collective-permute-done | bytes 3104 | tf_op jit(solution)/shard_map/ppermute | solution.py:23
  51.1 1.9 collective-permute-start.1
  53.1 3.4 %collective-permute-start = (bf16[2,3,256]{2,1,0:T(4,128)(2,1)S(1)}, bf16[2,3,256]{2,1,0:T(4,128)(2,1)S(1)}, u32[]{:S(2)}, u32[]{:S(2)}) collective-permute-start(bf16[2,3,256]{2,1,0:T(4,128)(2,1)S(1)} %get-tuple-element.18), channel_id=1, source_target_pairs={{0,4},{4,8},{8,12},{12,16},{16,20},{20,24},{24,28},{1,5},{5,9},{9,... | collective-permute-start | bytes 9224 | tf_op jit(solution)/shard_map/ppermute | solution.py:23
  62.2 3.3 %collective-permute-start.8 = (bf16[2,1024,256]{2,1,0:T(8,128)(2,1)}, bf16[2,1024,256]{2,1,0:T(8,128)(2,1)}, u32[]{:S(2)}, u32[]{:S(2)}) collective-permute-start(bf16[2,1024,256]{2,1,0:T(8,128)(2,1)} %maximum_bitcast_fusion.1), channel_id=1, source_target_pairs={{0,1},{1,0},{2,3},{3,2},{4,5},{5,4},{6,7},{7,6},{8,9},{9,8},{10,11... | collective-permute-start | bytes 3145736 | tf_op jit(solution)/shard_map/ppermute | solution.py:13
  68.5 12.5 %collective-permute-done.2 = bf16[1,1024,256]{2,1,0:T(8,128)(2,1)} collective-permute-done((bf16[1,1024,256]{2,1,0:T(8,128)(2,1)}, bf16[1,1024,256]{2,1,0:T(8,128)(2,1)}, u32[]{:S(2)}, u32[]{:S(2)}) %collective-permute-start.2) | collective-permute-done | bytes 524320 | tf_op jit(solution)/shard_map/ppermute | solution.py:13
  86.8 4.3 %fusion.37 = f32[1024,1024,1]{1,0,2:T(8,128)} fusion(bf16[4,1024,256]{2,1,0:T(8,128)(2,1)S(1)} %bitcast.162, bf16[4,256,1024]{2,1,0:T(8,128)(2,1)S(1)} %bitcast.154), kind=kOutput, calls=%fused_computation.106 | convolution fusion | flops 2147483648 | bytes 8388608 | tf_op jit(solution)/shard_map/dot_general | solution.py:104
  91.1 10.8 %convolution_bitcast_fusion = f32[1024,1024]{1,0:T(8,128)} fusion(bf16[1024,1024]{1,0:T(8,128)(2,1)} %param.21, f32[1024,1024,1]{1,0,2:T(8,128)} %fusion.37, bf16[4,1024,256]{2,1,0:T(8,128)(2,1)} %bitcast.163, bf16[4,256,1024]{2,1,0:T(8,128)(2,1)} %bitcast.200), kind=kOutput, calls=%fused_computation.15 | convolution fusion | flops 4301258752 | bytes 14680064 | tf_op jit(solution)/shard_map/dot_general | solution.py:118
  101.8 32.9 %rev.21 = f32[1024,1024]{1,0:T(8,128)} reverse(f32[1024,1024]{1,0:T(8,128)} %convolution_bitcast_fusion), dimensions={0} | reverse | bytes 8388608 | tf_op jit(solution)/shard_map/jit(_flip)/rev | solution.py:117
  137.6 4.4 %fusion.36 = f32[1024,1024,1]{1,0,2:T(8,128)} fusion(bf16[4,1024,256]{2,1,0:T(8,128)(2,1)S(1)} %bitcast.160, bf16[4,256,1024]{2,1,0:T(8,128)(2,1)S(1)} %bitcast.153), kind=kOutput, calls=%fused_computation.105 | convolution fusion | flops 2147483648 | bytes 8388608 | tf_op jit(solution)/shard_map/dot_general | solution.py:104
  142.0 11.9 %bitcast_add_fusion = f32[1024,1024]{1,0:T(8,128)} fusion(f32[1024,1024]{1,0:T(8,128)} %rev.21, bf16[1024,1024]{1,0:T(8,128)(2,1)} %param.21, f32[1024,1024,1]{1,0,2:T(8,128)} %fusion.36, bf16[4,1024,256]{2,1,0:T(8,128)(2,1)} %bitcast.161, bf16[4,256,1024]{2,1,0:T(8,128)(2,1)} %bitcast.201), kind=kOutput, calls=%fused_computation.7 | convolution fusion | flops 4302307328 | bytes 18874368 | tf_op jit(solution)/shard_map/dot_general | solution.py:117
  153.9 2.8 %select_bitcast_fusion = f32[2,256,1024]{2,1,0:T(8,128)S(1)} fusion(f32[2,2,256,1024]{3,2,1,0:T(8,128)} %bitcast.155, pred[]{:T(512)S(6)} %eq.81), kind=kLoop, calls=%fused_computation.22 | loop fusion | flops 524288 | bytes 6291457 | tf_op jit(solution)/shard_map/jit(_where)/select_n | solution.py:55
  156.8 4.1 %collective-permute-done.9 = f32[2,256,1024]{2,1,0:T(8,128)S(1)} collective-permute-done((f32[2,256,1024]{2,1,0:T(8,128)S(1)}, f32[2,256,1024]{2,1,0:T(8,128)S(1)}, u32[]{:S(2)}, u32[]{:S(2)}) %collective-permute-start.9) | collective-permute-done | bytes 2097184 | tf_op jit(solution)/shard_map/ppermute | solution.py:13
  163.2 12.1 %collective-permute-done.10 = bf16[1,256,1024]{2,1,0:T(8,128)(2,1)S(1)} collective-permute-done((bf16[1,256,1024]{2,1,0:T(8,128)(2,1)S(1)}, bf16[1,256,1024]{2,1,0:T(8,128)(2,1)S(1)}, u32[]{:S(2)}, u32[]{:S(2)}) %collective-permute-start.10) | collective-permute-done | bytes 524320 | tf_op jit(solution)/shard_map/ppermute | solution.py:13
  179.0 2.6 %collective-permute-start.11 = (s32[2,512]{1,0:T(2,128)S(1)}, s32[2,512]{1,0:T(2,128)S(1)}, u32[]{:S(2)}, u32[]{:S(2)}) collective-permute-start(s32[2,512]{1,0:T(2,128)S(1)} %get-tuple-element.7), channel_id=1, source_target_pairs={{0,28},{4,24},{8,20},{12,16},{16,12},{20,8},{24,4},{28,0},{1,29},{... | collective-permute-start | bytes 12296 | tf_op jit(solution)/shard_map/ppermute | solution.py:8
  181.6 23.6 %collective-permute-done.11 = s32[2,512]{1,0:T(2,128)S(1)} collective-permute-done((s32[2,512]{1,0:T(2,128)S(1)}, s32[2,512]{1,0:T(2,128)S(1)}, u32[]{:S(2)}, u32[]{:S(2)}) %collective-permute-start.11) | collective-permute-done | bytes 4128 | tf_op jit(solution)/shard_map/ppermute | solution.py:8
  205.5 3.0 %fusion.28 = f32[1024,256]{0,1:T(8,128)} fusion(bf16[1,256,1024]{2,1,0:T(8,128)(2,1)} %copy-done.12, f32[1,2,256,1024]{3,2,1,0:T(8,128)} %copy-done.1, pred[]{:T(512)S(6)} %eq.80), kind=kLoop, calls=%fused_computation.77 | loop fusion | flops 786432 | bytes 3670017 | tf_op jit(solution)/shard_map/transpose | solution.py:121
  208.5 2.6 %copy.20 = f32[1024,256]{1,0:T(8,128)} copy(f32[1024,256]{0,1:T(8,128)} %fusion.28) | data formatting | bytes 2097152 | tf_op jit(solution)/shard_map/transpose | solution.py:121
  211.1 6.3 %rev.24 = bf16[2,512,256]{2,1,0:T(8,128)(2,1)S(1)} reverse(bf16[2,512,256]{2,1,0:T(8,128)(2,1)} %collective-permute-done.12), dimensions={1} | reverse | bytes 1048576 | tf_op jit(solution)/shard_map/jit(_flip)/rev | solution.py:126
  217.5 6.3 %add_convert_fusion = (bf16[2,512,256]{2,1,0:T(8,128)(2,1)}, bf16[2,512,256]{2,1,0:T(8,128)(2,1)}) fusion(bf16[2,512,256]{2,1,0:T(8,128)(2,1)S(1)} %rev.24, bf16[2,512,256]{2,1,0:T(8,128)(2,1)} %param.14, f32[256]{0:T(256)S(1)} %bitcast.185, f32[256]{0:T(256)S(1)} %bitcast.181, f32[256]{0:T(256)S(1)} %bitcast.177, f32[256]{0:T(256)S(1)} %bitcast.173, ...), kind=kLoop, calls=%fused_computation.56 | loop fusion | flops 7077888 | bytes 3685376 | tf_op jit(solution)/shard_map/convert_element_type | solution.py:127
  (75 shorter events, 32.7 us)
Async XLA Ops:
  0.6 86.1 %copy-start = (bf16[1024,1024]{1,0:T(8,128)(2,1)S(1)}, bf16[1024,1024]{1,0:T(8,128)(2,1)}, u32[]{:S(2)}) copy-start(bf16[1024,1024]{1,0:T(8,128)(2,1)} %param.19) | copy-start | bytes 6291460
  0.6 37.5 %copy-start.14 = (f32[256]{0:T(256)S(1)}, f32[256]{0:T(256)}, u32[]{:S(2)}) copy-start(f32[256]{0:T(256)} %param.18) | copy-start | bytes 3076
  0.7 25.2 %collective-permute-start.4 = (bf16[2,512,256]{2,1,0:T(8,128)(2,1)}, bf16[2,512,256]{2,1,0:T(8,128)(2,1)S(1)}, u32[]{:S(2)}, u32[]{:S(2)}) collective-permute-start(bf16[2,512,256]{2,1,0:T(8,128)(2,1)} %param.14), channel_id=1, source_target_pairs={{0,28},{4,24},{8,20},{12,16},{16,12},{20,8},{24,4},{28,0},{1,29},{... | collective-permute-start | bytes 1572872 | tf_op jit(solution)/shard_map/ppermute | solution.py:8
  26.5 21.2 %copy-start.13 = (f32[256]{0:T(256)S(1)}, f32[256]{0:T(256)}, u32[]{:S(2)}) copy-start(f32[256]{0:T(256)} %param.17) | copy-start | bytes 3076
  39.3 5.3 %collective-permute-start.6 = (bf16[2,3,256]{2,1,0:T(4,128)(2,1)S(1)}, bf16[2,3,256]{2,1,0:T(4,128)(2,1)S(1)}, u32[]{:S(2)}, u32[]{:S(2)}) collective-permute-start(bf16[2,3,256]{2,1,0:T(4,128)(2,1)S(1)} %get-tuple-element.21), channel_id=1, source_target_pairs={{4,0},{8,4},{12,8},{16,12},{20,16},{24,20},{28,24},{5,1},{9,5},{13... | collective-permute-start | bytes 9224 | tf_op jit(solution)/shard_map/ppermute | solution.py:25
  42.4 5.3 %collective-permute-start.5 = (bf16[2,3,256]{2,1,0:T(4,128)(2,1)S(1)}, bf16[2,3,256]{2,1,0:T(4,128)(2,1)S(1)}, u32[]{:S(2)}, u32[]{:S(2)}) collective-permute-start(bf16[2,3,256]{2,1,0:T(4,128)(2,1)S(1)} %get-tuple-element.20), channel_id=1, source_target_pairs={{0,4},{4,8},{8,12},{12,16},{16,20},{20,24},{24,28},{1,5},{5,9},{9,... | collective-permute-start | bytes 9224 | tf_op jit(solution)/shard_map/ppermute | solution.py:23
  47.7 2.3 %copy-start.7 = (bf16[2,512,256]{2,1,0:T(8,128)(2,1)S(1)}, bf16[2,512,256]{2,1,0:T(8,128)(2,1)}, u32[]{:S(2)}) copy-start(bf16[2,512,256]{2,1,0:T(8,128)(2,1)} %param.13) | copy-start | bytes 1572868
  48.7 11.2 %copy-start.9 = (bf16[2,512,256]{2,1,0:T(8,128)(2,1)}, bf16[2,512,256]{2,1,0:T(8,128)(2,1)S(1)}, u32[]{:S(2)}) copy-start(bf16[2,512,256]{2,1,0:T(8,128)(2,1)S(1)} %fusion.12) | copy-start | bytes 1572868
  48.7 11.2 %collective-permute-start.7 = (bf16[1,1024,256]{2,1,0:T(8,128)(2,1)S(1)}, bf16[1,1024,256]{2,1,0:T(8,128)(2,1)}, u32[]{:S(2)}, u32[]{:S(2)}) collective-permute-start(bf16[1,1024,256]{2,1,0:T(8,128)(2,1)S(1)} %bitcast.158), channel_id=1, source_target_pairs={{0,2},{1,3},{2,0},{3,1},{4,6},{5,7},{6,4},{7,5},{8,10},{9,11},{10,... | collective-permute-start | bytes 1572872 | tf_op jit(solution)/shard_map/ppermute | solution.py:13
  51.1 5.3 %collective-permute-start.1 = (bf16[2,3,256]{2,1,0:T(4,128)(2,1)S(1)}, bf16[2,3,256]{2,1,0:T(4,128)(2,1)S(1)}, u32[]{:S(2)}, u32[]{:S(2)}) collective-permute-start(bf16[2,3,256]{2,1,0:T(4,128)(2,1)S(1)} %get-tuple-element.19), channel_id=1, source_target_pairs={{4,0},{8,4},{12,8},{16,12},{20,16},{24,20},{28,24},{5,1},{9,5},{13... | collective-permute-start | bytes 9224 | tf_op jit(solution)/shard_map/ppermute | solution.py:25
  53.1 5.3 %collective-permute-start = (bf16[2,3,256]{2,1,0:T(4,128)(2,1)S(1)}, bf16[2,3,256]{2,1,0:T(4,128)(2,1)S(1)}, u32[]{:S(2)}, u32[]{:S(2)}) collective-permute-start(bf16[2,3,256]{2,1,0:T(4,128)(2,1)S(1)} %get-tuple-element.18), channel_id=1, source_target_pairs={{0,4},{4,8},{8,12},{12,16},{16,20},{20,24},{24,28},{1,5},{5,9},{9,... | collective-permute-start | bytes 9224 | tf_op jit(solution)/shard_map/ppermute | solution.py:23
  62.2 22.8 %collective-permute-start.8 = (bf16[2,1024,256]{2,1,0:T(8,128)(2,1)}, bf16[2,1024,256]{2,1,0:T(8,128)(2,1)}, u32[]{:S(2)}, u32[]{:S(2)}) collective-permute-start(bf16[2,1024,256]{2,1,0:T(8,128)(2,1)} %maximum_bitcast_fusion.1), channel_id=1, source_target_pairs={{0,1},{1,0},{2,3},{3,2},{4,5},{5,4},{6,7},{7,6},{8,9},{9,8},{10,11... | collective-permute-start | bytes 3145736 | tf_op jit(solution)/shard_map/ppermute | solution.py:13
  67.2 13.8 %collective-permute-start.2 = (bf16[1,1024,256]{2,1,0:T(8,128)(2,1)}, bf16[1,1024,256]{2,1,0:T(8,128)(2,1)}, u32[]{:S(2)}, u32[]{:S(2)}) collective-permute-start(bf16[1,1024,256]{2,1,0:T(8,128)(2,1)} %bitcast.12), channel_id=1, source_target_pairs={{0,2},{1,3},{2,0},{3,1},{4,6},{5,7},{6,4},{7,5},{8,10},{9,11},{10,... | collective-permute-start | bytes 1572872 | tf_op jit(solution)/shard_map/ppermute | solution.py:13
  84.2 50.5 %collective-permute-start.3 = (bf16[2,1024,256]{2,1,0:T(8,128)(2,1)}, bf16[2,1024,256]{2,1,0:T(8,128)(2,1)}, u32[]{:S(2)}, u32[]{:S(2)}) collective-permute-start(bf16[2,1024,256]{2,1,0:T(8,128)(2,1)} %maximum_bitcast_fusion), channel_id=1, source_target_pairs={{0,1},{1,0},{2,3},{3,2},{4,5},{5,4},{6,7},{7,6},{8,9},{9,8},{10,11... | collective-permute-start | bytes 3145736 | tf_op jit(solution)/shard_map/ppermute | solution.py:13
  86.7 4.3 %copy-start.11 = (bf16[2,2,1024,256]{3,2,1,0:T(8,128)(2,1)}, bf16[2,2,1024,256]{3,2,1,0:T(8,128)(2,1)S(1)}, u32[]{:S(2)}) copy-start(bf16[2,2,1024,256]{3,2,1,0:T(8,128)(2,1)S(1)} %copy.14) | copy-start | bytes 6291460
  101.8 32.9 %copy-start.4 = (bf16[1,1,1024,256]{3,2,1,0:T(8,128)(2,1)S(1)}, bf16[1,1,1024,256]{3,2,1,0:T(8,128)(2,1)}, u32[]{:S(2)}) copy-start(bf16[1,1,1024,256]{3,2,1,0:T(8,128)(2,1)} %copy-done.3) | copy-start | bytes 1572868
  101.8 32.9 %copy-start.6 = (bf16[1,1,1024,256]{3,2,1,0:T(8,128)(2,1)S(1)}, bf16[1,1,1024,256]{3,2,1,0:T(8,128)(2,1)}, u32[]{:S(2)}) copy-start(bf16[1,1,1024,256]{3,2,1,0:T(8,128)(2,1)} %copy-done.5) | copy-start | bytes 1572868
  153.9 7.0 %copy-start.2 = (f32[1024,1024]{1,0:T(8,128)S(1)}, f32[1024,1024]{1,0:T(8,128)}, u32[]{:S(2)}) copy-start(f32[1024,1024]{1,0:T(8,128)} %bitcast_add_fusion) | copy-start | bytes 12582916
  156.7 4.2 %collective-permute-start.9 = (f32[2,256,1024]{2,1,0:T(8,128)S(1)}, f32[2,256,1024]{2,1,0:T(8,128)S(1)}, u32[]{:S(2)}, u32[]{:S(2)}) collective-permute-start(f32[2,256,1024]{2,1,0:T(8,128)S(1)} %select_bitcast_fusion), channel_id=1, source_target_pairs={{0,1},{1,0},{2,3},{3,2},{4,5},{5,4},{6,7},{7,6},{8,9},{9,8},{10,11... | collective-permute-start | bytes 6291464 | tf_op jit(solution)/shard_map/ppermute | solution.py:13
  161.8 13.5 %copy-start.1 = (f32[1,2,256,1024]{3,2,1,0:T(8,128)}, f32[1,2,256,1024]{3,2,1,0:T(8,128)S(1)}, u32[]{:S(2)}) copy-start(f32[1,2,256,1024]{3,2,1,0:T(8,128)S(1)} %fusion.10) | copy-start | bytes 6291460
  161.9 13.4 %collective-permute-start.10 = (bf16[1,256,1024]{2,1,0:T(8,128)(2,1)S(1)}, bf16[1,256,1024]{2,1,0:T(8,128)(2,1)S(1)}, u32[]{:S(2)}, u32[]{:S(2)}) collective-permute-start(bf16[1,256,1024]{2,1,0:T(8,128)(2,1)S(1)} %fusion.27), channel_id=1, source_target_pairs={{0,2},{1,3},{2,0},{3,1},{4,6},{5,7},{6,4},{7,5},{8,10},{9,11},{10,... | collective-permute-start | bytes 1572872 | tf_op jit(solution)/shard_map/ppermute | solution.py:13
  177.3 33.8 %collective-permute-start.12 = (bf16[2,512,256]{2,1,0:T(8,128)(2,1)S(1)}, bf16[2,512,256]{2,1,0:T(8,128)(2,1)}, u32[]{:S(2)}, u32[]{:S(2)}) collective-permute-start(bf16[2,512,256]{2,1,0:T(8,128)(2,1)S(1)} %bitcast.165), channel_id=1, source_target_pairs={{0,31},{1,30},{2,29},{3,28},{4,27},{5,26},{6,25},{7,24},{8,23},{9,... | collective-permute-start | bytes 1572872 | tf_op jit(solution)/shard_map/ppermute | solution.py:8
  179.0 26.2 %collective-permute-start.11 = (s32[2,512]{1,0:T(2,128)S(1)}, s32[2,512]{1,0:T(2,128)S(1)}, u32[]{:S(2)}, u32[]{:S(2)}) collective-permute-start(s32[2,512]{1,0:T(2,128)S(1)} %get-tuple-element.7), channel_id=1, source_target_pairs={{0,28},{4,24},{8,20},{12,16},{16,12},{20,8},{24,4},{28,0},{1,29},{... | collective-permute-start | bytes 12296 | tf_op jit(solution)/shard_map/ppermute | solution.py:8
  208.5 9.0 %copy-start.8 = (bf16[2,512,256]{2,1,0:T(8,128)(2,1)S(1)}, bf16[2,512,256]{2,1,0:T(8,128)(2,1)}, u32[]{:S(2)}) copy-start(bf16[2,512,256]{2,1,0:T(8,128)(2,1)} %param.13) | copy-start | bytes 1572868
  (4 other events, 4.8 us)
where the time goes:
time: 227 us; the launch traced here: 224 us
  waiting for transfers between devices  80.1 us (35%)
  local copies, waits for them, and re-layouts  48.6 us (21%)
  other arithmetic  32 us (14%)
  matrix products  31.3 us (14%)
  starting transfers between devices  24.1 us (11%)
  blocking collectives  6.62 us (3%)
    ppermute x3, waiting for transfers between devices, mirror(): return lax.ppermute(value, axes, [(k, count - 1 - k) for k in range(count)])  45 us
    rev x1, local copies, waits for them, and re-layouts, local(): jnp.flip(lax.dot_general(w_out, act_rev, contract, preferred_element_type...  32.9 us
    ppermute x6, waiting for transfers between devices, partner(): lax.ppermute(value, axis, [(k, k ^ mask) for k in range(lax.axis_size(axi...  30.2 us
    dot_general x1, matrix products, local(): lax.dot_general(w_out, act_fwd, contract, preferred_element_type=jnp.floa...  11.9 us
    dot_general x1, matrix products, local(): lax.dot_general(w_out, act_rev, contract, preferred_element_type=jnp.floa...  10.8 us
    dot_general x2, matrix products, activation(): lax.dot_general(pieces, w_gate.reshape(ch_count, local_width, -1), dims,...  8.68 us
    ppermute x6, starting transfers between devices, partner(): lax.ppermute(value, axis, [(k, k ^ mask) for k in range(lax.axis_size(axi...  8.14 us
    psum x1, blocking collectives, conv_rows(): square = lax.psum(jnp.sum(x * x, axis=-1), 'ch')  6.62 us
  transfers between devices with their start and end apart: 13, of which 8 were waited for; matrix products, arithmetic and copies ran while one was open for 28% of the time, Pallas kernels for 0%

commit v1 on v0

--- a/solution.py
+++ b/solution.py
@@ -48,15 +48,23 @@
 
 def scatter_blocks(part, bits, me):
     cur = part
+    rows, _, w = part.shape
     for bit in range(bits):
-        cur = cur.reshape((-1, 2) + part.shape[1:])
+        cur = cur.reshape(rows, -1, 2, w)
         low = ((me >> bit) & 1) == 0
-        keep = jnp.where(low, cur[:, 0], cur[:, 1])
-        give = jnp.where(low, cur[:, 1], cur[:, 0])
+        keep = jnp.where(low, cur[:, :, 0], cur[:, :, 1])
+        give = jnp.where(low, cur[:, :, 1], cur[:, :, 0])
         if bit > 0:
             give = give.astype(jnp.bfloat16)
         cur = keep + partner(give, "ch", bit).astype(jnp.float32)
-    return cur[0]
+    return cur[:, 0]
+
+
+def reversal(n, block):
+    rows = lax.broadcasted_iota(jnp.int32, (n, n), 0)
+    cols = lax.broadcasted_iota(jnp.int32, (n, n), 1)
+    same = rows // block == cols // block
+    return (same & (rows % block + cols % block == block - 1)).astype(jnp.bfloat16)
 
 
 def local(
@@ -113,17 +121,23 @@
     _, rows_rev = conv_rows(rev_here, comp, conv_kernel[::-1])
     act_fwd = activation(rows_fwd)
     act_rev = activation(rows_rev)
-    contract = (((0,), (1,)), ((), ()))
-    part = lax.dot_general(w_out, act_fwd, contract, preferred_element_type=jnp.float32) + jnp.flip(
-        lax.dot_general(w_out, act_rev, contract, preferred_element_type=jnp.float32), axis=0
+    lane_flip = reversal(local_width, local_width)
+    blocks = w_out.reshape(w_out.shape[0], ch_count, local_width)
+    w_flip = jnp.concatenate([blocks[:, k] for k in reversed(range(ch_count))], axis=1)
+    w_flip = jnp.dot(
+        w_flip.reshape(-1, local_width), lane_flip, preferred_element_type=jnp.float32
+    ).astype(jnp.bfloat16).reshape(w_out.shape)
+    part = jnp.dot(act_fwd, w_out, preferred_element_type=jnp.float32) + jnp.dot(
+        act_rev, w_flip, preferred_element_type=jnp.float32
     )
-    share = scatter_blocks(part.reshape(ch_count, local_width, -1), ch_bits, me)
-    out_forward = x_fwd + share.T.reshape(x_fwd.shape)
-    sent = mirror(
-        jnp.flip(share, axis=0).T.astype(jnp.bfloat16).reshape(x_fwd.shape), ("seq", "ch"), seq_count * ch_count
-    )
+    share = scatter_blocks(part.reshape(part.shape[0], ch_count, local_width), ch_bits, me)
+    out_forward = x_fwd + share.reshape(x_fwd.shape)
+    row_flip = reversal(share.shape[0], x_fwd.shape[1])
+    turned = jnp.dot(share.astype(jnp.bfloat16), lane_flip, preferred_element_type=jnp.float32)
+    turned = jnp.dot(row_flip, turned.astype(jnp.bfloat16), preferred_element_type=jnp.float32)
+    sent = mirror(turned.astype(jnp.bfloat16).reshape(x_fwd.shape), ("seq", "ch"), seq_count * ch_count)
     x_rev = hidden_reverse.astype(jnp.float32) + embedded(comp_back, table)
-    out_reverse = x_rev + jnp.flip(sent, axis=1).astype(jnp.float32)
+    out_reverse = x_rev + sent.astype(jnp.float32)
     return (out_forward.astype(jnp.bfloat16), out_reverse.astype(jnp.bfloat16))
 
 

time: 227 us -> 198 us (0.87)
  local copies, waits for them, and re-layouts: 48.6 us -> 29.7 us
  waiting for transfers between devices: 80.1 us -> 66.4 us
  matrix products: 31.3 us -> 38.5 us
  other arithmetic: 32 us -> 25.7 us
  starting transfers between devices: 24.1 us -> 28.1 us
    rev x3 -> x0, local copies, waits for them, and re-layouts: 39.9 us -> none  [the longest x1 32.9 us: local(): jnp.flip(lax.dot_general(w_out, act_rev, contract, preferred_element_type...]
    reshape x0 -> x2, local copies, waits for them, and re-layouts: none -> 8.74 us  [the longest x1 4.37 us: local(): w_flip = jnp.dot(w_flip.reshape(-1, local_width), lane_flip, preferred_el...]
    dot_general x2 -> x5, matrix products: 22.7 us -> 29.8 us  [the longest x1 11.6 us: local(): jnp.dot(act_rev, w_flip, preferred_element_type=jnp.float32)]
    ppermute x3, waiting for transfers between devices: 45 us -> 38.5 us  [mirror(): return lax.ppermute(value, axes, [(k, count - 1 - k) for k in range(count)])]
    rev x1, local copies, waits for them, and re-layouts: 0.62 us -> 6.35 us  [local(): rev_here = jnp.flip(mirror(hidden_reverse, 'seq', seq_count), axis=1)]
    ppermute x2, waiting for transfers between devices: 4.8 us -> 0.83 us  [padded_2(): lax.ppermute(tail, axis, [(i, (i + 1) % count) for i in range(ends)])]
    concatenate x0 -> x1, local copies, waits for them, and re-layouts: none -> 3.96 us  [local(): jnp.concatenate([blocks[:, k] for k in reversed(range(ch_count))], axis=1)]
    ppermute x6, starting transfers between devices: 8.14 us -> 11.5 us  [partner(): lax.ppermute(value, axis, [(k, k ^ mask) for k in range(lax.axis_size(axi...]
  transfers between devices with their start and end apart: 13 -> 13, of which waited for: 8 -> 7; matrix products, arithmetic and copies ran while one was open for 28% -> 18% of each run, Pallas kernels for 0% -> 0%
where the time goes in v1:
time: 198 us; the launch traced here: 196 us
  waiting for transfers between devices  66.4 us (34%)
  matrix products  38.5 us (19%)
  local copies, waits for them, and re-layouts  29.7 us (15%)
  starting transfers between devices  28.1 us (14%)
  other arithmetic  25.7 us (13%)
  blocking collectives  6.62 us (3%)
    ppermute x3, waiting for transfers between devices, mirror(): return lax.ppermute(value, axes, [(k, count - 1 - k) for k in range(count)])  38.5 us
    ppermute x6, waiting for transfers between devices, partner(): lax.ppermute(value, axis, [(k, k ^ mask) for k in range(lax.axis_size(axi...  27.1 us
    dot_general x1, matrix products, local(): jnp.dot(act_rev, w_flip, preferred_element_type=jnp.float32)  11.6 us
    ppermute x6, starting transfers between devices, partner(): lax.ppermute(value, axis, [(k, k ^ mask) for k in range(lax.axis_size(axi...  11.5 us
    dot_general x1, matrix products, local(): jnp.dot(act_fwd, w_out, preferred_element_type=jnp.float32)  10.9 us
    dot_general x2, matrix products, activation(): lax.dot_general(pieces, w_gate.reshape(ch_count, local_width, -1), dims,...  8.71 us
    ppermute x2, starting transfers between devices, padded_2(): lax.ppermute(head, axis, [((i + 1) % count, i) for i in range(ends)])  6.91 us
    psum x1, blocking collectives, conv_rows(): square = lax.psum(jnp.sum(x * x, axis=-1), 'ch')  6.62 us
  transfers between devices with their start and end apart: 13, of which 7 were waited for; matrix products, arithmetic and copies ran while one was open for 18% of the time, Pallas kernels for 0%

profile of v1, /device:TPU:17, one launch (start us, length us, event | category | flops | bytes accessed | tf_op | source)
XLA Modules:
  0.0 196.1 jit_solution(7383727596400277084)
XLA Ops:
  4.4 4.0 %copy.42 = bf16[1024,1024]{0,1:T(8,128)(2,1)} copy(bf16[1024,1024]{1,0:T(8,128)(2,1)} %param.21) | data formatting | bytes 4194304 | tf_op args[10]
  8.4 2.9 %slice_bitcast_fusion.3 = (bf16[1024,256]{0,1:T(8,128)(2,1)}, bf16[1024,256]{0,1:T(8,128)(2,1)}, bf16[1024,256]{0,1:T(8,128)(2,1)}, bf16[1024,256]{0,1:T(8,128)(2,1)}) fusion(bf16[1024,4,256]{0,2,1:T(8,128)(2,1)} %bitcast.160), kind=kLoop, calls=%fused_computation.96 | loop fusion | bytes 4194304 | tf_op jit(solution)/shard_map/squeeze | solution.py:126
  11.3 14.7 %collective-permute-done.4 = bf16[2,512,256]{2,1,0:T(8,128)(2,1)} collective-permute-done((bf16[2,512,256]{2,1,0:T(8,128)(2,1)}, bf16[2,512,256]{2,1,0:T(8,128)(2,1)}, u32[]{:S(2)}, u32[]{:S(2)}) %collective-permute-start.4) | collective-permute-done | bytes 524320 | tf_op jit(solution)/shard_map/ppermute | solution.py:8
  26.0 6.3 %rev.9 = bf16[2,512,256]{2,1,0:T(8,128)(2,1)S(1)} reverse(bf16[2,512,256]{2,1,0:T(8,128)(2,1)} %collective-permute-done.4), dimensions={1} | reverse | bytes 1048576 | tf_op jit(solution)/shard_map/jit(_flip)/rev | solution.py:90
  34.5 6.6 %all-reduce = (f32[2,512]{1,0:T(2,128)S(1)}, f32[2,512]{1,0:T(2,128)S(1)}) all-reduce(f32[2,512]{1,0:T(2,128)S(1)} %get-tuple-element.3, f32[2,512]{1,0:T(2,128)S(1)} %get-tuple-element.2), channel_id=1, replica_groups=mesh['seq'=8,'ch'=4] {'ch'}, use_global_device_ids=true, to_apply=%region_1.2 | all-reduce | flops 2048 | bytes 16384 | tf_op jit(solution)/shard_map/psum | solution.py:100
  43.5 3.0 %collective-permute-start.6 = (bf16[2,3,256]{2,1,0:T(4,128)(2,1)S(1)}, bf16[2,3,256]{2,1,0:T(4,128)(2,1)S(1)}, u32[]{:S(2)}, u32[]{:S(2)}) collective-permute-start(bf16[2,3,256]{2,1,0:T(4,128)(2,1)S(1)} %get-tuple-element.23), channel_id=1, source_target_pairs={{4,0},{8,4},{12,8},{16,12},{20,16},{24,20},{28,24},{5,1},{9,5},{13... | collective-permute-start | bytes 9224 | tf_op jit(solution)/shard_map/ppermute | solution.py:25
  48.8 3.9 %collective-permute-start.1 = (bf16[2,3,256]{2,1,0:T(4,128)(2,1)S(1)}, bf16[2,3,256]{2,1,0:T(4,128)(2,1)S(1)}, u32[]{:S(2)}, u32[]{:S(2)}) collective-permute-start(bf16[2,3,256]{2,1,0:T(4,128)(2,1)S(1)} %get-tuple-element.25), channel_id=1, source_target_pairs={{4,0},{8,4},{12,8},{16,12},{20,16},{24,20},{28,24},{5,1},{9,5},{13... | collective-permute-start | bytes 9224 | tf_op jit(solution)/shard_map/ppermute | solution.py:25
  61.9 5.7 %collective-permute-done.7 = bf16[1,1024,256]{2,1,0:T(8,128)(2,1)S(1)} collective-permute-done((bf16[1,1024,256]{2,1,0:T(8,128)(2,1)S(1)}, bf16[1,1024,256]{2,1,0:T(8,128)(2,1)S(1)}, u32[]{:S(2)}, u32[]{:S(2)}) %collective-permute-start.7) | collective-permute-done | bytes 524320 | tf_op jit(solution)/shard_map/ppermute | solution.py:13
  68.8 4.8 %collective-permute-start.8 = (bf16[2,1024,256]{2,1,0:T(8,128)(2,1)}, bf16[2,1024,256]{2,1,0:T(8,128)(2,1)}, u32[]{:S(2)}, u32[]{:S(2)}) collective-permute-start(bf16[2,1024,256]{2,1,0:T(8,128)(2,1)} %maximum_bitcast_fusion.1), channel_id=1, source_target_pairs={{0,1},{1,0},{2,3},{3,2},{4,5},{5,4},{6,7},{7,6},{8,9},{9,8},{10,11... | collective-permute-start | bytes 3145736 | tf_op jit(solution)/shard_map/ppermute | solution.py:13
  73.7 5.2 %collective-permute-done.2 = bf16[1,1024,256]{2,1,0:T(8,128)(2,1)S(1)} collective-permute-done((bf16[1,1024,256]{2,1,0:T(8,128)(2,1)S(1)}, bf16[1,1024,256]{2,1,0:T(8,128)(2,1)S(1)}, u32[]{:S(2)}, u32[]{:S(2)}) %collective-permute-start.2) | collective-permute-done | bytes 524320 | tf_op jit(solution)/shard_map/ppermute | solution.py:13
  82.6 4.0 %copy.45 = bf16[1024,1024]{1,0:T(8,128)(2,1)} copy(bf16[1024,1024]{0,1:T(8,128)(2,1)} %pad_maximum_fusion.2) | data formatting | bytes 4194304 | tf_op jit(solution)/shard_map/concatenate | solution.py:126
  86.6 4.4 %reshape.154 = bf16[4096,256]{1,0:T(8,128)(2,1)} reshape(bf16[1024,1024]{1,0:T(8,128)(2,1)} %copy.45) | data formatting | bytes 4194304 | tf_op jit(solution)/shard_map/reshape | solution.py:128
  91.0 3.9 %convolution_convert_fusion = bf16[4096,256]{1,0:T(8,128)(2,1)} fusion(bf16[4096,256]{1,0:T(8,128)(2,1)} %reshape.154, s32[256]{0:T(256)S(1)} %get-tuple-element.60, s32[256]{0:T(256)S(1)} %get-tuple-element.63, s32[256]{0:T(256)S(1)} %get-tuple-element.59, s32[256]{0:T(256)S(1)} %get-tuple-element.64, pred[256]{0:T(512)(128)(4,1)S(1)} %get-tuple-element.61, ...), kind=kOutput, calls=%fused_computation | convolution fusion | flops 538443776 | bytes 4198912 | tf_op jit(solution)/shard_map/dot_general | solution.py:127
  94.8 4.4 %reshape.155 = bf16[1024,1024]{1,0:T(8,128)(2,1)} reshape(bf16[4096,256]{1,0:T(8,128)(2,1)} %convolution_convert_fusion) | data formatting | bytes 4194304 | tf_op jit(solution)/shard_map/reshape | solution.py:129
  103.6 4.4 %fusion.71 = f32[1024,1024,1]{1,0,2:T(8,128)} fusion(bf16[4,1024,256]{2,1,0:T(8,128)(2,1)S(1)} %bitcast.168, bf16[4,256,1024]{2,1,0:T(8,128)(2,1)S(1)} %bitcast.156), kind=kOutput, calls=%fused_computation.151 | convolution fusion | flops 2147483648 | bytes 8388608 | tf_op jit(solution)/shard_map/dot_general | solution.py:112
  108.0 4.3 %fusion.72 = f32[1024,1024,1]{1,0,2:T(8,128)} fusion(bf16[4,1024,256]{2,1,0:T(8,128)(2,1)S(1)} %bitcast.166, bf16[4,256,1024]{2,1,0:T(8,128)(2,1)S(1)} %bitcast.157), kind=kOutput, calls=%fused_computation.152 | convolution fusion | flops 2147483648 | bytes 8388608 | tf_op jit(solution)/shard_map/dot_general | solution.py:112
  112.3 10.9 %fusion.27 = f32[1024,1024]{0,1:T(8,128)} fusion(bf16[1024,1024]{1,0:T(8,128)(2,1)} %param.21, f32[1024,1024,1]{1,0,2:T(8,128)} %fusion.71, bf16[4,1024,256]{2,1,0:T(8,128)(2,1)} %bitcast.169, bf16[4,256,1024]{2,1,0:T(8,128)(2,1)} %bitcast.204), kind=kOutput, calls=%fused_computation.41 | convolution fusion | flops 4301258752 | bytes 14680064 | tf_op jit(solution)/shard_map/dot_general | solution.py:130
  123.2 11.6 %convolution_add_fusion = f32[1024,1024]{0,1:T(8,128)} fusion(f32[1024,1024]{0,1:T(8,128)} %fusion.27, bf16[1024,1024]{1,0:T(8,128)(2,1)S(1)} %copy-done.6, f32[1024,1024,1]{1,0,2:T(8,128)} %fusion.72, bf16[4,1024,256]{2,1,0:T(8,128)(2,1)} %bitcast.167, bf16[4,256,1024]{2,1,0:T(8,128)(2,1)} %bitcast.205), kind=kOutput, calls=%fused_computation.40 | convolution fusion | flops 4302307328 | bytes 18874368 | tf_op jit(solution)/shard_map/dot_general | solution.py:130
  134.8 2.9 %select_bitcast_fusion = f32[1024,2,256]{0,2,1:T(8,128)S(1)} fusion(f32[1024,2,2,256]{0,3,2,1:T(8,128)} %bitcast.158, pred[]{:T(512)S(6)} %eq.109), kind=kLoop, calls=%fused_computation.35 | loop fusion | flops 524288 | bytes 6291457 | tf_op jit(solution)/shard_map/jit(_where)/select_n | solution.py:56
  137.8 4.1 %collective-permute-done.9 = f32[1024,2,256]{0,2,1:T(8,128)S(1)} collective-permute-done((f32[1024,2,256]{0,2,1:T(8,128)S(1)}, f32[1024,2,256]{0,2,1:T(8,128)S(1)}, u32[]{:S(2)}, u32[]{:S(2)}) %collective-permute-start.9) | collective-permute-done | bytes 2097184 | tf_op jit(solution)/shard_map/ppermute | solution.py:13
  144.1 12.1 %collective-permute-done.10 = bf16[1024,1,256]{0,2,1:T(8,128)(2,1)S(1)} collective-permute-done((bf16[1024,1,256]{0,2,1:T(8,128)(2,1)S(1)}, bf16[1024,1,256]{0,2,1:T(8,128)(2,1)S(1)}, u32[]{:S(2)}, u32[]{:S(2)}) %collective-permute-start.10) | collective-permute-done | bytes 524320 | tf_op jit(solution)/shard_map/ppermute | solution.py:13
  159.8 4.1 %collective-permute-start.12 = (bf16[2,512,256]{2,1,0:T(8,128)(2,1)}, bf16[2,512,256]{2,1,0:T(8,128)(2,1)}, u32[]{:S(2)}, u32[]{:S(2)}) collective-permute-start(bf16[2,512,256]{2,1,0:T(8,128)(2,1)} %bitcast.49), channel_id=1, source_target_pairs={{0,31},{1,30},{2,29},{3,28},{4,27},{5,26},{6,25},{7,24},{8,23},{9,... | collective-permute-start | bytes 1572872 | tf_op jit(solution)/shard_map/ppermute | solution.py:8
  164.1 23.8 %collective-permute-done.11 = s32[2,512]{1,0:T(2,128)S(1)} collective-permute-done((s32[2,512]{1,0:T(2,128)S(1)}, s32[2,512]{1,0:T(2,128)S(1)}, u32[]{:S(2)}, u32[]{:S(2)}) %collective-permute-start.11) | collective-permute-done | bytes 4128 | tf_op jit(solution)/shard_map/ppermute | solution.py:8
  189.6 6.4 %add_convert_fusion = (bf16[2,512,256]{2,1,0:T(8,128)(2,1)}, bf16[2,512,256]{2,1,0:T(8,128)(2,1)}) fusion(bf16[2,512,256]{2,1,0:T(8,128)(2,1)} %collective-permute-done.12, bf16[2,512,256]{2,1,0:T(8,128)(2,1)} %param.14, f32[256]{0:T(256)S(1)} %bitcast.189, f32[256]{0:T(256)S(1)} %bitcast.185, f32[256]{0:T(256)S(1)} %bitcast.181, f32[256]{0:T(256)S(1)} %bitcast.177, ...), kind=kLoop, calls=%fused_computation.77 | loop fusion | flops 7077888 | bytes 3685376 | tf_op jit(solution)/shard_map/convert_element_type | solution.py:141
  (85 shorter events, 36.6 us)
Async XLA Ops:
  0.6 103.0 %copy-start = (bf16[1024,1024]{1,0:T(8,128)(2,1)S(1)}, bf16[1024,1024]{1,0:T(8,128)(2,1)}, u32[]{:S(2)}) copy-start(bf16[1024,1024]{1,0:T(8,128)(2,1)} %param.19) | copy-start | bytes 6291460
  0.6 25.3 %collective-permute-start.4 = (bf16[2,512,256]{2,1,0:T(8,128)(2,1)}, bf16[2,512,256]{2,1,0:T(8,128)(2,1)}, u32[]{:S(2)}, u32[]{:S(2)}) collective-permute-start(bf16[2,512,256]{2,1,0:T(8,128)(2,1)} %param.14), channel_id=1, source_target_pairs={{0,28},{4,24},{8,20},{12,16},{16,12},{20,8},{24,4},{28,0},{1,29},{... | collective-permute-start | bytes 1572872 | tf_op jit(solution)/shard_map/ppermute | solution.py:8
  8.4 24.0 %copy-start.5 = (bf16[2,512,256]{2,1,0:T(8,128)(2,1)S(1)}, bf16[2,512,256]{2,1,0:T(8,128)(2,1)}, u32[]{:S(2)}) copy-start(bf16[2,512,256]{2,1,0:T(8,128)(2,1)} %param.13) | copy-start | bytes 1572868
  11.3 29.8 %copy-start.14 = (f32[256]{0:T(256)S(1)}, f32[256]{0:T(256)}, u32[]{:S(2)}) copy-start(f32[256]{0:T(256)} %param.18) | copy-start | bytes 3076
  34.5 20.4 %copy-start.13 = (f32[256]{0:T(256)S(1)}, f32[256]{0:T(256)}, u32[]{:S(2)}) copy-start(f32[256]{0:T(256)} %param.17) | copy-start | bytes 3076
  43.5 11.3 %collective-permute-start.6 = (bf16[2,3,256]{2,1,0:T(4,128)(2,1)S(1)}, bf16[2,3,256]{2,1,0:T(4,128)(2,1)S(1)}, u32[]{:S(2)}, u32[]{:S(2)}) collective-permute-start(bf16[2,3,256]{2,1,0:T(4,128)(2,1)S(1)} %get-tuple-element.23), channel_id=1, source_target_pairs={{4,0},{8,4},{12,8},{16,12},{20,16},{24,20},{28,24},{5,1},{9,5},{13... | collective-permute-start | bytes 9224 | tf_op jit(solution)/shard_map/ppermute | solution.py:25
  46.5 8.3 %collective-permute-start.5 = (bf16[2,3,256]{2,1,0:T(4,128)(2,1)S(1)}, bf16[2,3,256]{2,1,0:T(4,128)(2,1)S(1)}, u32[]{:S(2)}, u32[]{:S(2)}) collective-permute-start(bf16[2,3,256]{2,1,0:T(4,128)(2,1)S(1)} %get-tuple-element.22), channel_id=1, source_target_pairs={{0,4},{4,8},{8,12},{12,16},{16,20},{20,24},{24,28},{1,5},{5,9},{9,... | collective-permute-start | bytes 9224 | tf_op jit(solution)/shard_map/ppermute | solution.py:23
  48.8 8.3 %collective-permute-start.1 = (bf16[2,3,256]{2,1,0:T(4,128)(2,1)S(1)}, bf16[2,3,256]{2,1,0:T(4,128)(2,1)S(1)}, u32[]{:S(2)}, u32[]{:S(2)}) collective-permute-start(bf16[2,3,256]{2,1,0:T(4,128)(2,1)S(1)} %get-tuple-element.25), channel_id=1, source_target_pairs={{4,0},{8,4},{12,8},{16,12},{20,16},{24,20},{28,24},{5,1},{9,5},{13... | collective-permute-start | bytes 9224 | tf_op jit(solution)/shard_map/ppermute | solution.py:25
  52.7 5.3 %collective-permute-start = (bf16[2,3,256]{2,1,0:T(4,128)(2,1)S(1)}, bf16[2,3,256]{2,1,0:T(4,128)(2,1)S(1)}, u32[]{:S(2)}, u32[]{:S(2)}) collective-permute-start(bf16[2,3,256]{2,1,0:T(4,128)(2,1)S(1)} %get-tuple-element.24), channel_id=1, source_target_pairs={{0,4},{4,8},{8,12},{12,16},{16,20},{20,24},{24,28},{1,5},{5,9},{9,... | collective-permute-start | bytes 9224 | tf_op jit(solution)/shard_map/ppermute | solution.py:23
  55.8 11.8 %collective-permute-start.7 = (bf16[1,1024,256]{2,1,0:T(8,128)(2,1)S(1)}, bf16[1,1024,256]{2,1,0:T(8,128)(2,1)S(1)}, u32[]{:S(2)}, u32[]{:S(2)}) collective-permute-start(bf16[1,1024,256]{2,1,0:T(8,128)(2,1)S(1)} %bitcast.162), channel_id=1, source_target_pairs={{0,2},{1,3},{2,0},{3,1},{4,6},{5,7},{6,4},{7,5},{8,10},{9,11},{10,... | collective-permute-start | bytes 1572872 | tf_op jit(solution)/shard_map/ppermute | solution.py:13
  59.0 19.8 %collective-permute-start.2 = (bf16[1,1024,256]{2,1,0:T(8,128)(2,1)S(1)}, bf16[1,1024,256]{2,1,0:T(8,128)(2,1)S(1)}, u32[]{:S(2)}, u32[]{:S(2)}) collective-permute-start(bf16[1,1024,256]{2,1,0:T(8,128)(2,1)S(1)} %bitcast.164), channel_id=1, source_target_pairs={{0,2},{1,3},{2,0},{3,1},{4,6},{5,7},{6,4},{7,5},{8,10},{9,11},{10,... | collective-permute-start | bytes 1572872 | tf_op jit(solution)/shard_map/ppermute | solution.py:13
  67.7 11.2 %copy-start.3 = (bf16[1,1,1024,256]{3,2,1,0:T(8,128)(2,1)}, bf16[1,1,1024,256]{3,2,1,0:T(8,128)(2,1)S(1)}, u32[]{:S(2)}) copy-start(bf16[1,1,1024,256]{3,2,1,0:T(8,128)(2,1)S(1)} %get-tuple-element.18) | copy-start | bytes 1572868
  67.7 11.2 %copy-start.4 = (bf16[1,1,1024,256]{3,2,1,0:T(8,128)(2,1)}, bf16[1,1,1024,256]{3,2,1,0:T(8,128)(2,1)S(1)}, u32[]{:S(2)}) copy-start(bf16[1,1,1024,256]{3,2,1,0:T(8,128)(2,1)S(1)} %get-tuple-element.19) | copy-start | bytes 1572868
  68.8 30.4 %collective-permute-start.8 = (bf16[2,1024,256]{2,1,0:T(8,128)(2,1)}, bf16[2,1024,256]{2,1,0:T(8,128)(2,1)}, u32[]{:S(2)}, u32[]{:S(2)}) collective-permute-start(bf16[2,1024,256]{2,1,0:T(8,128)(2,1)} %maximum_bitcast_fusion.1), channel_id=1, source_target_pairs={{0,1},{1,0},{2,3},{3,2},{4,5},{5,4},{6,7},{7,6},{8,9},{9,8},{10,11... | collective-permute-start | bytes 3145736 | tf_op jit(solution)/shard_map/ppermute | solution.py:13
  80.0 21.2 %collective-permute-start.3 = (bf16[2,1024,256]{2,1,0:T(8,128)(2,1)}, bf16[2,1024,256]{2,1,0:T(8,128)(2,1)}, u32[]{:S(2)}, u32[]{:S(2)}) collective-permute-start(bf16[2,1024,256]{2,1,0:T(8,128)(2,1)} %maximum_bitcast_fusion), channel_id=1, source_target_pairs={{0,1},{1,0},{2,3},{3,2},{4,5},{5,4},{6,7},{7,6},{8,9},{9,8},{10,11... | collective-permute-start | bytes 3145736 | tf_op jit(solution)/shard_map/ppermute | solution.py:13
  101.2 6.8 %copy-start.7 = (bf16[2,2,1024,256]{3,2,1,0:T(8,128)(2,1)}, bf16[2,2,1024,256]{3,2,1,0:T(8,128)(2,1)S(1)}, u32[]{:S(2)}) copy-start(bf16[2,2,1024,256]{3,2,1,0:T(8,128)(2,1)S(1)} %copy.41) | copy-start | bytes 6291460
  103.6 4.4 %copy-start.8 = (bf16[2,2,1024,256]{3,2,1,0:T(8,128)(2,1)}, bf16[2,2,1024,256]{3,2,1,0:T(8,128)(2,1)S(1)}, u32[]{:S(2)}) copy-start(bf16[2,2,1024,256]{3,2,1,0:T(8,128)(2,1)S(1)} %pad_maximum_fusion) | copy-start | bytes 6291460
  112.3 10.9 %copy-start.6 = (bf16[1024,1024]{1,0:T(8,128)(2,1)S(1)}, bf16[1024,1024]{1,0:T(8,128)(2,1)}, u32[]{:S(2)}) copy-start(bf16[1024,1024]{1,0:T(8,128)(2,1)} %reshape.155) | copy-start | bytes 6291460
  134.8 7.2 %copy-start.2 = (f32[1024,1024]{0,1:T(8,128)S(1)}, f32[1024,1024]{0,1:T(8,128)}, u32[]{:S(2)}) copy-start(f32[1024,1024]{0,1:T(8,128)} %convolution_add_fusion) | copy-start | bytes 12582916
  137.7 4.2 %collective-permute-start.9 = (f32[1024,2,256]{0,2,1:T(8,128)S(1)}, f32[1024,2,256]{0,2,1:T(8,128)S(1)}, u32[]{:S(2)}, u32[]{:S(2)}) collective-permute-start(f32[1024,2,256]{0,2,1:T(8,128)S(1)} %select_bitcast_fusion), channel_id=1, source_target_pairs={{0,1},{1,0},{2,3},{3,2},{4,5},{5,4},{6,7},{7,6},{8,9},{9,8},{10,11... | collective-permute-start | bytes 6291464 | tf_op jit(solution)/shard_map/ppermute | solution.py:13
  142.7 13.4 %collective-permute-start.10 = (bf16[1024,1,256]{0,2,1:T(8,128)(2,1)S(1)}, bf16[1024,1,256]{0,2,1:T(8,128)(2,1)S(1)}, u32[]{:S(2)}, u32[]{:S(2)}) collective-permute-start(bf16[1024,1,256]{0,2,1:T(8,128)(2,1)S(1)} %fusion.47), channel_id=1, source_target_pairs={{0,2},{1,3},{2,0},{3,1},{4,6},{5,7},{6,4},{7,5},{8,10},{9,11},{10,... | collective-permute-start | bytes 1572872 | tf_op jit(solution)/shard_map/ppermute | solution.py:13
  159.8 29.7 %collective-permute-start.12 = (bf16[2,512,256]{2,1,0:T(8,128)(2,1)}, bf16[2,512,256]{2,1,0:T(8,128)(2,1)}, u32[]{:S(2)}, u32[]{:S(2)}) collective-permute-start(bf16[2,512,256]{2,1,0:T(8,128)(2,1)} %bitcast.49), channel_id=1, source_target_pairs={{0,31},{1,30},{2,29},{3,28},{4,27},{5,26},{6,25},{7,24},{8,23},{9,... | collective-permute-start | bytes 1572872 | tf_op jit(solution)/shard_map/ppermute | solution.py:8
  163.9 23.9 %collective-permute-start.11 = (s32[2,512]{1,0:T(2,128)S(1)}, s32[2,512]{1,0:T(2,128)S(1)}, u32[]{:S(2)}, u32[]{:S(2)}) collective-permute-start(s32[2,512]{1,0:T(2,128)S(1)} %get-tuple-element.34), channel_id=1, source_target_pairs={{0,28},{4,24},{8,20},{12,16},{16,12},{20,8},{24,4},{28,0},{1,29},{... | collective-permute-start | bytes 12296 | tf_op jit(solution)/shard_map/ppermute | solution.py:8
  188.2 7.7 %copy-start.1 = (bf16[1024,1024]{1,0:T(8,128)(2,1)S(1)}, bf16[1024,1024]{1,0:T(8,128)(2,1)}, u32[]{:S(2)}) copy-start(bf16[1024,1024]{1,0:T(8,128)(2,1)} %param.19) | copy-start | bytes 6291460
  (4 other events, 9.0 us)

commit v2 on v1

--- a/solution.py
+++ b/solution.py
@@ -87,8 +87,15 @@
     table = embed_table.astype(jnp.float32)
     base_in = jnp.where(masked == 1, 4, tokens)
     comp = jnp.where(masked == 1, 4, 3 - tokens)
-    rev_here = jnp.flip(mirror(hidden_reverse, "seq", seq_count), axis=1)
+    arrived = mirror(hidden_reverse, "seq", seq_count)
     comp_back = jnp.flip(mirror(comp, "seq", seq_count), axis=1)
+    x_rev = hidden_reverse.astype(jnp.float32) + embedded(comp_back, table)
+    arrived, x_rev = lax.optimization_barrier((arrived, x_rev))
+    span = arrived.shape[1]
+    rows_all = arrived.shape[0] * span
+    rev_here = jnp.dot(
+        reversal(rows_all, span), arrived.reshape(rows_all, -1), preferred_element_type=jnp.float32
+    ).astype(jnp.bfloat16).reshape(arrived.shape)
 
     local_width = hidden_forward.shape[-1]
     width = local_width * ch_count
@@ -122,11 +129,7 @@
     act_fwd = activation(rows_fwd)
     act_rev = activation(rows_rev)
     lane_flip = reversal(local_width, local_width)
-    blocks = w_out.reshape(w_out.shape[0], ch_count, local_width)
-    w_flip = jnp.concatenate([blocks[:, k] for k in reversed(range(ch_count))], axis=1)
-    w_flip = jnp.dot(
-        w_flip.reshape(-1, local_width), lane_flip, preferred_element_type=jnp.float32
-    ).astype(jnp.bfloat16).reshape(w_out.shape)
+    w_flip = jnp.dot(w_out, reversal(width, width), preferred_element_type=jnp.float32).astype(jnp.bfloat16)
     part = jnp.dot(act_fwd, w_out, preferred_element_type=jnp.float32) + jnp.dot(
         act_rev, w_flip, preferred_element_type=jnp.float32
     )
@@ -136,7 +139,6 @@
     turned = jnp.dot(share.astype(jnp.bfloat16), lane_flip, preferred_element_type=jnp.float32)
     turned = jnp.dot(row_flip, turned.astype(jnp.bfloat16), preferred_element_type=jnp.float32)
     sent = mirror(turned.astype(jnp.bfloat16).reshape(x_fwd.shape), ("seq", "ch"), seq_count * ch_count)
-    x_rev = hidden_reverse.astype(jnp.float32) + embedded(comp_back, table)
     out_reverse = x_rev + sent.astype(jnp.float32)
     return (out_forward.astype(jnp.bfloat16), out_reverse.astype(jnp.bfloat16))
 

time: 198 us -> 178 us (0.90)
  local copies, waits for them, and re-layouts: 29.7 us -> 4.61 us
  other arithmetic: 25.7 us -> 28.6 us
  starting transfers between devices: 28.1 us -> 30.5 us
    reshape x2 -> x0, local copies, waits for them, and re-layouts: 8.74 us -> none  [the longest x1 4.37 us: local(): w_flip = jnp.dot(w_flip.reshape(-1, local_width), lane_flip, preferred_el...]
    dot_general x1 -> x3, matrix products: 3.88 us -> 11.4 us  [the longest x1 4.64 us: local(): jnp.dot(w_out, reversal(width, width), preferred_element_type=jnp.float32)]
    dot_general x1, matrix products: 11.6 us -> 4.62 us  [local(): jnp.dot(act_rev, w_flip, preferred_element_type=jnp.float32)]
    rev x1 -> x0, local copies, waits for them, and re-layouts: 6.35 us -> none  [local(): rev_here = jnp.flip(mirror(hidden_reverse, 'seq', seq_count), axis=1)]
    concatenate x1 -> x0, local copies, waits for them, and re-layouts: 3.96 us -> none  [local(): jnp.concatenate([blocks[:, k] for k in reversed(range(ch_count))], axis=1)]
    reduce_sum x1, other arithmetic: 2.12 us -> 6.05 us  [conv_rows(): square = lax.psum(jnp.sum(x * x, axis=-1), 'ch')]
    unnamed x31 -> x26, local copies, waits for them, and re-layouts: 4.04 us -> 0.85 us
    squeeze x1 -> x0, local copies, waits for them, and re-layouts: 2.92 us -> none  [local(): blocks[:, k]]
  transfers between devices with their start and end apart: 13 -> 13, of which waited for: 7 -> 7; matrix products, arithmetic and copies ran while one was open for 18% -> 16% of each run, Pallas kernels for 0% -> 0%
where the time goes in v2:
time: 178 us; the launch traced here: 177 us
  waiting for transfers between devices  67.6 us (38%)
  matrix products  38.1 us (21%)
  starting transfers between devices  30.5 us (17%)
  other arithmetic  28.6 us (16%)
  blocking collectives  6.59 us (4%)
  local copies, waits for them, and re-layouts  4.61 us (3%)
    ppermute x3, waiting for transfers between devices, mirror(): return lax.ppermute(value, axes, [(k, count - 1 - k) for k in range(count)])  38.8 us
    ppermute x6, waiting for transfers between devices, partner(): lax.ppermute(value, axis, [(k, k ^ mask) for k in range(lax.axis_size(axi...  28.2 us
    ppermute x6, starting transfers between devices, partner(): lax.ppermute(value, axis, [(k, k ^ mask) for k in range(lax.axis_size(axi...  12.2 us
    dot_general x1, matrix products, local(): jnp.dot(act_fwd, w_out, preferred_element_type=jnp.float32)  12 us
    ppermute x2, starting transfers between devices, padded_2(): lax.ppermute(head, axis, [((i + 1) % count, i) for i in range(ends)])  6.91 us
    ppermute x3, starting transfers between devices, mirror(): return lax.ppermute(value, axes, [(k, count - 1 - k) for k in range(count)])  6.82 us
    dot_general x2, matrix products, activation(): lax.dot_general(pieces, w_gate.reshape(ch_count, local_width, -1), dims,...  6.66 us
    psum x1, blocking collectives, conv_rows(): square = lax.psum(jnp.sum(x * x, axis=-1), 'ch')  6.59 us
  transfers between devices with their start and end apart: 13, of which 7 were waited for; matrix products, arithmetic and copies ran while one was open for 16% of the time, Pallas kernels for 0%

profile of v2, /device:TPU:17, one launch (start us, length us, event | category | flops | bytes accessed | tf_op | source)
XLA Modules:
  0.0 177.0 jit_solution(3227596268245179730)
XLA Ops:
  5.9 20.2 %collective-permute-done.5 = s32[2,512]{1,0:T(2,128)S(1)} collective-permute-done((s32[2,512]{1,0:T(2,128)S(1)}, s32[2,512]{1,0:T(2,128)S(1)}, u32[]{:S(2)}, u32[]{:S(2)}) %collective-permute-start.5) | collective-permute-done | bytes 4128 | tf_op jit(solution)/shard_map/ppermute | solution.py:8
  26.4 6.0 %multiply_reduce_fusion.1 = (f32[2,512]{1,0:T(2,128)S(1)}, f32[2,512,256]{2,1,0:T(8,128)}) fusion(f32[256]{0:T(256)S(1)} %bitcast.185, pred[2,512]{1,0:T(4,128)(4,1)S(1)} %get-tuple-element.55, f32[256]{0:T(256)S(1)} %bitcast.180, pred[2,512]{1,0:T(4,128)(4,1)S(1)} %get-tuple-element.57, f32[256]{0:T(256)S(1)} %bitcast.175, ...), kind=kLoop, calls=%fused_computation.93 | loop fusion | flops 6290432 | bytes 2116608 | tf_op jit(solution)/shard_map/reduce_sum | solution.py:107
  33.3 4.1 %multiply_reduce_fusion = (f32[1024]{0:T(1024)S(1)}, f32[1024,256]{1,0:T(8,128)}) fusion(f32[256]{0:T(256)S(1)} %bitcast.186, f32[256]{0:T(256)S(1)} %bitcast.181, f32[256]{0:T(256)S(1)} %bitcast.176, f32[256]{0:T(256)S(1)} %bitcast.171, f32[256]{0:T(256)S(1)} %bitcast.166, pred[1024]{0:T(1024)(128)(4,1)S(1)} %broadcast_in_dim.215, ...), kind=kOutput, calls=%fused_computation.88 | convolution fusion | flops 548928512 | bytes 1605632 | tf_op jit(solution)/shard_map/dot_general | solution.py:96
  37.4 6.6 %all-reduce = (f32[2,512]{1,0:T(2,128)S(1)}, f32[2,512]{1,0:T(2,128)S(1)}) all-reduce(f32[2,512]{1,0:T(2,128)S(1)} %reduce_sum.22, f32[2,512]{1,0:T(2,128)S(1)} %get-tuple-element.33), channel_id=1, replica_groups=mesh['seq'=8,'ch'=4] {'ch'}, use_global_device_ids=true, to_apply=%region_3.4 | all-reduce | flops 2048 | bytes 16384 | tf_op jit(solution)/shard_map/psum | solution.py:107
  44.0 2.8 %multiply_convert_fusion = bf16[2,512,256]{2,1,0:T(8,128)(2,1)S(1)} fusion(f32[2,512,256]{2,1,0:T(8,128)} %bitcast.164, f32[2,512]{1,0:T(2,128)S(1)} %add_rsqrt_fusion, f32[256]{0:T(256)S(1)} %copy-done.8, f32[256]{0:T(256)S(1)} %bitcast.187, f32[256]{0:T(256)S(1)} %bitcast.182, f32[256]{0:T(256)S(1)} %bitcast.177, f32[256]{0:T(256)S(1)} %bitcast.172, ...), kind=kLoop, calls=%fused_computation.87 | loop fusion | flops 3407872 | bytes 1588224 | tf_op jit(solution)/shard_map/convert_element_type | solution.py:108
  46.9 3.0 %collective-permute-start.7 = (bf16[2,3,256]{2,1,0:T(4,128)(2,1)S(1)}, bf16[2,3,256]{2,1,0:T(4,128)(2,1)S(1)}, u32[]{:S(2)}, u32[]{:S(2)}) collective-permute-start(bf16[2,3,256]{2,1,0:T(4,128)(2,1)S(1)} %get-tuple-element.23), channel_id=1, source_target_pairs={{4,0},{8,4},{12,8},{16,12},{20,16},{24,20},{28,24},{5,1},{9,5},{13... | collective-permute-start | bytes 9224 | tf_op jit(solution)/shard_map/ppermute | solution.py:25
  53.3 3.9 %collective-permute-start.1 = (bf16[2,3,256]{2,1,0:T(4,128)(2,1)S(1)}, bf16[2,3,256]{2,1,0:T(4,128)(2,1)S(1)}, u32[]{:S(2)}, u32[]{:S(2)}) collective-permute-start(bf16[2,3,256]{2,1,0:T(4,128)(2,1)S(1)} %get-tuple-element.21), channel_id=1, source_target_pairs={{4,0},{8,4},{12,8},{16,12},{20,16},{24,20},{28,24},{5,1},{9,5},{13... | collective-permute-start | bytes 9224 | tf_op jit(solution)/shard_map/ppermute | solution.py:25
  64.9 7.5 %collective-permute-done.8 = bf16[1,1024,256]{2,1,0:T(8,128)(2,1)S(1)} collective-permute-done((bf16[1,1024,256]{2,1,0:T(8,128)(2,1)S(1)}, bf16[1,1024,256]{2,1,0:T(8,128)(2,1)S(1)}, u32[]{:S(2)}, u32[]{:S(2)}) %collective-permute-start.8) | collective-permute-done | bytes 524320 | tf_op jit(solution)/shard_map/ppermute | solution.py:13
  73.7 4.8 %collective-permute-start.9 = (bf16[2,1024,256]{2,1,0:T(8,128)(2,1)}, bf16[2,1024,256]{2,1,0:T(8,128)(2,1)}, u32[]{:S(2)}, u32[]{:S(2)}) collective-permute-start(bf16[2,1024,256]{2,1,0:T(8,128)(2,1)} %maximum_bitcast_fusion.1), channel_id=1, source_target_pairs={{0,1},{1,0},{2,3},{3,2},{4,5},{5,4},{6,7},{7,6},{8,9},{9,8},{10,11... | collective-permute-start | bytes 3145736 | tf_op jit(solution)/shard_map/ppermute | solution.py:13
  78.5 5.1 %collective-permute-done.2 = bf16[1,1024,256]{2,1,0:T(8,128)(2,1)S(1)} collective-permute-done((bf16[1,1024,256]{2,1,0:T(8,128)(2,1)S(1)}, bf16[1,1024,256]{2,1,0:T(8,128)(2,1)S(1)}, u32[]{:S(2)}, u32[]{:S(2)}) %collective-permute-start.2) | collective-permute-done | bytes 524320 | tf_op jit(solution)/shard_map/ppermute | solution.py:13
  84.7 2.6 %collective-permute-start.3 = (bf16[2,1024,256]{2,1,0:T(8,128)(2,1)}, bf16[2,1024,256]{2,1,0:T(8,128)(2,1)}, u32[]{:S(2)}, u32[]{:S(2)}) collective-permute-start(bf16[2,1024,256]{2,1,0:T(8,128)(2,1)} %maximum_bitcast_fusion), channel_id=1, source_target_pairs={{0,1},{1,0},{2,3},{3,2},{4,5},{5,4},{6,7},{7,6},{8,9},{9,8},{10,11... | collective-permute-start | bytes 3145736 | tf_op jit(solution)/shard_map/ppermute | solution.py:13
  87.3 4.6 %fusion.142 = bf16[1024,1024]{1,0:T(8,128)(2,1)} fusion(bf16[1024,1024]{1,0:T(8,128)(2,1)S(1)} %copy-done.10, s32[1024]{0:T(1024)S(1)} %get-tuple-element.66, s32[1024]{0:T(1024)S(1)} %get-tuple-element.67, s32[1024]{0:T(1024)S(1)} %get-tuple-element.65, s32[1024]{0:T(1024)S(1)} %get-tuple-element.68, pred[1024]{0:T(1024)(128)(4,1)S(1)} %get-tuple-element.69, ...), kind=kOutput, calls=%fused_computation.30.clone.1 | convolution fusion | flops 2157969408 | bytes 4212736 | tf_op jit(solution)/shard_map/dot_general | solution.py:132
  94.0 2.3 %fusion.111 = f32[1024,1024,1]{1,0,2:T(8,128)S(1)} fusion(bf16[4,1024,256]{2,1,0:T(8,128)(2,1)S(1)} %bitcast.160, bf16[4,256,1024]{2,1,0:T(8,128)(2,1)S(1)} %bitcast.152), kind=kOutput, calls=%fused_computation.174 | convolution fusion | flops 2147483648 | bytes 8388608 | tf_op jit(solution)/shard_map/dot_general | solution.py:119
  97.9 4.3 %fusion.110 = f32[1024,1024,1]{1,0,2:T(8,128)} fusion(bf16[4,1024,256]{2,1,0:T(8,128)(2,1)S(1)} %bitcast.162, bf16[4,256,1024]{2,1,0:T(8,128)(2,1)S(1)} %bitcast.151), kind=kOutput, calls=%fused_computation.173 | convolution fusion | flops 2147483648 | bytes 8388608 | tf_op jit(solution)/shard_map/dot_general | solution.py:119
  102.3 2.7 %fusion = bf16[1024,1024]{1,0:T(8,128)(2,1)S(1)} fusion(f32[1024,1024,1]{1,0,2:T(8,128)S(1)} %fusion.111, bf16[4,1024,256]{2,1,0:T(8,128)(2,1)S(1)} %bitcast.161, bf16[4,256,1024]{2,1,0:T(8,128)(2,1)S(1)} %bitcast.205), kind=kOutput, calls=%fused_computation.1 | convolution fusion | flops 2153775104 | bytes 10485760 | tf_op jit(solution)/shard_map/dot_general | solution.py:122
  105.0 4.6 %fusion.16 = f32[1024,1024]{0,1:T(8,128)} fusion(bf16[1024,1024]{1,0:T(8,128)(2,1)S(1)} %fusion, bf16[1024,1024]{1,0:T(8,128)(2,1)S(1)} %copy-done.12), kind=kOutput, calls=%fused_computation.29 | convolution fusion | flops 2147483648 | bytes 8388608 | tf_op jit(solution)/shard_map/dot_general | solution.py:133
  109.6 12.0 %convolution_add_fusion = f32[1024,1024]{0,1:T(8,128)} fusion(f32[1024,1024]{0,1:T(8,128)} %fusion.16, bf16[1024,1024]{1,0:T(8,128)(2,1)} %param.21, f32[1024,1024,1]{1,0,2:T(8,128)} %fusion.110, bf16[4,1024,256]{2,1,0:T(8,128)(2,1)} %bitcast.163, bf16[4,256,1024]{2,1,0:T(8,128)(2,1)} %bitcast.204), kind=kOutput, calls=%fused_computation.44 | convolution fusion | flops 4302307328 | bytes 18874368 | tf_op jit(solution)/shard_map/dot_general | solution.py:133
  121.6 2.8 %select_bitcast_fusion = f32[1024,2,256]{0,2,1:T(8,128)S(1)} fusion(f32[1024,2,2,256]{0,3,2,1:T(8,128)} %bitcast.153, pred[]{:T(512)S(6)} %eq.121), kind=kLoop, calls=%fused_computation.28 | loop fusion | flops 524288 | bytes 6291457 | tf_op jit(solution)/shard_map/jit(_where)/select_n | solution.py:56
  125.2 3.8 %collective-permute-done.10 = f32[1024,2,256]{0,2,1:T(8,128)S(1)} collective-permute-done((f32[1024,2,256]{0,2,1:T(8,128)S(1)}, f32[1024,2,256]{0,2,1:T(8,128)S(1)}, u32[]{:S(2)}, u32[]{:S(2)}) %collective-permute-start.10) | collective-permute-done | bytes 2097184 | tf_op jit(solution)/shard_map/ppermute | solution.py:13
  131.3 11.8 %collective-permute-done.11 = bf16[1024,1,256]{0,2,1:T(8,128)(2,1)S(1)} collective-permute-done((bf16[1024,1,256]{0,2,1:T(8,128)(2,1)S(1)}, bf16[1024,1,256]{0,2,1:T(8,128)(2,1)S(1)}, u32[]{:S(2)}, u32[]{:S(2)}) %collective-permute-start.11) | collective-permute-done | bytes 524320 | tf_op jit(solution)/shard_map/ppermute | solution.py:13
  144.0 2.8 %convolution_convert_fusion = bf16[1024,256]{1,0:T(8,128)(2,1)} fusion(s32[1024]{0:T(1024)S(1)} %get-tuple-element.60, s32[1024]{0:T(1024)S(1)} %get-tuple-element.61, s32[1024]{0:T(1024)S(1)} %get-tuple-element.59, s32[1024]{0:T(1024)S(1)} %get-tuple-element.62, pred[1024]{0:T(1024)(128)(4,1)S(1)} %get-tuple-element.63, ...), kind=kOutput, calls=%fused_computation.45 | convolution fusion | flops 545521664 | bytes 1067008 | tf_op jit(solution)/shard_map/dot_general | solution.py:140
  146.9 4.3 %collective-permute-start.12 = (bf16[2,512,256]{2,1,0:T(8,128)(2,1)}, bf16[2,512,256]{2,1,0:T(8,128)(2,1)}, u32[]{:S(2)}, u32[]{:S(2)}) collective-permute-start(bf16[2,512,256]{2,1,0:T(8,128)(2,1)} %bitcast.46), channel_id=1, source_target_pairs={{0,31},{1,30},{2,29},{3,28},{4,27},{5,26},{6,25},{7,24},{8,23},{9,... | collective-permute-start | bytes 1572872 | tf_op jit(solution)/shard_map/ppermute | solution.py:8
  152.5 3.9 %add_convert_fusion.1 = bf16[2,512,256]{2,1,0:T(8,128)(2,1)} fusion(f32[2,512,256]{2,1,0:T(8,128)} %bitcast.155, f32[256]{0:T(256)S(1)} %bitcast.189, pred[2,512]{1,0:T(4,128)(4,1)S(1)} %get-tuple-element.55, f32[256]{0:T(256)S(1)} %bitcast.184, pred[2,512]{1,0:T(4,128)(4,1)S(1)} %get-tuple-element.57, f32[256]{0:T(256)S(1)} %bitcast.179, ...), kind=kLoop, calls=%fused_computation.83 | loop fusion | flops 3407872 | bytes 2107392 | tf_op jit(solution)/shard_map/convert_element_type | solution.py:143
  156.4 18.6 %collective-permute-done.12 = bf16[2,512,256]{2,1,0:T(8,128)(2,1)} collective-permute-done((bf16[2,512,256]{2,1,0:T(8,128)(2,1)}, bf16[2,512,256]{2,1,0:T(8,128)(2,1)}, u32[]{:S(2)}, u32[]{:S(2)}) %collective-permute-start.12) | collective-permute-done | bytes 524320 | tf_op jit(solution)/shard_map/ppermute | solution.py:8
  (86 shorter events, 30.7 us)
Async XLA Ops:
  0.6 93.4 %copy-start = (bf16[1024,1024]{1,0:T(8,128)(2,1)S(1)}, bf16[1024,1024]{1,0:T(8,128)(2,1)}, u32[]{:S(2)}) copy-start(bf16[1024,1024]{1,0:T(8,128)(2,1)} %param.19) | copy-start | bytes 6291460
  0.6 31.8 %collective-permute-start.4 = (bf16[2,512,256]{2,1,0:T(8,128)(2,1)}, bf16[2,512,256]{2,1,0:T(8,128)(2,1)S(1)}, u32[]{:S(2)}, u32[]{:S(2)}) collective-permute-start(bf16[2,512,256]{2,1,0:T(8,128)(2,1)} %param.14), channel_id=1, source_target_pairs={{0,28},{4,24},{8,20},{12,16},{16,12},{20,8},{24,4},{28,0},{1,29},{... | collective-permute-start | bytes 1572872 | tf_op jit(solution)/shard_map/ppermute | solution.py:8
  2.5 23.5 %collective-permute-start.5 = (s32[2,512]{1,0:T(2,128)S(1)}, s32[2,512]{1,0:T(2,128)S(1)}, u32[]{:S(2)}, u32[]{:S(2)}) collective-permute-start(s32[2,512]{1,0:T(2,128)S(1)} %get-tuple-element.32), channel_id=1, source_target_pairs={{0,28},{4,24},{8,20},{12,16},{16,12},{20,8},{24,4},{28,0},{1,29},{... | collective-permute-start | bytes 12296 | tf_op jit(solution)/shard_map/ppermute | solution.py:8
  33.3 10.7 %copy-start.8 = (f32[256]{0:T(256)S(1)}, f32[256]{0:T(256)}, u32[]{:S(2)}) copy-start(f32[256]{0:T(256)} %param.18) | copy-start | bytes 3076
  33.3 18.9 %copy-start.4 = (bf16[2,512,256]{2,1,0:T(8,128)(2,1)S(1)}, bf16[2,512,256]{2,1,0:T(8,128)(2,1)}, u32[]{:S(2)}) copy-start(bf16[2,512,256]{2,1,0:T(8,128)(2,1)} %param.13) | copy-start | bytes 1572868
  44.0 15.6 %copy-start.7 = (f32[256]{0:T(256)S(1)}, f32[256]{0:T(256)}, u32[]{:S(2)}) copy-start(f32[256]{0:T(256)} %param.17) | copy-start | bytes 3076
  46.9 12.6 %collective-permute-start.7 = (bf16[2,3,256]{2,1,0:T(4,128)(2,1)S(1)}, bf16[2,3,256]{2,1,0:T(4,128)(2,1)S(1)}, u32[]{:S(2)}, u32[]{:S(2)}) collective-permute-start(bf16[2,3,256]{2,1,0:T(4,128)(2,1)S(1)} %get-tuple-element.23), channel_id=1, source_target_pairs={{4,0},{8,4},{12,8},{16,12},{20,16},{24,20},{28,24},{5,1},{9,5},{13... | collective-permute-start | bytes 9224 | tf_op jit(solution)/shard_map/ppermute | solution.py:25
  49.9 9.6 %collective-permute-start.6 = (bf16[2,3,256]{2,1,0:T(4,128)(2,1)S(1)}, bf16[2,3,256]{2,1,0:T(4,128)(2,1)S(1)}, u32[]{:S(2)}, u32[]{:S(2)}) collective-permute-start(bf16[2,3,256]{2,1,0:T(4,128)(2,1)S(1)} %get-tuple-element.22), channel_id=1, source_target_pairs={{0,4},{4,8},{8,12},{12,16},{16,20},{20,24},{24,28},{1,5},{5,9},{9,... | collective-permute-start | bytes 9224 | tf_op jit(solution)/shard_map/ppermute | solution.py:23
  53.3 8.5 %collective-permute-start.1 = (bf16[2,3,256]{2,1,0:T(4,128)(2,1)S(1)}, bf16[2,3,256]{2,1,0:T(4,128)(2,1)S(1)}, u32[]{:S(2)}, u32[]{:S(2)}) collective-permute-start(bf16[2,3,256]{2,1,0:T(4,128)(2,1)S(1)} %get-tuple-element.21), channel_id=1, source_target_pairs={{4,0},{8,4},{12,8},{16,12},{20,16},{24,20},{28,24},{5,1},{9,5},{13... | collective-permute-start | bytes 9224 | tf_op jit(solution)/shard_map/ppermute | solution.py:25
  57.3 5.3 %collective-permute-start = (bf16[2,3,256]{2,1,0:T(4,128)(2,1)S(1)}, bf16[2,3,256]{2,1,0:T(4,128)(2,1)S(1)}, u32[]{:S(2)}, u32[]{:S(2)}) collective-permute-start(bf16[2,3,256]{2,1,0:T(4,128)(2,1)S(1)} %get-tuple-element.20), channel_id=1, source_target_pairs={{0,4},{4,8},{8,12},{12,16},{16,20},{20,24},{24,28},{1,5},{5,9},{9,... | collective-permute-start | bytes 9224 | tf_op jit(solution)/shard_map/ppermute | solution.py:23
  60.5 11.8 %collective-permute-start.8 = (bf16[1,1024,256]{2,1,0:T(8,128)(2,1)S(1)}, bf16[1,1024,256]{2,1,0:T(8,128)(2,1)S(1)}, u32[]{:S(2)}, u32[]{:S(2)}) collective-permute-start(bf16[1,1024,256]{2,1,0:T(8,128)(2,1)S(1)} %bitcast.156), channel_id=1, source_target_pairs={{0,2},{1,3},{2,0},{3,1},{4,6},{5,7},{6,4},{7,5},{8,10},{9,11},{10,... | collective-permute-start | bytes 1572872 | tf_op jit(solution)/shard_map/ppermute | solution.py:13
  63.5 20.0 %collective-permute-start.2 = (bf16[1,1024,256]{2,1,0:T(8,128)(2,1)S(1)}, bf16[1,1024,256]{2,1,0:T(8,128)(2,1)S(1)}, u32[]{:S(2)}, u32[]{:S(2)}) collective-permute-start(bf16[1,1024,256]{2,1,0:T(8,128)(2,1)S(1)} %bitcast.158), channel_id=1, source_target_pairs={{0,2},{1,3},{2,0},{3,1},{4,6},{5,7},{6,4},{7,5},{8,10},{9,11},{10,... | collective-permute-start | bytes 1572872 | tf_op jit(solution)/shard_map/ppermute | solution.py:13
  72.4 11.2 %copy-start.2 = (bf16[1,1,1024,256]{3,2,1,0:T(8,128)(2,1)}, bf16[1,1,1024,256]{3,2,1,0:T(8,128)(2,1)S(1)}, u32[]{:S(2)}) copy-start(bf16[1,1,1024,256]{3,2,1,0:T(8,128)(2,1)S(1)} %get-tuple-element.18) | copy-start | bytes 1572868
  72.4 11.2 %copy-start.3 = (bf16[1,1,1024,256]{3,2,1,0:T(8,128)(2,1)}, bf16[1,1,1024,256]{3,2,1,0:T(8,128)(2,1)S(1)}, u32[]{:S(2)}) copy-start(bf16[1,1,1024,256]{3,2,1,0:T(8,128)(2,1)S(1)} %get-tuple-element.19) | copy-start | bytes 1572868
  73.7 18.3 %collective-permute-start.9 = (bf16[2,1024,256]{2,1,0:T(8,128)(2,1)}, bf16[2,1024,256]{2,1,0:T(8,128)(2,1)}, u32[]{:S(2)}, u32[]{:S(2)}) collective-permute-start(bf16[2,1024,256]{2,1,0:T(8,128)(2,1)} %maximum_bitcast_fusion.1), channel_id=1, source_target_pairs={{0,1},{1,0},{2,3},{3,2},{4,5},{5,4},{6,7},{7,6},{8,9},{9,8},{10,11... | collective-permute-start | bytes 3145736 | tf_op jit(solution)/shard_map/ppermute | solution.py:13
  83.6 3.8 %copy-start.10 = (bf16[1024,1024]{1,0:T(8,128)(2,1)S(1)}, bf16[1024,1024]{1,0:T(8,128)(2,1)}, u32[]{:S(2)}) copy-start(bf16[1024,1024]{1,0:T(8,128)(2,1)} %param.21) | copy-start | bytes 6291460
  84.7 11.6 %collective-permute-start.3 = (bf16[2,1024,256]{2,1,0:T(8,128)(2,1)}, bf16[2,1024,256]{2,1,0:T(8,128)(2,1)}, u32[]{:S(2)}, u32[]{:S(2)}) collective-permute-start(bf16[2,1024,256]{2,1,0:T(8,128)(2,1)} %maximum_bitcast_fusion), channel_id=1, source_target_pairs={{0,1},{1,0},{2,3},{3,2},{4,5},{5,4},{6,7},{7,6},{8,9},{9,8},{10,11... | collective-permute-start | bytes 3145736 | tf_op jit(solution)/shard_map/ppermute | solution.py:13
  97.9 4.3 %copy-start.6 = (bf16[2,2,1024,256]{3,2,1,0:T(8,128)(2,1)}, bf16[2,2,1024,256]{3,2,1,0:T(8,128)(2,1)S(1)}, u32[]{:S(2)}) copy-start(bf16[2,2,1024,256]{3,2,1,0:T(8,128)(2,1)S(1)} %pad_maximum_fusion) | copy-start | bytes 6291460
  97.9 4.3 %copy-start.9 = (bf16[1024,1024]{1,0:T(8,128)(2,1)S(1)}, bf16[1024,1024]{1,0:T(8,128)(2,1)}, u32[]{:S(2)}) copy-start(bf16[1024,1024]{1,0:T(8,128)(2,1)} %param.20) | copy-start | bytes 6291460
  121.5 7.4 %copy-start.1 = (f32[1024,1024]{0,1:T(8,128)S(1)}, f32[1024,1024]{0,1:T(8,128)}, u32[]{:S(2)}) copy-start(f32[1024,1024]{0,1:T(8,128)} %convolution_add_fusion) | copy-start | bytes 12582916
  124.3 4.6 %collective-permute-start.10 = (f32[1024,2,256]{0,2,1:T(8,128)S(1)}, f32[1024,2,256]{0,2,1:T(8,128)S(1)}, u32[]{:S(2)}, u32[]{:S(2)}) collective-permute-start(f32[1024,2,256]{0,2,1:T(8,128)S(1)} %select_bitcast_fusion), channel_id=1, source_target_pairs={{0,1},{1,0},{2,3},{3,2},{4,5},{5,4},{6,7},{7,6},{8,9},{9,8},{10,11... | collective-permute-start | bytes 6291464 | tf_op jit(solution)/shard_map/ppermute | solution.py:13
  129.9 13.2 %collective-permute-start.11 = (bf16[1024,1,256]{0,2,1:T(8,128)(2,1)S(1)}, bf16[1024,1,256]{0,2,1:T(8,128)(2,1)S(1)}, u32[]{:S(2)}, u32[]{:S(2)}) collective-permute-start(bf16[1024,1,256]{0,2,1:T(8,128)(2,1)S(1)} %fusion.52), channel_id=1, source_target_pairs={{0,2},{1,3},{2,0},{3,1},{4,6},{5,7},{6,4},{7,5},{8,10},{9,11},{10,... | collective-permute-start | bytes 1572872 | tf_op jit(solution)/shard_map/ppermute | solution.py:13
  146.9 28.2 %collective-permute-start.12 = (bf16[2,512,256]{2,1,0:T(8,128)(2,1)}, bf16[2,512,256]{2,1,0:T(8,128)(2,1)}, u32[]{:S(2)}, u32[]{:S(2)}) collective-permute-start(bf16[2,512,256]{2,1,0:T(8,128)(2,1)} %bitcast.46), channel_id=1, source_target_pairs={{0,31},{1,30},{2,29},{3,28},{4,27},{5,26},{6,25},{7,24},{8,23},{9,... | collective-permute-start | bytes 1572872 | tf_op jit(solution)/shard_map/ppermute | solution.py:8
  152.5 22.5 %copy-start.5 = (f32[2,512,256]{2,1,0:T(8,128)S(1)}, f32[2,512,256]{2,1,0:T(8,128)}, u32[]{:S(2)}) copy-start(f32[2,512,256]{2,1,0:T(8,128)} %get-tuple-element.5) | copy-start | bytes 3145732
  (2 other events, 3.5 us)

commit v3 on v2

v3 whole, which is shorter than its diff:
```python
import jax
import jax.numpy as jnp
from jax import lax
from jax.sharding import PartitionSpec as P


def mirror(value, axes, count):
    return lax.ppermute(value, axes, [(k, count - 1 - k) for k in range(count)])


def partner(value, axis, bit):
    mask = 1 << bit
    return lax.ppermute(value, axis, [(k, k ^ mask) for k in range(lax.axis_size(axis))])


def padded_2(cells, axis, dim, width):
    count = lax.axis_size(axis)
    ends = count - 1
    head = lax.slice_in_dim(cells, 0, width, axis=dim)
    tail = lax.slice_in_dim(cells, cells.shape[dim] - width, cells.shape[dim], axis=dim)
    return jnp.concatenate(
        [
            lax.ppermute(tail, axis, [(i, (i + 1) % count) for i in range(ends)]),
            cells,
            lax.ppermute(head, axis, [((i + 1) % count, i) for i in range(ends)]),
        ],
        axis=dim,
    )


def embedded(bases, table):
    out = jnp.zeros(bases.shape + (table.shape[1],), jnp.float32)
    for v in range(table.shape[0]):
        out = out + jnp.where(bases[..., None] == v, table[v], 0.0)
    return out


def gather_blocks(block, bits, me):
    cur = block[None]
    for bit in reversed(range(bits)):
        other = partner(cur, "ch", bit)
        low = ((me >> bit) & 1) == 0
        first = jnp.where(low, cur, other)
        second = jnp.where(low, other, cur)
        cur = jnp.stack([first, second], axis=1).reshape((-1,) + block.shape)
    return cur


def scatter_blocks(part, bits, me):
    cur = part
    rows, _, w = part.shape
    for bit in range(bits):
        cur = cur.reshape(rows, -1, 2, w)
        low = ((me >> bit) & 1) == 0
        keep = jnp.where(low, cur[:, :, 0], cur[:, :, 1])
        give = jnp.where(low, cur[:, :, 1], cur[:, :, 0])
        if bit > 0:
            give = give.astype(jnp.bfloat16)
        cur = keep + partner(give, "ch", bit).astype(jnp.float32)
    return cur[:, 0]


def reversal(n, block):
    rows = lax.broadcasted_iota(jnp.int32, (n, n), 0)
    cols = lax.broadcasted_iota(jnp.int32, (n, n), 1)
    same = rows // block == cols // block
    return (same & (rows % block + cols % block == block - 1)).astype(jnp.bfloat16)


def chain(
    tokens,
    masked,
    hidden_forward,
    hidden_reverse,
    table,
    conv_kernel,
    conv_bias,
    norm_gain,
    w_gate,
    w_value,
    w_out,
    w_flip,
    after,
):
    seq_count = lax.axis_size("seq")
    ch_count = lax.axis_size("ch")
    ch_bits = ch_count.bit_length() - 1
    me = lax.axis_index("ch")
    base_in = jnp.where(masked == 1, 4, tokens)
    comp = jnp.where(masked == 1, 4, 3 - tokens)
    arrived = mirror(hidden_reverse, "seq", seq_count)
    comp_back = jnp.flip(mirror(comp, "seq", seq_count), axis=1)
    x_rev = hidden_reverse.astype(jnp.float32) + embedded(comp_back, table)
    arrived, x_rev = lax.optimization_barrier((arrived, x_rev))
    span = arrived.shape[1]
    rows_all = arrived.shape[0] * span
    rev_here = jnp.dot(
        reversal(rows_all, span), arrived.reshape(rows_all, -1), preferred_element_type=jnp.float32
    ).astype(jnp.bfloat16).reshape(arrived.shape)

    local_width = hidden_forward.shape[-1]
    width = local_width * ch_count
    taps = conv_kernel.shape[0]
    half_width = taps // 2

    def conv_rows(hidden, bases, kernel):
        x = hidden.astype(jnp.float32) + embedded(bases, table)
        own = jnp.sum(x * x, axis=-1)
        if after is not None:
            own, _ = lax.optimization_barrier((own, after))
        square = lax.psum(own, "ch")
        normed = (x * lax.rsqrt(square[..., None] / width + 1e-05) * norm_gain).astype(jnp.bfloat16)
        length = normed.shape[1]
        padded = padded_2(normed, "seq", 1, half_width).astype(jnp.float32)
        conv = jnp.zeros(normed.shape, jnp.float32) + conv_bias
        for offset in range(taps):
            conv = conv + kernel[offset] * padded[:, offset : offset + length]
        return x, conv.astype(jnp.bfloat16).reshape(-1, local_width), square

    def activation(rows):
        pieces = gather_blocks(rows, ch_bits, me)
        dims = (((0, 2), (0, 1)), ((), ()))
        gate = lax.dot_general(
            pieces, w_gate.reshape(ch_count, local_width, -1), dims, preferred_element_type=jnp.float32
        )
        value = lax.dot_general(
            pieces, w_value.reshape(ch_count, local_width, -1), dims, preferred_element_type=jnp.float32
        )
        return (jax.nn.silu(gate) * value).astype(jnp.bfloat16)

    x_fwd, rows_fwd, square = conv_rows(hidden_forward, base_in, conv_kernel)
    _, rows_rev, square_rev = conv_rows(rev_here, comp, conv_kernel[::-1])
    act_fwd = activation(rows_fwd)
    act_rev = activation(rows_rev)
    part = jnp.dot(act_fwd, w_out, preferred_element_type=jnp.float32) + jnp.dot(
        act_rev, w_flip, preferred_element_type=jnp.float32
    )
    share = scatter_blocks(part.reshape(part.shape[0], ch_count, local_width), ch_bits, me)
    out_forward = x_fwd + share.reshape(x_fwd.shape)
    row_flip = reversal(share.shape[0], x_fwd.shape[1])
    turned = jnp.dot(share.astype(jnp.bfloat16), reversal(local_width, local_width), preferred_element_type=jnp.float32)
    turned = jnp.dot(row_flip, turned.astype(jnp.bfloat16), preferred_element_type=jnp.float32)
    sent = mirror(turned.astype(jnp.bfloat16).reshape(x_fwd.shape), ("seq", "ch"), seq_count * ch_count)
    out_reverse = x_rev + sent.astype(jnp.float32)
    return (out_forward.astype(jnp.bfloat16), out_reverse.astype(jnp.bfloat16)), (square, square_rev)


def local(
    tokens,
    masked,
    hidden_forward,
    hidden_reverse,
    embed_table,
    conv_kernel,
    conv_bias,
    norm_gain,
    w_gate,
    w_value,
    w_out,
):
    width = w_out.shape[1]
    table = embed_table.astype(jnp.float32)
    w_flip = jnp.dot(w_out, reversal(width, width), preferred_element_type=jnp.float32).astype(jnp.bfloat16)
    outs = []
    after = None
    for s in range(tokens.shape[0]):
        pick = slice(s, s + 1)
        out, after = chain(
            tokens[pick],
            masked[pick],
            hidden_forward[pick],
            hidden_reverse[pick],
            table,
            conv_kernel,
            conv_bias,
            norm_gain,
            w_gate,
            w_value,
            w_out,
            w_flip,
            after,
        )
        outs.append(out)
    return tuple(jnp.concatenate([o[k] for o in outs]) for k in range(2))


def solution(mesh):
    placed = (
        P(None, "seq"),
        P(None, "seq"),
        P(None, "seq", "ch"),
        P(None, "seq", "ch"),
        P(None, "ch"),
        P(None, "ch"),
        P("ch"),
        P("ch"),
        P(None, "ch"),
        P(None, "ch"),
        P("ch", None),
    )
    return jax.shard_map(
        local,
        mesh=mesh,
        in_specs=placed,
        out_specs=(P(None, "seq", "ch"), P(None, "seq", "ch")),
        check_vma=False,
    )
```

time: 178 us -> 207 us (1.16)
  waiting for transfers between devices: 67.6 us -> 21.9 us
  starting transfers between devices: 30.5 us -> 59.2 us
  local copies, waits for them, and re-layouts: 4.61 us -> 25.4 us
  matrix products: 38.1 us -> 55.1 us
  blocking collectives: 6.59 us -> 13.4 us
    ppermute x6 -> x12, waiting for transfers between devices: 28.2 us -> 4.94 us  [partner(): lax.ppermute(value, axis, [(k, k ^ mask) for k in range(lax.axis_size(axi...]
    ppermute x3 -> x6, waiting for transfers between devices: 38.8 us -> 17 us  [mirror(): return lax.ppermute(value, axes, [(k, count - 1 - k) for k in range(count)])]
    dot_general x6 -> x8, matrix products: 26.8 us -> 38.6 us  [the longest x2 14.9 us: chain(): jnp.dot(act_rev, w_flip, preferred_element_type=jnp.float32)]
    ppermute x6 -> x12, starting transfers between devices: 12.2 us -> 23.5 us  [partner(): lax.ppermute(value, axis, [(k, k ^ mask) for k in range(lax.axis_size(axi...]
    slice x0 -> x3, local copies, waits for them, and re-layouts: none -> 8.98 us  [the longest x2 7.06 us: scatter_blocks(): keep = jnp.where(low, cur[:, :, 0], cur[:, :, 1])]
    ppermute x2 -> x4, starting transfers between devices: 6.91 us -> 14.2 us  [padded_2(): lax.ppermute(head, axis, [((i + 1) % count, i) for i in range(ends)])]
    psum x1 -> x2, blocking collectives: 6.59 us -> 13.4 us  [conv_rows(): square = lax.psum(own, 'ch')]
    unnamed x26 -> x48, local copies, waits for them, and re-layouts: 0.85 us -> 6.62 us
  transfers between devices with their start and end apart: 13 -> 26, of which waited for: 7 -> 5; matrix products, arithmetic and copies ran while one was open for 16% -> 49% of each run, Pallas kernels for 0% -> 0%
where the time goes in v3:
time: 207 us; the launch traced here: 206 us
  starting transfers between devices  59.2 us (29%)
  matrix products  55.1 us (27%)
  other arithmetic  29.2 us (14%)
  local copies, waits for them, and re-layouts  25.4 us (12%)
  waiting for transfers between devices  21.9 us (11%)
  blocking collectives  13.4 us (6%)
    ppermute x12, starting transfers between devices, partner(): lax.ppermute(value, axis, [(k, k ^ mask) for k in range(lax.axis_size(axi...  23.5 us
    ppermute x6, waiting for transfers between devices, mirror(): return lax.ppermute(value, axes, [(k, count - 1 - k) for k in range(count)])  17 us
    dot_general x2, matrix products, chain(): jnp.dot(act_rev, w_flip, preferred_element_type=jnp.float32)  14.9 us
    ppermute x4, starting transfers between devices, padded_2(): lax.ppermute(head, axis, [((i + 1) % count, i) for i in range(ends)])  14.2 us
    dot_general x2, matrix products, chain(): jnp.dot(act_fwd, w_out, preferred_element_type=jnp.float32)  13.4 us
    psum x2, blocking collectives, conv_rows(): square = lax.psum(own, 'ch')  13.4 us
    ppermute x6, starting transfers between devices, mirror(): return lax.ppermute(value, axes, [(k, count - 1 - k) for k in range(count)])  12 us
    dot_general x4, matrix products, activation(): lax.dot_general(pieces, w_gate.reshape(ch_count, local_width, -1), dims,...  10.3 us
  transfers between devices with their start and end apart: 26, of which 5 were waited for; matrix products, arithmetic and copies ran while one was open for 49% of the time, Pallas kernels for 0%

profile of v3, /device:TPU:17, one launch (start us, length us, event | category | flops | bytes accessed | tf_op | source)
XLA Modules:
  0.0 205.6 jit_solution(2033050565371690695)
XLA Ops:
  11.5 6.2 %fusion.33 = bf16[1024,1024]{1,0:T(8,128)(2,1)} fusion(bf16[1024,1024]{1,0:T(8,128)(2,1)} %param.21, s32[1024]{0:T(1024)S(1)} %get-tuple-element.122, s32[1024]{0:T(1024)S(1)} %get-tuple-element.123, s32[1024]{0:T(1024)S(1)} %get-tuple-element.121, s32[1024]{0:T(1024)S(1)} %get-tuple-element.124, pred[1024]{0:T(1024)(128)(4,1)S(1)} %get-tuple-element.125, ...), kind=kOutput, calls=%fused_computation.46 | convolution fusion | flops 2157969408 | bytes 4212736 | tf_op jit(solution)/shard_map/dot_general | solution.py:163
  27.3 7.6 %all-reduce.1 = (f32[1,512]{1,0:T(1,128)S(1)}, f32[1,512]{1,0:T(1,128)S(1)}) all-reduce(f32[1,512]{1,0:T(1,128)S(1)} %bitcast.368, f32[1,512]{1,0:T(1,128)S(1)} %bitcast.373), channel_id=1, replica_groups=mesh['seq'=8,'ch'=4] {'ch'}, use_global_device_ids=true, to_apply=%region_1.2 | all-reduce | flops 1024 | bytes 8192 | tf_op jit(solution)/shard_map/psum | solution.py:111
  35.0 3.0 %multiply_reduce_fusion = (f32[512]{0:T(512)S(1)}, f32[512,256]{1,0:T(8,128)}) fusion(f32[256]{0:T(256)S(1)} %bitcast.362, pred[512]{0:T(512)(128)(4,1)S(1)} %copy-done.18, f32[256]{0:T(256)S(1)} %bitcast.354, pred[512]{0:T(512)(128)(4,1)S(1)} %copy-done.19, f32[256]{0:T(256)S(1)} %bitcast.346, pred[512]{0:T(512)(128)(4,1)S(1)} %copy-done.20, ...), kind=kOutput, calls=%fused_computation.158 | convolution fusion | flops 138149376 | bytes 805376 | tf_op jit(solution)/shard_map/dot_general | solution.py:97
  38.0 5.7 %all-reduce = (f32[1,512]{1,0:T(1,128)S(1)}, f32[1,512]{1,0:T(1,128)S(1)}) all-reduce(f32[1,512]{1,0:T(1,128)S(1)} %bitcast.367, f32[1,512]{1,0:T(1,128)S(1)} %bitcast.374), channel_id=1, replica_groups=mesh['seq'=8,'ch'=4] {'ch'}, use_global_device_ids=true, to_apply=%region_5.6 | all-reduce | flops 1024 | bytes 8192 | tf_op jit(solution)/shard_map/psum | solution.py:111
  44.5 2.8 %collective-permute-start.13 = (bf16[1,3,256]{2,1,0:T(4,128)(2,1)S(1)}, bf16[1,3,256]{2,1,0:T(4,128)(2,1)S(1)}, u32[]{:S(2)}, u32[]{:S(2)}) collective-permute-start(bf16[1,3,256]{2,1,0:T(4,128)(2,1)S(1)} %get-tuple-element.83), channel_id=1, source_target_pairs={{4,0},{8,4},{12,8},{16,12},{20,16},{24,20},{28,24},{5,1},{9,5},{13... | collective-permute-start | bytes 4616 | tf_op jit(solution)/shard_map/ppermute | solution.py:25
  51.1 3.7 %collective-permute-start.19 = (bf16[1,3,256]{2,1,0:T(4,128)(2,1)S(1)}, bf16[1,3,256]{2,1,0:T(4,128)(2,1)S(1)}, u32[]{:S(2)}, u32[]{:S(2)}) collective-permute-start(bf16[1,3,256]{2,1,0:T(4,128)(2,1)S(1)} %get-tuple-element.81), channel_id=1, source_target_pairs={{4,0},{8,4},{12,8},{16,12},{20,16},{24,20},{28,24},{5,1},{9,5},{13... | collective-permute-start | bytes 4616 | tf_op jit(solution)/shard_map/ppermute | solution.py:25
  57.7 3.9 %collective-permute-start.1 = (bf16[1,3,256]{2,1,0:T(4,128)(2,1)S(1)}, bf16[1,3,256]{2,1,0:T(4,128)(2,1)S(1)}, u32[]{:S(2)}, u32[]{:S(2)}) collective-permute-start(bf16[1,3,256]{2,1,0:T(4,128)(2,1)S(1)} %get-tuple-element.79), channel_id=1, source_target_pairs={{4,0},{8,4},{12,8},{16,12},{20,16},{24,20},{28,24},{5,1},{9,5},{13... | collective-permute-start | bytes 4616 | tf_op jit(solution)/shard_map/ppermute | solution.py:25
  64.0 3.9 %collective-permute-start.7 = (bf16[1,3,256]{2,1,0:T(4,128)(2,1)S(1)}, bf16[1,3,256]{2,1,0:T(4,128)(2,1)S(1)}, u32[]{:S(2)}, u32[]{:S(2)}) collective-permute-start(bf16[1,3,256]{2,1,0:T(4,128)(2,1)S(1)} %get-tuple-element.77), channel_id=1, source_target_pairs={{4,0},{8,4},{12,8},{16,12},{20,16},{24,20},{28,24},{5,1},{9,5},{13... | collective-permute-start | bytes 4616 | tf_op jit(solution)/shard_map/ppermute | solution.py:25
  76.8 7.5 %collective-permute-start.15 = (bf16[2,512,256]{2,1,0:T(8,128)(2,1)S(1)}, bf16[2,512,256]{2,1,0:T(8,128)(2,1)S(1)}, u32[]{:S(2)}, u32[]{:S(2)}) collective-permute-start(bf16[2,512,256]{2,1,0:T(8,128)(2,1)S(1)} %maximum_bitcast_fusion.2), channel_id=1, source_target_pairs={{0,1},{1,0},{2,3},{3,2},{4,5},{5,4},{6,7},{7,6},{8,9},{9,8},{10,11... | collective-permute-start | bytes 1572872 | tf_op jit(solution)/shard_map/ppermute | solution.py:13
  84.8 5.0 %collective-permute-start.21 = (bf16[2,512,256]{2,1,0:T(8,128)(2,1)S(1)}, bf16[2,512,256]{2,1,0:T(8,128)(2,1)S(1)}, u32[]{:S(2)}, u32[]{:S(2)}) collective-permute-start(bf16[2,512,256]{2,1,0:T(8,128)(2,1)S(1)} %maximum_bitcast_fusion.3), channel_id=1, source_target_pairs={{0,1},{1,0},{2,3},{3,2},{4,5},{5,4},{6,7},{7,6},{8,9},{9,8},{10,11... | collective-permute-start | bytes 1572872 | tf_op jit(solution)/shard_map/ppermute | solution.py:13
  91.4 3.8 %collective-permute-start.3 = (bf16[2,512,256]{2,1,0:T(8,128)(2,1)}, bf16[2,512,256]{2,1,0:T(8,128)(2,1)}, u32[]{:S(2)}, u32[]{:S(2)}) collective-permute-start(bf16[2,512,256]{2,1,0:T(8,128)(2,1)} %maximum_bitcast_fusion), channel_id=1, source_target_pairs={{0,1},{1,0},{2,3},{3,2},{4,5},{5,4},{6,7},{7,6},{8,9},{9,8},{10,11... | collective-permute-start | bytes 1572872 | tf_op jit(solution)/shard_map/ppermute | solution.py:13
  103.6 6.6 %fusion.43 = f32[512,1024]{1,0:T(8,128)} fusion(bf16[1024,1024]{1,0:T(8,128)(2,1)} %param.21, f32[512,1024,1]{1,0,2:T(8,128)} %fusion.138, bf16[4,512,256]{2,1,0:T(8,128)(2,1)S(1)} %bitcast.264, bf16[4,256,1024]{2,1,0:T(8,128)(2,1)} %bitcast.375), kind=kOutput, calls=%fused_computation.62 | convolution fusion | flops 2150629376 | bytes 9437184 | tf_op jit(solution)/shard_map/dot_general | solution.py:135
  110.2 7.5 %convolution_add_fusion = f32[512,1024]{1,0:T(8,128)} fusion(f32[512,1024]{1,0:T(8,128)} %fusion.43, bf16[1024,1024]{1,0:T(8,128)(2,1)} %fusion.33, f32[512,1024,1]{1,0,2:T(8,128)} %fusion.139, bf16[4,512,256]{2,1,0:T(8,128)(2,1)} %bitcast.266, bf16[4,256,1024]{2,1,0:T(8,128)(2,1)} %bitcast.376), kind=kOutput, calls=%fused_computation.47 | convolution fusion | flops 2151153664 | bytes 11534336 | tf_op jit(solution)/shard_map/dot_general | solution.py:135
  117.7 2.9 %copy.22 = f32[512,1024]{0,1:T(8,128)} copy(f32[512,1024]{1,0:T(8,128)} %convolution_add_fusion) | data formatting | bytes 4194304 | tf_op jit(solution)/shard_map/add | solution.py:135
  120.6 3.0 %fusion.128 = (f32[512,2,1,256]{0,3,2,1:T(8,128)}, f32[512,2,1,256]{0,3,2,1:T(8,128)}) fusion(f32[512,2,2,256]{0,3,2,1:T(8,128)} %bitcast.262), kind=kLoop, calls=%fused_computation.273 | loop fusion | bytes 4194304 | tf_op jit(solution)/shard_map/slice | solution.py:55
  135.2 6.8 %fusion.42 = f32[512,1024]{1,0:T(8,128)} fusion(bf16[1024,1024]{1,0:T(8,128)(2,1)} %param.21, f32[512,1024,1]{1,0,2:T(8,128)} %fusion.136, bf16[4,512,256]{2,1,0:T(8,128)(2,1)} %bitcast.270, bf16[4,256,1024]{2,1,0:T(8,128)(2,1)} %bitcast.377), kind=kOutput, calls=%fused_computation.61 | convolution fusion | flops 2150629376 | bytes 9437184 | tf_op jit(solution)/shard_map/dot_general | solution.py:135
  146.9 7.4 %convolution_add_fusion.1 = f32[512,1024]{1,0:T(8,128)} fusion(f32[512,1024]{1,0:T(8,128)} %fusion.42, bf16[1024,1024]{1,0:T(8,128)(2,1)} %fusion.33, f32[512,1024,1]{1,0,2:T(8,128)} %fusion.137, bf16[4,512,256]{2,1,0:T(8,128)(2,1)} %bitcast.268, bf16[4,256,1024]{2,1,0:T(8,128)(2,1)} %bitcast.378), kind=kOutput, calls=%fused_computation.48 | convolution fusion | flops 2151153664 | bytes 11534336 | tf_op jit(solution)/shard_map/dot_general | solution.py:135
  154.4 4.0 %reshape_reshape.6 = f32[512,2,2,256]{3,2,1,0:T(2,128)} reshape(f32[512,1024]{1,0:T(8,128)} %convolution_add_fusion.1) | data formatting | bytes 4194304 | tf_op jit(solution)/shard_map/reshape;reshape | solution.py:53
  158.4 4.0 %fusion.127 = (f32[512,2,1,256]{3,2,1,0:T(1,128)S(1)}, f32[512,2,1,256]{3,2,1,0:T(1,128)S(1)}) fusion(f32[512,2,2,256]{3,2,1,0:T(2,128)} %reshape_reshape.6), kind=kLoop, calls=%fused_computation.272 | loop fusion | bytes 4194304 | tf_op jit(solution)/shard_map/slice | solution.py:55
  168.2 4.4 %collective-permute-done.23 = bf16[512,1,256]{2,0,1:T(8,128)(2,1)S(1)} collective-permute-done((bf16[512,1,256]{2,0,1:T(8,128)(2,1)S(1)}, bf16[512,1,256]{2,0,1:T(8,128)(2,1)S(1)}, u32[]{:S(2)}, u32[]{:S(2)}) %collective-permute-start.23) | collective-permute-done | bytes 262176 | tf_op jit(solution)/shard_map/ppermute | solution.py:13
  172.6 2.8 %fusion.41 = bf16[1,512,256]{2,1,0:T(8,128)(2,1)} fusion(bf16[512,1,256]{2,0,1:T(8,128)(2,1)S(1)} %collective-permute-done.23, f32[512,1,2,256]{3,0,2,1:T(8,128)} %copy-done.2, pred[]{:T(512)S(6)} %eq.427, s32[256]{0:T(256)S(1)} %get-tuple-element.128, s32[256]{0:T(256)S(1)} %get-tuple-element.131, s32[256]{0:T(256)S(1)} %get-tuple-element.127, ...), kind=kOutput, calls=%fused_computation.60 | convolution fusion | flops 204734464 | bytes 1601537 | tf_op jit(solution)/shard_map/dot_general | solution.py:142
  175.4 5.3 %collective-permute-start.25 = (bf16[1,512,256]{2,1,0:T(8,128)(2,1)}, bf16[1,512,256]{2,1,0:T(8,128)(2,1)}, u32[]{:S(2)}, u32[]{:S(2)}) collective-permute-start(bf16[1,512,256]{2,1,0:T(8,128)(2,1)} %fusion.41), channel_id=1, source_target_pairs={{0,31},{1,30},{2,29},{3,28},{4,27},{5,26},{6,25},{7,24},{8,23},{9,... | collective-permute-start | bytes 786440 | tf_op jit(solution)/shard_map/ppermute | solution.py:8
  189.4 9.9 %collective-permute-done.25 = bf16[1,512,256]{2,1,0:T(8,128)(2,1)} collective-permute-done((bf16[1,512,256]{2,1,0:T(8,128)(2,1)}, bf16[1,512,256]{2,1,0:T(8,128)(2,1)}, u32[]{:S(2)}, u32[]{:S(2)}) %collective-permute-start.25) | collective-permute-done | bytes 262176 | tf_op jit(solution)/shard_map/ppermute | solution.py:8
  200.3 4.4 %collective-permute-done.24 = bf16[1,512,256]{2,1,0:T(8,128)(2,1)S(1)} collective-permute-done((bf16[1,512,256]{2,1,0:T(8,128)(2,1)}, bf16[1,512,256]{2,1,0:T(8,128)(2,1)S(1)}, u32[]{:S(2)}, u32[]{:S(2)}) %collective-permute-start.24) | collective-permute-done | bytes 262176 | tf_op jit(solution)/shard_map/ppermute | solution.py:8
  (167 shorter events, 82.0 us)
Async XLA Ops:
  2.6 22.8 %collective-permute-start.4 = (bf16[1,512,256]{2,1,0:T(8,128)(2,1)}, bf16[1,512,256]{2,1,0:T(8,128)(2,1)}, u32[]{:S(2)}, u32[]{:S(2)}) collective-permute-start(bf16[1,512,256]{2,1,0:T(8,128)(2,1)} %get-tuple-element.75), channel_id=1, source_target_pairs={{0,28},{4,24},{8,20},{12,16},{16,12},{20,8},{24,4},{28,0},{1,29},{... | collective-permute-start | bytes 786440 | tf_op jit(solution)/shard_map/ppermute | solution.py:8
  5.1 17.2 %collective-permute-start.17 = (s32[1,512]{1,0:T(1,128)S(1)}, s32[1,512]{1,0:T(1,128)S(1)}, u32[]{:S(2)}, u32[]{:S(2)}) collective-permute-start(s32[1,512]{1,0:T(1,128)S(1)} %get-tuple-element.50), channel_id=1, source_target_pairs={{0,28},{4,24},{8,20},{12,16},{16,12},{20,8},{24,4},{28,0},{1,29},{... | collective-permute-start | bytes 6152 | tf_op jit(solution)/shard_map/ppermute | solution.py:8
  6.4 16.4 %collective-permute-start.5 = (s32[1,512]{1,0:T(1,128)S(1)}, s32[1,512]{1,0:T(1,128)S(1)}, u32[]{:S(2)}, u32[]{:S(2)}) collective-permute-start(s32[1,512]{1,0:T(1,128)S(1)} %get-tuple-element.96), channel_id=1, source_target_pairs={{0,28},{4,24},{8,20},{12,16},{16,12},{20,8},{24,4},{28,0},{1,29},{... | collective-permute-start | bytes 6152 | tf_op jit(solution)/shard_map/ppermute | solution.py:8
  7.5 27.5 %collective-permute-start.16 = (bf16[1,512,256]{2,1,0:T(8,128)(2,1)S(1)}, bf16[1,512,256]{2,1,0:T(8,128)(2,1)}, u32[]{:S(2)}, u32[]{:S(2)}) collective-permute-start(bf16[1,512,256]{2,1,0:T(8,128)(2,1)S(1)} %get-tuple-element.74), channel_id=1, source_target_pairs={{0,28},{4,24},{8,20},{12,16},{16,12},{20,8},{24,4},{28,0},{1,29},{... | collective-permute-start | bytes 786440 | tf_op jit(solution)/shard_map/ppermute | solution.py:8
  44.5 17.2 %collective-permute-start.13 = (bf16[1,3,256]{2,1,0:T(4,128)(2,1)S(1)}, bf16[1,3,256]{2,1,0:T(4,128)(2,1)S(1)}, u32[]{:S(2)}, u32[]{:S(2)}) collective-permute-start(bf16[1,3,256]{2,1,0:T(4,128)(2,1)S(1)} %get-tuple-element.83), channel_id=1, source_target_pairs={{4,0},{8,4},{12,8},{16,12},{20,16},{24,20},{28,24},{5,1},{9,5},{13... | collective-permute-start | bytes 4616 | tf_op jit(solution)/shard_map/ppermute | solution.py:25
  47.3 16.7 %collective-permute-start.12 = (bf16[1,3,256]{2,1,0:T(4,128)(2,1)S(1)}, bf16[1,3,256]{2,1,0:T(4,128)(2,1)S(1)}, u32[]{:S(2)}, u32[]{:S(2)}) collective-permute-start(bf16[1,3,256]{2,1,0:T(4,128)(2,1)S(1)} %get-tuple-element.82), channel_id=1, source_target_pairs={{0,4},{4,8},{8,12},{12,16},{16,20},{20,24},{24,28},{1,5},{5,9},{9,... | collective-permute-start | bytes 4616 | tf_op jit(solution)/shard_map/ppermute | solution.py:23
  51.1 17.3 %collective-permute-start.19 = (bf16[1,3,256]{2,1,0:T(4,128)(2,1)S(1)}, bf16[1,3,256]{2,1,0:T(4,128)(2,1)S(1)}, u32[]{:S(2)}, u32[]{:S(2)}) collective-permute-start(bf16[1,3,256]{2,1,0:T(4,128)(2,1)S(1)} %get-tuple-element.81), channel_id=1, source_target_pairs={{4,0},{8,4},{12,8},{16,12},{20,16},{24,20},{28,24},{5,1},{9,5},{13... | collective-permute-start | bytes 4616 | tf_op jit(solution)/shard_map/ppermute | solution.py:25
  54.7 16.1 %collective-permute-start.18 = (bf16[1,3,256]{2,1,0:T(4,128)(2,1)S(1)}, bf16[1,3,256]{2,1,0:T(4,128)(2,1)S(1)}, u32[]{:S(2)}, u32[]{:S(2)}) collective-permute-start(bf16[1,3,256]{2,1,0:T(4,128)(2,1)S(1)} %get-tuple-element.80), channel_id=1, source_target_pairs={{0,4},{4,8},{8,12},{12,16},{16,20},{20,24},{24,28},{1,5},{5,9},{9,... | collective-permute-start | bytes 4616 | tf_op jit(solution)/shard_map/ppermute | solution.py:23
  57.7 15.1 %collective-permute-start.1 = (bf16[1,3,256]{2,1,0:T(4,128)(2,1)S(1)}, bf16[1,3,256]{2,1,0:T(4,128)(2,1)S(1)}, u32[]{:S(2)}, u32[]{:S(2)}) collective-permute-start(bf16[1,3,256]{2,1,0:T(4,128)(2,1)S(1)} %get-tuple-element.79), channel_id=1, source_target_pairs={{4,0},{8,4},{12,8},{16,12},{20,16},{24,20},{28,24},{5,1},{9,5},{13... | collective-permute-start | bytes 4616 | tf_op jit(solution)/shard_map/ppermute | solution.py:25
  61.7 11.4 %collective-permute-start = (bf16[1,3,256]{2,1,0:T(4,128)(2,1)S(1)}, bf16[1,3,256]{2,1,0:T(4,128)(2,1)S(1)}, u32[]{:S(2)}, u32[]{:S(2)}) collective-permute-start(bf16[1,3,256]{2,1,0:T(4,128)(2,1)S(1)} %get-tuple-element.78), channel_id=1, source_target_pairs={{0,4},{4,8},{8,12},{12,16},{16,20},{20,24},{24,28},{1,5},{5,9},{9,... | collective-permute-start | bytes 4616 | tf_op jit(solution)/shard_map/ppermute | solution.py:23
  64.0 11.0 %collective-permute-start.7 = (bf16[1,3,256]{2,1,0:T(4,128)(2,1)S(1)}, bf16[1,3,256]{2,1,0:T(4,128)(2,1)S(1)}, u32[]{:S(2)}, u32[]{:S(2)}) collective-permute-start(bf16[1,3,256]{2,1,0:T(4,128)(2,1)S(1)} %get-tuple-element.77), channel_id=1, source_target_pairs={{4,0},{8,4},{12,8},{16,12},{20,16},{24,20},{28,24},{5,1},{9,5},{13... | collective-permute-start | bytes 4616 | tf_op jit(solution)/shard_map/ppermute | solution.py:25
  68.4 6.6 %collective-permute-start.6 = (bf16[1,3,256]{2,1,0:T(4,128)(2,1)S(1)}, bf16[1,3,256]{2,1,0:T(4,128)(2,1)S(1)}, u32[]{:S(2)}, u32[]{:S(2)}) collective-permute-start(bf16[1,3,256]{2,1,0:T(4,128)(2,1)S(1)} %get-tuple-element.76), channel_id=1, source_target_pairs={{0,4},{4,8},{8,12},{12,16},{16,20},{20,24},{24,28},{1,5},{5,9},{9,... | collective-permute-start | bytes 4616 | tf_op jit(solution)/shard_map/ppermute | solution.py:23
  72.8 11.4 %collective-permute-start.20 = (bf16[1,512,256]{2,1,0:T(8,128)(2,1)S(1)}, bf16[1,512,256]{2,1,0:T(8,128)(2,1)S(1)}, u32[]{:S(2)}, u32[]{:S(2)}) collective-permute-start(bf16[1,512,256]{2,1,0:T(8,128)(2,1)S(1)} %fusion.52), channel_id=1, source_target_pairs={{0,2},{1,3},{2,0},{3,1},{4,6},{5,7},{6,4},{7,5},{8,10},{9,11},{10,... | collective-permute-start | bytes 786440 | tf_op jit(solution)/shard_map/ppermute | solution.py:13
  73.5 16.3 %collective-permute-start.2 = (bf16[1,512,256]{2,1,0:T(8,128)(2,1)S(1)}, bf16[1,512,256]{2,1,0:T(8,128)(2,1)S(1)}, u32[]{:S(2)}, u32[]{:S(2)}) collective-permute-start(bf16[1,512,256]{2,1,0:T(8,128)(2,1)S(1)} %fusion.76), channel_id=1, source_target_pairs={{0,2},{1,3},{2,0},{3,1},{4,6},{5,7},{6,4},{7,5},{8,10},{9,11},{10,... | collective-permute-start | bytes 786440 | tf_op jit(solution)/shard_map/ppermute | solution.py:13
  75.5 19.7 %collective-permute-start.8 = (bf16[1,512,256]{2,1,0:T(8,128)(2,1)S(1)}, bf16[1,512,256]{2,1,0:T(8,128)(2,1)S(1)}, u32[]{:S(2)}, u32[]{:S(2)}) collective-permute-start(bf16[1,512,256]{2,1,0:T(8,128)(2,1)S(1)} %fusion.68), channel_id=1, source_target_pairs={{0,2},{1,3},{2,0},{3,1},{4,6},{5,7},{6,4},{7,5},{8,10},{9,11},{10,... | collective-permute-start | bytes 786440 | tf_op jit(solution)/shard_map/ppermute | solution.py:13
  76.8 21.2 %collective-permute-start.15 = (bf16[2,512,256]{2,1,0:T(8,128)(2,1)S(1)}, bf16[2,512,256]{2,1,0:T(8,128)(2,1)S(1)}, u32[]{:S(2)}, u32[]{:S(2)}) collective-permute-start(bf16[2,512,256]{2,1,0:T(8,128)(2,1)S(1)} %maximum_bitcast_fusion.2), channel_id=1, source_target_pairs={{0,1},{1,0},{2,3},{3,2},{4,5},{5,4},{6,7},{7,6},{8,9},{9,8},{10,11... | collective-permute-start | bytes 1572872 | tf_op jit(solution)/shard_map/ppermute | solution.py:13
  84.8 13.4 %collective-permute-start.21 = (bf16[2,512,256]{2,1,0:T(8,128)(2,1)S(1)}, bf16[2,512,256]{2,1,0:T(8,128)(2,1)S(1)}, u32[]{:S(2)}, u32[]{:S(2)}) collective-permute-start(bf16[2,512,256]{2,1,0:T(8,128)(2,1)S(1)} %maximum_bitcast_fusion.3), channel_id=1, source_target_pairs={{0,1},{1,0},{2,3},{3,2},{4,5},{5,4},{6,7},{7,6},{8,9},{9,8},{10,11... | collective-permute-start | bytes 1572872 | tf_op jit(solution)/shard_map/ppermute | solution.py:13
  91.4 38.9 %collective-permute-start.3 = (bf16[2,512,256]{2,1,0:T(8,128)(2,1)}, bf16[2,512,256]{2,1,0:T(8,128)(2,1)}, u32[]{:S(2)}, u32[]{:S(2)}) collective-permute-start(bf16[2,512,256]{2,1,0:T(8,128)(2,1)} %maximum_bitcast_fusion), channel_id=1, source_target_pairs={{0,1},{1,0},{2,3},{3,2},{4,5},{5,4},{6,7},{7,6},{8,9},{9,8},{10,11... | collective-permute-start | bytes 1572872 | tf_op jit(solution)/shard_map/ppermute | solution.py:13
  96.6 45.4 %collective-permute-start.9 = (bf16[2,512,256]{2,1,0:T(8,128)(2,1)}, bf16[2,512,256]{2,1,0:T(8,128)(2,1)}, u32[]{:S(2)}, u32[]{:S(2)}) collective-permute-start(bf16[2,512,256]{2,1,0:T(8,128)(2,1)} %maximum_bitcast_fusion.1), channel_id=1, source_target_pairs={{0,1},{1,0},{2,3},{3,2},{4,5},{5,4},{6,7},{7,6},{8,9},{9,8},{10,11... | collective-permute-start | bytes 1572872 | tf_op jit(solution)/shard_map/ppermute | solution.py:13
  130.3 32.9 %collective-permute-start.22 = (f32[512,2,256]{2,0,1:T(8,128)}, f32[512,2,256]{2,0,1:T(8,128)}, u32[]{:S(2)}, u32[]{:S(2)}) collective-permute-start(f32[512,2,256]{2,0,1:T(8,128)} %select_bitcast_fusion), channel_id=1, source_target_pairs={{0,1},{1,0},{2,3},{3,2},{4,5},{5,4},{6,7},{7,6},{8,9},{9,8},{10,11... | collective-permute-start | bytes 3145736 | tf_op jit(solution)/shard_map/ppermute | solution.py:13
  165.2 7.4 %collective-permute-start.23 = (bf16[512,1,256]{2,0,1:T(8,128)(2,1)S(1)}, bf16[512,1,256]{2,0,1:T(8,128)(2,1)S(1)}, u32[]{:S(2)}, u32[]{:S(2)}) collective-permute-start(bf16[512,1,256]{2,0,1:T(8,128)(2,1)S(1)} %fusion.88), channel_id=1, source_target_pairs={{0,2},{1,3},{2,0},{3,1},{4,6},{5,7},{6,4},{7,5},{8,10},{9,11},{10,... | collective-permute-start | bytes 786440 | tf_op jit(solution)/shard_map/ppermute | solution.py:13
  167.6 13.1 %collective-permute-start.11 = (bf16[512,1,256]{2,0,1:T(8,128)(2,1)}, bf16[512,1,256]{2,0,1:T(8,128)(2,1)}, u32[]{:S(2)}, u32[]{:S(2)}) collective-permute-start(bf16[512,1,256]{2,0,1:T(8,128)(2,1)} %fusion.86), channel_id=1, source_target_pairs={{0,2},{1,3},{2,0},{3,1},{4,6},{5,7},{6,4},{7,5},{8,10},{9,11},{10,... | collective-permute-start | bytes 786440 | tf_op jit(solution)/shard_map/ppermute | solution.py:13
  175.4 23.9 %collective-permute-start.25 = (bf16[1,512,256]{2,1,0:T(8,128)(2,1)}, bf16[1,512,256]{2,1,0:T(8,128)(2,1)}, u32[]{:S(2)}, u32[]{:S(2)}) collective-permute-start(bf16[1,512,256]{2,1,0:T(8,128)(2,1)} %fusion.41), channel_id=1, source_target_pairs={{0,31},{1,30},{2,29},{3,28},{4,27},{5,26},{6,25},{7,24},{8,23},{9,... | collective-permute-start | bytes 786440 | tf_op jit(solution)/shard_map/ppermute | solution.py:8
  183.2 21.5 %collective-permute-start.24 = (bf16[1,512,256]{2,1,0:T(8,128)(2,1)}, bf16[1,512,256]{2,1,0:T(8,128)(2,1)S(1)}, u32[]{:S(2)}, u32[]{:S(2)}) collective-permute-start(bf16[1,512,256]{2,1,0:T(8,128)(2,1)} %fusion.40), channel_id=1, source_target_pairs={{0,31},{1,30},{2,29},{3,28},{4,27},{5,26},{6,25},{7,24},{8,23},{9,... | collective-permute-start | bytes 786440 | tf_op jit(solution)/shard_map/ppermute | solution.py:8
  (25 other events, 276.0 us)

commit v4 on v2

--- a/solution.py
+++ b/solution.py
@@ -102,32 +102,38 @@
     taps = conv_kernel.shape[0]
     half_width = taps // 2
 
-    def conv_rows(hidden, bases, kernel):
-        x = hidden.astype(jnp.float32) + embedded(bases, table)
-        square = lax.psum(jnp.sum(x * x, axis=-1), "ch")
-        normed = (x * lax.rsqrt(square[..., None] / width + 1e-05) * norm_gain).astype(jnp.bfloat16)
-        length = normed.shape[1]
-        padded = padded_2(normed, "seq", 1, half_width).astype(jnp.float32)
-        conv = jnp.zeros(normed.shape, jnp.float32) + conv_bias
-        for offset in range(taps):
-            conv = conv + kernel[offset] * padded[:, offset : offset + length]
-        return x, conv.astype(jnp.bfloat16).reshape(-1, local_width)
-
-    def activation(rows):
-        pieces = gather_blocks(rows, ch_bits, me)
-        dims = (((0, 2), (0, 1)), ((), ()))
-        gate = lax.dot_general(
-            pieces, w_gate.reshape(ch_count, local_width, -1), dims, preferred_element_type=jnp.float32
-        )
-        value = lax.dot_general(
-            pieces, w_value.reshape(ch_count, local_width, -1), dims, preferred_element_type=jnp.float32
-        )
-        return (jax.nn.silu(gate) * value).astype(jnp.bfloat16)
-
-    x_fwd, rows_fwd = conv_rows(hidden_forward, base_in, conv_kernel)
-    _, rows_rev = conv_rows(rev_here, comp, conv_kernel[::-1])
-    act_fwd = activation(rows_fwd)
-    act_rev = activation(rows_rev)
+    x_fwd = hidden_forward.astype(jnp.float32) + embedded(base_in, table)
+    x_rfp = rev_here.astype(jnp.float32) + embedded(comp, table)
+    square_fwd, square_rev = lax.psum(
+        (jnp.sum(x_fwd * x_fwd, axis=-1), jnp.sum(x_rfp * x_rfp, axis=-1)), "ch"
+    )
+    normed_fwd = (x_fwd * lax.rsqrt(square_fwd[..., None] / width + 1e-05) * norm_gain).astype(
+        jnp.bfloat16
+    )
+    normed_rev = (x_rfp * lax.rsqrt(square_rev[..., None] / width + 1e-05) * norm_gain).astype(
+        jnp.bfloat16
+    )
+    stacked = jnp.stack([normed_fwd, normed_rev])
+    length = stacked.shape[2]
+    padded = padded_2(stacked, "seq", 2, half_width).astype(jnp.float32)
+    conv_f = jnp.zeros(normed_fwd.shape, jnp.float32) + conv_bias
+    conv_r = jnp.zeros(normed_rev.shape, jnp.float32) + conv_bias
+    for offset in range(taps):
+        conv_f = conv_f + conv_kernel[offset] * padded[0, :, offset : offset + length]
+        conv_r = conv_r + conv_kernel[taps - 1 - offset] * padded[1, :, offset : offset + length]
+    rows = jnp.concatenate([conv_f, conv_r]).astype(jnp.bfloat16).reshape(-1, local_width)
+    pieces = gather_blocks(rows, ch_bits, me)
+    dims = (((0, 2), (0, 1)), ((), ()))
+    gate = lax.dot_general(
+        pieces, w_gate.reshape(ch_count, local_width, -1), dims, preferred_element_type=jnp.float32
+    )
+    value = lax.dot_general(
+        pieces, w_value.reshape(ch_count, local_width, -1), dims, preferred_element_type=jnp.float32
+    )
+    act = (jax.nn.silu(gate) * value).astype(jnp.bfloat16)
+    half = act.shape[0] // 2
+    act_fwd = act[:half]
+    act_rev = act[half:]
     lane_flip = reversal(local_width, local_width)
     w_flip = jnp.dot(w_out, reversal(width, width), preferred_element_type=jnp.float32).astype(jnp.bfloat16)
     part = jnp.dot(act_fwd, w_out, preferred_element_type=jnp.float32) + jnp.dot(

time: 178 us -> 173 us (0.972)
  starting transfers between devices: 30.5 us -> 19 us
  waiting for transfers between devices: 67.6 us -> 76.9 us
  matrix products: 38.1 us -> 33.3 us
  local copies, waits for them, and re-layouts: 4.61 us -> 8 us
  other arithmetic: 28.6 us -> 26.3 us
    ppermute x6 -> x4, waiting for transfers between devices: 28.2 us -> 41.5 us  [partner(): lax.ppermute(value, axis, [(k, k ^ mask) for k in range(lax.axis_size(axi...]
    ppermute x6 -> x4, starting transfers between devices: 12.2 us -> 5.74 us  [partner(): lax.ppermute(value, axis, [(k, k ^ mask) for k in range(lax.axis_size(axi...]
    dot_general x1, matrix products: 12 us -> 6.08 us  [local(): jnp.dot(act_fwd, w_out, preferred_element_type=jnp.float32)]
    dot_general x1, matrix products: 4.62 us -> 9.71 us  [local(): jnp.dot(act_rev, w_flip, preferred_element_type=jnp.float32)]
    ppermute x3, waiting for transfers between devices: 38.8 us -> 34.7 us  [mirror(): return lax.ppermute(value, axes, [(k, count - 1 - k) for k in range(count)])]
    dot_general x4 -> x2, matrix products: 14 us -> 9.98 us  [the longest x1 5.45 us: local(): lax.dot_general(pieces, w_value.reshape(ch_count, local_width, -1), dims,...]
    convert_element_type x6 -> x2, other arithmetic: 5.98 us -> 3.02 us  [the longest x1 2.8 us: local(): (x_rfp * lax.rsqrt(square_rev[..., None] / width + 1e-05) * norm_gain).as...]
    another operation x0 -> x3, other arithmetic: none -> 2.95 us
  transfers between devices with their start and end apart: 13 -> 9, of which waited for: 7 -> 7; matrix products, arithmetic and copies ran while one was open for 16% -> 7% of each run, Pallas kernels for 0% -> 0%
where the time goes in v4:
time: 173 us; the launch traced here: 171 us
  waiting for transfers between devices  76.9 us (44%)
  matrix products  33.3 us (19%)
  other arithmetic  26.3 us (15%)
  starting transfers between devices  19 us (11%)
  local copies, waits for them, and re-layouts  8 us (5%)
  blocking collectives  6.83 us (4%)
    ppermute x4, waiting for transfers between devices, partner(): lax.ppermute(value, axis, [(k, k ^ mask) for k in range(lax.axis_size(axi...  41.5 us
    ppermute x3, waiting for transfers between devices, mirror(): return lax.ppermute(value, axes, [(k, count - 1 - k) for k in range(count)])  34.7 us
    dot_general x1, matrix products, local(): jnp.dot(act_rev, w_flip, preferred_element_type=jnp.float32)  9.71 us
    ppermute x3, starting transfers between devices, mirror(): return lax.ppermute(value, axes, [(k, count - 1 - k) for k in range(count)])  7.11 us
    psum x1, blocking collectives, local(): lax.psum((jnp.sum(x_fwd * x_fwd, axis=-1), jnp.sum(x_rfp * x_rfp, axis=-1...  6.83 us
    dot_general x1, matrix products, local(): jnp.dot(act_fwd, w_out, preferred_element_type=jnp.float32)  6.08 us
    convert_element_type x2, other arithmetic, local(): return (out_forward.astype(jnp.bfloat16), out_reverse.astype(jnp.bfloat16))  6.07 us
    reduce_sum x1, other arithmetic, local(): jnp.sum(x_fwd * x_fwd, axis=-1)  6.04 us
  transfers between devices with their start and end apart: 9, of which 7 were waited for; matrix products, arithmetic and copies ran while one was open for 7% of the time, Pallas kernels for 0%

profile of v4, /device:TPU:17, one launch (start us, length us, event | category | flops | bytes accessed | tf_op | source)
XLA Modules:
  0.0 171.4 jit_solution(14099082988878685399)
XLA Ops:
  5.3 6.0 %multiply_reduce_fusion.1 = (f32[2,512]{1,0:T(2,128)S(1)}, f32[2,512,256]{2,1,0:T(8,128)}) fusion(f32[256]{0:T(256)S(1)} %bitcast.248, pred[2,512]{1,0:T(4,128)(4,1)S(1)} %get-tuple-element.49, f32[256]{0:T(256)S(1)} %bitcast.243, pred[2,512]{1,0:T(4,128)(4,1)S(1)} %get-tuple-element.51, f32[256]{0:T(256)S(1)} %bitcast.238, ...), kind=kLoop, calls=%fused_computation.103 | loop fusion | flops 6290432 | bytes 2116608 | tf_op jit(solution)/shard_map/reduce_sum | solution.py:108
  11.4 16.3 %collective-permute-done = bf16[2,512,256]{2,1,0:T(8,128)(2,1)S(1)} collective-permute-done((bf16[2,512,256]{2,1,0:T(8,128)(2,1)}, bf16[2,512,256]{2,1,0:T(8,128)(2,1)S(1)}, u32[]{:S(2)}, u32[]{:S(2)}) %collective-permute-start) | collective-permute-done | bytes 524320 | tf_op jit(solution)/shard_map/ppermute | solution.py:8
  28.5 4.1 %multiply_reduce_fusion = (f32[1024]{0:T(1024)S(1)}, f32[1024,256]{1,0:T(8,128)}) fusion(f32[256]{0:T(256)S(1)} %bitcast.249, f32[256]{0:T(256)S(1)} %bitcast.244, f32[256]{0:T(256)S(1)} %bitcast.239, f32[256]{0:T(256)S(1)} %bitcast.234, f32[256]{0:T(256)S(1)} %bitcast.229, pred[1024]{0:T(1024)(128)(4,1)S(1)} %broadcast_in_dim.233, ...), kind=kOutput, calls=%fused_computation.100 | convolution fusion | flops 548928512 | bytes 1605632 | tf_op jit(solution)/shard_map/dot_general | solution.py:96
  32.6 6.8 %all-reduce = (f32[2,512]{1,0:T(2,128)S(1)}, f32[2,512]{1,0:T(2,128)S(1)}) all-reduce(f32[2,512]{1,0:T(2,128)S(1)} %reduce_sum.22, f32[2,512]{1,0:T(2,128)S(1)} %get-tuple-element.27), channel_id=1, replica_groups=mesh['seq'=8,'ch'=4] {'ch'}, use_global_device_ids=true, to_apply=%region_3.4 | all-reduce | flops 2048 | bytes 16384 | tf_op jit(solution)/shard_map/psum | solution.py:107
  40.7 2.8 %multiply_convert_fusion = bf16[1,2,512,256]{3,2,1,0:T(8,128)(2,1)S(1)} fusion(f32[1,2,512,256]{3,2,1,0:T(8,128)} %bitcast.227, f32[256]{0:T(256)S(1)} %copy-done.7, f32[2,512]{1,0:T(2,128)S(1)} %add_rsqrt_fusion, f32[256]{0:T(256)S(1)} %bitcast.251, f32[256]{0:T(256)S(1)} %bitcast.246, f32[256]{0:T(256)S(1)} %bitcast.241, f32[256]{0:T(256)S(1)} %bitcast.236, ...), kind=kLoop, calls=%fused_computation.99 | loop fusion | flops 3407872 | bytes 1588224 | tf_op jit(solution)/shard_map/convert_element_type | solution.py:113
  43.5 2.2 %collective-permute-start.2 = (bf16[2,2,3,256]{3,2,1,0:T(4,128)(2,1)S(1)}, bf16[2,2,3,256]{3,2,1,0:T(4,128)(2,1)S(1)}, u32[]{:S(2)}, u32[]{:S(2)}) collective-permute-start(bf16[2,2,3,256]{3,2,1,0:T(4,128)(2,1)S(1)} %get-tuple-element.16), channel_id=1, source_target_pairs={{0,4},{4,8},{8,12},{12,16},{16,20},{20,24},{24,28},{1,5},{5,9},{9,... | collective-permute-start | bytes 18440 | tf_op jit(solution)/shard_map/ppermute | solution.py:23
  45.7 4.0 %collective-permute-start.3 = (bf16[2,2,3,256]{3,2,1,0:T(4,128)(2,1)S(1)}, bf16[2,2,3,256]{3,2,1,0:T(4,128)(2,1)S(1)}, u32[]{:S(2)}, u32[]{:S(2)}) collective-permute-start(bf16[2,2,3,256]{3,2,1,0:T(4,128)(2,1)S(1)} %get-tuple-element.17), channel_id=1, source_target_pairs={{4,0},{8,4},{12,8},{16,12},{20,16},{24,20},{28,24},{5,1},{9,5},{13... | collective-permute-start | bytes 18440 | tf_op jit(solution)/shard_map/ppermute | solution.py:25
  54.0 21.8 %collective-permute-done.4 = bf16[1,2048,256]{2,1,0:T(8,128)(2,1)} collective-permute-done((bf16[1,2048,256]{2,1,0:T(8,128)(2,1)S(1)}, bf16[1,2048,256]{2,1,0:T(8,128)(2,1)}, u32[]{:S(2)}, u32[]{:S(2)}) %collective-permute-start.4) | collective-permute-done | bytes 1048608 | tf_op jit(solution)/shard_map/ppermute | solution.py:13
  75.7 1.7 select_bitcast_fusion.4
  79.9 2.7 %collective-permute-start.5 = (bf16[2,2048,256]{2,1,0:T(8,128)(2,1)}, bf16[2,2048,256]{2,1,0:T(8,128)(2,1)}, u32[]{:S(2)}, u32[]{:S(2)}) collective-permute-start(bf16[2,2048,256]{2,1,0:T(8,128)(2,1)} %maximum_bitcast_fusion), channel_id=1, source_target_pairs={{0,1},{1,0},{2,3},{3,2},{4,5},{5,4},{6,7},{7,6},{8,9},{9,8},{10,11... | collective-permute-start | bytes 6291464 | tf_op jit(solution)/shard_map/ppermute | solution.py:13
  82.6 4.1 %collective-permute-done.5 = bf16[2,2048,256]{2,1,0:T(8,128)(2,1)} collective-permute-done((bf16[2,2048,256]{2,1,0:T(8,128)(2,1)}, bf16[2,2048,256]{2,1,0:T(8,128)(2,1)}, u32[]{:S(2)}, u32[]{:S(2)}) %collective-permute-start.5) | collective-permute-done | bytes 2097184 | tf_op jit(solution)/shard_map/ppermute | solution.py:13
  86.7 2.1 %select_bitcast_fusion.2 = (bf16[2,1,2048,256]{3,2,1,0:T(8,128)(2,1)S(1)}, bf16[2,1,2048,256]{3,2,1,0:T(8,128)(2,1)S(1)}) fusion(bf16[2,2048,256]{2,1,0:T(8,128)(2,1)} %collective-permute-done.5, pred[]{:T(512)S(6)} %eq.119, bf16[1,1,2048,256]{3,2,1,0:T(8,128)(2,1)} %copy-done.1, bf16[1,1,2048,256]{3,2,1,0:T(8,128)(2,1)S(1)} %get-tuple-element.14), kind=kLoop, calls=%fused_computation.37 | loop fusion | flops 3145728 | bytes 8388609 | tf_op jit(solution)/shard_map/stack | solution.py:45
  89.2 4.5 %fusion.124 = f32[2048,1024,1]{1,0,2:T(8,128)S(1)} fusion(bf16[4,2048,256]{2,1,0:T(8,128)(2,1)S(1)} %bitcast.224, bf16[4,256,1024]{2,1,0:T(8,128)(2,1)S(1)} %bitcast.219), kind=kOutput, calls=%fused_computation.177 | convolution fusion | flops 4294967296 | bytes 14680064 | tf_op jit(solution)/shard_map/dot_general | solution.py:127
  93.8 5.5 %fusion = bf16[2048,1024]{1,0:T(8,128)(2,1)S(1)} fusion(f32[2048,1024,1]{1,0,2:T(8,128)S(1)} %fusion.124, bf16[4,2048,256]{2,1,0:T(8,128)(2,1)S(1)} %bitcast.225, bf16[4,256,1024]{2,1,0:T(8,128)(2,1)S(1)} %bitcast.267), kind=kOutput, calls=%fused_computation.1 | convolution fusion | flops 4307550208 | bytes 18874368 | tf_op jit(solution)/shard_map/dot_general | solution.py:130
  99.2 1.9 %copy-done.4 = bf16[2048,1024]{1,0:T(8,128)(2,1)} copy-done((bf16[2048,1024]{1,0:T(8,128)(2,1)}, bf16[2048,1024]{1,0:T(8,128)(2,1)S(1)}, u32[]{:S(2)}) %copy-start.4) | copy-done | bytes 4194328
  102.7 9.7 %fusion.9 = f32[1024,1024]{0,1:T(8,128)} fusion(bf16[1024,1024]{1,0:T(8,128)(2,1)} %param.21, s32[1024]{0:T(1024)S(1)} %get-tuple-element.60, s32[1024]{0:T(1024)S(1)} %get-tuple-element.61, s32[1024]{0:T(1024)S(1)} %get-tuple-element.59, s32[1024]{0:T(1024)S(1)} %get-tuple-element.62, pred[1024]{0:T(1024)(128)(4,1)S(1)} %get-tuple-element.63, ...), kind=kOutput, calls=%fused_computation.16 | convolution fusion | flops 4305453056 | bytes 8407040 | tf_op jit(solution)/shard_map/dot_general | solution.py:139
  112.4 6.1 %fusion.30 = f32[1024,1024]{0,1:T(8,128)S(1)} fusion(f32[1024,1024]{0,1:T(8,128)} %fusion.9, bf16[1024,1024]{1,0:T(8,128)(2,1)} %param.21, bf16[2048,1024]{1,0:T(8,128)(2,1)} %copy-done.4), kind=kOutput, calls=%fused_computation.42 | convolution fusion | flops 2148532224 | bytes 12582912 | tf_op jit(solution)/shard_map/dot_general | solution.py:139
  119.4 3.8 %collective-permute-done.6 = f32[1024,2,256]{0,2,1:T(8,128)S(1)} collective-permute-done((f32[1024,2,256]{0,2,1:T(8,128)S(1)}, f32[1024,2,256]{0,2,1:T(8,128)S(1)}, u32[]{:S(2)}, u32[]{:S(2)}) %collective-permute-start.6) | collective-permute-done | bytes 2097184 | tf_op jit(solution)/shard_map/ppermute | solution.py:13
  125.3 11.8 %collective-permute-done.7 = bf16[1024,1,256]{0,2,1:T(8,128)(2,1)S(1)} collective-permute-done((bf16[1024,1,256]{0,2,1:T(8,128)(2,1)S(1)}, bf16[1024,1,256]{0,2,1:T(8,128)(2,1)S(1)}, u32[]{:S(2)}, u32[]{:S(2)}) %collective-permute-start.7) | collective-permute-done | bytes 524320 | tf_op jit(solution)/shard_map/ppermute | solution.py:13
  138.1 2.8 %convolution_convert_fusion = bf16[1024,256]{1,0:T(8,128)(2,1)} fusion(s32[1024]{0:T(1024)S(1)} %get-tuple-element.54, s32[1024]{0:T(1024)S(1)} %get-tuple-element.55, s32[1024]{0:T(1024)S(1)} %get-tuple-element.53, s32[1024]{0:T(1024)S(1)} %get-tuple-element.56, pred[1024]{0:T(1024)(128)(4,1)S(1)} %get-tuple-element.57, ...), kind=kOutput, calls=%fused_computation.43 | convolution fusion | flops 545521664 | bytes 1067008 | tf_op jit(solution)/shard_map/dot_general | solution.py:146
  140.9 4.7 %collective-permute-start.8 = (bf16[2,512,256]{2,1,0:T(8,128)(2,1)}, bf16[2,512,256]{2,1,0:T(8,128)(2,1)}, u32[]{:S(2)}, u32[]{:S(2)}) collective-permute-start(bf16[2,512,256]{2,1,0:T(8,128)(2,1)} %bitcast.52), channel_id=1, source_target_pairs={{0,31},{1,30},{2,29},{3,28},{4,27},{5,26},{6,25},{7,24},{8,23},{9,... | collective-permute-start | bytes 1572872 | tf_op jit(solution)/shard_map/ppermute | solution.py:8
  146.9 3.8 %add_convert_fusion.1 = bf16[2,512,256]{2,1,0:T(8,128)(2,1)} fusion(f32[2,512,256]{2,1,0:T(8,128)} %bitcast.226, f32[256]{0:T(256)S(1)} %bitcast.252, pred[2,512]{1,0:T(4,128)(4,1)S(1)} %get-tuple-element.49, f32[256]{0:T(256)S(1)} %bitcast.247, pred[2,512]{1,0:T(4,128)(4,1)S(1)} %get-tuple-element.51, f32[256]{0:T(256)S(1)} %bitcast.242, ...), kind=kLoop, calls=%fused_computation.95 | loop fusion | flops 3407872 | bytes 2107392 | tf_op jit(solution)/shard_map/convert_element_type | solution.py:149
  150.7 18.4 %collective-permute-done.8 = bf16[2,512,256]{2,1,0:T(8,128)(2,1)} collective-permute-done((bf16[2,512,256]{2,1,0:T(8,128)(2,1)}, bf16[2,512,256]{2,1,0:T(8,128)(2,1)}, u32[]{:S(2)}, u32[]{:S(2)}) %collective-permute-start.8) | collective-permute-done | bytes 524320 | tf_op jit(solution)/shard_map/ppermute | solution.py:8
  169.1 2.3 %add_convert_fusion = bf16[2,512,256]{2,1,0:T(8,128)(2,1)} fusion(f32[2,512,256]{2,1,0:T(8,128)} %get-tuple-element.5, bf16[2,512,256]{2,1,0:T(8,128)(2,1)} %collective-permute-done.8), kind=kLoop, calls=%fused_computation.94 | loop fusion | flops 786432 | bytes 2097152 | tf_op jit(solution)/shard_map/convert_element_type | solution.py:149
  (65 shorter events, 20.5 us)
Async XLA Ops:
  0.6 88.6 %copy-start = (bf16[1024,1024]{1,0:T(8,128)(2,1)S(1)}, bf16[1024,1024]{1,0:T(8,128)(2,1)}, u32[]{:S(2)}) copy-start(bf16[1024,1024]{1,0:T(8,128)(2,1)} %param.19) | copy-start | bytes 6291460
  1.5 3.4 %collective-permute-start.1 = (s32[2,512]{1,0:T(2,128)S(1)}, s32[2,512]{1,0:T(2,128)S(1)}, u32[]{:S(2)}, u32[]{:S(2)}) collective-permute-start(s32[2,512]{1,0:T(2,128)S(1)} %get-tuple-element.26), channel_id=1, source_target_pairs={{0,28},{4,24},{8,20},{12,16},{16,12},{20,8},{24,4},{28,0},{1,29},{... | collective-permute-start | bytes 12296 | tf_op jit(solution)/shard_map/ppermute | solution.py:8
  2.7 25.0 %collective-permute-start = (bf16[2,512,256]{2,1,0:T(8,128)(2,1)}, bf16[2,512,256]{2,1,0:T(8,128)(2,1)S(1)}, u32[]{:S(2)}, u32[]{:S(2)}) collective-permute-start(bf16[2,512,256]{2,1,0:T(8,128)(2,1)} %param.14), channel_id=1, source_target_pairs={{0,28},{4,24},{8,20},{12,16},{16,12},{20,8},{24,4},{28,0},{1,29},{... | collective-permute-start | bytes 1572872 | tf_op jit(solution)/shard_map/ppermute | solution.py:8
  27.7 0.8 copy-start.9
  28.5 11.0 %copy-start.2 = (bf16[2,512,256]{2,1,0:T(8,128)(2,1)S(1)}, bf16[2,512,256]{2,1,0:T(8,128)(2,1)}, u32[]{:S(2)}) copy-start(bf16[2,512,256]{2,1,0:T(8,128)(2,1)} %param.13) | copy-start | bytes 1572868
  28.5 11.0 %copy-start.7 = (f32[256]{0:T(256)S(1)}, f32[256]{0:T(256)}, u32[]{:S(2)}) copy-start(f32[256]{0:T(256)} %param.18) | copy-start | bytes 3076
  28.5 21.2 %copy-start.5 = (f32[7,256]{1,0:T(8,128)S(1)}, f32[7,256]{1,0:T(8,128)}, u32[]{:S(2)}) copy-start(f32[7,256]{1,0:T(8,128)} %param.16) | copy-start | bytes 21508
  32.6 18.1 %copy-start.6 = (f32[256]{0:T(256)S(1)}, f32[256]{0:T(256)}, u32[]{:S(2)}) copy-start(f32[256]{0:T(256)} %param.17) | copy-start | bytes 3076
  43.5 6.2 %collective-permute-start.2 = (bf16[2,2,3,256]{3,2,1,0:T(4,128)(2,1)S(1)}, bf16[2,2,3,256]{3,2,1,0:T(4,128)(2,1)S(1)}, u32[]{:S(2)}, u32[]{:S(2)}) collective-permute-start(bf16[2,2,3,256]{3,2,1,0:T(4,128)(2,1)S(1)} %get-tuple-element.16), channel_id=1, source_target_pairs={{0,4},{4,8},{8,12},{12,16},{16,20},{20,24},{24,28},{1,5},{5,9},{9,... | collective-permute-start | bytes 18440 | tf_op jit(solution)/shard_map/ppermute | solution.py:23
  45.7 4.8 %collective-permute-start.3 = (bf16[2,2,3,256]{3,2,1,0:T(4,128)(2,1)S(1)}, bf16[2,2,3,256]{3,2,1,0:T(4,128)(2,1)S(1)}, u32[]{:S(2)}, u32[]{:S(2)}) collective-permute-start(bf16[2,2,3,256]{3,2,1,0:T(4,128)(2,1)S(1)} %get-tuple-element.17), channel_id=1, source_target_pairs={{4,0},{8,4},{12,8},{16,12},{20,16},{24,20},{28,24},{5,1},{9,5},{13... | collective-permute-start | bytes 18440 | tf_op jit(solution)/shard_map/ppermute | solution.py:25
  52.6 23.1 %copy-start.3 = (bf16[4,512,256]{2,1,0:T(8,128)(2,1)}, bf16[4,512,256]{2,1,0:T(8,128)(2,1)S(1)}, u32[]{:S(2)}) copy-start(bf16[4,512,256]{2,1,0:T(8,128)(2,1)S(1)} %pad_maximum_fusion.1) | copy-start | bytes 3145732
  52.6 23.1 %collective-permute-start.4 = (bf16[1,2048,256]{2,1,0:T(8,128)(2,1)S(1)}, bf16[1,2048,256]{2,1,0:T(8,128)(2,1)}, u32[]{:S(2)}, u32[]{:S(2)}) collective-permute-start(bf16[1,2048,256]{2,1,0:T(8,128)(2,1)S(1)} %bitcast.222), channel_id=1, source_target_pairs={{0,2},{1,3},{2,0},{3,1},{4,6},{5,7},{6,4},{7,5},{8,10},{9,11},{10,... | collective-permute-start | bytes 3145736 | tf_op jit(solution)/shard_map/ppermute | solution.py:13
  77.4 1.0 copy-start.1
  79.9 6.8 %collective-permute-start.5 = (bf16[2,2048,256]{2,1,0:T(8,128)(2,1)}, bf16[2,2048,256]{2,1,0:T(8,128)(2,1)}, u32[]{:S(2)}, u32[]{:S(2)}) collective-permute-start(bf16[2,2048,256]{2,1,0:T(8,128)(2,1)} %maximum_bitcast_fusion), channel_id=1, source_target_pairs={{0,1},{1,0},{2,3},{3,2},{4,5},{5,4},{6,7},{7,6},{8,9},{9,8},{10,11... | collective-permute-start | bytes 6291464 | tf_op jit(solution)/shard_map/ppermute | solution.py:13
  89.2 4.5 %copy-start.8 = (bf16[1024,1024]{1,0:T(8,128)(2,1)S(1)}, bf16[1024,1024]{1,0:T(8,128)(2,1)}, u32[]{:S(2)}) copy-start(bf16[1024,1024]{1,0:T(8,128)(2,1)} %param.20) | copy-start | bytes 6291460
  99.2 2.0 %copy-start.4 = (bf16[2048,1024]{1,0:T(8,128)(2,1)}, bf16[2048,1024]{1,0:T(8,128)(2,1)S(1)}, u32[]{:S(2)}) copy-start(bf16[2048,1024]{1,0:T(8,128)(2,1)S(1)} %fusion) | copy-start | bytes 12582916
  118.9 4.2 %collective-permute-start.6 = (f32[1024,2,256]{0,2,1:T(8,128)S(1)}, f32[1024,2,256]{0,2,1:T(8,128)S(1)}, u32[]{:S(2)}, u32[]{:S(2)}) collective-permute-start(f32[1024,2,256]{0,2,1:T(8,128)S(1)} %select_bitcast_fusion), channel_id=1, source_target_pairs={{0,1},{1,0},{2,3},{3,2},{4,5},{5,4},{6,7},{7,6},{8,9},{9,8},{10,11... | collective-permute-start | bytes 6291464 | tf_op jit(solution)/shard_map/ppermute | solution.py:13
  124.0 13.2 %collective-permute-start.7 = (bf16[1024,1,256]{0,2,1:T(8,128)(2,1)S(1)}, bf16[1024,1,256]{0,2,1:T(8,128)(2,1)S(1)}, u32[]{:S(2)}, u32[]{:S(2)}) collective-permute-start(bf16[1024,1,256]{0,2,1:T(8,128)(2,1)S(1)} %fusion.69), channel_id=1, source_target_pairs={{0,2},{1,3},{2,0},{3,1},{4,6},{5,7},{6,4},{7,5},{8,10},{9,11},{10,... | collective-permute-start | bytes 1572872 | tf_op jit(solution)/shard_map/ppermute | solution.py:13
  140.9 28.2 %collective-permute-start.8 = (bf16[2,512,256]{2,1,0:T(8,128)(2,1)}, bf16[2,512,256]{2,1,0:T(8,128)(2,1)}, u32[]{:S(2)}, u32[]{:S(2)}) collective-permute-start(bf16[2,512,256]{2,1,0:T(8,128)(2,1)} %bitcast.52), channel_id=1, source_target_pairs={{0,31},{1,30},{2,29},{3,28},{4,27},{5,26},{6,25},{7,24},{8,23},{9,... | collective-permute-start | bytes 1572872 | tf_op jit(solution)/shard_map/ppermute | solution.py:8

commit v5 on v4

--- a/solution.py
+++ b/solution.py
@@ -29,10 +29,8 @@
 
 
 def embedded(bases, table):
-    out = jnp.zeros(bases.shape + (table.shape[1],), jnp.float32)
-    for v in range(table.shape[0]):
-        out = out + jnp.where(bases[..., None] == v, table[v], 0.0)
-    return out
+    onehot = (bases[..., None] == jnp.arange(table.shape[0], dtype=jnp.int32)).astype(table.dtype)
+    return jnp.einsum("sbv,vc->sbc", onehot, table, preferred_element_type=jnp.float32)
 
 
 def gather_blocks(block, bits, me):
@@ -84,7 +82,7 @@
     ch_count = lax.axis_size("ch")
     ch_bits = ch_count.bit_length() - 1
     me = lax.axis_index("ch")
-    table = embed_table.astype(jnp.float32)
+    table = embed_table
     base_in = jnp.where(masked == 1, 4, tokens)
     comp = jnp.where(masked == 1, 4, 3 - tokens)
     arrived = mirror(hidden_reverse, "seq", seq_count)

time: 173 us -> 175 us (1.012)
  other arithmetic: 26.3 us -> 15.4 us
  waiting for transfers between devices: 76.9 us -> 83.9 us
  matrix products: 33.3 us -> 35.6 us
  local copies, waits for them, and re-layouts: 8 us -> 10.2 us
  starting transfers between devices: 19 us -> 20.8 us
    ppermute x3, waiting for transfers between devices: 34.7 us -> 41.7 us  [mirror(): return lax.ppermute(value, axes, [(k, count - 1 - k) for k in range(count)])]
    reduce_sum x1 -> x0, other arithmetic: 6.04 us -> none  [local(): jnp.sum(x_fwd * x_fwd, axis=-1)]
    dot_general x0 -> x3, matrix products: none -> 5.29 us  [embedded(): jnp.einsum('sbv,vc->sbc', onehot, table, preferred_element_type=jnp.float32)]
    convert_element_type x2, other arithmetic: 6.07 us -> 1.9 us  [local(): return (out_forward.astype(jnp.bfloat16), out_reverse.astype(jnp.bfloat16))]
    unnamed x20 -> x28, local copies, waits for them, and re-layouts: 3.77 us -> 6.88 us
    convert_element_type x1 -> x0, other arithmetic: 2.8 us -> none  [local(): (x_rfp * lax.rsqrt(square_rev[..., None] / width + 1e-05) * norm_gain).as...]
  transfers between devices with their start and end apart: 9 -> 9, of which waited for: 7 -> 7; matrix products, arithmetic and copies ran while one was open for 7% -> 3% of each run, Pallas kernels for 0% -> 0%
where the time goes in v5:
time: 175 us; the launch traced here: 174 us
  waiting for transfers between devices  83.9 us (48%)
  matrix products  35.6 us (20%)
  starting transfers between devices  20.8 us (12%)
  other arithmetic  15.4 us (9%)
  local copies, waits for them, and re-layouts  10.2 us (6%)
  blocking collectives  6.83 us (4%)
    ppermute x3, waiting for transfers between devices, mirror(): return lax.ppermute(value, axes, [(k, count - 1 - k) for k in range(count)])  41.7 us
    ppermute x4, waiting for transfers between devices, partner(): lax.ppermute(value, axis, [(k, k ^ mask) for k in range(lax.axis_size(axi...  41.5 us
    dot_general x1, matrix products, local(): jnp.dot(act_rev, w_flip, preferred_element_type=jnp.float32)  9.01 us
    ppermute x4, starting transfers between devices, partner(): lax.ppermute(value, axis, [(k, k ^ mask) for k in range(lax.axis_size(axi...  7.49 us
    ppermute x3, starting transfers between devices, mirror(): return lax.ppermute(value, axes, [(k, count - 1 - k) for k in range(count)])  7.1 us
    unnamed x28, local copies, waits for them, and re-layouts  6.88 us
    psum x1, blocking collectives, local(): lax.psum((jnp.sum(x_fwd * x_fwd, axis=-1), jnp.sum(x_rfp * x_rfp, axis=-1...  6.83 us
    dot_general x1, matrix products, local(): jnp.dot(act_fwd, w_out, preferred_element_type=jnp.float32)  6.08 us
  transfers between devices with their start and end apart: 9, of which 7 were waited for; matrix products, arithmetic and copies ran while one was open for 3% of the time, Pallas kernels for 0%

profile of v5, /device:TPU:17, one launch (start us, length us, event | category | flops | bytes accessed | tf_op | source)
XLA Modules:
  0.0 173.8 jit_solution(11345908673375927651)
XLA Ops:
  5.8 2.4 %convolution_add_fusion.1 = f32[2,512,256]{2,1,0:T(8,128)} fusion(bf16[2,512,256]{2,1,0:T(8,128)(2,1)} %param.14, s32[2,512]{1,0:T(2,128)S(1)} %rev.4, bf16[5,256]{1,0:T(8,128)(2,1)} %param.15), kind=kOutput, calls=%fused_computation.42 | convolution fusion | flops 3150848 | bytes 1579520 | tf_op jit(solution)/shard_map/sbv,vc->sbc/dot_general | solution.py:33
  8.2 19.5 %collective-permute-done = bf16[2,512,256]{2,1,0:T(8,128)(2,1)} collective-permute-done((bf16[2,512,256]{2,1,0:T(8,128)(2,1)}, bf16[2,512,256]{2,1,0:T(8,128)(2,1)}, u32[]{:S(2)}, u32[]{:S(2)}) %collective-permute-start) | collective-permute-done | bytes 524320 | tf_op jit(solution)/shard_map/ppermute | solution.py:8
  27.7 2.6 %convolution_convert_fusion.2 = bf16[1024,256]{1,0:T(8,128)(2,1)S(1)} fusion(bf16[1024,256]{1,0:T(8,128)(2,1)} %bitcast.3, s32[1024]{0:T(1024)S(1)} %get-tuple-element.32, s32[1024]{0:T(1024)S(1)} %get-tuple-element.33, s32[1024]{0:T(1024)S(1)} %get-tuple-element.31, s32[1024]{0:T(1024)S(1)} %get-tuple-element.34, ...), kind=kOutput, calls=%fused_computation.46 | convolution fusion | flops 545521664 | bytes 1067008 | tf_op jit(solution)/shard_map/dot_general | solution.py:94
  31.8 6.8 %all-reduce = (f32[2,512]{1,0:T(2,128)S(1)}, f32[2,512]{1,0:T(2,128)S(1)}) all-reduce(f32[2,512]{1,0:T(2,128)S(1)} %get-tuple-element.27, f32[2,512]{1,0:T(2,128)S(1)} %get-tuple-element.29), channel_id=1, replica_groups=mesh['seq'=8,'ch'=4] {'ch'}, use_global_device_ids=true, to_apply=%region_3.4 | all-reduce | flops 2048 | bytes 16384 | tf_op jit(solution)/shard_map/psum | solution.py:105
  40.2 2.2 %collective-permute-start.2 = (bf16[2,2,3,256]{3,2,1,0:T(4,128)(2,1)S(1)}, bf16[2,2,3,256]{3,2,1,0:T(4,128)(2,1)S(1)}, u32[]{:S(2)}, u32[]{:S(2)}) collective-permute-start(bf16[2,2,3,256]{3,2,1,0:T(4,128)(2,1)S(1)} %get-tuple-element.14), channel_id=1, source_target_pairs={{0,4},{4,8},{8,12},{12,16},{16,20},{20,24},{24,28},{1,5},{5,9},{9,... | collective-permute-start | bytes 18440 | tf_op jit(solution)/shard_map/ppermute | solution.py:23
  42.5 4.0 %collective-permute-start.3 = (bf16[2,2,3,256]{3,2,1,0:T(4,128)(2,1)S(1)}, bf16[2,2,3,256]{3,2,1,0:T(4,128)(2,1)S(1)}, u32[]{:S(2)}, u32[]{:S(2)}) collective-permute-start(bf16[2,2,3,256]{3,2,1,0:T(4,128)(2,1)S(1)} %get-tuple-element.15), channel_id=1, source_target_pairs={{4,0},{8,4},{12,8},{16,12},{20,16},{24,20},{28,24},{5,1},{9,5},{13... | collective-permute-start | bytes 18440 | tf_op jit(solution)/shard_map/ppermute | solution.py:25
  50.7 21.8 %collective-permute-done.4 = bf16[1,2048,256]{2,1,0:T(8,128)(2,1)} collective-permute-done((bf16[1,2048,256]{2,1,0:T(8,128)(2,1)S(1)}, bf16[1,2048,256]{2,1,0:T(8,128)(2,1)}, u32[]{:S(2)}, u32[]{:S(2)}) %collective-permute-start.4) | collective-permute-done | bytes 1048608 | tf_op jit(solution)/shard_map/ppermute | solution.py:13
  72.4 2.7 %select_bitcast_fusion.4 = (bf16[1,1,2048,256]{3,2,1,0:T(8,128)(2,1)S(1)}, bf16[1,1,2048,256]{3,2,1,0:T(8,128)(2,1)}) fusion(bf16[1,2048,256]{2,1,0:T(8,128)(2,1)} %collective-permute-done.4, pred[]{:T(512)S(6)} %eq.95, bf16[1,2048,256]{2,1,0:T(8,128)(2,1)} %bitcast.213), kind=kLoop, calls=%fused_computation.98 | loop fusion | flops 1048576 | bytes 4194305 | tf_op jit(solution)/shard_map/stack | solution.py:43
  75.1 2.7 %maximum_bitcast_fusion = bf16[2,2048,256]{2,1,0:T(8,128)(2,1)} fusion(bf16[1,1,2048,256]{3,2,1,0:T(8,128)(2,1)} %get-tuple-element.13, bf16[1,1,2048,256]{3,2,1,0:T(8,128)(2,1)S(1)} %get-tuple-element.12), kind=kLoop, calls=%fused_computation.20 | loop fusion | flops 1048576 | bytes 4194304 | tf_op jit(solution)/shard_map/reshape | solution.py:43
  77.9 2.7 %collective-permute-start.5 = (bf16[2,2048,256]{2,1,0:T(8,128)(2,1)}, bf16[2,2048,256]{2,1,0:T(8,128)(2,1)}, u32[]{:S(2)}, u32[]{:S(2)}) collective-permute-start(bf16[2,2048,256]{2,1,0:T(8,128)(2,1)} %maximum_bitcast_fusion), channel_id=1, source_target_pairs={{0,1},{1,0},{2,3},{3,2},{4,5},{5,4},{6,7},{7,6},{8,9},{9,8},{10,11... | collective-permute-start | bytes 6291464 | tf_op jit(solution)/shard_map/ppermute | solution.py:13
  80.6 4.1 %collective-permute-done.5 = bf16[2,2048,256]{2,1,0:T(8,128)(2,1)} collective-permute-done((bf16[2,2048,256]{2,1,0:T(8,128)(2,1)}, bf16[2,2048,256]{2,1,0:T(8,128)(2,1)}, u32[]{:S(2)}, u32[]{:S(2)}) %collective-permute-start.5) | collective-permute-done | bytes 2097184 | tf_op jit(solution)/shard_map/ppermute | solution.py:13
  84.7 2.1 %select_bitcast_fusion.2 = (bf16[2,1,2048,256]{3,2,0,1:T(8,128)(2,1)S(1)}, bf16[2,1,2048,256]{3,2,0,1:T(8,128)(2,1)S(1)}) fusion(bf16[2,2048,256]{2,1,0:T(8,128)(2,1)} %collective-permute-done.5, pred[]{:T(512)S(6)} %eq.96, bf16[1,1,2048,256]{3,2,1,0:T(8,128)(2,1)} %get-tuple-element.13, bf16[1,1,2048,256]{3,2,1,0:T(8,128)(2,1)S(1)} %get-tuple-element.12), kind=kLoop, calls=%fused_computation.35 | loop fusion | flops 3145728 | bytes 8388609 | tf_op jit(solution)/shard_map/stack | solution.py:43
  87.5 4.5 %fusion.128 = f32[2048,1024,1]{1,0,2:T(8,128)S(1)} fusion(bf16[4,2048,256]{2,1,0:T(8,128)(2,1)S(1)} %bitcast.215, bf16[4,256,1024]{2,1,0:T(8,128)(2,1)S(1)} %bitcast.210), kind=kOutput, calls=%fused_computation.170 | convolution fusion | flops 4294967296 | bytes 14680064 | tf_op jit(solution)/shard_map/dot_general | solution.py:125
  92.1 5.4 %fusion = bf16[2048,1024]{1,0:T(8,128)(2,1)S(1)} fusion(f32[2048,1024,1]{1,0,2:T(8,128)S(1)} %fusion.128, bf16[4,2048,256]{2,1,0:T(8,128)(2,1)S(1)} %bitcast.216, bf16[4,256,1024]{2,1,0:T(8,128)(2,1)S(1)} %bitcast.232), kind=kOutput, calls=%fused_computation.1 | convolution fusion | flops 4307550208 | bytes 18874368 | tf_op jit(solution)/shard_map/dot_general | solution.py:128
  99.7 9.0 %fusion.9 = f32[1024,1024]{0,1:T(8,128)} fusion(bf16[1024,1024]{1,0:T(8,128)(2,1)} %param.21, s32[1024]{0:T(1024)S(1)} %get-tuple-element.38, s32[1024]{0:T(1024)S(1)} %get-tuple-element.39, s32[1024]{0:T(1024)S(1)} %get-tuple-element.37, s32[1024]{0:T(1024)S(1)} %get-tuple-element.40, pred[1024]{0:T(1024)(128)(4,1)S(1)} %get-tuple-element.41, ...), kind=kOutput, calls=%fused_computation.16 | convolution fusion | flops 4305453056 | bytes 8407040 | tf_op jit(solution)/shard_map/dot_general | solution.py:137
  108.7 6.1 %fusion.28 = f32[1024,1024]{0,1:T(8,128)S(1)} fusion(f32[1024,1024]{0,1:T(8,128)} %fusion.9, bf16[1024,1024]{1,0:T(8,128)(2,1)} %param.21, bf16[2048,1024]{1,0:T(8,128)(2,1)} %copy-done.7), kind=kOutput, calls=%fused_computation.40 | convolution fusion | flops 2148532224 | bytes 12582912 | tf_op jit(solution)/shard_map/dot_general | solution.py:137
  114.8 2.5 %fusion.126 = (f32[1024,2,1,256]{0,3,2,1:T(8,128)}, f32[1024,2,1,256]{0,3,2,1:T(8,128)}) fusion(f32[1024,2,2,256]{0,3,2,1:T(8,128)S(1)} %bitcast.214), kind=kLoop, calls=%fused_computation.168 | loop fusion | bytes 8388608 | tf_op jit(solution)/shard_map/slice | solution.py:53
  119.3 2.9 %copy.17 = f32[1024,2,1,256]{3,0,1,2:T(8,128)} copy(f32[1024,2,1,256]{0,3,2,1:T(8,128)} %get-tuple-element.9) | data formatting | bytes 4194304
  122.4 2.2 %collective-permute-start.6 = (f32[1024,2,256]{2,0,1:T(8,128)S(1)}, f32[1024,2,256]{2,0,1:T(8,128)S(1)}, u32[]{:S(2)}, u32[]{:S(2)}) collective-permute-start(f32[1024,2,256]{2,0,1:T(8,128)S(1)} %select_bitcast_fusion), channel_id=1, source_target_pairs={{0,1},{1,0},{2,3},{3,2},{4,5},{5,4},{6,7},{7,6},{8,9},{9,8},{10,11... | collective-permute-start | bytes 6291464 | tf_op jit(solution)/shard_map/ppermute | solution.py:13
  124.6 3.8 %collective-permute-done.6 = f32[1024,2,256]{2,0,1:T(8,128)S(1)} collective-permute-done((f32[1024,2,256]{2,0,1:T(8,128)S(1)}, f32[1024,2,256]{2,0,1:T(8,128)S(1)}, u32[]{:S(2)}, u32[]{:S(2)}) %collective-permute-start.6) | collective-permute-done | bytes 2097184 | tf_op jit(solution)/shard_map/ppermute | solution.py:13
  130.2 11.8 %collective-permute-done.7 = bf16[1024,1,256]{2,0,1:T(8,128)(2,1)S(1)} collective-permute-done((bf16[1024,1,256]{2,0,1:T(8,128)(2,1)S(1)}, bf16[1024,1,256]{2,0,1:T(8,128)(2,1)S(1)}, u32[]{:S(2)}, u32[]{:S(2)}) %collective-permute-start.7) | collective-permute-done | bytes 524320 | tf_op jit(solution)/shard_map/ppermute | solution.py:13
  142.8 2.1 %convolution_convert_fusion = bf16[1024,256]{1,0:T(8,128)(2,1)S(1)} fusion(s32[1024]{0:T(1024)S(1)} %get-tuple-element.32, s32[1024]{0:T(1024)S(1)} %get-tuple-element.33, s32[1024]{0:T(1024)S(1)} %get-tuple-element.31, s32[1024]{0:T(1024)S(1)} %get-tuple-element.34, pred[1024]{0:T(1024)(128)(4,1)S(1)} %get-tuple-element.35, ...), kind=kOutput, calls=%fused_computation.44 | convolution fusion | flops 545521664 | bytes 1067008 | tf_op jit(solution)/shard_map/dot_general | solution.py:144
  144.9 4.7 %collective-permute-start.8 = (bf16[2,512,256]{2,1,0:T(8,128)(2,1)S(1)}, bf16[2,512,256]{2,1,0:T(8,128)(2,1)S(1)}, u32[]{:S(2)}, u32[]{:S(2)}) collective-permute-start(bf16[2,512,256]{2,1,0:T(8,128)(2,1)S(1)} %bitcast.233), channel_id=1, source_target_pairs={{0,31},{1,30},{2,29},{3,28},{4,27},{5,26},{6,25},{7,24},{8,23},{9,... | collective-permute-start | bytes 1572872 | tf_op jit(solution)/shard_map/ppermute | solution.py:8
  150.6 22.2 %collective-permute-done.8 = bf16[2,512,256]{2,1,0:T(8,128)(2,1)S(1)} collective-permute-done((bf16[2,512,256]{2,1,0:T(8,128)(2,1)S(1)}, bf16[2,512,256]{2,1,0:T(8,128)(2,1)S(1)}, u32[]{:S(2)}, u32[]{:S(2)}) %collective-permute-start.8) | collective-permute-done | bytes 524320 | tf_op jit(solution)/shard_map/ppermute | solution.py:8
  (66 shorter events, 21.8 us)
Async XLA Ops:
  0.6 86.9 %copy-start = (bf16[1024,1024]{1,0:T(8,128)(2,1)S(1)}, bf16[1024,1024]{1,0:T(8,128)(2,1)}, u32[]{:S(2)}) copy-start(bf16[1024,1024]{1,0:T(8,128)(2,1)} %param.19) | copy-start | bytes 6291460
  1.5 3.9 %collective-permute-start.1 = (s32[2,512]{1,0:T(2,128)S(1)}, s32[2,512]{1,0:T(2,128)S(1)}, u32[]{:S(2)}, u32[]{:S(2)}) collective-permute-start(s32[2,512]{1,0:T(2,128)S(1)} %get-tuple-element.23), channel_id=1, source_target_pairs={{0,28},{4,24},{8,20},{12,16},{16,12},{20,8},{24,4},{28,0},{1,29},{... | collective-permute-start | bytes 12296 | tf_op jit(solution)/shard_map/ppermute | solution.py:8
  2.6 25.1 %collective-permute-start = (bf16[2,512,256]{2,1,0:T(8,128)(2,1)}, bf16[2,512,256]{2,1,0:T(8,128)(2,1)}, u32[]{:S(2)}, u32[]{:S(2)}) collective-permute-start(bf16[2,512,256]{2,1,0:T(8,128)(2,1)} %param.14), channel_id=1, source_target_pairs={{0,28},{4,24},{8,20},{12,16},{16,12},{20,8},{24,4},{28,0},{1,29},{... | collective-permute-start | bytes 1572872 | tf_op jit(solution)/shard_map/ppermute | solution.py:8
  5.4 33.2 %copy-start.3 = (f32[2,512,256]{2,1,0:T(8,128)}, f32[2,512,256]{2,1,0:T(8,128)S(1)}, u32[]{:S(2)}) copy-start(f32[2,512,256]{2,1,0:T(8,128)S(1)} %get-tuple-element.30) | copy-start | bytes 3145732
  27.7 2.7 %copy-start.8 = (bf16[5,256]{1,0:T(8,128)(2,1)S(1)}, bf16[5,256]{1,0:T(8,128)(2,1)}, u32[]{:S(2)}) copy-start(bf16[5,256]{1,0:T(8,128)(2,1)} %param.15) | copy-start | bytes 7684
  27.7 10.9 %copy-start.11 = (f32[256]{0:T(256)S(1)}, f32[256]{0:T(256)}, u32[]{:S(2)}) copy-start(f32[256]{0:T(256)} %param.18) | copy-start | bytes 3076
  30.4 16.1 %copy-start.9 = (f32[7,256]{1,0:T(8,128)S(1)}, f32[7,256]{1,0:T(8,128)}, u32[]{:S(2)}) copy-start(f32[7,256]{1,0:T(8,128)} %param.16) | copy-start | bytes 21508
  30.4 17.0 %copy-start.10 = (f32[256]{0:T(256)S(1)}, f32[256]{0:T(256)}, u32[]{:S(2)}) copy-start(f32[256]{0:T(256)} %param.17) | copy-start | bytes 3076
  40.2 6.2 %collective-permute-start.2 = (bf16[2,2,3,256]{3,2,1,0:T(4,128)(2,1)S(1)}, bf16[2,2,3,256]{3,2,1,0:T(4,128)(2,1)S(1)}, u32[]{:S(2)}, u32[]{:S(2)}) collective-permute-start(bf16[2,2,3,256]{3,2,1,0:T(4,128)(2,1)S(1)} %get-tuple-element.14), channel_id=1, source_target_pairs={{0,4},{4,8},{8,12},{12,16},{16,20},{20,24},{24,28},{1,5},{5,9},{9,... | collective-permute-start | bytes 18440 | tf_op jit(solution)/shard_map/ppermute | solution.py:23
  42.5 4.8 %collective-permute-start.3 = (bf16[2,2,3,256]{3,2,1,0:T(4,128)(2,1)S(1)}, bf16[2,2,3,256]{3,2,1,0:T(4,128)(2,1)S(1)}, u32[]{:S(2)}, u32[]{:S(2)}) collective-permute-start(bf16[2,2,3,256]{3,2,1,0:T(4,128)(2,1)S(1)} %get-tuple-element.15), channel_id=1, source_target_pairs={{4,0},{8,4},{12,8},{16,12},{20,16},{24,20},{28,24},{5,1},{9,5},{13... | collective-permute-start | bytes 18440 | tf_op jit(solution)/shard_map/ppermute | solution.py:25
  49.4 23.1 %copy-start.5 = (bf16[4,512,256]{2,1,0:T(8,128)(2,1)}, bf16[4,512,256]{2,1,0:T(8,128)(2,1)S(1)}, u32[]{:S(2)}) copy-start(bf16[4,512,256]{2,1,0:T(8,128)(2,1)S(1)} %pad_maximum_fusion.1) | copy-start | bytes 3145732
  49.4 23.1 %collective-permute-start.4 = (bf16[1,2048,256]{2,1,0:T(8,128)(2,1)S(1)}, bf16[1,2048,256]{2,1,0:T(8,128)(2,1)}, u32[]{:S(2)}, u32[]{:S(2)}) collective-permute-start(bf16[1,2048,256]{2,1,0:T(8,128)(2,1)S(1)} %bitcast.212), channel_id=1, source_target_pairs={{0,2},{1,3},{2,0},{3,1},{4,6},{5,7},{6,4},{7,5},{8,10},{9,11},{10,... | collective-permute-start | bytes 3145736 | tf_op jit(solution)/shard_map/ppermute | solution.py:13
  77.9 6.8 %collective-permute-start.5 = (bf16[2,2048,256]{2,1,0:T(8,128)(2,1)}, bf16[2,2048,256]{2,1,0:T(8,128)(2,1)}, u32[]{:S(2)}, u32[]{:S(2)}) collective-permute-start(bf16[2,2048,256]{2,1,0:T(8,128)(2,1)} %maximum_bitcast_fusion), channel_id=1, source_target_pairs={{0,1},{1,0},{2,3},{3,2},{4,5},{5,4},{6,7},{7,6},{8,9},{9,8},{10,11... | collective-permute-start | bytes 6291464 | tf_op jit(solution)/shard_map/ppermute | solution.py:13
  87.5 4.5 %copy-start.12 = (bf16[1024,1024]{1,0:T(8,128)(2,1)S(1)}, bf16[1024,1024]{1,0:T(8,128)(2,1)}, u32[]{:S(2)}) copy-start(bf16[1024,1024]{1,0:T(8,128)(2,1)} %param.20) | copy-start | bytes 6291460
  97.5 2.0 %copy-start.7 = (bf16[2048,1024]{1,0:T(8,128)(2,1)}, bf16[2048,1024]{1,0:T(8,128)(2,1)S(1)}, u32[]{:S(2)}) copy-start(bf16[2048,1024]{1,0:T(8,128)(2,1)S(1)} %fusion) | copy-start | bytes 12582916
  122.1 6.2 %copy-start.2 = (f32[1024,2,1,256]{3,0,1,2:T(8,128)S(1)}, f32[1024,2,1,256]{3,0,1,2:T(8,128)}, u32[]{:S(2)}) copy-start(f32[1024,2,1,256]{3,0,1,2:T(8,128)} %copy.17) | copy-start | bytes 6291460
  122.4 6.0 %collective-permute-start.6 = (f32[1024,2,256]{2,0,1:T(8,128)S(1)}, f32[1024,2,256]{2,0,1:T(8,128)S(1)}, u32[]{:S(2)}, u32[]{:S(2)}) collective-permute-start(f32[1024,2,256]{2,0,1:T(8,128)S(1)} %select_bitcast_fusion), channel_id=1, source_target_pairs={{0,1},{1,0},{2,3},{3,2},{4,5},{5,4},{6,7},{7,6},{8,9},{9,8},{10,11... | collective-permute-start | bytes 6291464 | tf_op jit(solution)/shard_map/ppermute | solution.py:13
  128.9 13.2 %collective-permute-start.7 = (bf16[1024,1,256]{2,0,1:T(8,128)(2,1)S(1)}, bf16[1024,1,256]{2,0,1:T(8,128)(2,1)S(1)}, u32[]{:S(2)}, u32[]{:S(2)}) collective-permute-start(bf16[1024,1,256]{2,0,1:T(8,128)(2,1)S(1)} %fusion.67), channel_id=1, source_target_pairs={{0,2},{1,3},{2,0},{3,1},{4,6},{5,7},{6,4},{7,5},{8,10},{9,11},{10,... | collective-permute-start | bytes 1572872 | tf_op jit(solution)/shard_map/ppermute | solution.py:13
  142.8 6.8 %copy-start.4 = (f32[2,512,256]{2,1,0:T(8,128)S(1)}, f32[2,512,256]{2,1,0:T(8,128)}, u32[]{:S(2)}) copy-start(f32[2,512,256]{2,1,0:T(8,128)} %copy-done.3) | copy-start | bytes 3145732
  142.8 30.0 %copy-start.6 = (f32[2,512,256]{2,1,0:T(8,128)S(1)}, f32[2,512,256]{2,1,0:T(8,128)}, u32[]{:S(2)}) copy-start(f32[2,512,256]{2,1,0:T(8,128)} %convolution_add_fusion.1) | copy-start | bytes 3145732
  142.8 31.0 %copy-start.1 = (bf16[1024,1024]{1,0:T(8,128)(2,1)S(1)}, bf16[1024,1024]{1,0:T(8,128)(2,1)}, u32[]{:S(2)}) copy-start(bf16[1024,1024]{1,0:T(8,128)(2,1)} %param.19) | copy-start | bytes 6291460
  144.9 27.9 %collective-permute-start.8 = (bf16[2,512,256]{2,1,0:T(8,128)(2,1)S(1)}, bf16[2,512,256]{2,1,0:T(8,128)(2,1)S(1)}, u32[]{:S(2)}, u32[]{:S(2)}) collective-permute-start(bf16[2,512,256]{2,1,0:T(8,128)(2,1)S(1)} %bitcast.233), channel_id=1, source_target_pairs={{0,31},{1,30},{2,29},{3,28},{4,27},{5,26},{6,25},{7,24},{8,23},{9,... | collective-permute-start | bytes 1572872 | tf_op jit(solution)/shard_map/ppermute | solution.py:8

commit v6 on v4

--- a/solution.py
+++ b/solution.py
@@ -102,20 +102,49 @@
     taps = conv_kernel.shape[0]
     half_width = taps // 2
 
+    n = seq_count
+    place = lax.axis_index("seq")
+    code = tokens + 4 * masked
+    up = [(k, k + 1) for k in range(n - 1)]
+    down = [(k + 1, k) for k in range(n - 1)]
+    left_f, left_code = lax.ppermute((hidden_forward[:, -half_width:], code[:, -half_width:]), "seq", up)
+    right_f, right_code = lax.ppermute((hidden_forward[:, :half_width], code[:, :half_width]), "seq", down)
+    left_r = lax.ppermute(hidden_reverse[:, :half_width], "seq", [(k, n - k) for k in range(1, n)])
+    right_r = lax.ppermute(hidden_reverse[:, -half_width:], "seq", [(k, n - 2 - k) for k in range(n - 1)])
+    edge_code = jnp.concatenate([left_code, right_code], axis=1)
+    edge_masked = edge_code >= 4
+    edge_f = jnp.concatenate([left_f, right_f], axis=1).astype(jnp.float32) + embedded(
+        jnp.where(edge_masked, 4, edge_code), table
+    )
+    edge_r = jnp.concatenate([jnp.flip(left_r, axis=1), jnp.flip(right_r, axis=1)], axis=1).astype(
+        jnp.float32
+    ) + embedded(jnp.where(edge_masked, 4, 3 - edge_code), table)
+    side = jnp.arange(2 * half_width) < half_width
+    valid = jnp.where(side, place > 0, place < n - 1)[None, :, None]
+
     x_fwd = hidden_forward.astype(jnp.float32) + embedded(base_in, table)
     x_rfp = rev_here.astype(jnp.float32) + embedded(comp, table)
-    square_fwd, square_rev = lax.psum(
-        (jnp.sum(x_fwd * x_fwd, axis=-1), jnp.sum(x_rfp * x_rfp, axis=-1)), "ch"
-    )
-    normed_fwd = (x_fwd * lax.rsqrt(square_fwd[..., None] / width + 1e-05) * norm_gain).astype(
-        jnp.bfloat16
-    )
-    normed_rev = (x_rfp * lax.rsqrt(square_rev[..., None] / width + 1e-05) * norm_gain).astype(
-        jnp.bfloat16
-    )
+    square_fwd, square_rev, square_ef, square_er = lax.psum(
+        (
+            jnp.sum(x_fwd * x_fwd, axis=-1),
+            jnp.sum(x_rfp * x_rfp, axis=-1),
+            jnp.sum(edge_f * edge_f, axis=-1),
+            jnp.sum(edge_r * edge_r, axis=-1),
+        ),
+        "ch",
+    )
+
+    def normed(x, square):
+        return (x * lax.rsqrt(square[..., None] / width + 1e-05) * norm_gain).astype(jnp.bfloat16)
+
+    normed_fwd = normed(x_fwd, square_fwd)
+    normed_rev = normed(x_rfp, square_rev)
+    edges = jnp.where(valid, jnp.stack([normed(edge_f, square_ef), normed(edge_r, square_er)]), 0)
     stacked = jnp.stack([normed_fwd, normed_rev])
     length = stacked.shape[2]
-    padded = padded_2(stacked, "seq", 2, half_width).astype(jnp.float32)
+    padded = jnp.concatenate(
+        [edges[:, :, :half_width], stacked, edges[:, :, half_width:]], axis=2
+    ).astype(jnp.float32)
     conv_f = jnp.zeros(normed_fwd.shape, jnp.float32) + conv_bias
     conv_r = jnp.zeros(normed_rev.shape, jnp.float32) + conv_bias
     for offset in range(taps):

time: 173 us -> 184 us (1.064)
  starting transfers between devices: 19 us -> 23.8 us
  blocking collectives: 6.83 us -> 10.6 us
  local copies, waits for them, and re-layouts: 8 us -> 10.6 us
    ppermute x2 -> x6, starting transfers between devices: 6.18 us -> 18.4 us  [the longest x2 7.94 us: local(): lax.ppermute((hidden_forward[:, :half_width], code[:, :half_width]), 'seq...]
    ppermute x3, starting transfers between devices: 7.11 us -> 2.35 us  [mirror(): return lax.ppermute(value, axes, [(k, count - 1 - k) for k in range(count)])]
    psum x1, blocking collectives: 6.83 us -> 10.6 us  [local(): lax.psum((jnp.sum(x_fwd * x_fwd, axis=-1), jnp.sum(x_rfp * x_rfp, axis=-1...]
    ppermute x3, waiting for transfers between devices: 34.7 us -> 31.3 us  [mirror(): return lax.ppermute(value, axes, [(k, count - 1 - k) for k in range(count)])]
    ppermute x4, starting transfers between devices: 5.74 us -> 3.04 us  [partner(): lax.ppermute(value, axis, [(k, k ^ mask) for k in range(lax.axis_size(axi...]
    ppermute x4, waiting for transfers between devices: 41.5 us -> 44.2 us  [partner(): lax.ppermute(value, axis, [(k, k ^ mask) for k in range(lax.axis_size(axi...]
    unnamed x20 -> x18, local copies, waits for them, and re-layouts: 3.77 us -> 3.79 us
  transfers between devices with their start and end apart: 9 -> 13, of which waited for: 7 -> 7; matrix products, arithmetic and copies ran while one was open for 7% -> 9% of each run, Pallas kernels for 0% -> 0%
where the time goes in v6:
time: 184 us; the launch traced here: 183 us
  waiting for transfers between devices  75.8 us (41%)
  matrix products  33.4 us (18%)
  other arithmetic  27.6 us (15%)
  starting transfers between devices  23.8 us (13%)
  local copies, waits for them, and re-layouts  10.6 us (6%)
  blocking collectives  10.6 us (6%)
    ppermute x4, waiting for transfers between devices, partner(): lax.ppermute(value, axis, [(k, k ^ mask) for k in range(lax.axis_size(axi...  44.2 us
    ppermute x3, waiting for transfers between devices, mirror(): return lax.ppermute(value, axes, [(k, count - 1 - k) for k in range(count)])  31.3 us
    psum x1, blocking collectives, local(): lax.psum((jnp.sum(x_fwd * x_fwd, axis=-1), jnp.sum(x_rfp * x_rfp, axis=-1...  10.6 us
    dot_general x1, matrix products, local(): jnp.dot(act_rev, w_flip, preferred_element_type=jnp.float32)  9.71 us
    ppermute x2, starting transfers between devices, local(): lax.ppermute((hidden_forward[:, :half_width], code[:, :half_width]), 'seq...  7.94 us
    dot_general x1, matrix products, local(): jnp.dot(act_fwd, w_out, preferred_element_type=jnp.float32)  6.08 us
    convert_element_type x2, other arithmetic, local(): return (out_forward.astype(jnp.bfloat16), out_reverse.astype(jnp.bfloat16))  6.07 us
    reduce_sum x1, other arithmetic, local(): jnp.sum(x_fwd * x_fwd, axis=-1)  6.04 us
  transfers between devices with their start and end apart: 13, of which 7 were waited for; matrix products, arithmetic and copies ran while one was open for 9% of the time, Pallas kernels for 0%

profile of v6, /device:TPU:17, one launch (start us, length us, event | category | flops | bytes accessed | tf_op | source)
XLA Modules:
  0.0 182.9 jit_solution(2299449737289376548)
XLA Ops:
  3.5 2.2 %collective-permute-start.2 = (s32[2,3]{1,0:T(2,128)S(1)}, s32[2,3]{1,0:T(2,128)S(1)}, u32[]{:S(2)}, u32[]{:S(2)}) collective-permute-start(s32[2,3]{1,0:T(2,128)S(1)} %get-tuple-element.54), channel_id=1, source_target_pairs={{0,4},{4,8},{8,12},{12,16},{16,20},{20,24},{24,28},{1,5},{5,9},{9,... | collective-permute-start | bytes 80 | tf_op jit(solution)/shard_map/ppermute | solution.py:110
  5.6 4.0 %collective-permute-start.3 = (s32[2,3]{1,0:T(2,128)S(1)}, s32[2,3]{1,0:T(2,128)S(1)}, u32[]{:S(2)}, u32[]{:S(2)}) collective-permute-start(s32[2,3]{1,0:T(2,128)S(1)} %get-tuple-element.55), channel_id=1, source_target_pairs={{4,0},{8,4},{12,8},{16,12},{20,16},{24,20},{28,24},{5,1},{9,5},{13... | collective-permute-start | bytes 80 | tf_op jit(solution)/shard_map/ppermute | solution.py:111
  11.0 5.4 %collective-permute-start.5 = (bf16[2,3,256]{2,1,0:T(4,128)(2,1)S(1)}, bf16[2,3,256]{2,1,0:T(4,128)(2,1)S(1)}, u32[]{:S(2)}, u32[]{:S(2)}) collective-permute-start(bf16[2,3,256]{2,1,0:T(4,128)(2,1)S(1)} %get-tuple-element.27), channel_id=1, source_target_pairs={{0,24},{4,20},{8,16},{12,12},{16,8},{20,4},{24,0},{1,25},{5,21},{9... | collective-permute-start | bytes 9224 | tf_op jit(solution)/shard_map/ppermute | solution.py:113
  19.2 2.3 %collective-permute-start = (bf16[2,3,256]{2,1,0:T(4,128)(2,1)S(1)}, bf16[2,3,256]{2,1,0:T(4,128)(2,1)S(1)}, u32[]{:S(2)}, u32[]{:S(2)}) collective-permute-start(bf16[2,3,256]{2,1,0:T(4,128)(2,1)S(1)} %get-tuple-element.24), channel_id=1, source_target_pairs={{0,4},{4,8},{8,12},{12,16},{16,20},{20,24},{24,28},{1,5},{5,9},{9,... | collective-permute-start | bytes 9224 | tf_op jit(solution)/shard_map/ppermute | solution.py:110
  21.5 3.9 %collective-permute-start.1 = (bf16[2,3,256]{2,1,0:T(4,128)(2,1)S(1)}, bf16[2,3,256]{2,1,0:T(4,128)(2,1)S(1)}, u32[]{:S(2)}, u32[]{:S(2)}) collective-permute-start(bf16[2,3,256]{2,1,0:T(4,128)(2,1)S(1)} %get-tuple-element.25), channel_id=1, source_target_pairs={{4,0},{8,4},{12,8},{16,12},{20,16},{24,20},{28,24},{5,1},{9,5},{13... | collective-permute-start | bytes 9224 | tf_op jit(solution)/shard_map/ppermute | solution.py:111
  26.7 6.0 %multiply_reduce_fusion.1 = (f32[2,512]{1,0:T(2,128)S(1)}, f32[2,512,256]{2,1,0:T(8,128)}) fusion(f32[256]{0:T(256)S(1)} %bitcast.265, pred[2,512]{1,0:T(4,128)(4,1)S(1)} %get-tuple-element.77, f32[256]{0:T(256)S(1)} %bitcast.257, pred[2,512]{1,0:T(4,128)(4,1)S(1)} %get-tuple-element.79, f32[256]{0:T(256)S(1)} %bitcast.249, ...), kind=kLoop, calls=%fused_computation.103 | loop fusion | flops 6290432 | bytes 2116608 | tf_op jit(solution)/shard_map/reduce_sum | solution.py:129
  32.7 18.2 %collective-permute-done.6 = bf16[2,512,256]{2,1,0:T(8,128)(2,1)S(1)} collective-permute-done((bf16[2,512,256]{2,1,0:T(8,128)(2,1)}, bf16[2,512,256]{2,1,0:T(8,128)(2,1)S(1)}, u32[]{:S(2)}, u32[]{:S(2)}) %collective-permute-start.6) | collective-permute-done | bytes 524320 | tf_op jit(solution)/shard_map/ppermute | solution.py:8
  51.7 4.1 %multiply_reduce_fusion = (f32[1024]{0:T(1024)S(1)}, f32[1024,256]{1,0:T(8,128)}) fusion(f32[256]{0:T(256)S(1)} %bitcast.266, f32[256]{0:T(256)S(1)} %bitcast.258, f32[256]{0:T(256)S(1)} %bitcast.250, f32[256]{0:T(256)S(1)} %bitcast.242, f32[256]{0:T(256)S(1)} %bitcast.234, pred[1024]{0:T(1024)(128)(4,1)S(1)} %broadcast_in_dim.426, ...), kind=kOutput, calls=%fused_computation.100 | convolution fusion | flops 548928512 | bytes 1605632 | tf_op jit(solution)/shard_map/dot_general | solution.py:96
  55.8 10.6 %all-reduce = (f32[2,6]{1,0:T(2,128)S(1)}, f32[2,6]{1,0:T(2,128)S(1)}, f32[2,512]{1,0:T(2,128)S(1)}, f32[2,512]{1,0:T(2,128)S(1)}) all-reduce(f32[2,6]{1,0:T(2,128)S(1)} %get-tuple-element.7, f32[2,6]{1,0:T(2,128)S(1)} %get-tuple-element.6, f32[2,512]{1,0:T(2,128)S(1)} %reduce_sum.42, ...), channel_id=1, replica_groups=mesh['seq'=8,'ch'=4] {'ch'}, use_global_device_ids=true, to_apply=%region_3.4 | all-reduce | flops 2072 | bytes 16576 | tf_op jit(solution)/shard_map/psum | solution.py:127
  68.0 2.8 %multiply_convert_fusion = bf16[1,2,512,256]{3,2,1,0:T(8,128)(2,1)S(1)} fusion(f32[1,2,512,256]{3,2,1,0:T(8,128)} %bitcast.231, f32[256]{0:T(256)S(1)} %copy-done.5, f32[2,512]{1,0:T(2,128)S(1)} %add_rsqrt_fusion, f32[256]{0:T(256)S(1)} %bitcast.270, f32[256]{0:T(256)S(1)} %bitcast.262, f32[256]{0:T(256)S(1)} %bitcast.254, f32[256]{0:T(256)S(1)} %bitcast.246, ...), kind=kLoop, calls=%fused_computation.99 | loop fusion | flops 3407872 | bytes 1588224 | tf_op jit(solution)/shard_map/convert_element_type | solution.py:138
  73.2 23.4 %collective-permute-done.8 = bf16[1,2048,256]{2,1,0:T(8,128)(2,1)} collective-permute-done((bf16[1,2048,256]{2,1,0:T(8,128)(2,1)S(1)}, bf16[1,2048,256]{2,1,0:T(8,128)(2,1)}, u32[]{:S(2)}, u32[]{:S(2)}) %collective-permute-start.8) | collective-permute-done | bytes 1048608 | tf_op jit(solution)/shard_map/ppermute | solution.py:13
  100.9 2.0 %collective-permute-start.9 = (bf16[2,2048,256]{2,1,0:T(8,128)(2,1)}, bf16[2,2048,256]{2,1,0:T(8,128)(2,1)}, u32[]{:S(2)}, u32[]{:S(2)}) collective-permute-start(bf16[2,2048,256]{2,1,0:T(8,128)(2,1)} %maximum_bitcast_fusion), channel_id=1, source_target_pairs={{0,1},{1,0},{2,3},{3,2},{4,5},{5,4},{6,7},{7,6},{8,9},{9,8},{10,11... | collective-permute-start | bytes 6291464 | tf_op jit(solution)/shard_map/ppermute | solution.py:13
  102.9 4.1 %collective-permute-done.9 = bf16[2,2048,256]{2,1,0:T(8,128)(2,1)} collective-permute-done((bf16[2,2048,256]{2,1,0:T(8,128)(2,1)}, bf16[2,2048,256]{2,1,0:T(8,128)(2,1)}, u32[]{:S(2)}, u32[]{:S(2)}) %collective-permute-start.9) | collective-permute-done | bytes 2097184 | tf_op jit(solution)/shard_map/ppermute | solution.py:13
  107.0 2.1 %select_bitcast_fusion.2 = (bf16[2,1,2048,256]{3,2,1,0:T(8,128)(2,1)S(1)}, bf16[2,1,2048,256]{3,2,1,0:T(8,128)(2,1)S(1)}) fusion(bf16[2,2048,256]{2,1,0:T(8,128)(2,1)} %collective-permute-done.9, pred[]{:T(512)S(6)} %eq.199, bf16[1,1,2048,256]{3,2,1,0:T(8,128)(2,1)} %copy-done.1, bf16[1,1,2048,256]{3,2,1,0:T(8,128)(2,1)S(1)} %get-tuple-element.22), kind=kLoop, calls=%fused_computation.37 | loop fusion | flops 3145728 | bytes 8388609 | tf_op jit(solution)/shard_map/stack | solution.py:45
  109.6 4.5 %fusion.128 = f32[2048,1024,1]{1,0,2:T(8,128)S(1)} fusion(bf16[4,2048,256]{2,1,0:T(8,128)(2,1)S(1)} %bitcast.228, bf16[4,256,1024]{2,1,0:T(8,128)(2,1)S(1)} %bitcast.223), kind=kOutput, calls=%fused_computation.201 | convolution fusion | flops 4294967296 | bytes 14680064 | tf_op jit(solution)/shard_map/dot_general | solution.py:156
  114.1 5.5 %fusion = bf16[2048,1024]{1,0:T(8,128)(2,1)S(1)} fusion(f32[2048,1024,1]{1,0,2:T(8,128)S(1)} %fusion.128, bf16[4,2048,256]{2,1,0:T(8,128)(2,1)S(1)} %bitcast.229, bf16[4,256,1024]{2,1,0:T(8,128)(2,1)S(1)} %bitcast.290), kind=kOutput, calls=%fused_computation.1 | convolution fusion | flops 4307550208 | bytes 18874368 | tf_op jit(solution)/shard_map/dot_general | solution.py:159
  123.1 9.7 %fusion.9 = f32[1024,1024]{0,1:T(8,128)} fusion(bf16[1024,1024]{1,0:T(8,128)(2,1)} %param.21, s32[1024]{0:T(1024)S(1)} %get-tuple-element.88, s32[1024]{0:T(1024)S(1)} %get-tuple-element.89, s32[1024]{0:T(1024)S(1)} %get-tuple-element.87, s32[1024]{0:T(1024)S(1)} %get-tuple-element.90, pred[1024]{0:T(1024)(128)(4,1)S(1)} %get-tuple-element.91, ...), kind=kOutput, calls=%fused_computation.16 | convolution fusion | flops 4305453056 | bytes 8407040 | tf_op jit(solution)/shard_map/dot_general | solution.py:168
  132.8 6.1 %fusion.30 = f32[1024,1024]{0,1:T(8,128)S(1)} fusion(f32[1024,1024]{0,1:T(8,128)} %fusion.9, bf16[1024,1024]{1,0:T(8,128)(2,1)} %param.21, bf16[2048,1024]{1,0:T(8,128)(2,1)} %copy-done.4), kind=kOutput, calls=%fused_computation.42 | convolution fusion | flops 2148532224 | bytes 12582912 | tf_op jit(solution)/shard_map/dot_general | solution.py:168
  139.7 3.8 %collective-permute-done.10 = f32[1024,2,256]{0,2,1:T(8,128)S(1)} collective-permute-done((f32[1024,2,256]{0,2,1:T(8,128)S(1)}, f32[1024,2,256]{0,2,1:T(8,128)S(1)}, u32[]{:S(2)}, u32[]{:S(2)}) %collective-permute-start.10) | collective-permute-done | bytes 2097184 | tf_op jit(solution)/shard_map/ppermute | solution.py:13
  144.7 12.9 %collective-permute-done.11 = bf16[1024,1,256]{0,2,1:T(8,128)(2,1)S(1)} collective-permute-done((bf16[1024,1,256]{0,2,1:T(8,128)(2,1)S(1)}, bf16[1024,1,256]{0,2,1:T(8,128)(2,1)S(1)}, u32[]{:S(2)}, u32[]{:S(2)}) %collective-permute-start.11) | collective-permute-done | bytes 524320 | tf_op jit(solution)/shard_map/ppermute | solution.py:13
  158.4 2.8 %convolution_convert_fusion = bf16[1024,256]{1,0:T(8,128)(2,1)} fusion(s32[1024]{0:T(1024)S(1)} %get-tuple-element.82, s32[1024]{0:T(1024)S(1)} %get-tuple-element.83, s32[1024]{0:T(1024)S(1)} %get-tuple-element.81, s32[1024]{0:T(1024)S(1)} %get-tuple-element.84, pred[1024]{0:T(1024)(128)(4,1)S(1)} %get-tuple-element.85, ...), kind=kOutput, calls=%fused_computation.43 | convolution fusion | flops 545521664 | bytes 1067008 | tf_op jit(solution)/shard_map/dot_general | solution.py:175
  163.7 3.8 %add_convert_fusion.1 = bf16[2,512,256]{2,1,0:T(8,128)(2,1)} fusion(f32[2,512,256]{2,1,0:T(8,128)} %bitcast.230, f32[256]{0:T(256)S(1)} %bitcast.271, pred[2,512]{1,0:T(4,128)(4,1)S(1)} %get-tuple-element.77, f32[256]{0:T(256)S(1)} %bitcast.263, pred[2,512]{1,0:T(4,128)(4,1)S(1)} %get-tuple-element.79, f32[256]{0:T(256)S(1)} %bitcast.255, ...), kind=kLoop, calls=%fused_computation.95 | loop fusion | flops 3407872 | bytes 2107392 | tf_op jit(solution)/shard_map/convert_element_type | solution.py:178
  167.5 13.1 %collective-permute-done.12 = bf16[2,512,256]{2,1,0:T(8,128)(2,1)} collective-permute-done((bf16[2,512,256]{2,1,0:T(8,128)(2,1)}, bf16[2,512,256]{2,1,0:T(8,128)(2,1)}, u32[]{:S(2)}, u32[]{:S(2)}) %collective-permute-start.12) | collective-permute-done | bytes 524320 | tf_op jit(solution)/shard_map/ppermute | solution.py:8
  180.6 2.3 %add_convert_fusion = bf16[2,512,256]{2,1,0:T(8,128)(2,1)} fusion(f32[2,512,256]{2,1,0:T(8,128)} %get-tuple-element.5, bf16[2,512,256]{2,1,0:T(8,128)(2,1)} %collective-permute-done.12), kind=kLoop, calls=%fused_computation.94 | loop fusion | flops 786432 | bytes 2097152 | tf_op jit(solution)/shard_map/convert_element_type | solution.py:178
  (86 shorter events, 26.2 us)
Async XLA Ops:
  0.6 108.9 %copy-start = (bf16[1024,1024]{1,0:T(8,128)(2,1)S(1)}, bf16[1024,1024]{1,0:T(8,128)(2,1)}, u32[]{:S(2)}) copy-start(bf16[1024,1024]{1,0:T(8,128)(2,1)} %param.19) | copy-start | bytes 6291460
  1.5 24.8 %collective-permute-start.7 = (s32[2,512]{1,0:T(2,128)S(1)}, s32[2,512]{1,0:T(2,128)S(1)}, u32[]{:S(2)}, u32[]{:S(2)}) collective-permute-start(s32[2,512]{1,0:T(2,128)S(1)} %get-tuple-element.38), channel_id=1, source_target_pairs={{0,28},{4,24},{8,20},{12,16},{16,12},{20,8},{24,4},{28,0},{1,29},{... | collective-permute-start | bytes 12296 | tf_op jit(solution)/shard_map/ppermute | solution.py:8
  3.5 15.7 %collective-permute-start.2 = (s32[2,3]{1,0:T(2,128)S(1)}, s32[2,3]{1,0:T(2,128)S(1)}, u32[]{:S(2)}, u32[]{:S(2)}) collective-permute-start(s32[2,3]{1,0:T(2,128)S(1)} %get-tuple-element.54), channel_id=1, source_target_pairs={{0,4},{4,8},{8,12},{12,16},{16,20},{20,24},{24,28},{1,5},{5,9},{9,... | collective-permute-start | bytes 80 | tf_op jit(solution)/shard_map/ppermute | solution.py:110
  5.6 15.8 %collective-permute-start.3 = (s32[2,3]{1,0:T(2,128)S(1)}, s32[2,3]{1,0:T(2,128)S(1)}, u32[]{:S(2)}, u32[]{:S(2)}) collective-permute-start(s32[2,3]{1,0:T(2,128)S(1)} %get-tuple-element.55), channel_id=1, source_target_pairs={{4,0},{8,4},{12,8},{16,12},{20,16},{24,20},{28,24},{5,1},{9,5},{13... | collective-permute-start | bytes 80 | tf_op jit(solution)/shard_map/ppermute | solution.py:111
  10.4 15.1 %collective-permute-start.4 = (bf16[2,3,256]{2,1,0:T(4,128)(2,1)S(1)}, bf16[2,3,256]{2,1,0:T(4,128)(2,1)S(1)}, u32[]{:S(2)}, u32[]{:S(2)}) collective-permute-start(bf16[2,3,256]{2,1,0:T(4,128)(2,1)S(1)} %get-tuple-element.26), channel_id=1, source_target_pairs={{4,28},{8,24},{12,20},{16,16},{20,12},{24,8},{28,4},{5,29},{9,25},... | collective-permute-start | bytes 9224 | tf_op jit(solution)/shard_map/ppermute | solution.py:112
  11.0 14.7 %collective-permute-start.5 = (bf16[2,3,256]{2,1,0:T(4,128)(2,1)S(1)}, bf16[2,3,256]{2,1,0:T(4,128)(2,1)S(1)}, u32[]{:S(2)}, u32[]{:S(2)}) collective-permute-start(bf16[2,3,256]{2,1,0:T(4,128)(2,1)S(1)} %get-tuple-element.27), channel_id=1, source_target_pairs={{0,24},{4,20},{8,16},{12,12},{16,8},{20,4},{24,0},{1,25},{5,21},{9... | collective-permute-start | bytes 9224 | tf_op jit(solution)/shard_map/ppermute | solution.py:113
  19.2 6.6 %collective-permute-start = (bf16[2,3,256]{2,1,0:T(4,128)(2,1)S(1)}, bf16[2,3,256]{2,1,0:T(4,128)(2,1)S(1)}, u32[]{:S(2)}, u32[]{:S(2)}) collective-permute-start(bf16[2,3,256]{2,1,0:T(4,128)(2,1)S(1)} %get-tuple-element.24), channel_id=1, source_target_pairs={{0,4},{4,8},{8,12},{12,16},{16,20},{20,24},{24,28},{1,5},{5,9},{9,... | collective-permute-start | bytes 9224 | tf_op jit(solution)/shard_map/ppermute | solution.py:110
  21.5 4.7 %collective-permute-start.1 = (bf16[2,3,256]{2,1,0:T(4,128)(2,1)S(1)}, bf16[2,3,256]{2,1,0:T(4,128)(2,1)S(1)}, u32[]{:S(2)}, u32[]{:S(2)}) collective-permute-start(bf16[2,3,256]{2,1,0:T(4,128)(2,1)S(1)} %get-tuple-element.25), channel_id=1, source_target_pairs={{4,0},{8,4},{12,8},{16,12},{20,16},{24,20},{28,24},{5,1},{9,5},{13... | collective-permute-start | bytes 9224 | tf_op jit(solution)/shard_map/ppermute | solution.py:111
  25.5 25.4 %collective-permute-start.6 = (bf16[2,512,256]{2,1,0:T(8,128)(2,1)}, bf16[2,512,256]{2,1,0:T(8,128)(2,1)S(1)}, u32[]{:S(2)}, u32[]{:S(2)}) collective-permute-start(bf16[2,512,256]{2,1,0:T(8,128)(2,1)} %param.14), channel_id=1, source_target_pairs={{0,28},{4,24},{8,20},{12,16},{16,12},{20,8},{24,4},{28,0},{1,29},{... | collective-permute-start | bytes 1572872 | tf_op jit(solution)/shard_map/ppermute | solution.py:8
  50.9 0.8 copy-start.8
  51.7 14.8 %copy-start.2 = (bf16[2,512,256]{2,1,0:T(8,128)(2,1)S(1)}, bf16[2,512,256]{2,1,0:T(8,128)(2,1)}, u32[]{:S(2)}) copy-start(bf16[2,512,256]{2,1,0:T(8,128)(2,1)} %param.13) | copy-start | bytes 1572868
  51.7 14.8 %copy-start.5 = (f32[256]{0:T(256)S(1)}, f32[256]{0:T(256)}, u32[]{:S(2)}) copy-start(f32[256]{0:T(256)} %param.18) | copy-start | bytes 3076
  55.8 15.2 %copy-start.6 = (f32[256]{0:T(256)S(1)}, f32[256]{0:T(256)}, u32[]{:S(2)}) copy-start(f32[256]{0:T(256)} %param.17) | copy-start | bytes 3076
  72.9 23.7 %copy-start.3 = (bf16[4,512,256]{2,1,0:T(8,128)(2,1)}, bf16[4,512,256]{2,1,0:T(8,128)(2,1)S(1)}, u32[]{:S(2)}) copy-start(bf16[4,512,256]{2,1,0:T(8,128)(2,1)S(1)} %pad_maximum_fusion.1) | copy-start | bytes 3145732
  72.9 23.7 %collective-permute-start.8 = (bf16[1,2048,256]{2,1,0:T(8,128)(2,1)S(1)}, bf16[1,2048,256]{2,1,0:T(8,128)(2,1)}, u32[]{:S(2)}, u32[]{:S(2)}) collective-permute-start(bf16[1,2048,256]{2,1,0:T(8,128)(2,1)S(1)} %bitcast.226), channel_id=1, source_target_pairs={{0,2},{1,3},{2,0},{3,1},{4,6},{5,7},{6,4},{7,5},{8,10},{9,11},{10,... | collective-permute-start | bytes 3145736 | tf_op jit(solution)/shard_map/ppermute | solution.py:13
  98.4 1.0 copy-start.1
  100.9 6.1 %collective-permute-start.9 = (bf16[2,2048,256]{2,1,0:T(8,128)(2,1)}, bf16[2,2048,256]{2,1,0:T(8,128)(2,1)}, u32[]{:S(2)}, u32[]{:S(2)}) collective-permute-start(bf16[2,2048,256]{2,1,0:T(8,128)(2,1)} %maximum_bitcast_fusion), channel_id=1, source_target_pairs={{0,1},{1,0},{2,3},{3,2},{4,5},{5,4},{6,7},{7,6},{8,9},{9,8},{10,11... | collective-permute-start | bytes 6291464 | tf_op jit(solution)/shard_map/ppermute | solution.py:13
  109.6 4.5 %copy-start.7 = (bf16[1024,1024]{1,0:T(8,128)(2,1)S(1)}, bf16[1024,1024]{1,0:T(8,128)(2,1)}, u32[]{:S(2)}) copy-start(bf16[1024,1024]{1,0:T(8,128)(2,1)} %param.20) | copy-start | bytes 6291460
  119.6 2.0 %copy-start.4 = (bf16[2048,1024]{1,0:T(8,128)(2,1)}, bf16[2048,1024]{1,0:T(8,128)(2,1)S(1)}, u32[]{:S(2)}) copy-start(bf16[2048,1024]{1,0:T(8,128)(2,1)S(1)} %fusion) | copy-start | bytes 12582916
  139.3 4.2 %collective-permute-start.10 = (f32[1024,2,256]{0,2,1:T(8,128)S(1)}, f32[1024,2,256]{0,2,1:T(8,128)S(1)}, u32[]{:S(2)}, u32[]{:S(2)}) collective-permute-start(f32[1024,2,256]{0,2,1:T(8,128)S(1)} %select_bitcast_fusion), channel_id=1, source_target_pairs={{0,1},{1,0},{2,3},{3,2},{4,5},{5,4},{6,7},{7,6},{8,9},{9,8},{10,11... | collective-permute-start | bytes 6291464 | tf_op jit(solution)/shard_map/ppermute | solution.py:13
  144.4 13.2 %collective-permute-start.11 = (bf16[1024,1,256]{0,2,1:T(8,128)(2,1)S(1)}, bf16[1024,1,256]{0,2,1:T(8,128)(2,1)S(1)}, u32[]{:S(2)}, u32[]{:S(2)}) collective-permute-start(bf16[1024,1,256]{0,2,1:T(8,128)(2,1)S(1)} %fusion.69), channel_id=1, source_target_pairs={{0,2},{1,3},{2,0},{3,1},{4,6},{5,7},{6,4},{7,5},{8,10},{9,11},{10,... | collective-permute-start | bytes 1572872 | tf_op jit(solution)/shard_map/ppermute | solution.py:13
  161.3 19.3 %collective-permute-start.12 = (bf16[2,512,256]{2,1,0:T(8,128)(2,1)}, bf16[2,512,256]{2,1,0:T(8,128)(2,1)}, u32[]{:S(2)}, u32[]{:S(2)}) collective-permute-start(bf16[2,512,256]{2,1,0:T(8,128)(2,1)} %bitcast.56), channel_id=1, source_target_pairs={{0,31},{1,30},{2,29},{3,28},{4,27},{5,26},{6,25},{7,24},{8,23},{9,... | collective-permute-start | bytes 1572872 | tf_op jit(solution)/shard_map/ppermute | solution.py:8

commit v7 on v4

--- a/solution.py
+++ b/solution.py
@@ -54,9 +54,7 @@
         low = ((me >> bit) & 1) == 0
         keep = jnp.where(low, cur[:, :, 0], cur[:, :, 1])
         give = jnp.where(low, cur[:, :, 1], cur[:, :, 0])
-        if bit > 0:
-            give = give.astype(jnp.bfloat16)
-        cur = keep + partner(give, "ch", bit).astype(jnp.float32)
+        cur = keep + partner(give.astype(jnp.bfloat16), "ch", bit).astype(jnp.float32)
     return cur[:, 0]
 
 
@@ -87,8 +85,19 @@
     table = embed_table.astype(jnp.float32)
     base_in = jnp.where(masked == 1, 4, tokens)
     comp = jnp.where(masked == 1, 4, 3 - tokens)
-    arrived = mirror(hidden_reverse, "seq", seq_count)
-    comp_back = jnp.flip(mirror(comp, "seq", seq_count), axis=1)
+    span = hidden_reverse.shape[1]
+    lanes = hidden_reverse.shape[2]
+    if span % lanes == 0:
+        extra = span // lanes
+        packed = jnp.concatenate(
+            [hidden_reverse, comp.astype(jnp.bfloat16).reshape(comp.shape[0], extra, lanes)], axis=1
+        )
+        packed = mirror(packed, "seq", seq_count)
+        arrived = packed[:, :span]
+        comp_back = jnp.flip(packed[:, span:].reshape(comp.shape).astype(jnp.int32), axis=1)
+    else:
+        arrived = mirror(hidden_reverse, "seq", seq_count)
+        comp_back = jnp.flip(mirror(comp, "seq", seq_count), axis=1)
     x_rev = hidden_reverse.astype(jnp.float32) + embedded(comp_back, table)
     arrived, x_rev = lax.optimization_barrier((arrived, x_rev))
     span = arrived.shape[1]

time: 173 us -> 176 us (1.017)
  waiting for transfers between devices: 76.9 us -> 83.1 us
    ppermute x3 -> x2, waiting for transfers between devices: 34.7 us -> 42.2 us  [mirror(): return lax.ppermute(value, axes, [(k, count - 1 - k) for k in range(count)])]
    ppermute x4, waiting for transfers between devices: 41.5 us -> 39.6 us  [partner(): lax.ppermute(value, axis, [(k, k ^ mask) for k in range(lax.axis_size(axi...]
    ppermute x3 -> x2, starting transfers between devices: 7.11 us -> 5.3 us  [mirror(): return lax.ppermute(value, axes, [(k, count - 1 - k) for k in range(count)])]
    unnamed x20 -> x19, local copies, waits for them, and re-layouts: 3.77 us -> 2.99 us
  transfers between devices with their start and end apart: 9 -> 8, of which waited for: 7 -> 7; matrix products, arithmetic and copies ran while one was open for 7% -> 4% of each run, Pallas kernels for 0% -> 0%
where the time goes in v7:
time: 176 us; the launch traced here: 175 us
  waiting for transfers between devices  83.1 us (47%)
  matrix products  32.6 us (19%)
  other arithmetic  27.1 us (15%)
  starting transfers between devices  17.6 us (10%)
  local copies, waits for them, and re-layouts  7.3 us (4%)
  blocking collectives  6.6 us (4%)
    ppermute x2, waiting for transfers between devices, mirror(): return lax.ppermute(value, axes, [(k, count - 1 - k) for k in range(count)])  42.2 us
    ppermute x4, waiting for transfers between devices, partner(): lax.ppermute(value, axis, [(k, k ^ mask) for k in range(lax.axis_size(axi...  39.6 us
    dot_general x1, matrix products, local(): jnp.dot(act_rev, w_flip, preferred_element_type=jnp.float32)  9.71 us
    psum x1, blocking collectives, local(): lax.psum((jnp.sum(x_fwd * x_fwd, axis=-1), jnp.sum(x_rfp * x_rfp, axis=-1...  6.6 us
    ppermute x4, starting transfers between devices, partner(): lax.ppermute(value, axis, [(k, k ^ mask) for k in range(lax.axis_size(axi...  6.14 us
    dot_general x1, matrix products, local(): jnp.dot(act_fwd, w_out, preferred_element_type=jnp.float32)  6.08 us
    convert_element_type x2, other arithmetic, local(): return (out_forward.astype(jnp.bfloat16), out_reverse.astype(jnp.bfloat16))  6.07 us
    reduce_sum x1, other arithmetic, local(): jnp.sum(x_fwd * x_fwd, axis=-1)  6.03 us
  transfers between devices with their start and end apart: 8, of which 7 were waited for; matrix products, arithmetic and copies ran while one was open for 4% of the time, Pallas kernels for 0%

profile of v7, /device:TPU:17, one launch (start us, length us, event | category | flops | bytes accessed | tf_op | source)
XLA Modules:
  0.0 175.3 jit_solution(10990226588023671067)
XLA Ops:
  4.8 23.2 %collective-permute-done = bf16[2,514,256]{2,1,0:T(8,128)(2,1)S(1)} collective-permute-done((bf16[2,514,256]{2,1,0:T(8,128)(2,1)S(1)}, bf16[2,514,256]{2,1,0:T(8,128)(2,1)S(1)}, u32[]{:S(2)}, u32[]{:S(2)}) %collective-permute-start) | collective-permute-done | bytes 526368 | tf_op jit(solution)/shard_map/ppermute | solution.py:8
  28.4 6.0 %multiply_reduce_fusion.1 = (f32[2,512]{1,0:T(2,128)S(1)}, f32[2,512,256]{2,1,0:T(8,128)}) fusion(f32[256]{0:T(256)S(1)} %bitcast.254, pred[2,512]{1,0:T(4,128)(4,1)S(1)} %get-tuple-element.49, f32[256]{0:T(256)S(1)} %bitcast.249, pred[2,512]{1,0:T(4,128)(4,1)S(1)} %get-tuple-element.51, f32[256]{0:T(256)S(1)} %bitcast.244, ...), kind=kLoop, calls=%fused_computation.104 | loop fusion | flops 6290432 | bytes 2116608 | tf_op jit(solution)/shard_map/reduce_sum | solution.py:117
  34.5 3.4 %multiply_reduce_fusion = (f32[1024]{0:T(1024)S(1)}, f32[1024,256]{1,0:T(8,128)}) fusion(f32[256]{0:T(256)S(1)} %bitcast.255, f32[256]{0:T(256)S(1)} %bitcast.250, f32[256]{0:T(256)S(1)} %bitcast.245, f32[256]{0:T(256)S(1)} %bitcast.240, f32[256]{0:T(256)S(1)} %bitcast.235, pred[1024]{0:T(1024)(128)(4,1)S(1)} %broadcast_in_dim.233, ...), kind=kOutput, calls=%fused_computation.101 | convolution fusion | flops 548928512 | bytes 1605632 | tf_op jit(solution)/shard_map/dot_general | solution.py:105
  37.9 6.6 %all-reduce = (f32[2,512]{1,0:T(2,128)S(1)}, f32[2,512]{1,0:T(2,128)S(1)}) all-reduce(f32[2,512]{1,0:T(2,128)S(1)} %reduce_sum.22, f32[2,512]{1,0:T(2,128)S(1)} %get-tuple-element.27), channel_id=1, replica_groups=mesh['seq'=8,'ch'=4] {'ch'}, use_global_device_ids=true, to_apply=%region_3.4 | all-reduce | flops 2048 | bytes 16384 | tf_op jit(solution)/shard_map/psum | solution.py:116
  45.7 2.8 %multiply_convert_fusion = bf16[1,2,512,256]{3,2,1,0:T(8,128)(2,1)S(1)} fusion(f32[1,2,512,256]{3,2,1,0:T(8,128)} %bitcast.232, f32[256]{0:T(256)S(1)} %copy-done.7, f32[2,512]{1,0:T(2,128)S(1)} %add_rsqrt_fusion, f32[256]{0:T(256)S(1)} %bitcast.257, f32[256]{0:T(256)S(1)} %bitcast.252, f32[256]{0:T(256)S(1)} %bitcast.247, f32[256]{0:T(256)S(1)} %bitcast.242, ...), kind=kLoop, calls=%fused_computation.100 | loop fusion | flops 3407872 | bytes 1588224 | tf_op jit(solution)/shard_map/convert_element_type | solution.py:122
  48.5 3.1 %collective-permute-start.1 = (bf16[2,2,3,256]{3,2,1,0:T(4,128)(2,1)S(1)}, bf16[2,2,3,256]{3,2,1,0:T(4,128)(2,1)S(1)}, u32[]{:S(2)}, u32[]{:S(2)}) collective-permute-start(bf16[2,2,3,256]{3,2,1,0:T(4,128)(2,1)S(1)} %get-tuple-element.16), channel_id=1, source_target_pairs={{0,4},{4,8},{8,12},{12,16},{16,20},{20,24},{24,28},{1,5},{5,9},{9,... | collective-permute-start | bytes 18440 | tf_op jit(solution)/shard_map/ppermute | solution.py:23
  51.6 3.1 %collective-permute-start.2 = (bf16[2,2,3,256]{3,2,1,0:T(4,128)(2,1)S(1)}, bf16[2,2,3,256]{3,2,1,0:T(4,128)(2,1)S(1)}, u32[]{:S(2)}, u32[]{:S(2)}) collective-permute-start(bf16[2,2,3,256]{3,2,1,0:T(4,128)(2,1)S(1)} %get-tuple-element.17), channel_id=1, source_target_pairs={{4,0},{8,4},{12,8},{16,12},{20,16},{24,20},{28,24},{5,1},{9,5},{13... | collective-permute-start | bytes 18440 | tf_op jit(solution)/shard_map/ppermute | solution.py:25
  59.5 21.4 %collective-permute-done.3 = bf16[1,2048,256]{2,1,0:T(8,128)(2,1)} collective-permute-done((bf16[1,2048,256]{2,1,0:T(8,128)(2,1)S(1)}, bf16[1,2048,256]{2,1,0:T(8,128)(2,1)}, u32[]{:S(2)}, u32[]{:S(2)}) %collective-permute-start.3) | collective-permute-done | bytes 1048608 | tf_op jit(solution)/shard_map/ppermute | solution.py:13
  80.9 1.7 select_bitcast_fusion.3
  85.1 3.1 %collective-permute-start.4 = (bf16[2,2048,256]{2,1,0:T(8,128)(2,1)}, bf16[2,2048,256]{2,1,0:T(8,128)(2,1)}, u32[]{:S(2)}, u32[]{:S(2)}) collective-permute-start(bf16[2,2048,256]{2,1,0:T(8,128)(2,1)} %maximum_bitcast_fusion), channel_id=1, source_target_pairs={{0,1},{1,0},{2,3},{3,2},{4,5},{5,4},{6,7},{7,6},{8,9},{9,8},{10,11... | collective-permute-start | bytes 6291464 | tf_op jit(solution)/shard_map/ppermute | solution.py:13
  88.2 4.1 %collective-permute-done.4 = bf16[2,2048,256]{2,1,0:T(8,128)(2,1)} collective-permute-done((bf16[2,2048,256]{2,1,0:T(8,128)(2,1)}, bf16[2,2048,256]{2,1,0:T(8,128)(2,1)}, u32[]{:S(2)}, u32[]{:S(2)}) %collective-permute-start.4) | collective-permute-done | bytes 2097184 | tf_op jit(solution)/shard_map/ppermute | solution.py:13
  92.3 2.1 %select_bitcast_fusion.1 = (bf16[2,1,2048,256]{3,2,1,0:T(8,128)(2,1)S(1)}, bf16[2,1,2048,256]{3,2,1,0:T(8,128)(2,1)S(1)}) fusion(bf16[2,2048,256]{2,1,0:T(8,128)(2,1)} %collective-permute-done.4, pred[]{:T(512)S(6)} %eq.119, bf16[1,1,2048,256]{3,2,1,0:T(8,128)(2,1)} %copy-done.1, bf16[1,1,2048,256]{3,2,1,0:T(8,128)(2,1)S(1)} %get-tuple-element.14), kind=kLoop, calls=%fused_computation.37 | loop fusion | flops 3145728 | bytes 8388609 | tf_op jit(solution)/shard_map/stack | solution.py:45
  94.8 4.5 %fusion.125 = f32[2048,1024,1]{1,0,2:T(8,128)S(1)} fusion(bf16[4,2048,256]{2,1,0:T(8,128)(2,1)S(1)} %bitcast.229, bf16[4,256,1024]{2,1,0:T(8,128)(2,1)S(1)} %bitcast.224), kind=kOutput, calls=%fused_computation.180 | convolution fusion | flops 4294967296 | bytes 14680064 | tf_op jit(solution)/shard_map/dot_general | solution.py:136
  99.4 5.4 %fusion = bf16[2048,1024]{1,0:T(8,128)(2,1)S(1)} fusion(f32[2048,1024,1]{1,0,2:T(8,128)S(1)} %fusion.125, bf16[4,2048,256]{2,1,0:T(8,128)(2,1)S(1)} %bitcast.230, bf16[4,256,1024]{2,1,0:T(8,128)(2,1)S(1)} %bitcast.274), kind=kOutput, calls=%fused_computation.1 | convolution fusion | flops 4307550208 | bytes 18874368 | tf_op jit(solution)/shard_map/dot_general | solution.py:139
  104.8 1.9 %copy-done.4 = bf16[2048,1024]{1,0:T(8,128)(2,1)} copy-done((bf16[2048,1024]{1,0:T(8,128)(2,1)}, bf16[2048,1024]{1,0:T(8,128)(2,1)S(1)}, u32[]{:S(2)}) %copy-start.4) | copy-done | bytes 4194328
  108.3 9.7 %fusion.9 = f32[1024,1024]{0,1:T(8,128)} fusion(bf16[1024,1024]{1,0:T(8,128)(2,1)} %param.21, s32[1024]{0:T(1024)S(1)} %get-tuple-element.60, s32[1024]{0:T(1024)S(1)} %get-tuple-element.61, s32[1024]{0:T(1024)S(1)} %get-tuple-element.59, s32[1024]{0:T(1024)S(1)} %get-tuple-element.62, pred[1024]{0:T(1024)(128)(4,1)S(1)} %get-tuple-element.63, ...), kind=kOutput, calls=%fused_computation.16 | convolution fusion | flops 4305453056 | bytes 8407040 | tf_op jit(solution)/shard_map/dot_general | solution.py:148
  118.0 6.1 %fusion.30 = f32[1024,1024]{0,1:T(8,128)S(1)} fusion(f32[1024,1024]{0,1:T(8,128)} %fusion.9, bf16[1024,1024]{1,0:T(8,128)(2,1)} %param.21, bf16[2048,1024]{1,0:T(8,128)(2,1)} %copy-done.4), kind=kOutput, calls=%fused_computation.42 | convolution fusion | flops 2148532224 | bytes 12582912 | tf_op jit(solution)/shard_map/dot_general | solution.py:148
  124.8 2.3 %collective-permute-done.5 = bf16[1024,2,256]{0,2,1:T(8,128)(2,1)S(1)} collective-permute-done((bf16[1024,2,256]{0,2,1:T(8,128)(2,1)S(1)}, bf16[1024,2,256]{0,2,1:T(8,128)(2,1)S(1)}, u32[]{:S(2)}, u32[]{:S(2)}) %collective-permute-start.5) | collective-permute-done | bytes 1048608 | tf_op jit(solution)/shard_map/ppermute | solution.py:13
  129.1 11.8 %collective-permute-done.6 = bf16[1024,1,256]{0,2,1:T(8,128)(2,1)S(1)} collective-permute-done((bf16[1024,1,256]{0,2,1:T(8,128)(2,1)S(1)}, bf16[1024,1,256]{0,2,1:T(8,128)(2,1)S(1)}, u32[]{:S(2)}, u32[]{:S(2)}) %collective-permute-start.6) | collective-permute-done | bytes 524320 | tf_op jit(solution)/shard_map/ppermute | solution.py:13
  141.8 2.8 %convolution_convert_fusion = bf16[1024,256]{1,0:T(8,128)(2,1)} fusion(s32[1024]{0:T(1024)S(1)} %get-tuple-element.54, s32[1024]{0:T(1024)S(1)} %get-tuple-element.55, s32[1024]{0:T(1024)S(1)} %get-tuple-element.53, s32[1024]{0:T(1024)S(1)} %get-tuple-element.56, pred[1024]{0:T(1024)(128)(4,1)S(1)} %get-tuple-element.57, ...), kind=kOutput, calls=%fused_computation.43 | convolution fusion | flops 545521664 | bytes 1067008 | tf_op jit(solution)/shard_map/dot_general | solution.py:155
  144.7 4.1 %collective-permute-start.7 = (bf16[2,512,256]{2,1,0:T(8,128)(2,1)}, bf16[2,512,256]{2,1,0:T(8,128)(2,1)}, u32[]{:S(2)}, u32[]{:S(2)}) collective-permute-start(bf16[2,512,256]{2,1,0:T(8,128)(2,1)} %bitcast.52), channel_id=1, source_target_pairs={{0,31},{1,30},{2,29},{3,28},{4,27},{5,26},{6,25},{7,24},{8,23},{9,... | collective-permute-start | bytes 1572872 | tf_op jit(solution)/shard_map/ppermute | solution.py:8
  150.1 3.8 %add_convert_fusion.1 = bf16[2,512,256]{2,1,0:T(8,128)(2,1)} fusion(f32[2,512,256]{2,1,0:T(8,128)} %bitcast.231, f32[256]{0:T(256)S(1)} %bitcast.258, pred[2,512]{1,0:T(4,128)(4,1)S(1)} %get-tuple-element.49, f32[256]{0:T(256)S(1)} %bitcast.253, pred[2,512]{1,0:T(4,128)(4,1)S(1)} %get-tuple-element.51, f32[256]{0:T(256)S(1)} %bitcast.248, ...), kind=kLoop, calls=%fused_computation.96 | loop fusion | flops 3407872 | bytes 2107392 | tf_op jit(solution)/shard_map/convert_element_type | solution.py:158
  154.0 19.1 %collective-permute-done.7 = bf16[2,512,256]{2,1,0:T(8,128)(2,1)} collective-permute-done((bf16[2,512,256]{2,1,0:T(8,128)(2,1)}, bf16[2,512,256]{2,1,0:T(8,128)(2,1)}, u32[]{:S(2)}, u32[]{:S(2)}) %collective-permute-start.7) | collective-permute-done | bytes 524320 | tf_op jit(solution)/shard_map/ppermute | solution.py:8
  173.0 2.3 %add_convert_fusion = bf16[2,512,256]{2,1,0:T(8,128)(2,1)} fusion(f32[2,512,256]{2,1,0:T(8,128)} %get-tuple-element.5, bf16[2,512,256]{2,1,0:T(8,128)(2,1)} %collective-permute-done.7), kind=kLoop, calls=%fused_computation.95 | loop fusion | flops 786432 | bytes 2097152 | tf_op jit(solution)/shard_map/convert_element_type | solution.py:158
  (67 shorter events, 19.9 us)
Async XLA Ops:
  0.6 94.2 %copy-start = (bf16[1024,1024]{1,0:T(8,128)(2,1)S(1)}, bf16[1024,1024]{1,0:T(8,128)(2,1)}, u32[]{:S(2)}) copy-start(bf16[1024,1024]{1,0:T(8,128)(2,1)} %param.19) | copy-start | bytes 6291460
  2.6 25.4 %collective-permute-start = (bf16[2,514,256]{2,1,0:T(8,128)(2,1)S(1)}, bf16[2,514,256]{2,1,0:T(8,128)(2,1)S(1)}, u32[]{:S(2)}, u32[]{:S(2)}) collective-permute-start(bf16[2,514,256]{2,1,0:T(8,128)(2,1)S(1)} %pad_maximum_fusion.2), channel_id=1, source_target_pairs={{0,28},{4,24},{8,20},{12,16},{16,12},{20,8},{24,4},{28,0},{1,29},{... | collective-permute-start | bytes 1579016 | tf_op jit(solution)/shard_map/ppermute | solution.py:8
  34.4 10.1 %copy-start.2 = (bf16[2,512,256]{2,1,0:T(8,128)(2,1)S(1)}, bf16[2,512,256]{2,1,0:T(8,128)(2,1)}, u32[]{:S(2)}) copy-start(bf16[2,512,256]{2,1,0:T(8,128)(2,1)} %param.13) | copy-start | bytes 1572868
  34.5 10.1 %copy-start.7 = (f32[256]{0:T(256)S(1)}, f32[256]{0:T(256)}, u32[]{:S(2)}) copy-start(f32[256]{0:T(256)} %param.18) | copy-start | bytes 3076
  34.5 20.2 %copy-start.5 = (f32[7,256]{1,0:T(8,128)S(1)}, f32[7,256]{1,0:T(8,128)}, u32[]{:S(2)}) copy-start(f32[7,256]{1,0:T(8,128)} %param.16) | copy-start | bytes 21508
  37.9 18.4 %copy-start.6 = (f32[256]{0:T(256)S(1)}, f32[256]{0:T(256)}, u32[]{:S(2)}) copy-start(f32[256]{0:T(256)} %param.17) | copy-start | bytes 3076
  48.5 6.2 %collective-permute-start.1 = (bf16[2,2,3,256]{3,2,1,0:T(4,128)(2,1)S(1)}, bf16[2,2,3,256]{3,2,1,0:T(4,128)(2,1)S(1)}, u32[]{:S(2)}, u32[]{:S(2)}) collective-permute-start(bf16[2,2,3,256]{3,2,1,0:T(4,128)(2,1)S(1)} %get-tuple-element.16), channel_id=1, source_target_pairs={{0,4},{4,8},{8,12},{12,16},{16,20},{20,24},{24,28},{1,5},{5,9},{9,... | collective-permute-start | bytes 18440 | tf_op jit(solution)/shard_map/ppermute | solution.py:23
  51.6 4.4 %collective-permute-start.2 = (bf16[2,2,3,256]{3,2,1,0:T(4,128)(2,1)S(1)}, bf16[2,2,3,256]{3,2,1,0:T(4,128)(2,1)S(1)}, u32[]{:S(2)}, u32[]{:S(2)}) collective-permute-start(bf16[2,2,3,256]{3,2,1,0:T(4,128)(2,1)S(1)} %get-tuple-element.17), channel_id=1, source_target_pairs={{4,0},{8,4},{12,8},{16,12},{20,16},{24,20},{28,24},{5,1},{9,5},{13... | collective-permute-start | bytes 18440 | tf_op jit(solution)/shard_map/ppermute | solution.py:25
  58.2 22.7 %copy-start.3 = (bf16[4,512,256]{2,1,0:T(8,128)(2,1)}, bf16[4,512,256]{2,1,0:T(8,128)(2,1)S(1)}, u32[]{:S(2)}) copy-start(bf16[4,512,256]{2,1,0:T(8,128)(2,1)S(1)} %pad_maximum_fusion.1) | copy-start | bytes 3145732
  58.2 22.7 %collective-permute-start.3 = (bf16[1,2048,256]{2,1,0:T(8,128)(2,1)S(1)}, bf16[1,2048,256]{2,1,0:T(8,128)(2,1)}, u32[]{:S(2)}, u32[]{:S(2)}) collective-permute-start(bf16[1,2048,256]{2,1,0:T(8,128)(2,1)S(1)} %bitcast.227), channel_id=1, source_target_pairs={{0,2},{1,3},{2,0},{3,1},{4,6},{5,7},{6,4},{7,5},{8,10},{9,11},{10,... | collective-permute-start | bytes 3145736 | tf_op jit(solution)/shard_map/ppermute | solution.py:13
  82.6 1.0 copy-start.1
  85.1 7.2 %collective-permute-start.4 = (bf16[2,2048,256]{2,1,0:T(8,128)(2,1)}, bf16[2,2048,256]{2,1,0:T(8,128)(2,1)}, u32[]{:S(2)}, u32[]{:S(2)}) collective-permute-start(bf16[2,2048,256]{2,1,0:T(8,128)(2,1)} %maximum_bitcast_fusion), channel_id=1, source_target_pairs={{0,1},{1,0},{2,3},{3,2},{4,5},{5,4},{6,7},{7,6},{8,9},{9,8},{10,11... | collective-permute-start | bytes 6291464 | tf_op jit(solution)/shard_map/ppermute | solution.py:13
  94.8 4.5 %copy-start.8 = (bf16[1024,1024]{1,0:T(8,128)(2,1)S(1)}, bf16[1024,1024]{1,0:T(8,128)(2,1)}, u32[]{:S(2)}) copy-start(bf16[1024,1024]{1,0:T(8,128)(2,1)} %param.20) | copy-start | bytes 6291460
  104.8 1.9 %copy-start.4 = (bf16[2048,1024]{1,0:T(8,128)(2,1)}, bf16[2048,1024]{1,0:T(8,128)(2,1)S(1)}, u32[]{:S(2)}) copy-start(bf16[2048,1024]{1,0:T(8,128)(2,1)S(1)} %fusion) | copy-start | bytes 12582916
  124.3 2.7 %collective-permute-start.5 = (bf16[1024,2,256]{0,2,1:T(8,128)(2,1)S(1)}, bf16[1024,2,256]{0,2,1:T(8,128)(2,1)S(1)}, u32[]{:S(2)}, u32[]{:S(2)}) collective-permute-start(bf16[1024,2,256]{0,2,1:T(8,128)(2,1)S(1)} %fusion.38), channel_id=1, source_target_pairs={{0,1},{1,0},{2,3},{3,2},{4,5},{5,4},{6,7},{7,6},{8,9},{9,8},{10,11... | collective-permute-start | bytes 3145736 | tf_op jit(solution)/shard_map/ppermute | solution.py:13
  127.8 13.2 %collective-permute-start.6 = (bf16[1024,1,256]{0,2,1:T(8,128)(2,1)S(1)}, bf16[1024,1,256]{0,2,1:T(8,128)(2,1)S(1)}, u32[]{:S(2)}, u32[]{:S(2)}) collective-permute-start(bf16[1024,1,256]{0,2,1:T(8,128)(2,1)S(1)} %fusion.70), channel_id=1, source_target_pairs={{0,2},{1,3},{2,0},{3,1},{4,6},{5,7},{6,4},{7,5},{8,10},{9,11},{10,... | collective-permute-start | bytes 1572872 | tf_op jit(solution)/shard_map/ppermute | solution.py:13
  144.7 28.3 %collective-permute-start.7 = (bf16[2,512,256]{2,1,0:T(8,128)(2,1)}, bf16[2,512,256]{2,1,0:T(8,128)(2,1)}, u32[]{:S(2)}, u32[]{:S(2)}) collective-permute-start(bf16[2,512,256]{2,1,0:T(8,128)(2,1)} %bitcast.52), channel_id=1, source_target_pairs={{0,31},{1,30},{2,29},{3,28},{4,27},{5,26},{6,25},{7,24},{8,23},{9,... | collective-permute-start | bytes 1572872 | tf_op jit(solution)/shard_map/ppermute | solution.py:8

commit v8 on v2

--- a/solution.py
+++ b/solution.py
@@ -87,31 +87,40 @@
     table = embed_table.astype(jnp.float32)
     base_in = jnp.where(masked == 1, 4, tokens)
     comp = jnp.where(masked == 1, 4, 3 - tokens)
-    arrived = mirror(hidden_reverse, "seq", seq_count)
     comp_back = jnp.flip(mirror(comp, "seq", seq_count), axis=1)
-    x_rev = hidden_reverse.astype(jnp.float32) + embedded(comp_back, table)
-    arrived, x_rev = lax.optimization_barrier((arrived, x_rev))
-    span = arrived.shape[1]
-    rows_all = arrived.shape[0] * span
-    rev_here = jnp.dot(
-        reversal(rows_all, span), arrived.reshape(rows_all, -1), preferred_element_type=jnp.float32
-    ).astype(jnp.bfloat16).reshape(arrived.shape)
 
     local_width = hidden_forward.shape[-1]
     width = local_width * ch_count
     taps = conv_kernel.shape[0]
     half_width = taps // 2
 
-    def conv_rows(hidden, bases, kernel):
-        x = hidden.astype(jnp.float32) + embedded(bases, table)
-        square = lax.psum(jnp.sum(x * x, axis=-1), "ch")
-        normed = (x * lax.rsqrt(square[..., None] / width + 1e-05) * norm_gain).astype(jnp.bfloat16)
-        length = normed.shape[1]
-        padded = padded_2(normed, "seq", 1, half_width).astype(jnp.float32)
-        conv = jnp.zeros(normed.shape, jnp.float32) + conv_bias
-        for offset in range(taps):
-            conv = conv + kernel[offset] * padded[:, offset : offset + length]
-        return x, conv.astype(jnp.bfloat16).reshape(-1, local_width)
+    x_fwd = hidden_forward.astype(jnp.float32) + embedded(base_in, table)
+    x_rev = hidden_reverse.astype(jnp.float32) + embedded(comp_back, table)
+    square_fwd, square_rev = lax.psum(
+        (jnp.sum(x_fwd * x_fwd, axis=-1), jnp.sum(x_rev * x_rev, axis=-1)), "ch"
+    )
+    normed_fwd = (x_fwd * lax.rsqrt(square_fwd[..., None] / width + 1e-05) * norm_gain).astype(
+        jnp.bfloat16
+    )
+    normed_rev = (x_rev * lax.rsqrt(square_rev[..., None] / width + 1e-05) * norm_gain).astype(
+        jnp.bfloat16
+    )
+    stacked = jnp.stack([normed_fwd, normed_rev])
+    length = stacked.shape[2]
+    padded = padded_2(stacked, "seq", 2, half_width).astype(jnp.float32)
+    conv = jnp.zeros(stacked.shape, jnp.float32) + conv_bias
+    for offset in range(taps):
+        conv = conv + conv_kernel[offset] * padded[:, :, offset : offset + length]
+    conv = conv.astype(jnp.bfloat16)
+    rows_fwd = conv[0].reshape(-1, local_width)
+    rows_all = rows_fwd.shape[0]
+    rows_rev = mirror(
+        jnp.dot(
+            reversal(rows_all, length), conv[1].reshape(rows_all, -1), preferred_element_type=jnp.float32
+        ).astype(jnp.bfloat16),
+        "seq",
+        seq_count,
+    )
 
     def activation(rows):
         pieces = gather_blocks(rows, ch_bits, me)
@@ -124,8 +133,6 @@
         )
         return (jax.nn.silu(gate) * value).astype(jnp.bfloat16)
 
-    x_fwd, rows_fwd = conv_rows(hidden_forward, base_in, conv_kernel)
-    _, rows_rev = conv_rows(rev_here, comp, conv_kernel[::-1])
     act_fwd = activation(rows_fwd)
     act_rev = activation(rows_rev)
     lane_flip = reversal(local_width, local_width)

time: 178 us -> 163 us (0.916)
  starting transfers between devices: 30.5 us -> 21.7 us
  waiting for transfers between devices: 67.6 us -> 61.1 us
  other arithmetic: 28.6 us -> 31.1 us
    ppermute x6, waiting for transfers between devices: 28.2 us -> 19.6 us  [partner(): lax.ppermute(value, axis, [(k, k ^ mask) for k in range(lax.axis_size(axi...]
    ppermute x2 -> x1, starting transfers between devices: 6.91 us -> 3.01 us  [padded_2(): lax.ppermute(head, axis, [((i + 1) % count, i) for i in range(ends)])]
    convert_element_type x6 -> x2, other arithmetic: 5.98 us -> 2.1 us  [the longest x1 1.88 us: local(): conv = conv.astype(jnp.bfloat16)]
    another operation x0 -> x2, other arithmetic: none -> 3.86 us  [local(): stacked = jnp.stack([normed_fwd, normed_rev])]
    ppermute x2 -> x1, waiting for transfers between devices: 0.65 us -> 2.98 us  [padded_2(): lax.ppermute(tail, axis, [(i, (i + 1) % count) for i in range(ends)])]
    ppermute x2 -> x1, starting transfers between devices: 4.49 us -> 2.28 us  [padded_2(): lax.ppermute(tail, axis, [(i, (i + 1) % count) for i in range(ends)])]
    another operation x6, other arithmetic: 3.56 us -> 5.64 us  [gather_blocks(): cur = jnp.stack([first, second], axis=1).reshape((-1,) + block.shape)]
    convert_element_type x2 -> x1, other arithmetic: 5.84 us -> 6.41 us  [local(): return (out_forward.astype(jnp.bfloat16), out_reverse.astype(jnp.bfloat16))]
  transfers between devices with their start and end apart: 13 -> 11, of which waited for: 7 -> 6; matrix products, arithmetic and copies ran while one was open for 16% -> 12% of each run, Pallas kernels for 0% -> 0%
where the time goes in v8:
time: 163 us; the launch traced here: 162 us
  waiting for transfers between devices  61.1 us (37%)
  matrix products  36.8 us (23%)
  other arithmetic  31.1 us (19%)
  starting transfers between devices  21.7 us (13%)
  blocking collectives  6.56 us (4%)
  local copies, waits for them, and re-layouts  3.92 us (2%)
    ppermute x3, waiting for transfers between devices, mirror(): return lax.ppermute(value, axes, [(k, count - 1 - k) for k in range(count)])  38.5 us
    ppermute x6, waiting for transfers between devices, partner(): lax.ppermute(value, axis, [(k, k ^ mask) for k in range(lax.axis_size(axi...  19.6 us
    dot_general x1, matrix products, local(): jnp.dot(act_fwd, w_out, preferred_element_type=jnp.float32)  12.2 us
    ppermute x6, starting transfers between devices, partner(): lax.ppermute(value, axis, [(k, k ^ mask) for k in range(lax.axis_size(axi...  11.3 us
    dot_general x2, matrix products, activation(): lax.dot_general(pieces, w_gate.reshape(ch_count, local_width, -1), dims,...  6.66 us
    psum x1, blocking collectives, local(): lax.psum((jnp.sum(x_fwd * x_fwd, axis=-1), jnp.sum(x_rev * x_rev, axis=-1...  6.56 us
    convert_element_type x1, other arithmetic, local(): return (out_forward.astype(jnp.bfloat16), out_reverse.astype(jnp.bfloat16))  6.41 us
    another operation x6, other arithmetic, gather_blocks(): cur = jnp.stack([first, second], axis=1).reshape((-1,) + block.shape)  5.64 us
  transfers between devices with their start and end apart: 11, of which 6 were waited for; matrix products, arithmetic and copies ran while one was open for 12% of the time, Pallas kernels for 0%

profile of v8, /device:TPU:17, one launch (start us, length us, event | category | flops | bytes accessed | tf_op | source)
XLA Modules:
  0.0 162.2 jit_solution(6488824932861065860)
XLA Ops:
  5.6 5.2 %multiply_reduce_fusion.1 = (f32[2,512]{1,0:T(2,128)S(1)}, f32[2,512]{1,0:T(2,128)S(1)}) fusion(f32[256]{0:T(256)S(1)} %bitcast.178, pred[2,512]{1,0:T(4,128)(4,1)S(1)} %get-tuple-element.42, f32[256]{0:T(256)S(1)} %bitcast.174, pred[2,512]{1,0:T(4,128)(4,1)S(1)} %get-tuple-element.40, f32[256]{0:T(256)S(1)} %bitcast.170, ...), kind=kLoop, calls=%fused_computation.78 | loop fusion | flops 6813696 | bytes 1072128 | tf_op jit(solution)/shard_map/reduce_sum | solution.py:100
  10.8 6.6 %all-reduce = (f32[2,512]{1,0:T(2,128)S(1)}, f32[2,512]{1,0:T(2,128)S(1)}) all-reduce(f32[2,512]{1,0:T(2,128)S(1)} %get-tuple-element.3, f32[2,512]{1,0:T(2,128)S(1)} %get-tuple-element.2), channel_id=1, replica_groups=mesh['seq'=8,'ch'=4] {'ch'}, use_global_device_ids=true, to_apply=%region_3.4 | all-reduce | flops 2048 | bytes 16384 | tf_op jit(solution)/shard_map/psum | solution.py:99
  17.4 2.7 %fusion.44 = bf16[1,2,512,256]{3,2,1,0:T(8,128)(2,1)S(1)} fusion(f32[2,512]{1,0:T(2,128)S(1)} %get-tuple-element.43, f32[256]{0:T(256)} %param.18, f32[256]{0:T(256)S(1)} %bitcast.179, pred[2,512]{1,0:T(4,128)(4,1)S(1)} %get-tuple-element.30, f32[256]{0:T(256)S(1)} %bitcast.175, pred[2,512]{1,0:T(4,128)(4,1)S(1)} %get-tuple-element.31, f32[256]{0:T(256)S(1)} %bitcast.171, ...), kind=kLoop, calls=%fused_computation.81 | loop fusion | flops 3670016 | bytes 1063936 | tf_op jit(solution)/shard_map/stack | solution.py:108
  21.3 3.0 %collective-permute-start.2 = (bf16[2,2,3,256]{3,2,1,0:T(4,128)(2,1)S(1)}, bf16[2,2,3,256]{3,2,1,0:T(4,128)(2,1)S(1)}, u32[]{:S(2)}, u32[]{:S(2)}) collective-permute-start(bf16[2,2,3,256]{3,2,1,0:T(4,128)(2,1)S(1)} %get-tuple-element.19), channel_id=1, source_target_pairs={{4,0},{8,4},{12,8},{16,12},{20,16},{24,20},{28,24},{5,1},{9,5},{13... | collective-permute-start | bytes 18440 | tf_op jit(solution)/shard_map/ppermute | solution.py:25
  24.3 2.3 %collective-permute-start.1 = (bf16[2,2,3,256]{3,2,1,0:T(4,128)(2,1)S(1)}, bf16[2,2,3,256]{3,2,1,0:T(4,128)(2,1)S(1)}, u32[]{:S(2)}, u32[]{:S(2)}) collective-permute-start(bf16[2,2,3,256]{3,2,1,0:T(4,128)(2,1)S(1)} %get-tuple-element.18), channel_id=1, source_target_pairs={{0,4},{4,8},{8,12},{12,16},{16,20},{20,24},{24,28},{1,5},{5,9},{9,... | collective-permute-start | bytes 18440 | tf_op jit(solution)/shard_map/ppermute | solution.py:23
  26.6 3.0 %collective-permute-done.1 = bf16[2,2,3,256]{3,2,1,0:T(4,128)(2,1)S(1)} collective-permute-done((bf16[2,2,3,256]{3,2,1,0:T(4,128)(2,1)S(1)}, bf16[2,2,3,256]{3,2,1,0:T(4,128)(2,1)S(1)}, u32[]{:S(2)}, u32[]{:S(2)}) %collective-permute-start.1) | collective-permute-done | bytes 6176 | tf_op jit(solution)/shard_map/ppermute | solution.py:23
  31.8 2.8 %convolution_convert_fusion.2 = bf16[1024,256]{1,0:T(8,128)(2,1)} fusion(bf16[1024,256]{1,0:T(8,128)(2,1)S(1)} %bitcast.161, s32[1024]{0:T(1024)S(1)} %get-tuple-element.46, s32[1024]{0:T(1024)S(1)} %get-tuple-element.47, s32[1024]{0:T(1024)S(1)} %get-tuple-element.45, s32[1024]{0:T(1024)S(1)} %get-tuple-element.48, ...), kind=kOutput, calls=%fused_computation.62 | convolution fusion | flops 545521664 | bytes 1067008 | tf_op jit(solution)/shard_map/dot_general | solution.py:118
  36.7 21.5 %collective-permute-done.5 = bf16[1024,256]{1,0:T(8,128)(2,1)S(1)} collective-permute-done((bf16[1024,256]{1,0:T(8,128)(2,1)}, bf16[1024,256]{1,0:T(8,128)(2,1)S(1)}, u32[]{:S(2)}, u32[]{:S(2)}) %collective-permute-start.5) | collective-permute-done | bytes 524320 | tf_op jit(solution)/shard_map/ppermute | solution.py:8
  61.8 3.4 %collective-permute-start.4 = (bf16[2,1024,256]{2,1,0:T(8,128)(2,1)}, bf16[2,1024,256]{2,1,0:T(8,128)(2,1)}, u32[]{:S(2)}, u32[]{:S(2)}) collective-permute-start(bf16[2,1024,256]{2,1,0:T(8,128)(2,1)} %maximum_bitcast_fusion), channel_id=1, source_target_pairs={{0,1},{1,0},{2,3},{3,2},{4,5},{5,4},{6,7},{7,6},{8,9},{9,8},{10,11... | collective-permute-start | bytes 3145736 | tf_op jit(solution)/shard_map/ppermute | solution.py:13
  65.2 3.4 %collective-permute-done.6 = bf16[1,1024,256]{2,1,0:T(8,128)(2,1)S(1)} collective-permute-done((bf16[1,1024,256]{2,1,0:T(8,128)(2,1)S(1)}, bf16[1,1024,256]{2,1,0:T(8,128)(2,1)S(1)}, u32[]{:S(2)}, u32[]{:S(2)}) %collective-permute-start.6) | collective-permute-done | bytes 524320 | tf_op jit(solution)/shard_map/ppermute | solution.py:13
  70.8 4.0 %collective-permute-start.7 = (bf16[2,1024,256]{2,1,0:T(8,128)(2,1)}, bf16[2,1024,256]{2,1,0:T(8,128)(2,1)}, u32[]{:S(2)}, u32[]{:S(2)}) collective-permute-start(bf16[2,1024,256]{2,1,0:T(8,128)(2,1)} %maximum_bitcast_fusion.1), channel_id=1, source_target_pairs={{0,1},{1,0},{2,3},{3,2},{4,5},{5,4},{6,7},{7,6},{8,9},{9,8},{10,11... | collective-permute-start | bytes 3145736 | tf_op jit(solution)/shard_map/ppermute | solution.py:13
  74.7 4.6 %fusion.134 = bf16[1024,1024]{1,0:T(8,128)(2,1)} fusion(bf16[1024,1024]{1,0:T(8,128)(2,1)S(1)} %copy-done.10, s32[1024]{0:T(1024)S(1)} %get-tuple-element.52, s32[1024]{0:T(1024)S(1)} %get-tuple-element.53, s32[1024]{0:T(1024)S(1)} %get-tuple-element.51, s32[1024]{0:T(1024)S(1)} %get-tuple-element.54, pred[1024]{0:T(1024)(128)(4,1)S(1)} %get-tuple-element.55, ...), kind=kOutput, calls=%fused_computation.45.clone.1 | convolution fusion | flops 2157969408 | bytes 4212736 | tf_op jit(solution)/shard_map/dot_general | solution.py:139
  81.4 4.3 %fusion.102 = f32[1024,1024,1]{1,0,2:T(8,128)} fusion(bf16[4,1024,256]{2,1,0:T(8,128)(2,1)S(1)} %bitcast.155, bf16[4,256,1024]{2,1,0:T(8,128)(2,1)S(1)} %bitcast.150), kind=kOutput, calls=%fused_computation.154 | convolution fusion | flops 2147483648 | bytes 8388608 | tf_op jit(solution)/shard_map/dot_general | solution.py:128
  87.4 2.3 %fusion.103 = f32[1024,1024,1]{1,0,2:T(8,128)S(1)} fusion(bf16[4,1024,256]{2,1,0:T(8,128)(2,1)S(1)} %bitcast.157, bf16[4,256,1024]{2,1,0:T(8,128)(2,1)S(1)} %bitcast.151), kind=kOutput, calls=%fused_computation.155 | convolution fusion | flops 2147483648 | bytes 8388608 | tf_op jit(solution)/shard_map/dot_general | solution.py:128
  89.8 2.7 %fusion = bf16[1024,1024]{1,0:T(8,128)(2,1)S(1)} fusion(f32[1024,1024,1]{1,0,2:T(8,128)S(1)} %fusion.103, bf16[4,1024,256]{2,1,0:T(8,128)(2,1)S(1)} %bitcast.158, bf16[4,256,1024]{2,1,0:T(8,128)(2,1)S(1)} %bitcast.190), kind=kOutput, calls=%fused_computation.1 | convolution fusion | flops 2153775104 | bytes 10485760 | tf_op jit(solution)/shard_map/dot_general | solution.py:131
  92.5 4.4 %fusion.24 = f32[1024,1024]{0,1:T(8,128)} fusion(bf16[1024,1024]{1,0:T(8,128)(2,1)S(1)} %fusion, bf16[1024,1024]{1,0:T(8,128)(2,1)S(1)} %copy-done.11), kind=kOutput, calls=%fused_computation.44 | convolution fusion | flops 2147483648 | bytes 8388608 | tf_op jit(solution)/shard_map/dot_general | solution.py:140
  96.9 12.2 %convolution_add_fusion = f32[1024,1024]{0,1:T(8,128)} fusion(f32[1024,1024]{0,1:T(8,128)} %fusion.24, bf16[1024,1024]{1,0:T(8,128)(2,1)} %param.21, f32[1024,1024,1]{1,0,2:T(8,128)} %fusion.102, bf16[4,1024,256]{2,1,0:T(8,128)(2,1)} %bitcast.156, bf16[4,256,1024]{2,1,0:T(8,128)(2,1)} %bitcast.189), kind=kOutput, calls=%fused_computation.59 | convolution fusion | flops 4302307328 | bytes 18874368 | tf_op jit(solution)/shard_map/dot_general | solution.py:140
  109.1 2.8 %select_bitcast_fusion = f32[1024,2,256]{0,2,1:T(8,128)S(1)} fusion(f32[1024,2,2,256]{0,3,2,1:T(8,128)} %bitcast.152, pred[]{:T(512)S(6)} %eq.101), kind=kLoop, calls=%fused_computation.43 | loop fusion | flops 524288 | bytes 6291457 | tf_op jit(solution)/shard_map/jit(_where)/select_n | solution.py:56
  111.9 4.1 %collective-permute-done.8 = f32[1024,2,256]{0,2,1:T(8,128)S(1)} collective-permute-done((f32[1024,2,256]{0,2,1:T(8,128)S(1)}, f32[1024,2,256]{0,2,1:T(8,128)S(1)}, u32[]{:S(2)}, u32[]{:S(2)}) %collective-permute-start.8) | collective-permute-done | bytes 2097184 | tf_op jit(solution)/shard_map/ppermute | solution.py:13
  118.4 12.1 %collective-permute-done.9 = bf16[1024,1,256]{0,2,1:T(8,128)(2,1)S(1)} collective-permute-done((bf16[1024,1,256]{0,2,1:T(8,128)(2,1)S(1)}, bf16[1024,1,256]{0,2,1:T(8,128)(2,1)S(1)}, u32[]{:S(2)}, u32[]{:S(2)}) %collective-permute-start.9) | collective-permute-done | bytes 524320 | tf_op jit(solution)/shard_map/ppermute | solution.py:13
  131.4 2.8 %convolution_convert_fusion = bf16[1024,256]{1,0:T(8,128)(2,1)} fusion(s32[1024]{0:T(1024)S(1)} %get-tuple-element.46, s32[1024]{0:T(1024)S(1)} %get-tuple-element.47, s32[1024]{0:T(1024)S(1)} %get-tuple-element.45, s32[1024]{0:T(1024)S(1)} %get-tuple-element.48, pred[1024]{0:T(1024)(128)(4,1)S(1)} %get-tuple-element.49, ...), kind=kOutput, calls=%fused_computation.60 | convolution fusion | flops 545521664 | bytes 1067008 | tf_op jit(solution)/shard_map/dot_general | solution.py:147
  134.2 3.3 %collective-permute-start.10 = (bf16[2,512,256]{2,1,0:T(8,128)(2,1)}, bf16[2,512,256]{2,1,0:T(8,128)(2,1)}, u32[]{:S(2)}, u32[]{:S(2)}) collective-permute-start(bf16[2,512,256]{2,1,0:T(8,128)(2,1)} %bitcast.46), channel_id=1, source_target_pairs={{0,31},{1,30},{2,29},{3,28},{4,27},{5,26},{6,25},{7,24},{8,23},{9,... | collective-permute-start | bytes 1572872 | tf_op jit(solution)/shard_map/ppermute | solution.py:8
  138.8 17.0 %collective-permute-done.10 = bf16[2,512,256]{2,1,0:T(8,128)(2,1)} collective-permute-done((bf16[2,512,256]{2,1,0:T(8,128)(2,1)}, bf16[2,512,256]{2,1,0:T(8,128)(2,1)}, u32[]{:S(2)}, u32[]{:S(2)}) %collective-permute-start.10) | collective-permute-done | bytes 524320 | tf_op jit(solution)/shard_map/ppermute | solution.py:8
  155.8 6.4 %add_convert_fusion = (bf16[2,512,256]{2,1,0:T(8,128)(2,1)}, bf16[2,512,256]{2,1,0:T(8,128)(2,1)}) fusion(bf16[2,512,256]{2,1,0:T(8,128)(2,1)} %collective-permute-done.10, f32[256]{0:T(256)S(1)} %bitcast.181, pred[2,512]{1,0:T(4,128)(4,1)S(1)} %get-tuple-element.30, f32[256]{0:T(256)S(1)} %bitcast.177, pred[2,512]{1,0:T(4,128)(4,1)S(1)} %get-tuple-element.31, ...), kind=kLoop, calls=%fused_computation.67 | loop fusion | flops 7077888 | bytes 3685376 | tf_op jit(solution)/shard_map/convert_element_type | solution.py:150
  (72 shorter events, 24.4 us)
Async XLA Ops:
  0.6 80.7 %copy-start = (bf16[1024,1024]{1,0:T(8,128)(2,1)S(1)}, bf16[1024,1024]{1,0:T(8,128)(2,1)}, u32[]{:S(2)}) copy-start(bf16[1024,1024]{1,0:T(8,128)(2,1)} %param.19) | copy-start | bytes 6291460
  0.6 19.4 %copy-start.4 = (bf16[2,512,256]{2,1,0:T(8,128)(2,1)S(1)}, bf16[2,512,256]{2,1,0:T(8,128)(2,1)}, u32[]{:S(2)}) copy-start(bf16[2,512,256]{2,1,0:T(8,128)(2,1)} %param.13) | copy-start | bytes 1572868
  0.7 19.4 %copy-start.7 = (f32[256]{0:T(256)S(1)}, f32[256]{0:T(256)}, u32[]{:S(2)}) copy-start(f32[256]{0:T(256)} %param.18) | copy-start | bytes 3076
  1.5 3.7 %collective-permute-start = (s32[2,512]{1,0:T(2,128)S(1)}, s32[2,512]{1,0:T(2,128)S(1)}, u32[]{:S(2)}, u32[]{:S(2)}) collective-permute-start(s32[2,512]{1,0:T(2,128)S(1)} %subtract_select_fusion), channel_id=1, source_target_pairs={{0,28},{4,24},{8,20},{12,16},{16,12},{20,8},{24,4},{28,0},{1,29},{... | collective-permute-start | bytes 12296 | tf_op jit(solution)/shard_map/ppermute | solution.py:8
  21.3 8.6 %copy-start.8 = (f32[256]{0:T(256)S(1)}, f32[256]{0:T(256)}, u32[]{:S(2)}) copy-start(f32[256]{0:T(256)} %param.17) | copy-start | bytes 3076
  21.3 5.3 %collective-permute-start.2 = (bf16[2,2,3,256]{3,2,1,0:T(4,128)(2,1)S(1)}, bf16[2,2,3,256]{3,2,1,0:T(4,128)(2,1)S(1)}, u32[]{:S(2)}, u32[]{:S(2)}) collective-permute-start(bf16[2,2,3,256]{3,2,1,0:T(4,128)(2,1)S(1)} %get-tuple-element.19), channel_id=1, source_target_pairs={{4,0},{8,4},{12,8},{16,12},{20,16},{24,20},{28,24},{5,1},{9,5},{13... | collective-permute-start | bytes 18440 | tf_op jit(solution)/shard_map/ppermute | solution.py:25
  24.3 5.3 %collective-permute-start.1 = (bf16[2,2,3,256]{3,2,1,0:T(4,128)(2,1)S(1)}, bf16[2,2,3,256]{3,2,1,0:T(4,128)(2,1)S(1)}, u32[]{:S(2)}, u32[]{:S(2)}) collective-permute-start(bf16[2,2,3,256]{3,2,1,0:T(4,128)(2,1)S(1)} %get-tuple-element.18), channel_id=1, source_target_pairs={{0,4},{4,8},{8,12},{12,16},{16,20},{20,24},{24,28},{1,5},{5,9},{9,... | collective-permute-start | bytes 18440 | tf_op jit(solution)/shard_map/ppermute | solution.py:23
  34.6 23.6 %collective-permute-start.5 = (bf16[1024,256]{1,0:T(8,128)(2,1)}, bf16[1024,256]{1,0:T(8,128)(2,1)S(1)}, u32[]{:S(2)}, u32[]{:S(2)}) collective-permute-start(bf16[1024,256]{1,0:T(8,128)(2,1)} %convolution_convert_fusion.2), channel_id=1, source_target_pairs={{0,28},{4,24},{8,20},{12,16},{16,12},{20,8},{24,4},{28,0},{1,29},{... | collective-permute-start | bytes 1572872 | tf_op jit(solution)/shard_map/ppermute | solution.py:8
  35.4 24.0 %collective-permute-start.3 = (bf16[1,1024,256]{2,1,0:T(8,128)(2,1)S(1)}, bf16[1,1024,256]{2,1,0:T(8,128)(2,1)}, u32[]{:S(2)}, u32[]{:S(2)}) collective-permute-start(bf16[1,1024,256]{2,1,0:T(8,128)(2,1)S(1)} %bitcast.159), channel_id=1, source_target_pairs={{0,2},{1,3},{2,0},{3,1},{4,6},{5,7},{6,4},{7,5},{8,10},{9,11},{10,... | collective-permute-start | bytes 1572872 | tf_op jit(solution)/shard_map/ppermute | solution.py:13
  58.2 3.6 %copy-start.6 = (bf16[1024,256]{1,0:T(8,128)(2,1)}, bf16[1024,256]{1,0:T(8,128)(2,1)S(1)}, u32[]{:S(2)}) copy-start(bf16[1024,256]{1,0:T(8,128)(2,1)S(1)} %collective-permute-done.5) | copy-start | bytes 1572868
  58.2 10.4 %collective-permute-start.6 = (bf16[1,1024,256]{2,1,0:T(8,128)(2,1)S(1)}, bf16[1,1024,256]{2,1,0:T(8,128)(2,1)S(1)}, u32[]{:S(2)}, u32[]{:S(2)}) collective-permute-start(bf16[1,1024,256]{2,1,0:T(8,128)(2,1)S(1)} %bitcast.160), channel_id=1, source_target_pairs={{0,2},{1,3},{2,0},{3,1},{4,6},{5,7},{6,4},{7,5},{8,10},{9,11},{10,... | collective-permute-start | bytes 1572872 | tf_op jit(solution)/shard_map/ppermute | solution.py:13
  60.6 9.1 %copy-start.2 = (bf16[1,1,1024,256]{3,2,1,0:T(8,128)(2,1)}, bf16[1,1,1024,256]{3,2,1,0:T(8,128)(2,1)S(1)}, u32[]{:S(2)}) copy-start(bf16[1,1,1024,256]{3,2,1,0:T(8,128)(2,1)S(1)} %get-tuple-element.12) | copy-start | bytes 1572868
  60.6 9.1 %copy-start.3 = (bf16[1,1,1024,256]{3,2,1,0:T(8,128)(2,1)}, bf16[1,1,1024,256]{3,2,1,0:T(8,128)(2,1)S(1)}, u32[]{:S(2)}) copy-start(bf16[1,1,1024,256]{3,2,1,0:T(8,128)(2,1)S(1)} %get-tuple-element.13) | copy-start | bytes 1572868
  61.8 12.9 %copy-start.10 = (bf16[1024,1024]{1,0:T(8,128)(2,1)S(1)}, bf16[1024,1024]{1,0:T(8,128)(2,1)}, u32[]{:S(2)}) copy-start(bf16[1024,1024]{1,0:T(8,128)(2,1)} %param.21) | copy-start | bytes 6291460
  61.8 17.6 %collective-permute-start.4 = (bf16[2,1024,256]{2,1,0:T(8,128)(2,1)}, bf16[2,1024,256]{2,1,0:T(8,128)(2,1)}, u32[]{:S(2)}, u32[]{:S(2)}) collective-permute-start(bf16[2,1024,256]{2,1,0:T(8,128)(2,1)} %maximum_bitcast_fusion), channel_id=1, source_target_pairs={{0,1},{1,0},{2,3},{3,2},{4,5},{5,4},{6,7},{7,6},{8,9},{9,8},{10,11... | collective-permute-start | bytes 3145736 | tf_op jit(solution)/shard_map/ppermute | solution.py:13
  70.8 15.0 %collective-permute-start.7 = (bf16[2,1024,256]{2,1,0:T(8,128)(2,1)}, bf16[2,1024,256]{2,1,0:T(8,128)(2,1)}, u32[]{:S(2)}, u32[]{:S(2)}) collective-permute-start(bf16[2,1024,256]{2,1,0:T(8,128)(2,1)} %maximum_bitcast_fusion.1), channel_id=1, source_target_pairs={{0,1},{1,0},{2,3},{3,2},{4,5},{5,4},{6,7},{7,6},{8,9},{9,8},{10,11... | collective-permute-start | bytes 3145736 | tf_op jit(solution)/shard_map/ppermute | solution.py:13
  81.4 4.3 %copy-start.5 = (bf16[2,2,1024,256]{3,2,1,0:T(8,128)(2,1)}, bf16[2,2,1024,256]{3,2,1,0:T(8,128)(2,1)S(1)}, u32[]{:S(2)}) copy-start(bf16[2,2,1024,256]{3,2,1,0:T(8,128)(2,1)S(1)} %copy.19) | copy-start | bytes 6291460
  87.4 2.4 %copy-start.9 = (bf16[1024,1024]{1,0:T(8,128)(2,1)S(1)}, bf16[1024,1024]{1,0:T(8,128)(2,1)}, u32[]{:S(2)}) copy-start(bf16[1024,1024]{1,0:T(8,128)(2,1)} %param.20) | copy-start | bytes 6291460
  89.8 2.7 %copy-start.11 = (bf16[1024,1024]{1,0:T(8,128)(2,1)S(1)}, bf16[1024,1024]{1,0:T(8,128)(2,1)}, u32[]{:S(2)}) copy-start(bf16[1024,1024]{1,0:T(8,128)(2,1)} %fusion.134) | copy-start | bytes 6291460
  109.1 7.0 %copy-start.1 = (f32[1024,1024]{0,1:T(8,128)S(1)}, f32[1024,1024]{0,1:T(8,128)}, u32[]{:S(2)}) copy-start(f32[1024,1024]{0,1:T(8,128)} %convolution_add_fusion) | copy-start | bytes 12582916
  111.9 4.2 %collective-permute-start.8 = (f32[1024,2,256]{0,2,1:T(8,128)S(1)}, f32[1024,2,256]{0,2,1:T(8,128)S(1)}, u32[]{:S(2)}, u32[]{:S(2)}) collective-permute-start(f32[1024,2,256]{0,2,1:T(8,128)S(1)} %select_bitcast_fusion), channel_id=1, source_target_pairs={{0,1},{1,0},{2,3},{3,2},{4,5},{5,4},{6,7},{7,6},{8,9},{9,8},{10,11... | collective-permute-start | bytes 6291464 | tf_op jit(solution)/shard_map/ppermute | solution.py:13
  117.1 13.4 %collective-permute-start.9 = (bf16[1024,1,256]{0,2,1:T(8,128)(2,1)S(1)}, bf16[1024,1,256]{0,2,1:T(8,128)(2,1)S(1)}, u32[]{:S(2)}, u32[]{:S(2)}) collective-permute-start(bf16[1024,1,256]{0,2,1:T(8,128)(2,1)S(1)} %fusion.45), channel_id=1, source_target_pairs={{0,2},{1,3},{2,0},{3,1},{4,6},{5,7},{6,4},{7,5},{8,10},{9,11},{10,... | collective-permute-start | bytes 1572872 | tf_op jit(solution)/shard_map/ppermute | solution.py:13
  134.2 21.6 %collective-permute-start.10 = (bf16[2,512,256]{2,1,0:T(8,128)(2,1)}, bf16[2,512,256]{2,1,0:T(8,128)(2,1)}, u32[]{:S(2)}, u32[]{:S(2)}) collective-permute-start(bf16[2,512,256]{2,1,0:T(8,128)(2,1)} %bitcast.46), channel_id=1, source_target_pairs={{0,31},{1,30},{2,29},{3,28},{4,27},{5,26},{6,25},{7,24},{8,23},{9,... | collective-permute-start | bytes 1572872 | tf_op jit(solution)/shard_map/ppermute | solution.py:8

commit v9 on v8

--- a/solution.py
+++ b/solution.py
@@ -95,7 +95,7 @@
     half_width = taps // 2
 
     x_fwd = hidden_forward.astype(jnp.float32) + embedded(base_in, table)
-    x_rev = hidden_reverse.astype(jnp.float32) + embedded(comp_back, table)
+    x_rev = lax.optimization_barrier(hidden_reverse.astype(jnp.float32) + embedded(comp_back, table))
     square_fwd, square_rev = lax.psum(
         (jnp.sum(x_fwd * x_fwd, axis=-1), jnp.sum(x_rev * x_rev, axis=-1)), "ch"
     )
@@ -114,13 +114,11 @@
     conv = conv.astype(jnp.bfloat16)
     rows_fwd = conv[0].reshape(-1, local_width)
     rows_all = rows_fwd.shape[0]
-    rows_rev = mirror(
-        jnp.dot(
-            reversal(rows_all, length), conv[1].reshape(rows_all, -1), preferred_element_type=jnp.float32
-        ).astype(jnp.bfloat16),
-        "seq",
-        seq_count,
-    )
+    turned_rev = jnp.dot(
+        reversal(rows_all, length), conv[1].reshape(rows_all, -1), preferred_element_type=jnp.float32
+    ).astype(jnp.bfloat16)
+    rows_fwd, turned_rev = lax.optimization_barrier((rows_fwd, turned_rev))
+    rows_rev = mirror(turned_rev, "seq", seq_count)
 
     def activation(rows):
         pieces = gather_blocks(rows, ch_bits, me)
@@ -134,12 +132,12 @@
         return (jax.nn.silu(gate) * value).astype(jnp.bfloat16)
 
     act_fwd = activation(rows_fwd)
+    part_fwd = jnp.dot(act_fwd, w_out, preferred_element_type=jnp.float32)
+    w_flip = jnp.dot(w_out, reversal(width, width), preferred_element_type=jnp.float32).astype(jnp.bfloat16)
+    rows_rev, part_fwd, w_flip = lax.optimization_barrier((rows_rev, part_fwd, w_flip))
     act_rev = activation(rows_rev)
     lane_flip = reversal(local_width, local_width)
-    w_flip = jnp.dot(w_out, reversal(width, width), preferred_element_type=jnp.float32).astype(jnp.bfloat16)
-    part = jnp.dot(act_fwd, w_out, preferred_element_type=jnp.float32) + jnp.dot(
-        act_rev, w_flip, preferred_element_type=jnp.float32
-    )
+    part = part_fwd + jnp.dot(act_rev, w_flip, preferred_element_type=jnp.float32)
     share = scatter_blocks(part.reshape(part.shape[0], ch_count, local_width), ch_bits, me)
     out_forward = x_fwd + share.reshape(x_fwd.shape)
     row_flip = reversal(share.shape[0], x_fwd.shape[1])

time: 163 us -> 184 us (1.13)
  local copies, waits for them, and re-layouts: 3.92 us -> 19.2 us
  waiting for transfers between devices: 61.1 us -> 68.1 us
  matrix products: 36.8 us -> 41.7 us
  other arithmetic: 31.1 us -> 26.5 us
  starting transfers between devices: 21.7 us -> 19.4 us
    ppermute x6, waiting for transfers between devices: 19.6 us -> 39.6 us  [partner(): lax.ppermute(value, axis, [(k, k ^ mask) for k in range(lax.axis_size(axi...]
    ppermute x3, waiting for transfers between devices: 38.5 us -> 25.5 us  [mirror(): return lax.ppermute(value, axes, [(k, count - 1 - k) for k in range(count)])]
    slice x1 -> x2, local copies, waits for them, and re-layouts: 0.07 us -> 7.92 us  [the longest x1 7.06 us: scatter_blocks(): keep = jnp.where(low, cur[:, :, 0], cur[:, :, 1])]
    add x0 -> x1, other arithmetic: none -> 6.8 us  [local(): part_fwd + jnp.dot(act_rev, w_flip, preferred_element_type=jnp.float32)]
    another operation x0 -> x1, local copies, waits for them, and re-layouts: none -> 6.66 us  [scatter_blocks(): cur = cur.reshape(rows, -1, 2, w)]
    dot_general x1, matrix products: 4.4 us -> 10.8 us  [local(): jnp.dot(act_rev, w_flip, preferred_element_type=jnp.float32)]
    dot_general x2 -> x1, matrix products: 14.8 us -> 10.5 us  [local(): part_fwd = jnp.dot(act_fwd, w_out, preferred_element_type=jnp.float32)]
    convert_element_type x1 -> x2, other arithmetic: 6.41 us -> 2.97 us  [local(): return (out_forward.astype(jnp.bfloat16), out_reverse.astype(jnp.bfloat16))]
  transfers between devices with their start and end apart: 11 -> 11, of which waited for: 6 -> 8; matrix products, arithmetic and copies ran while one was open for 12% -> 15% of each run, Pallas kernels for 0% -> 0%
where the time goes in v9:
time: 184 us; the launch traced here: 182 us
  waiting for transfers between devices  68.1 us (37%)
  matrix products  41.7 us (23%)
  other arithmetic  26.5 us (14%)
  starting transfers between devices  19.4 us (11%)
  local copies, waits for them, and re-layouts  19.2 us (10%)
  blocking collectives  6.55 us (4%)
    ppermute x6, waiting for transfers between devices, partner(): lax.ppermute(value, axis, [(k, k ^ mask) for k in range(lax.axis_size(axi...  39.6 us
    ppermute x3, waiting for transfers between devices, mirror(): return lax.ppermute(value, axes, [(k, count - 1 - k) for k in range(count)])  25.5 us
    dot_general x1, matrix products, local(): jnp.dot(act_rev, w_flip, preferred_element_type=jnp.float32)  10.8 us
    dot_general x1, matrix products, local(): part_fwd = jnp.dot(act_fwd, w_out, preferred_element_type=jnp.float32)  10.5 us
    ppermute x6, starting transfers between devices, partner(): lax.ppermute(value, axis, [(k, k ^ mask) for k in range(lax.axis_size(axi...  9.33 us
    dot_general x2, matrix products, activation(): lax.dot_general(pieces, w_gate.reshape(ch_count, local_width, -1), dims,...  8.71 us
    slice x1, local copies, waits for them, and re-layouts, scatter_blocks(): keep = jnp.where(low, cur[:, :, 0], cur[:, :, 1])  7.06 us
    add x1, other arithmetic, local(): part_fwd + jnp.dot(act_rev, w_flip, preferred_element_type=jnp.float32)  6.8 us
  transfers between devices with their start and end apart: 11, of which 8 were waited for; matrix products, arithmetic and copies ran while one was open for 15% of the time, Pallas kernels for 0%

profile of v9, /device:TPU:17, one launch (start us, length us, event | category | flops | bytes accessed | tf_op | source)
XLA Modules:
  0.0 182.4 jit_solution(8981133580456805938)
XLA Ops:
  5.6 3.6 %multiply_reduce_fusion.1 = (f32[2,512]{1,0:T(2,128)S(1)}, f32[2,512,256]{2,1,0:T(8,128)S(1)}) fusion(f32[256]{0:T(256)S(1)} %bitcast.155, pred[2,512]{1,0:T(4,128)(4,1)S(1)} %get-tuple-element.42, f32[256]{0:T(256)S(1)} %bitcast.152, pred[2,512]{1,0:T(4,128)(4,1)S(1)} %get-tuple-element.40, f32[256]{0:T(256)S(1)} %bitcast.149, ...), kind=kLoop, calls=%fused_computation.76 | loop fusion | flops 6290432 | bytes 2116608 | tf_op jit(solution)/shard_map/reduce_sum | solution.py:100
  9.4 6.6 %all-reduce = (f32[2,512]{1,0:T(2,128)S(1)}, f32[2,512]{1,0:T(2,128)S(1)}) all-reduce(f32[2,512]{1,0:T(2,128)S(1)} %multiply_reduce_fusion, f32[2,512]{1,0:T(2,128)S(1)} %get-tuple-element.37), channel_id=1, replica_groups=mesh['seq'=8,'ch'=4] {'ch'}, use_global_device_ids=true, to_apply=%region_3.4 | all-reduce | flops 2048 | bytes 16384 | tf_op jit(solution)/shard_map/psum | solution.py:99
  16.0 2.8 %fusion.39 = (bf16[1,2,512,256]{3,2,1,0:T(8,128)(2,1)S(1)}, bf16[1,2,512,256]{3,2,1,0:T(8,128)(2,1)S(1)}) fusion(f32[256]{0:T(256)S(1)} %copy-done.9, f32[2,512]{1,0:T(2,128)S(1)} %get-tuple-element.56, f32[256]{0:T(256)S(1)} %bitcast.156, pred[2,512]{1,0:T(4,128)(4,1)S(1)} %get-tuple-element.42, f32[256]{0:T(256)S(1)} %bitcast.153, ...), kind=kLoop, calls=%fused_computation.78 | loop fusion | flops 4456448 | bytes 2640896 | tf_op jit(solution)/shard_map/stack | solution.py:108
  18.8 3.0 %collective-permute-start.2 = (bf16[2,2,3,256]{3,2,1,0:T(4,128)(2,1)S(1)}, bf16[2,2,3,256]{3,2,1,0:T(4,128)(2,1)S(1)}, u32[]{:S(2)}, u32[]{:S(2)}) collective-permute-start(bf16[2,2,3,256]{3,2,1,0:T(4,128)(2,1)S(1)} %get-tuple-element.29), channel_id=1, source_target_pairs={{4,0},{8,4},{12,8},{16,12},{20,16},{24,20},{28,24},{5,1},{9,5},{13... | collective-permute-start | bytes 18440 | tf_op jit(solution)/shard_map/ppermute | solution.py:25
  21.9 2.3 %collective-permute-start.1 = (bf16[2,2,3,256]{3,2,1,0:T(4,128)(2,1)S(1)}, bf16[2,2,3,256]{3,2,1,0:T(4,128)(2,1)S(1)}, u32[]{:S(2)}, u32[]{:S(2)}) collective-permute-start(bf16[2,2,3,256]{3,2,1,0:T(4,128)(2,1)S(1)} %get-tuple-element.28), channel_id=1, source_target_pairs={{0,4},{4,8},{8,12},{12,16},{16,20},{20,24},{24,28},{1,5},{5,9},{9,... | collective-permute-start | bytes 18440 | tf_op jit(solution)/shard_map/ppermute | solution.py:23
  24.2 3.0 %collective-permute-done.1 = bf16[2,2,3,256]{3,2,1,0:T(4,128)(2,1)S(1)} collective-permute-done((bf16[2,2,3,256]{3,2,1,0:T(4,128)(2,1)S(1)}, bf16[2,2,3,256]{3,2,1,0:T(4,128)(2,1)S(1)}, u32[]{:S(2)}, u32[]{:S(2)}) %collective-permute-start.1) | collective-permute-done | bytes 6176 | tf_op jit(solution)/shard_map/ppermute | solution.py:23
  30.1 2.8 %convolution_convert_fusion.2 = bf16[1024,256]{1,0:T(8,128)(2,1)} fusion(bf16[1024,256]{1,0:T(8,128)(2,1)S(1)} %bitcast.142, s32[1024]{0:T(1024)S(1)} %get-tuple-element.58, s32[1024]{0:T(1024)S(1)} %get-tuple-element.59, s32[1024]{0:T(1024)S(1)} %get-tuple-element.57, s32[1024]{0:T(1024)S(1)} %get-tuple-element.60, ...), kind=kOutput, calls=%fused_computation.60 | convolution fusion | flops 545521664 | bytes 1067008 | tf_op jit(solution)/shard_map/dot_general | solution.py:117
  34.2 10.1 %collective-permute-done.4 = bf16[1,1024,256]{2,1,0:T(8,128)(2,1)} collective-permute-done((bf16[1,1024,256]{2,1,0:T(8,128)(2,1)}, bf16[1,1024,256]{2,1,0:T(8,128)(2,1)}, u32[]{:S(2)}, u32[]{:S(2)}) %collective-permute-start.4) | collective-permute-done | bytes 524320 | tf_op jit(solution)/shard_map/ppermute | solution.py:13
  47.4 3.3 %collective-permute-start.5 = (bf16[2,1024,256]{2,1,0:T(8,128)(2,1)}, bf16[2,1024,256]{2,1,0:T(8,128)(2,1)}, u32[]{:S(2)}, u32[]{:S(2)}) collective-permute-start(bf16[2,1024,256]{2,1,0:T(8,128)(2,1)} %maximum_bitcast_fusion), channel_id=1, source_target_pairs={{0,1},{1,0},{2,3},{3,2},{4,5},{5,4},{6,7},{7,6},{8,9},{9,8},{10,11... | collective-permute-start | bytes 3145736 | tf_op jit(solution)/shard_map/ppermute | solution.py:13
  50.8 6.2 %convert_bitcast_fusion = bf16[1024,1024]{0,1:T(8,128)(2,1)} fusion(bf16[1024,1024]{1,0:T(8,128)(2,1)} %param.21, s32[1024]{0:T(1024)S(1)} %get-tuple-element.64, s32[1024]{0:T(1024)S(1)} %get-tuple-element.65, s32[1024]{0:T(1024)S(1)} %get-tuple-element.63, s32[1024]{0:T(1024)S(1)} %get-tuple-element.66, pred[1024]{0:T(1024)(128)(4,1)S(1)} %get-tuple-element.67, ...), kind=kOutput, calls=%fused_computation.42 | convolution fusion | flops 2157969408 | bytes 4212736 | tf_op jit(solution)/shard_map/dot_general | solution.py:136
  59.5 4.4 %fusion.99 = f32[1024,1024,1]{1,0,2:T(8,128)} fusion(bf16[4,1024,256]{2,1,0:T(8,128)(2,1)S(1)} %bitcast.140, bf16[4,256,1024]{2,1,0:T(8,128)(2,1)S(1)} %bitcast.135), kind=kOutput, calls=%fused_computation.154 | convolution fusion | flops 2147483648 | bytes 8388608 | tf_op jit(solution)/shard_map/dot_general | solution.py:126
  63.9 10.5 %fusion.37 = f32[1024,1024]{1,0:T(8,128)} fusion(bf16[1024,1024]{1,0:T(8,128)(2,1)} %param.21, f32[1024,1024,1]{1,0,2:T(8,128)} %fusion.99, bf16[4,1024,256]{2,1,0:T(8,128)(2,1)} %bitcast.141, bf16[4,256,1024]{2,1,0:T(8,128)(2,1)} %bitcast.165), kind=kOutput, calls=%fused_computation.56 | convolution fusion | flops 4301258752 | bytes 14680064 | tf_op jit(solution)/shard_map/dot_general | solution.py:135
  74.5 8.5 %collective-permute-done.3 = bf16[1024,256]{1,0:T(8,128)(2,1)} collective-permute-done((bf16[1024,256]{1,0:T(8,128)(2,1)}, bf16[1024,256]{1,0:T(8,128)(2,1)}, u32[]{:S(2)}, u32[]{:S(2)}) %collective-permute-start.3) | collective-permute-done | bytes 524320 | tf_op jit(solution)/shard_map/ppermute | solution.py:8
  84.2 11.6 %collective-permute-done.6 = bf16[1,1024,256]{2,1,0:T(8,128)(2,1)S(1)} collective-permute-done((bf16[1,1024,256]{2,1,0:T(8,128)(2,1)}, bf16[1,1024,256]{2,1,0:T(8,128)(2,1)S(1)}, u32[]{:S(2)}, u32[]{:S(2)}) %collective-permute-start.6) | collective-permute-done | bytes 524320 | tf_op jit(solution)/shard_map/ppermute | solution.py:13
  98.8 2.3 %collective-permute-done.7 = bf16[2,1024,256]{2,1,0:T(8,128)(2,1)S(1)} collective-permute-done((bf16[2,1024,256]{2,1,0:T(8,128)(2,1)S(1)}, bf16[2,1024,256]{2,1,0:T(8,128)(2,1)S(1)}, u32[]{:S(2)}, u32[]{:S(2)}) %collective-permute-start.7) | collective-permute-done | bytes 1048608 | tf_op jit(solution)/shard_map/ppermute | solution.py:13
  102.8 4.3 %fusion.100 = f32[1024,1024,1]{1,0,2:T(8,128)} fusion(bf16[4,1024,256]{2,1,0:T(8,128)(2,1)S(1)} %bitcast.138, bf16[4,256,1024]{2,1,0:T(8,128)(2,1)S(1)} %bitcast.136), kind=kOutput, calls=%fused_computation.155 | convolution fusion | flops 2147483648 | bytes 8388608 | tf_op jit(solution)/shard_map/dot_general | solution.py:126
  107.2 10.8 %fusion.38 = f32[1024,1024]{1,0:T(8,128)} fusion(bf16[1024,1024]{0,1:T(8,128)(2,1)} %convert_bitcast_fusion, f32[1024,1024,1]{1,0,2:T(8,128)} %fusion.100, bf16[4,1024,256]{2,1,0:T(8,128)(2,1)} %bitcast.139, bf16[4,256,1024]{2,1,0:T(8,128)(2,1)} %bitcast.166), kind=kOutput, calls=%fused_computation.57 | convolution fusion | flops 4301258752 | bytes 14680064 | tf_op jit(solution)/shard_map/dot_general | solution.py:140
  118.0 6.8 %add.174 = f32[1024,1024]{1,0:T(8,128)} add(f32[1024,1024]{1,0:T(8,128)} %fusion.37, f32[1024,1024]{1,0:T(8,128)} %fusion.38) | non-fusion elementwise | flops 1048576 | bytes 12582912 | tf_op jit(solution)/shard_map/add | solution.py:140
  124.8 6.7 %reshape_reshape.3 = f32[1024,2,2,256]{3,2,1,0:T(2,128)} reshape(f32[1024,1024]{1,0:T(8,128)} %add.174) | data formatting | bytes 8388608 | tf_op jit(solution)/shard_map/reshape;reshape | solution.py:53
  131.5 7.1 %fusion.95 = (f32[1024,2,1,256]{3,2,1,0:T(1,128)S(1)}, f32[1024,2,1,256]{3,2,1,0:T(1,128)S(1)}) fusion(f32[1024,2,2,256]{3,2,1,0:T(2,128)} %reshape_reshape.3), kind=kLoop, calls=%fused_computation.150 | loop fusion | bytes 8388608 | tf_op jit(solution)/shard_map/slice | solution.py:55
  139.2 3.8 %collective-permute-done.8 = f32[1024,2,256]{2,0,1:T(8,128)S(1)} collective-permute-done((f32[1024,2,256]{2,0,1:T(8,128)S(1)}, f32[1024,2,256]{2,0,1:T(8,128)S(1)}, u32[]{:S(2)}, u32[]{:S(2)}) %collective-permute-start.8) | collective-permute-done | bytes 2097184 | tf_op jit(solution)/shard_map/ppermute | solution.py:13
  144.9 11.8 %collective-permute-done.9 = bf16[1024,1,256]{2,0,1:T(8,128)(2,1)S(1)} collective-permute-done((bf16[1024,1,256]{2,0,1:T(8,128)(2,1)S(1)}, bf16[1024,1,256]{2,0,1:T(8,128)(2,1)S(1)}, u32[]{:S(2)}, u32[]{:S(2)}) %collective-permute-start.9) | collective-permute-done | bytes 524320 | tf_op jit(solution)/shard_map/ppermute | solution.py:13
  159.5 2.9 %collective-permute-start.10 = (bf16[2,512,256]{2,1,0:T(8,128)(2,1)S(1)}, bf16[2,512,256]{2,1,0:T(8,128)(2,1)S(1)}, u32[]{:S(2)}, u32[]{:S(2)}) collective-permute-start(bf16[2,512,256]{2,1,0:T(8,128)(2,1)S(1)} %bitcast.167), channel_id=1, source_target_pairs={{0,31},{1,30},{2,29},{3,28},{4,27},{5,26},{6,25},{7,24},{8,23},{9,... | collective-permute-start | bytes 1572872 | tf_op jit(solution)/shard_map/ppermute | solution.py:8
  164.5 17.0 %collective-permute-done.10 = bf16[2,512,256]{2,1,0:T(8,128)(2,1)S(1)} collective-permute-done((bf16[2,512,256]{2,1,0:T(8,128)(2,1)S(1)}, bf16[2,512,256]{2,1,0:T(8,128)(2,1)S(1)}, u32[]{:S(2)}, u32[]{:S(2)}) %collective-permute-start.10) | collective-permute-done | bytes 524320 | tf_op jit(solution)/shard_map/ppermute | solution.py:8
  (72 shorter events, 29.3 us)
Async XLA Ops:
  0.6 58.9 %copy-start = (bf16[1024,1024]{1,0:T(8,128)(2,1)S(1)}, bf16[1024,1024]{1,0:T(8,128)(2,1)}, u32[]{:S(2)}) copy-start(bf16[1024,1024]{1,0:T(8,128)(2,1)} %param.19) | copy-start | bytes 6291460
  0.6 15.3 %copy-start.9 = (f32[256]{0:T(256)S(1)}, f32[256]{0:T(256)}, u32[]{:S(2)}) copy-start(f32[256]{0:T(256)} %param.18) | copy-start | bytes 3076
  1.5 3.7 %collective-permute-start = (s32[2,512]{1,0:T(2,128)S(1)}, s32[2,512]{1,0:T(2,128)S(1)}, u32[]{:S(2)}, u32[]{:S(2)}) collective-permute-start(s32[2,512]{1,0:T(2,128)S(1)} %subtract_select_fusion), channel_id=1, source_target_pairs={{0,28},{4,24},{8,20},{12,16},{16,12},{20,8},{24,4},{28,0},{1,29},{... | collective-permute-start | bytes 12296 | tf_op jit(solution)/shard_map/ppermute | solution.py:8
  18.8 8.6 %copy-start.10 = (f32[256]{0:T(256)S(1)}, f32[256]{0:T(256)}, u32[]{:S(2)}) copy-start(f32[256]{0:T(256)} %param.17) | copy-start | bytes 3076
  18.8 5.3 %collective-permute-start.2 = (bf16[2,2,3,256]{3,2,1,0:T(4,128)(2,1)S(1)}, bf16[2,2,3,256]{3,2,1,0:T(4,128)(2,1)S(1)}, u32[]{:S(2)}, u32[]{:S(2)}) collective-permute-start(bf16[2,2,3,256]{3,2,1,0:T(4,128)(2,1)S(1)} %get-tuple-element.29), channel_id=1, source_target_pairs={{4,0},{8,4},{12,8},{16,12},{20,16},{24,20},{28,24},{5,1},{9,5},{13... | collective-permute-start | bytes 18440 | tf_op jit(solution)/shard_map/ppermute | solution.py:25
  21.9 5.3 %collective-permute-start.1 = (bf16[2,2,3,256]{3,2,1,0:T(4,128)(2,1)S(1)}, bf16[2,2,3,256]{3,2,1,0:T(4,128)(2,1)S(1)}, u32[]{:S(2)}, u32[]{:S(2)}) collective-permute-start(bf16[2,2,3,256]{3,2,1,0:T(4,128)(2,1)S(1)} %get-tuple-element.28), channel_id=1, source_target_pairs={{0,4},{4,8},{8,12},{12,16},{16,20},{20,24},{24,28},{1,5},{5,9},{9,... | collective-permute-start | bytes 18440 | tf_op jit(solution)/shard_map/ppermute | solution.py:23
  33.0 11.4 %collective-permute-start.4 = (bf16[1,1024,256]{2,1,0:T(8,128)(2,1)}, bf16[1,1024,256]{2,1,0:T(8,128)(2,1)}, u32[]{:S(2)}, u32[]{:S(2)}) collective-permute-start(bf16[1,1024,256]{2,1,0:T(8,128)(2,1)} %bitcast.16), channel_id=1, source_target_pairs={{0,2},{1,3},{2,0},{3,1},{4,6},{5,7},{6,4},{7,5},{8,10},{9,11},{10,... | collective-permute-start | bytes 1572872 | tf_op jit(solution)/shard_map/ppermute | solution.py:13
  45.6 0.8 copy-start.3
  45.6 1.8 %copy-start.5 = (bf16[1,1,1024,256]{3,2,1,0:T(8,128)(2,1)}, bf16[1,1,1024,256]{3,2,1,0:T(8,128)(2,1)S(1)}, u32[]{:S(2)}) copy-start(bf16[1,1,1024,256]{3,2,1,0:T(8,128)(2,1)S(1)} %get-tuple-element.25) | copy-start | bytes 1572868
  47.4 10.3 %collective-permute-start.5 = (bf16[2,1024,256]{2,1,0:T(8,128)(2,1)}, bf16[2,1024,256]{2,1,0:T(8,128)(2,1)}, u32[]{:S(2)}, u32[]{:S(2)}) collective-permute-start(bf16[2,1024,256]{2,1,0:T(8,128)(2,1)} %maximum_bitcast_fusion), channel_id=1, source_target_pairs={{0,1},{1,0},{2,3},{3,2},{4,5},{5,4},{6,7},{7,6},{8,9},{9,8},{10,11... | collective-permute-start | bytes 3145736 | tf_op jit(solution)/shard_map/ppermute | solution.py:13
  50.8 7.0 %copy-start.4 = (bf16[1,1,1024,256]{3,2,1,0:T(8,128)(2,1)S(1)}, bf16[1,1,1024,256]{3,2,1,0:T(8,128)(2,1)}, u32[]{:S(2)}) copy-start(bf16[1,1,1024,256]{3,2,1,0:T(8,128)(2,1)} %copy-done.3) | copy-start | bytes 1572868
  50.8 7.0 %copy-start.6 = (bf16[1,1,1024,256]{3,2,1,0:T(8,128)(2,1)S(1)}, bf16[1,1,1024,256]{3,2,1,0:T(8,128)(2,1)}, u32[]{:S(2)}) copy-start(bf16[1,1,1024,256]{3,2,1,0:T(8,128)(2,1)} %copy-done.5) | copy-start | bytes 1572868
  57.0 25.9 %collective-permute-start.3 = (bf16[1024,256]{1,0:T(8,128)(2,1)}, bf16[1024,256]{1,0:T(8,128)(2,1)}, u32[]{:S(2)}, u32[]{:S(2)}) collective-permute-start(bf16[1024,256]{1,0:T(8,128)(2,1)} %convolution_convert_fusion.2), channel_id=1, source_target_pairs={{0,28},{4,24},{8,20},{12,16},{16,12},{20,8},{24,4},{28,0},{1,29},{... | collective-permute-start | bytes 1572872 | tf_op jit(solution)/shard_map/ppermute | solution.py:8
  59.5 4.4 %copy-start.8 = (bf16[2,2,1024,256]{3,2,1,0:T(8,128)(2,1)}, bf16[2,2,1024,256]{3,2,1,0:T(8,128)(2,1)S(1)}, u32[]{:S(2)}) copy-start(bf16[2,2,1024,256]{3,2,1,0:T(8,128)(2,1)S(1)} %copy.22) | copy-start | bytes 6291460
  82.9 12.8 %collective-permute-start.6 = (bf16[1,1024,256]{2,1,0:T(8,128)(2,1)}, bf16[1,1024,256]{2,1,0:T(8,128)(2,1)S(1)}, u32[]{:S(2)}, u32[]{:S(2)}) collective-permute-start(bf16[1,1024,256]{2,1,0:T(8,128)(2,1)} %bitcast.28), channel_id=1, source_target_pairs={{0,2},{1,3},{2,0},{3,1},{4,6},{5,7},{6,4},{7,5},{8,10},{9,11},{10,... | collective-permute-start | bytes 1572872 | tf_op jit(solution)/shard_map/ppermute | solution.py:13
  97.0 4.1 %collective-permute-start.7 = (bf16[2,1024,256]{2,1,0:T(8,128)(2,1)S(1)}, bf16[2,1024,256]{2,1,0:T(8,128)(2,1)S(1)}, u32[]{:S(2)}, u32[]{:S(2)}) collective-permute-start(bf16[2,1024,256]{2,1,0:T(8,128)(2,1)S(1)} %maximum_bitcast_fusion.1), channel_id=1, source_target_pairs={{0,1},{1,0},{2,3},{3,2},{4,5},{5,4},{6,7},{7,6},{8,9},{9,8},{10,11... | collective-permute-start | bytes 3145736 | tf_op jit(solution)/shard_map/ppermute | solution.py:13
  101.5 1.3 copy-start.7
  138.8 4.2 %collective-permute-start.8 = (f32[1024,2,256]{2,0,1:T(8,128)S(1)}, f32[1024,2,256]{2,0,1:T(8,128)S(1)}, u32[]{:S(2)}, u32[]{:S(2)}) collective-permute-start(f32[1024,2,256]{2,0,1:T(8,128)S(1)} %select_bitcast_fusion), channel_id=1, source_target_pairs={{0,1},{1,0},{2,3},{3,2},{4,5},{5,4},{6,7},{7,6},{8,9},{9,8},{10,11... | collective-permute-start | bytes 6291464 | tf_op jit(solution)/shard_map/ppermute | solution.py:13
  143.6 13.2 %collective-permute-start.9 = (bf16[1024,1,256]{2,0,1:T(8,128)(2,1)S(1)}, bf16[1024,1,256]{2,0,1:T(8,128)(2,1)S(1)}, u32[]{:S(2)}, u32[]{:S(2)}) collective-permute-start(bf16[1024,1,256]{2,0,1:T(8,128)(2,1)S(1)} %fusion.41), channel_id=1, source_target_pairs={{0,2},{1,3},{2,0},{3,1},{4,6},{5,7},{6,4},{7,5},{8,10},{9,11},{10,... | collective-permute-start | bytes 1572872 | tf_op jit(solution)/shard_map/ppermute | solution.py:13
  157.5 5.0 %copy-start.2 = (bf16[2,512,256]{2,1,0:T(8,128)(2,1)S(1)}, bf16[2,512,256]{2,1,0:T(8,128)(2,1)}, u32[]{:S(2)}) copy-start(bf16[2,512,256]{2,1,0:T(8,128)(2,1)} %param.13) | copy-start | bytes 1572868
  159.5 22.0 %collective-permute-start.10 = (bf16[2,512,256]{2,1,0:T(8,128)(2,1)S(1)}, bf16[2,512,256]{2,1,0:T(8,128)(2,1)S(1)}, u32[]{:S(2)}, u32[]{:S(2)}) collective-permute-start(bf16[2,512,256]{2,1,0:T(8,128)(2,1)S(1)} %bitcast.167), channel_id=1, source_target_pairs={{0,31},{1,30},{2,29},{3,28},{4,27},{5,26},{6,25},{7,24},{8,23},{9,... | collective-permute-start | bytes 1572872 | tf_op jit(solution)/shard_map/ppermute | solution.py:8
  162.5 20.0 %copy-start.1 = (bf16[1024,1024]{1,0:T(8,128)(2,1)S(1)}, bf16[1024,1024]{1,0:T(8,128)(2,1)}, u32[]{:S(2)}) copy-start(bf16[1024,1024]{1,0:T(8,128)(2,1)} %param.19) | copy-start | bytes 6291460

commit v10 on v8

--- a/solution.py
+++ b/solution.py
@@ -95,7 +95,7 @@
     half_width = taps // 2
 
     x_fwd = hidden_forward.astype(jnp.float32) + embedded(base_in, table)
-    x_rev = hidden_reverse.astype(jnp.float32) + embedded(comp_back, table)
+    x_rev = lax.optimization_barrier(hidden_reverse.astype(jnp.float32) + embedded(comp_back, table))
     square_fwd, square_rev = lax.psum(
         (jnp.sum(x_fwd * x_fwd, axis=-1), jnp.sum(x_rev * x_rev, axis=-1)), "ch"
     )

time: 163 us -> 157 us (0.963)
  waiting for transfers between devices: 61.1 us -> 56 us
  local copies, waits for them, and re-layouts: 3.92 us -> 6.75 us
  other arithmetic: 31.1 us -> 28.4 us
    ppermute x3, waiting for transfers between devices: 38.5 us -> 33.4 us  [mirror(): return lax.ppermute(value, axes, [(k, count - 1 - k) for k in range(count)])]
    another operation x2 -> x1, other arithmetic: 3.86 us -> 2.82 us  [local(): stacked = jnp.stack([normed_fwd, normed_rev])]
    convert_element_type x1 -> x2, other arithmetic: 6.41 us -> 5.9 us  [local(): return (out_forward.astype(jnp.bfloat16), out_reverse.astype(jnp.bfloat16))]
  transfers between devices with their start and end apart: 11 -> 11, of which waited for: 6 -> 6; matrix products, arithmetic and copies ran while one was open for 12% -> 16% of each run, Pallas kernels for 0% -> 0%
where the time goes in v10:
time: 157 us
  waiting for transfers between devices  56 us (36%)
  matrix products  36.2 us (23%)
  other arithmetic  28.4 us (18%)
  starting transfers between devices  21.7 us (14%)
  local copies, waits for them, and re-layouts  6.75 us (4%)
  blocking collectives  6.55 us (4%)
    ppermute x3, waiting for transfers between devices, mirror(): return lax.ppermute(value, axes, [(k, count - 1 - k) for k in range(count)])  33.4 us
    ppermute x6, waiting for transfers between devices, partner(): lax.ppermute(value, axis, [(k, k ^ mask) for k in range(lax.axis_size(axi...  19.7 us
    dot_general x1, matrix products, local(): jnp.dot(act_fwd, w_out, preferred_element_type=jnp.float32)  11.6 us
    ppermute x6, starting transfers between devices, partner(): lax.ppermute(value, axis, [(k, k ^ mask) for k in range(lax.axis_size(axi...  11.3 us
    dot_general x2, matrix products, activation(): lax.dot_general(pieces, w_gate.reshape(ch_count, local_width, -1), dims,...  6.67 us
    psum x1, blocking collectives, local(): lax.psum((jnp.sum(x_fwd * x_fwd, axis=-1), jnp.sum(x_rev * x_rev, axis=-1...  6.55 us
    convert_element_type x2, other arithmetic, local(): return (out_forward.astype(jnp.bfloat16), out_reverse.astype(jnp.bfloat16))  5.9 us
    another operation x6, other arithmetic, gather_blocks(): cur = jnp.stack([first, second], axis=1).reshape((-1,) + block.shape)  5.8 us
  transfers between devices with their start and end apart: 11, of which 6 were waited for; matrix products, arithmetic and copies ran while one was open for 16% of the time, Pallas kernels for 0%

profile of v10, /device:TPU:17, one launch (start us, length us, event | category | flops | bytes accessed | tf_op | source)
XLA Modules:
  0.0 156.7 jit_solution(4088712540140729232)
XLA Ops:
  5.6 3.6 %multiply_reduce_fusion.1 = (f32[2,512]{1,0:T(2,128)S(1)}, f32[2,512,256]{2,1,0:T(8,128)S(1)}) fusion(f32[256]{0:T(256)S(1)} %bitcast.172, pred[2,512]{1,0:T(4,128)(4,1)S(1)} %get-tuple-element.30, f32[256]{0:T(256)S(1)} %bitcast.169, pred[2,512]{1,0:T(4,128)(4,1)S(1)} %get-tuple-element.28, f32[256]{0:T(256)S(1)} %bitcast.166, ...), kind=kLoop, calls=%fused_computation.78 | loop fusion | flops 6290432 | bytes 2116608 | tf_op jit(solution)/shard_map/reduce_sum | solution.py:100
  9.4 6.6 %all-reduce = (f32[2,512]{1,0:T(2,128)S(1)}, f32[2,512]{1,0:T(2,128)S(1)}) all-reduce(f32[2,512]{1,0:T(2,128)S(1)} %multiply_reduce_fusion, f32[2,512]{1,0:T(2,128)S(1)} %get-tuple-element.25), channel_id=1, replica_groups=mesh['seq'=8,'ch'=4] {'ch'}, use_global_device_ids=true, to_apply=%region_3.4 | all-reduce | flops 2048 | bytes 16384 | tf_op jit(solution)/shard_map/psum | solution.py:99
  16.0 2.8 %fusion.43 = (bf16[1,2,512,256]{3,2,1,0:T(8,128)(2,1)S(1)}, bf16[1,2,512,256]{3,2,1,0:T(8,128)(2,1)S(1)}) fusion(f32[256]{0:T(256)S(1)} %copy-done.12, f32[2,512]{1,0:T(2,128)S(1)} %get-tuple-element.44, f32[256]{0:T(256)S(1)} %bitcast.173, pred[2,512]{1,0:T(4,128)(4,1)S(1)} %get-tuple-element.30, f32[256]{0:T(256)S(1)} %bitcast.170, ...), kind=kLoop, calls=%fused_computation.80 | loop fusion | flops 4456448 | bytes 2640896 | tf_op jit(solution)/shard_map/stack | solution.py:108
  18.8 3.0 %collective-permute-start.2 = (bf16[2,2,3,256]{3,2,1,0:T(4,128)(2,1)S(1)}, bf16[2,2,3,256]{3,2,1,0:T(4,128)(2,1)S(1)}, u32[]{:S(2)}, u32[]{:S(2)}) collective-permute-start(bf16[2,2,3,256]{3,2,1,0:T(4,128)(2,1)S(1)} %get-tuple-element.17), channel_id=1, source_target_pairs={{4,0},{8,4},{12,8},{16,12},{20,16},{24,20},{28,24},{5,1},{9,5},{13... | collective-permute-start | bytes 18440 | tf_op jit(solution)/shard_map/ppermute | solution.py:25
  24.2 3.0 %collective-permute-done.1 = bf16[2,2,3,256]{3,2,1,0:T(4,128)(2,1)S(1)} collective-permute-done((bf16[2,2,3,256]{3,2,1,0:T(4,128)(2,1)S(1)}, bf16[2,2,3,256]{3,2,1,0:T(4,128)(2,1)S(1)}, u32[]{:S(2)}, u32[]{:S(2)}) %collective-permute-start.1) | collective-permute-done | bytes 6176 | tf_op jit(solution)/shard_map/ppermute | solution.py:23
  30.1 2.8 %convolution_convert_fusion.2 = bf16[1024,256]{1,0:T(8,128)(2,1)} fusion(bf16[1024,256]{1,0:T(8,128)(2,1)S(1)} %bitcast.159, s32[1024]{0:T(1024)S(1)} %get-tuple-element.46, s32[1024]{0:T(1024)S(1)} %get-tuple-element.47, s32[1024]{0:T(1024)S(1)} %get-tuple-element.45, s32[1024]{0:T(1024)S(1)} %get-tuple-element.48, ...), kind=kOutput, calls=%fused_computation.62 | convolution fusion | flops 545521664 | bytes 1067008 | tf_op jit(solution)/shard_map/dot_general | solution.py:118
  35.0 21.6 %collective-permute-done.5 = bf16[1024,256]{1,0:T(8,128)(2,1)} collective-permute-done((bf16[1024,256]{1,0:T(8,128)(2,1)}, bf16[1024,256]{1,0:T(8,128)(2,1)}, u32[]{:S(2)}, u32[]{:S(2)}) %collective-permute-start.5) | collective-permute-done | bytes 524320 | tf_op jit(solution)/shard_map/ppermute | solution.py:8
  60.3 3.4 %collective-permute-start.4 = (bf16[2,1024,256]{2,1,0:T(8,128)(2,1)}, bf16[2,1024,256]{2,1,0:T(8,128)(2,1)}, u32[]{:S(2)}, u32[]{:S(2)}) collective-permute-start(bf16[2,1024,256]{2,1,0:T(8,128)(2,1)} %maximum_bitcast_fusion), channel_id=1, source_target_pairs={{0,1},{1,0},{2,3},{3,2},{4,5},{5,4},{6,7},{7,6},{8,9},{9,8},{10,11... | collective-permute-start | bytes 3145736 | tf_op jit(solution)/shard_map/ppermute | solution.py:13
  63.8 3.4 %collective-permute-done.6 = bf16[1,1024,256]{2,1,0:T(8,128)(2,1)S(1)} collective-permute-done((bf16[1,1024,256]{2,1,0:T(8,128)(2,1)}, bf16[1,1024,256]{2,1,0:T(8,128)(2,1)S(1)}, u32[]{:S(2)}, u32[]{:S(2)}) %collective-permute-start.6) | collective-permute-done | bytes 524320 | tf_op jit(solution)/shard_map/ppermute | solution.py:13
  70.2 4.0 %collective-permute-start.7 = (bf16[2,1024,256]{2,1,0:T(8,128)(2,1)}, bf16[2,1024,256]{2,1,0:T(8,128)(2,1)}, u32[]{:S(2)}, u32[]{:S(2)}) collective-permute-start(bf16[2,1024,256]{2,1,0:T(8,128)(2,1)} %maximum_bitcast_fusion.1), channel_id=1, source_target_pairs={{0,1},{1,0},{2,3},{3,2},{4,5},{5,4},{6,7},{7,6},{8,9},{9,8},{10,11... | collective-permute-start | bytes 3145736 | tf_op jit(solution)/shard_map/ppermute | solution.py:13
  74.2 4.6 %fusion.134 = bf16[1024,1024]{1,0:T(8,128)(2,1)} fusion(bf16[1024,1024]{1,0:T(8,128)(2,1)S(1)} %copy-done.15, s32[1024]{0:T(1024)S(1)} %get-tuple-element.52, s32[1024]{0:T(1024)S(1)} %get-tuple-element.53, s32[1024]{0:T(1024)S(1)} %get-tuple-element.51, s32[1024]{0:T(1024)S(1)} %get-tuple-element.54, pred[1024]{0:T(1024)(128)(4,1)S(1)} %get-tuple-element.55, ...), kind=kOutput, calls=%fused_computation.45.clone.1 | convolution fusion | flops 2157969408 | bytes 4212736 | tf_op jit(solution)/shard_map/dot_general | solution.py:139
  80.8 4.3 %fusion.102 = f32[1024,1024,1]{1,0,2:T(8,128)} fusion(bf16[4,1024,256]{2,1,0:T(8,128)(2,1)S(1)} %bitcast.155, bf16[4,256,1024]{2,1,0:T(8,128)(2,1)S(1)} %bitcast.150), kind=kOutput, calls=%fused_computation.154 | convolution fusion | flops 2147483648 | bytes 8388608 | tf_op jit(solution)/shard_map/dot_general | solution.py:128
  86.9 2.3 %fusion.103 = f32[1024,1024,1]{1,0,2:T(8,128)S(1)} fusion(bf16[4,1024,256]{2,1,0:T(8,128)(2,1)S(1)} %bitcast.157, bf16[4,256,1024]{2,1,0:T(8,128)(2,1)S(1)} %bitcast.151), kind=kOutput, calls=%fused_computation.155 | convolution fusion | flops 2147483648 | bytes 8388608 | tf_op jit(solution)/shard_map/dot_general | solution.py:128
  89.3 2.7 %fusion = bf16[1024,1024]{1,0:T(8,128)(2,1)S(1)} fusion(f32[1024,1024,1]{1,0,2:T(8,128)S(1)} %fusion.103, bf16[4,1024,256]{2,1,0:T(8,128)(2,1)S(1)} %bitcast.158, bf16[4,256,1024]{2,1,0:T(8,128)(2,1)S(1)} %bitcast.183), kind=kOutput, calls=%fused_computation.1 | convolution fusion | flops 2153775104 | bytes 10485760 | tf_op jit(solution)/shard_map/dot_general | solution.py:131
  91.9 4.4 %fusion.24 = f32[1024,1024]{0,1:T(8,128)} fusion(bf16[1024,1024]{1,0:T(8,128)(2,1)S(1)} %fusion, bf16[1024,1024]{1,0:T(8,128)(2,1)S(1)} %copy-done.16), kind=kOutput, calls=%fused_computation.44 | convolution fusion | flops 2147483648 | bytes 8388608 | tf_op jit(solution)/shard_map/dot_general | solution.py:140
  96.4 11.6 %convolution_add_fusion = f32[1024,1024]{0,1:T(8,128)} fusion(f32[1024,1024]{0,1:T(8,128)} %fusion.24, bf16[1024,1024]{1,0:T(8,128)(2,1)} %param.21, f32[1024,1024,1]{1,0,2:T(8,128)} %fusion.102, bf16[4,1024,256]{2,1,0:T(8,128)(2,1)S(1)} %bitcast.156, bf16[4,256,1024]{2,1,0:T(8,128)(2,1)} %bitcast.182), kind=kOutput, calls=%fused_computation.59 | convolution fusion | flops 4302307328 | bytes 18874368 | tf_op jit(solution)/shard_map/dot_general | solution.py:140
  108.0 2.9 %select_bitcast_fusion = f32[1024,2,256]{0,2,1:T(8,128)S(1)} fusion(f32[1024,2,2,256]{0,3,2,1:T(8,128)} %bitcast.152, pred[]{:T(512)S(6)} %eq.101), kind=kLoop, calls=%fused_computation.43 | loop fusion | flops 524288 | bytes 6291457 | tf_op jit(solution)/shard_map/jit(_where)/select_n | solution.py:56
  111.0 4.1 %collective-permute-done.8 = f32[1024,2,256]{0,2,1:T(8,128)S(1)} collective-permute-done((f32[1024,2,256]{0,2,1:T(8,128)S(1)}, f32[1024,2,256]{0,2,1:T(8,128)S(1)}, u32[]{:S(2)}, u32[]{:S(2)}) %collective-permute-start.8) | collective-permute-done | bytes 2097184 | tf_op jit(solution)/shard_map/ppermute | solution.py:13
  117.4 12.1 %collective-permute-done.9 = bf16[1024,1,256]{0,2,1:T(8,128)(2,1)S(1)} collective-permute-done((bf16[1024,1,256]{0,2,1:T(8,128)(2,1)S(1)}, bf16[1024,1,256]{0,2,1:T(8,128)(2,1)S(1)}, u32[]{:S(2)}, u32[]{:S(2)}) %collective-permute-start.9) | collective-permute-done | bytes 524320 | tf_op jit(solution)/shard_map/ppermute | solution.py:13
  130.4 2.8 %convolution_convert_fusion = bf16[1024,256]{1,0:T(8,128)(2,1)} fusion(s32[1024]{0:T(1024)S(1)} %get-tuple-element.46, s32[1024]{0:T(1024)S(1)} %get-tuple-element.47, s32[1024]{0:T(1024)S(1)} %get-tuple-element.45, s32[1024]{0:T(1024)S(1)} %get-tuple-element.48, pred[1024]{0:T(1024)(128)(4,1)S(1)} %get-tuple-element.49, ...), kind=kOutput, calls=%fused_computation.60 | convolution fusion | flops 545521664 | bytes 1067008 | tf_op jit(solution)/shard_map/dot_general | solution.py:147
  133.2 3.3 %collective-permute-start.10 = (bf16[2,512,256]{2,1,0:T(8,128)(2,1)}, bf16[2,512,256]{2,1,0:T(8,128)(2,1)}, u32[]{:S(2)}, u32[]{:S(2)}) collective-permute-start(bf16[2,512,256]{2,1,0:T(8,128)(2,1)} %bitcast.46), channel_id=1, source_target_pairs={{0,31},{1,30},{2,29},{3,28},{4,27},{5,26},{6,25},{7,24},{8,23},{9,... | collective-permute-start | bytes 1572872 | tf_op jit(solution)/shard_map/ppermute | solution.py:8
  136.5 2.5 %copy.25 = f32[1024,1,256]{2,0,1:T(8,128)} copy(f32[1024,1,256]{0,2,1:T(8,128)} %copy-done.3) | data formatting | bytes 2097152 | tf_op jit(solution)/shard_map/add | solution.py:59
  139.0 4.0 %add_convert_fusion.1 = bf16[2,512,256]{2,1,0:T(8,128)(2,1)} fusion(f32[2,512,256]{2,1,0:T(8,128)} %bitcast.154, f32[256]{0:T(256)S(1)} %bitcast.174, pred[2,512]{1,0:T(4,128)(4,1)S(1)} %get-tuple-element.30, f32[256]{0:T(256)S(1)} %bitcast.171, pred[2,512]{1,0:T(4,128)(4,1)S(1)} %get-tuple-element.28, f32[256]{0:T(256)S(1)} %bitcast.168, ...), kind=kLoop, calls=%fused_computation.68 | loop fusion | flops 3407872 | bytes 2107392 | tf_op jit(solution)/shard_map/convert_element_type | solution.py:150
  143.0 11.8 %collective-permute-done.10 = bf16[2,512,256]{2,1,0:T(8,128)(2,1)} collective-permute-done((bf16[2,512,256]{2,1,0:T(8,128)(2,1)}, bf16[2,512,256]{2,1,0:T(8,128)(2,1)}, u32[]{:S(2)}, u32[]{:S(2)}) %collective-permute-start.10) | collective-permute-done | bytes 524320 | tf_op jit(solution)/shard_map/ppermute | solution.py:8
  (83 shorter events, 28.1 us)
Async XLA Ops:
  0.6 80.1 %copy-start = (bf16[1024,1024]{1,0:T(8,128)(2,1)S(1)}, bf16[1024,1024]{1,0:T(8,128)(2,1)}, u32[]{:S(2)}) copy-start(bf16[1024,1024]{1,0:T(8,128)(2,1)} %param.19) | copy-start | bytes 6291460
  0.6 15.3 %copy-start.12 = (f32[256]{0:T(256)S(1)}, f32[256]{0:T(256)}, u32[]{:S(2)}) copy-start(f32[256]{0:T(256)} %param.18) | copy-start | bytes 3076
  1.5 3.7 %collective-permute-start = (s32[2,512]{1,0:T(2,128)S(1)}, s32[2,512]{1,0:T(2,128)S(1)}, u32[]{:S(2)}, u32[]{:S(2)}) collective-permute-start(s32[2,512]{1,0:T(2,128)S(1)} %subtract_select_fusion), channel_id=1, source_target_pairs={{0,28},{4,24},{8,20},{12,16},{16,12},{20,8},{24,4},{28,0},{1,29},{... | collective-permute-start | bytes 12296 | tf_op jit(solution)/shard_map/ppermute | solution.py:8
  18.8 8.6 %copy-start.13 = (f32[256]{0:T(256)S(1)}, f32[256]{0:T(256)}, u32[]{:S(2)}) copy-start(f32[256]{0:T(256)} %param.17) | copy-start | bytes 3076
  18.8 5.3 %collective-permute-start.2 = (bf16[2,2,3,256]{3,2,1,0:T(4,128)(2,1)S(1)}, bf16[2,2,3,256]{3,2,1,0:T(4,128)(2,1)S(1)}, u32[]{:S(2)}, u32[]{:S(2)}) collective-permute-start(bf16[2,2,3,256]{3,2,1,0:T(4,128)(2,1)S(1)} %get-tuple-element.17), channel_id=1, source_target_pairs={{4,0},{8,4},{12,8},{16,12},{20,16},{24,20},{28,24},{5,1},{9,5},{13... | collective-permute-start | bytes 18440 | tf_op jit(solution)/shard_map/ppermute | solution.py:25
  21.9 5.3 %collective-permute-start.1 = (bf16[2,2,3,256]{3,2,1,0:T(4,128)(2,1)S(1)}, bf16[2,2,3,256]{3,2,1,0:T(4,128)(2,1)S(1)}, u32[]{:S(2)}, u32[]{:S(2)}) collective-permute-start(bf16[2,2,3,256]{3,2,1,0:T(4,128)(2,1)S(1)} %get-tuple-element.16), channel_id=1, source_target_pairs={{0,4},{4,8},{8,12},{12,16},{16,20},{20,24},{24,28},{1,5},{5,9},{9,... | collective-permute-start | bytes 18440 | tf_op jit(solution)/shard_map/ppermute | solution.py:23
  33.0 23.7 %collective-permute-start.5 = (bf16[1024,256]{1,0:T(8,128)(2,1)}, bf16[1024,256]{1,0:T(8,128)(2,1)}, u32[]{:S(2)}, u32[]{:S(2)}) collective-permute-start(bf16[1024,256]{1,0:T(8,128)(2,1)} %convolution_convert_fusion.2), channel_id=1, source_target_pairs={{0,28},{4,24},{8,20},{12,16},{16,12},{20,8},{24,4},{28,0},{1,29},{... | collective-permute-start | bytes 1572872 | tf_op jit(solution)/shard_map/ppermute | solution.py:8
  33.8 24.1 %collective-permute-start.3 = (bf16[1,1024,256]{2,1,0:T(8,128)(2,1)}, bf16[1,1024,256]{2,1,0:T(8,128)(2,1)}, u32[]{:S(2)}, u32[]{:S(2)}) collective-permute-start(bf16[1,1024,256]{2,1,0:T(8,128)(2,1)} %bitcast.14), channel_id=1, source_target_pairs={{0,2},{1,3},{2,0},{3,1},{4,6},{5,7},{6,4},{7,5},{8,10},{9,11},{10,... | collective-permute-start | bytes 1572872 | tf_op jit(solution)/shard_map/ppermute | solution.py:13
  56.6 10.6 %collective-permute-start.6 = (bf16[1,1024,256]{2,1,0:T(8,128)(2,1)}, bf16[1,1024,256]{2,1,0:T(8,128)(2,1)S(1)}, u32[]{:S(2)}, u32[]{:S(2)}) collective-permute-start(bf16[1,1024,256]{2,1,0:T(8,128)(2,1)} %bitcast.26), channel_id=1, source_target_pairs={{0,2},{1,3},{2,0},{3,1},{4,6},{5,7},{6,4},{7,5},{8,10},{9,11},{10,... | collective-permute-start | bytes 1572872 | tf_op jit(solution)/shard_map/ppermute | solution.py:13
  59.2 4.6 %copy-start.8 = (bf16[1,1,1024,256]{3,2,1,0:T(8,128)(2,1)}, bf16[1,1,1024,256]{3,2,1,0:T(8,128)(2,1)S(1)}, u32[]{:S(2)}) copy-start(bf16[1,1,1024,256]{3,2,1,0:T(8,128)(2,1)S(1)} %get-tuple-element.10) | copy-start | bytes 1572868
  59.2 4.6 %copy-start.9 = (bf16[1,1,1024,256]{3,2,1,0:T(8,128)(2,1)}, bf16[1,1,1024,256]{3,2,1,0:T(8,128)(2,1)S(1)}, u32[]{:S(2)}) copy-start(bf16[1,1,1024,256]{3,2,1,0:T(8,128)(2,1)S(1)} %get-tuple-element.11) | copy-start | bytes 1572868
  60.3 13.8 %copy-start.15 = (bf16[1024,1024]{1,0:T(8,128)(2,1)S(1)}, bf16[1024,1024]{1,0:T(8,128)(2,1)}, u32[]{:S(2)}) copy-start(bf16[1024,1024]{1,0:T(8,128)(2,1)} %param.21) | copy-start | bytes 6291460
  60.3 18.4 %collective-permute-start.4 = (bf16[2,1024,256]{2,1,0:T(8,128)(2,1)}, bf16[2,1024,256]{2,1,0:T(8,128)(2,1)}, u32[]{:S(2)}, u32[]{:S(2)}) collective-permute-start(bf16[2,1024,256]{2,1,0:T(8,128)(2,1)} %maximum_bitcast_fusion), channel_id=1, source_target_pairs={{0,1},{1,0},{2,3},{3,2},{4,5},{5,4},{6,7},{7,6},{8,9},{9,8},{10,11... | collective-permute-start | bytes 3145736 | tf_op jit(solution)/shard_map/ppermute | solution.py:13
  70.2 15.0 %collective-permute-start.7 = (bf16[2,1024,256]{2,1,0:T(8,128)(2,1)}, bf16[2,1024,256]{2,1,0:T(8,128)(2,1)}, u32[]{:S(2)}, u32[]{:S(2)}) collective-permute-start(bf16[2,1024,256]{2,1,0:T(8,128)(2,1)} %maximum_bitcast_fusion.1), channel_id=1, source_target_pairs={{0,1},{1,0},{2,3},{3,2},{4,5},{5,4},{6,7},{7,6},{8,9},{9,8},{10,11... | collective-permute-start | bytes 3145736 | tf_op jit(solution)/shard_map/ppermute | solution.py:13
  80.8 4.4 %copy-start.10 = (bf16[2,2,1024,256]{3,2,1,0:T(8,128)(2,1)}, bf16[2,2,1024,256]{3,2,1,0:T(8,128)(2,1)S(1)}, u32[]{:S(2)}) copy-start(bf16[2,2,1024,256]{3,2,1,0:T(8,128)(2,1)S(1)} %copy.19) | copy-start | bytes 6291460
  80.8 4.4 %copy-start.5 = (bf16[1,1,1024,256]{3,2,1,0:T(8,128)(2,1)S(1)}, bf16[1,1,1024,256]{3,2,1,0:T(8,128)(2,1)}, u32[]{:S(2)}) copy-start(bf16[1,1,1024,256]{3,2,1,0:T(8,128)(2,1)} %copy-done.4) | copy-start | bytes 1572868
  80.8 4.4 %copy-start.7 = (bf16[1,1,1024,256]{3,2,1,0:T(8,128)(2,1)S(1)}, bf16[1,1,1024,256]{3,2,1,0:T(8,128)(2,1)}, u32[]{:S(2)}) copy-start(bf16[1,1,1024,256]{3,2,1,0:T(8,128)(2,1)} %copy-done.6) | copy-start | bytes 1572868
  91.9 4.4 %copy-start.11 = (bf16[2,2,1024,256]{3,2,1,0:T(8,128)(2,1)S(1)}, bf16[2,2,1024,256]{3,2,1,0:T(8,128)(2,1)}, u32[]{:S(2)}) copy-start(bf16[2,2,1024,256]{3,2,1,0:T(8,128)(2,1)} %copy-done.10) | copy-start | bytes 6291460
  108.0 7.2 %copy-start.2 = (f32[1024,1024]{0,1:T(8,128)S(1)}, f32[1024,1024]{0,1:T(8,128)}, u32[]{:S(2)}) copy-start(f32[1024,1024]{0,1:T(8,128)} %convolution_add_fusion) | copy-start | bytes 12582916
  110.9 4.2 %collective-permute-start.8 = (f32[1024,2,256]{0,2,1:T(8,128)S(1)}, f32[1024,2,256]{0,2,1:T(8,128)S(1)}, u32[]{:S(2)}, u32[]{:S(2)}) collective-permute-start(f32[1024,2,256]{0,2,1:T(8,128)S(1)} %select_bitcast_fusion), channel_id=1, source_target_pairs={{0,1},{1,0},{2,3},{3,2},{4,5},{5,4},{6,7},{7,6},{8,9},{9,8},{10,11... | collective-permute-start | bytes 6291464 | tf_op jit(solution)/shard_map/ppermute | solution.py:13
  116.1 13.4 %collective-permute-start.9 = (bf16[1024,1,256]{0,2,1:T(8,128)(2,1)S(1)}, bf16[1024,1,256]{0,2,1:T(8,128)(2,1)S(1)}, u32[]{:S(2)}, u32[]{:S(2)}) collective-permute-start(bf16[1024,1,256]{0,2,1:T(8,128)(2,1)S(1)} %fusion.45), channel_id=1, source_target_pairs={{0,2},{1,3},{2,0},{3,1},{4,6},{5,7},{6,4},{7,5},{8,10},{9,11},{10,... | collective-permute-start | bytes 1572872 | tf_op jit(solution)/shard_map/ppermute | solution.py:13
  129.8 3.5 %copy-start.3 = (f32[1024,1,256]{0,2,1:T(8,128)}, f32[1024,1,256]{0,2,1:T(8,128)S(1)}, u32[]{:S(2)}) copy-start(f32[1024,1,256]{0,2,1:T(8,128)S(1)} %bitcast_add_fusion) | copy-start | bytes 3145732
  133.2 21.6 %collective-permute-start.10 = (bf16[2,512,256]{2,1,0:T(8,128)(2,1)}, bf16[2,512,256]{2,1,0:T(8,128)(2,1)}, u32[]{:S(2)}, u32[]{:S(2)}) collective-permute-start(bf16[2,512,256]{2,1,0:T(8,128)(2,1)} %bitcast.46), channel_id=1, source_target_pairs={{0,31},{1,30},{2,29},{3,28},{4,27},{5,26},{6,25},{7,24},{8,23},{9,... | collective-permute-start | bytes 1572872 | tf_op jit(solution)/shard_map/ppermute | solution.py:8
  139.0 17.7 %copy-start.1 = (bf16[1024,1024]{1,0:T(8,128)(2,1)S(1)}, bf16[1024,1024]{1,0:T(8,128)(2,1)}, u32[]{:S(2)}) copy-start(bf16[1024,1024]{1,0:T(8,128)(2,1)} %param.19) | copy-start | bytes 6291460
  (4 other events, 7.7 us)

commit v11 on v10

--- a/solution.py
+++ b/solution.py
@@ -39,10 +39,9 @@
     cur = block[None]
     for bit in reversed(range(bits)):
         other = partner(cur, "ch", bit)
-        low = ((me >> bit) & 1) == 0
-        first = jnp.where(low, cur, other)
-        second = jnp.where(low, other, cur)
-        cur = jnp.stack([first, second], axis=1).reshape((-1,) + block.shape)
+        high = (me >> bit) & 1
+        both = jnp.stack([cur, other, cur], axis=1)
+        cur = lax.dynamic_slice_in_dim(both, high, 2, axis=1).reshape((-1,) + block.shape)
     return cur
 
 
@@ -51,9 +50,9 @@
     rows, _, w = part.shape
     for bit in range(bits):
         cur = cur.reshape(rows, -1, 2, w)
-        low = ((me >> bit) & 1) == 0
-        keep = jnp.where(low, cur[:, :, 0], cur[:, :, 1])
-        give = jnp.where(low, cur[:, :, 1], cur[:, :, 0])
+        high = (me >> bit) & 1
+        keep = lax.dynamic_index_in_dim(cur, high, axis=2, keepdims=False)
+        give = lax.dynamic_index_in_dim(cur, 1 - high, axis=2, keepdims=False)
         if bit > 0:
             give = give.astype(jnp.bfloat16)
         cur = keep + partner(give, "ch", bit).astype(jnp.float32)

time: 157 us -> 163 us (1.038)
  local copies, waits for them, and re-layouts: 6.75 us -> 16.2 us
    unnamed x34 -> x18, local copies, waits for them, and re-layouts: 0.86 us -> 7.24 us
    dynamic_slice x0 -> x2, local copies, waits for them, and re-layouts: none -> 5 us  [the longest x1 4.86 us: scatter_blocks(): keep = lax.dynamic_index_in_dim(cur, high, axis=2, keepdims=False)]
    ppermute x6, waiting for transfers between devices: 19.7 us -> 15 us  [partner(): lax.ppermute(value, axis, [(k, k ^ mask) for k in range(lax.axis_size(axi...]
    ppermute x3, waiting for transfers between devices: 33.4 us -> 38 us  [mirror(): return lax.ppermute(value, axes, [(k, count - 1 - k) for k in range(count)])]
    add x1 -> x2, other arithmetic: 0.24 us -> 3.98 us  [scatter_blocks(): cur = keep + partner(give, 'ch', bit).astype(jnp.float32)]
    convert_element_type x2, other arithmetic: 5.9 us -> 2.96 us  [local(): return (out_forward.astype(jnp.bfloat16), out_reverse.astype(jnp.bfloat16))]
    select_n x1 -> x0, other arithmetic: 2.93 us -> none  [scatter_blocks(): give = jnp.where(low, cur[:, :, 1], cur[:, :, 0])]
    add x1 -> x0, local copies, waits for them, and re-layouts: 2.53 us -> none  [scatter_blocks(): cur = keep + partner(give, 'ch', bit).astype(jnp.float32)]
  transfers between devices with their start and end apart: 11 -> 11, of which waited for: 6 -> 6; matrix products, arithmetic and copies ran while one was open for 16% -> 15% of each run, Pallas kernels for 0% -> 0%
where the time goes in v11:
time: 163 us; the launch traced here: 162 us
  waiting for transfers between devices  56 us (34%)
  matrix products  34.6 us (21%)
  other arithmetic  27 us (17%)
  starting transfers between devices  20.9 us (13%)
  local copies, waits for them, and re-layouts  16.2 us (10%)
  blocking collectives  6.55 us (4%)
    ppermute x3, waiting for transfers between devices, mirror(): return lax.ppermute(value, axes, [(k, count - 1 - k) for k in range(count)])  38 us
    ppermute x6, waiting for transfers between devices, partner(): lax.ppermute(value, axis, [(k, k ^ mask) for k in range(lax.axis_size(axi...  15 us
    dot_general x1, matrix products, local(): jnp.dot(act_fwd, w_out, preferred_element_type=jnp.float32)  12 us
    ppermute x6, starting transfers between devices, partner(): lax.ppermute(value, axis, [(k, k ^ mask) for k in range(lax.axis_size(axi...  10.8 us
    unnamed x18, local copies, waits for them, and re-layouts  7.24 us
    dot_general x2, matrix products, activation(): lax.dot_general(pieces, w_gate.reshape(ch_count, local_width, -1), dims,...  6.65 us
    psum x1, blocking collectives, local(): lax.psum((jnp.sum(x_fwd * x_fwd, axis=-1), jnp.sum(x_rev * x_rev, axis=-1...  6.55 us
    another operation x4, other arithmetic, gather_blocks(): both = jnp.stack([cur, other, cur], axis=1)  5.98 us
  transfers between devices with their start and end apart: 11, of which 6 were waited for; matrix products, arithmetic and copies ran while one was open for 15% of the time, Pallas kernels for 0%

profile of v11, /device:TPU:17, one launch (start us, length us, event | category | flops | bytes accessed | tf_op | source)
XLA Modules:
  0.0 162.0 jit_solution(3072938705849858487)
XLA Ops:
  5.6 3.6 %multiply_reduce_fusion.1 = (f32[2,512]{1,0:T(2,128)S(1)}, f32[2,512,256]{2,1,0:T(8,128)S(1)}) fusion(f32[256]{0:T(256)S(1)} %bitcast.133, pred[2,512]{1,0:T(4,128)(4,1)S(1)} %get-tuple-element.24, f32[256]{0:T(256)S(1)} %bitcast.130, pred[2,512]{1,0:T(4,128)(4,1)S(1)} %get-tuple-element.22, f32[256]{0:T(256)S(1)} %bitcast.127, ...), kind=kLoop, calls=%fused_computation.86 | loop fusion | flops 6290432 | bytes 2116608 | tf_op jit(solution)/shard_map/reduce_sum | solution.py:99
  9.4 6.6 %all-reduce = (f32[2,512]{1,0:T(2,128)S(1)}, f32[2,512]{1,0:T(2,128)S(1)}) all-reduce(f32[2,512]{1,0:T(2,128)S(1)} %multiply_reduce_fusion, f32[2,512]{1,0:T(2,128)S(1)} %get-tuple-element.19), channel_id=1, replica_groups=mesh['seq'=8,'ch'=4] {'ch'}, use_global_device_ids=true, to_apply=%region_3.4 | all-reduce | flops 2048 | bytes 16384 | tf_op jit(solution)/shard_map/psum | solution.py:98
  16.0 2.8 %fusion.48 = (bf16[1,2,512,256]{3,2,1,0:T(8,128)(2,1)S(1)}, bf16[1,2,512,256]{3,2,1,0:T(8,128)(2,1)S(1)}) fusion(f32[256]{0:T(256)S(1)} %copy-done.4, f32[2,512]{1,0:T(2,128)S(1)} %get-tuple-element.44, f32[256]{0:T(256)S(1)} %bitcast.134, pred[2,512]{1,0:T(4,128)(4,1)S(1)} %get-tuple-element.24, f32[256]{0:T(256)S(1)} %bitcast.131, ...), kind=kLoop, calls=%fused_computation.88 | loop fusion | flops 4456448 | bytes 2640896 | tf_op jit(solution)/shard_map/stack | solution.py:107
  18.8 3.0 %collective-permute-start.2 = (bf16[2,2,3,256]{3,2,1,0:T(4,128)(2,1)S(1)}, bf16[2,2,3,256]{3,2,1,0:T(4,128)(2,1)S(1)}, u32[]{:S(2)}, u32[]{:S(2)}) collective-permute-start(bf16[2,2,3,256]{3,2,1,0:T(4,128)(2,1)S(1)} %get-tuple-element.11), channel_id=1, source_target_pairs={{4,0},{8,4},{12,8},{16,12},{20,16},{24,20},{28,24},{5,1},{9,5},{13... | collective-permute-start | bytes 18440 | tf_op jit(solution)/shard_map/ppermute | solution.py:25
  21.9 2.3 %collective-permute-start.1 = (bf16[2,2,3,256]{3,2,1,0:T(4,128)(2,1)S(1)}, bf16[2,2,3,256]{3,2,1,0:T(4,128)(2,1)S(1)}, u32[]{:S(2)}, u32[]{:S(2)}) collective-permute-start(bf16[2,2,3,256]{3,2,1,0:T(4,128)(2,1)S(1)} %get-tuple-element.10), channel_id=1, source_target_pairs={{0,4},{4,8},{8,12},{12,16},{16,20},{20,24},{24,28},{1,5},{5,9},{9,... | collective-permute-start | bytes 18440 | tf_op jit(solution)/shard_map/ppermute | solution.py:23
  24.2 3.0 %collective-permute-done.1 = bf16[2,2,3,256]{3,2,1,0:T(4,128)(2,1)S(1)} collective-permute-done((bf16[2,2,3,256]{3,2,1,0:T(4,128)(2,1)S(1)}, bf16[2,2,3,256]{3,2,1,0:T(4,128)(2,1)S(1)}, u32[]{:S(2)}, u32[]{:S(2)}) %collective-permute-start.1) | collective-permute-done | bytes 6176 | tf_op jit(solution)/shard_map/ppermute | solution.py:23
  30.1 2.8 %convolution_convert_fusion.2 = bf16[1024,256]{1,0:T(8,128)(2,1)} fusion(bf16[1024,256]{1,0:T(8,128)(2,1)S(1)} %bitcast.120, s32[1024]{0:T(1024)S(1)} %get-tuple-element.46, s32[1024]{0:T(1024)S(1)} %get-tuple-element.47, s32[1024]{0:T(1024)S(1)} %get-tuple-element.45, s32[1024]{0:T(1024)S(1)} %get-tuple-element.48, ...), kind=kOutput, calls=%fused_computation.72 | convolution fusion | flops 545521664 | bytes 1067008 | tf_op jit(solution)/shard_map/dot_general | solution.py:117
  35.0 21.6 %collective-permute-done.5 = bf16[1024,256]{1,0:T(8,128)(2,1)} collective-permute-done((bf16[1024,256]{1,0:T(8,128)(2,1)}, bf16[1024,256]{1,0:T(8,128)(2,1)}, u32[]{:S(2)}, u32[]{:S(2)}) %collective-permute-start.5) | collective-permute-done | bytes 524320 | tf_op jit(solution)/shard_map/ppermute | solution.py:8
  59.8 3.5 %collective-permute-start.4 = (bf16[2,1024,256]{2,1,0:T(8,128)(2,1)S(1)}, bf16[2,1024,256]{2,1,0:T(8,128)(2,1)S(1)}, u32[]{:S(2)}, u32[]{:S(2)}) collective-permute-start(bf16[2,1024,256]{2,1,0:T(8,128)(2,1)S(1)} %fusion.120), channel_id=1, source_target_pairs={{0,1},{1,0},{2,3},{3,2},{4,5},{5,4},{6,7},{7,6},{8,9},{9,8},{10,11... | collective-permute-start | bytes 3145736 | tf_op jit(solution)/shard_map/ppermute | solution.py:13
  63.3 3.2 %fusion.142 = bf16[1024,1024]{1,0:T(8,128)(2,1)S(1)} fusion(bf16[1024,1024]{1,0:T(8,128)(2,1)S(1)} %copy-done.7, s32[1024]{0:T(1024)S(1)} %get-tuple-element.50, s32[1024]{0:T(1024)S(1)} %get-tuple-element.51, s32[1024]{0:T(1024)S(1)} %get-tuple-element.49, s32[1024]{0:T(1024)S(1)} %get-tuple-element.52, pred[1024]{0:T(1024)(128)(4,1)S(1)} %get-tuple-element.39, ...), kind=kOutput, calls=%fused_computation.49.clone.1 | convolution fusion | flops 2157969408 | bytes 4212736 | tf_op jit(solution)/shard_map/dot_general | solution.py:138
  69.0 4.0 %collective-permute-start.7 = (bf16[2,1024,256]{2,1,0:T(8,128)(2,1)S(1)}, bf16[2,1024,256]{2,1,0:T(8,128)(2,1)S(1)}, u32[]{:S(2)}, u32[]{:S(2)}) collective-permute-start(bf16[2,1024,256]{2,1,0:T(8,128)(2,1)S(1)} %fusion.122), channel_id=1, source_target_pairs={{0,1},{1,0},{2,3},{3,2},{4,5},{5,4},{6,7},{7,6},{8,9},{9,8},{10,11... | collective-permute-start | bytes 3145736 | tf_op jit(solution)/shard_map/ppermute | solution.py:13
  77.9 4.3 %fusion.106 = f32[1024,1024,1]{1,0,2:T(8,128)} fusion(bf16[4,1024,256]{2,1,0:T(8,128)(2,1)S(1)} %bitcast.113, bf16[4,256,1024]{2,1,0:T(8,128)(2,1)S(1)} %bitcast.107), kind=kOutput, calls=%fused_computation.159 | convolution fusion | flops 2147483648 | bytes 8388608 | tf_op jit(solution)/shard_map/dot_general | solution.py:127
  83.5 2.3 %fusion.107 = f32[1024,1024,1]{1,0,2:T(8,128)S(1)} fusion(bf16[4,1024,256]{2,1,0:T(8,128)(2,1)S(1)} %bitcast.116, bf16[4,256,1024]{2,1,0:T(8,128)(2,1)S(1)} %bitcast.108), kind=kOutput, calls=%fused_computation.160 | convolution fusion | flops 2147483648 | bytes 8388608 | tf_op jit(solution)/shard_map/dot_general | solution.py:127
  85.9 2.9 %fusion = bf16[1024,1024]{1,0:T(8,128)(2,1)S(1)} fusion(f32[1024,1024,1]{1,0,2:T(8,128)S(1)} %fusion.107, bf16[4,1024,256]{2,1,0:T(8,128)(2,1)S(1)} %bitcast.117, bf16[4,256,1024]{2,1,0:T(8,128)(2,1)S(1)} %bitcast.144), kind=kOutput, calls=%fused_computation.1 | convolution fusion | flops 2153775104 | bytes 10485760 | tf_op jit(solution)/shard_map/dot_general | solution.py:130
  88.8 4.4 %fusion.25 = f32[1024,1024]{0,1:T(8,128)} fusion(bf16[1024,1024]{1,0:T(8,128)(2,1)S(1)} %fusion, bf16[1024,1024]{1,0:T(8,128)(2,1)S(1)} %fusion.142), kind=kOutput, calls=%fused_computation.48 | convolution fusion | flops 2147483648 | bytes 8388608 | tf_op jit(solution)/shard_map/dot_general | solution.py:139
  93.2 12.0 %convolution_add_fusion = f32[1024,1024]{0,1:T(8,128)} fusion(f32[1024,1024]{0,1:T(8,128)} %fusion.25, bf16[1024,1024]{1,0:T(8,128)(2,1)} %param.21, f32[1024,1024,1]{1,0,2:T(8,128)} %fusion.106, bf16[4,1024,256]{2,1,0:T(8,128)(2,1)} %bitcast.114, bf16[4,256,1024]{2,1,0:T(8,128)(2,1)} %bitcast.143), kind=kOutput, calls=%fused_computation.63 | convolution fusion | flops 4302307328 | bytes 18874368 | tf_op jit(solution)/shard_map/dot_general | solution.py:139
  105.1 4.9 %constant_dynamic-slice_fusion.1 = (f32[1024,2,1,256]{0,3,2,1:T(8,128)}, f32[1024,2,1,256]{0,3,2,1:T(8,128)}) fusion(f32[1024,2,2,256]{0,3,2,1:T(8,128)} %bitcast.110, s32[]{:T(128)S(6)} %select_n.147, s32[]{:T(128)S(6)} %select_n.148), kind=kLoop, calls=%fused_computation.130 | loop fusion | bytes 8388616 | tf_op jit(solution)/shard_map/jit(dynamic_index_in_dim)/dynamic_slice | solution.py:54
  110.0 2.9 %copy.18 = f32[1024,2,1,256]{3,0,2,1:T(8,128)} copy(f32[1024,2,1,256]{0,3,2,1:T(8,128)} %get-tuple-element.7) | data formatting | bytes 4194304
  112.9 3.0 %copy.17 = f32[1024,2,1,256]{3,0,2,1:T(8,128)} copy(f32[1024,2,1,256]{0,3,2,1:T(8,128)} %get-tuple-element.6) | data formatting | bytes 4194304
  117.4 2.5 %bitcast_add_fusion = f32[1024,2,256]{2,0,1:T(8,128)S(1)} fusion(f32[1024,2,256]{2,0,1:T(8,128)} %collective-permute-done.8, f32[1024,2,1,256]{3,0,2,1:T(8,128)} %copy.17), kind=kLoop, calls=%fused_computation.47 | loop fusion | flops 524288 | bytes 6291456 | tf_op jit(solution)/shard_map/add | solution.py:58
  122.8 12.9 %collective-permute-done.9 = bf16[1024,1,256]{2,0,1:T(8,128)(2,1)} collective-permute-done((bf16[1024,1,256]{2,0,1:T(8,128)(2,1)}, bf16[1024,1,256]{2,0,1:T(8,128)(2,1)}, u32[]{:S(2)}, u32[]{:S(2)}) %collective-permute-start.9) | collective-permute-done | bytes 524320 | tf_op jit(solution)/shard_map/ppermute | solution.py:13
  137.8 2.1 %convolution_convert_fusion = bf16[1024,256]{1,0:T(8,128)(2,1)S(1)} fusion(s32[1024]{0:T(1024)S(1)} %get-tuple-element.46, s32[1024]{0:T(1024)S(1)} %get-tuple-element.47, s32[1024]{0:T(1024)S(1)} %get-tuple-element.45, s32[1024]{0:T(1024)S(1)} %get-tuple-element.48, pred[1024]{0:T(1024)(128)(4,1)S(1)} %get-tuple-element.37, ...), kind=kOutput, calls=%fused_computation.70 | convolution fusion | flops 545521664 | bytes 1067008 | tf_op jit(solution)/shard_map/dot_general | solution.py:146
  139.8 2.9 %collective-permute-start.10 = (bf16[2,512,256]{2,1,0:T(8,128)(2,1)S(1)}, bf16[2,512,256]{2,1,0:T(8,128)(2,1)S(1)}, u32[]{:S(2)}, u32[]{:S(2)}) collective-permute-start(bf16[2,512,256]{2,1,0:T(8,128)(2,1)S(1)} %bitcast.145), channel_id=1, source_target_pairs={{0,31},{1,30},{2,29},{3,28},{4,27},{5,26},{6,25},{7,24},{8,23},{9,... | collective-permute-start | bytes 1572872 | tf_op jit(solution)/shard_map/ppermute | solution.py:8
  144.8 16.4 %collective-permute-done.10 = bf16[2,512,256]{2,1,0:T(8,128)(2,1)S(1)} collective-permute-done((bf16[2,512,256]{2,1,0:T(8,128)(2,1)S(1)}, bf16[2,512,256]{2,1,0:T(8,128)(2,1)S(1)}, u32[]{:S(2)}, u32[]{:S(2)}) %collective-permute-start.10) | collective-permute-done | bytes 524320 | tf_op jit(solution)/shard_map/ppermute | solution.py:8
  (63 shorter events, 31.5 us)
Async XLA Ops:
  0.6 77.3 %copy-start = (bf16[1024,1024]{1,0:T(8,128)(2,1)S(1)}, bf16[1024,1024]{1,0:T(8,128)(2,1)}, u32[]{:S(2)}) copy-start(bf16[1024,1024]{1,0:T(8,128)(2,1)} %param.19) | copy-start | bytes 6291460
  0.6 15.3 %copy-start.4 = (f32[256]{0:T(256)S(1)}, f32[256]{0:T(256)}, u32[]{:S(2)}) copy-start(f32[256]{0:T(256)} %param.18) | copy-start | bytes 3076
  1.5 3.7 %collective-permute-start = (s32[2,512]{1,0:T(2,128)S(1)}, s32[2,512]{1,0:T(2,128)S(1)}, u32[]{:S(2)}, u32[]{:S(2)}) collective-permute-start(s32[2,512]{1,0:T(2,128)S(1)} %subtract_select_fusion), channel_id=1, source_target_pairs={{0,28},{4,24},{8,20},{12,16},{16,12},{20,8},{24,4},{28,0},{1,29},{... | collective-permute-start | bytes 12296 | tf_op jit(solution)/shard_map/ppermute | solution.py:8
  18.8 8.6 %copy-start.5 = (f32[256]{0:T(256)S(1)}, f32[256]{0:T(256)}, u32[]{:S(2)}) copy-start(f32[256]{0:T(256)} %param.17) | copy-start | bytes 3076
  18.8 5.3 %collective-permute-start.2 = (bf16[2,2,3,256]{3,2,1,0:T(4,128)(2,1)S(1)}, bf16[2,2,3,256]{3,2,1,0:T(4,128)(2,1)S(1)}, u32[]{:S(2)}, u32[]{:S(2)}) collective-permute-start(bf16[2,2,3,256]{3,2,1,0:T(4,128)(2,1)S(1)} %get-tuple-element.11), channel_id=1, source_target_pairs={{4,0},{8,4},{12,8},{16,12},{20,16},{24,20},{28,24},{5,1},{9,5},{13... | collective-permute-start | bytes 18440 | tf_op jit(solution)/shard_map/ppermute | solution.py:25
  21.9 5.3 %collective-permute-start.1 = (bf16[2,2,3,256]{3,2,1,0:T(4,128)(2,1)S(1)}, bf16[2,2,3,256]{3,2,1,0:T(4,128)(2,1)S(1)}, u32[]{:S(2)}, u32[]{:S(2)}) collective-permute-start(bf16[2,2,3,256]{3,2,1,0:T(4,128)(2,1)S(1)} %get-tuple-element.10), channel_id=1, source_target_pairs={{0,4},{4,8},{8,12},{12,16},{16,20},{20,24},{24,28},{1,5},{5,9},{9,... | collective-permute-start | bytes 18440 | tf_op jit(solution)/shard_map/ppermute | solution.py:23
  33.0 23.7 %collective-permute-start.5 = (bf16[1024,256]{1,0:T(8,128)(2,1)}, bf16[1024,256]{1,0:T(8,128)(2,1)}, u32[]{:S(2)}, u32[]{:S(2)}) collective-permute-start(bf16[1024,256]{1,0:T(8,128)(2,1)} %convolution_convert_fusion.2), channel_id=1, source_target_pairs={{0,28},{4,24},{8,20},{12,16},{16,12},{20,8},{24,4},{28,0},{1,29},{... | collective-permute-start | bytes 1572872 | tf_op jit(solution)/shard_map/ppermute | solution.py:8
  33.8 24.1 %collective-permute-start.3 = (bf16[1,1024,256]{2,1,0:T(8,128)(2,1)}, bf16[1,1024,256]{2,1,0:T(8,128)(2,1)}, u32[]{:S(2)}, u32[]{:S(2)}) collective-permute-start(bf16[1,1024,256]{2,1,0:T(8,128)(2,1)} %bitcast.15), channel_id=1, source_target_pairs={{0,2},{1,3},{2,0},{3,1},{4,6},{5,7},{6,4},{7,5},{8,10},{9,11},{10,... | collective-permute-start | bytes 1572872 | tf_op jit(solution)/shard_map/ppermute | solution.py:13
  35.0 28.3 %copy-start.7 = (bf16[1024,1024]{1,0:T(8,128)(2,1)S(1)}, bf16[1024,1024]{1,0:T(8,128)(2,1)}, u32[]{:S(2)}) copy-start(bf16[1024,1024]{1,0:T(8,128)(2,1)} %param.21) | copy-start | bytes 6291460
  56.6 10.6 %collective-permute-start.6 = (bf16[1,1024,256]{2,1,0:T(8,128)(2,1)}, bf16[1,1024,256]{2,1,0:T(8,128)(2,1)S(1)}, u32[]{:S(2)}, u32[]{:S(2)}) collective-permute-start(bf16[1,1024,256]{2,1,0:T(8,128)(2,1)} %bitcast.27), channel_id=1, source_target_pairs={{0,2},{1,3},{2,0},{3,1},{4,6},{5,7},{6,4},{7,5},{8,10},{9,11},{10,... | collective-permute-start | bytes 1572872 | tf_op jit(solution)/shard_map/ppermute | solution.py:13
  59.8 16.9 %collective-permute-start.4 = (bf16[2,1024,256]{2,1,0:T(8,128)(2,1)S(1)}, bf16[2,1024,256]{2,1,0:T(8,128)(2,1)S(1)}, u32[]{:S(2)}, u32[]{:S(2)}) collective-permute-start(bf16[2,1024,256]{2,1,0:T(8,128)(2,1)S(1)} %fusion.120), channel_id=1, source_target_pairs={{0,1},{1,0},{2,3},{3,2},{4,5},{5,4},{6,7},{7,6},{8,9},{9,8},{10,11... | collective-permute-start | bytes 3145736 | tf_op jit(solution)/shard_map/ppermute | solution.py:13
  69.0 13.2 %collective-permute-start.7 = (bf16[2,1024,256]{2,1,0:T(8,128)(2,1)S(1)}, bf16[2,1024,256]{2,1,0:T(8,128)(2,1)S(1)}, u32[]{:S(2)}, u32[]{:S(2)}) collective-permute-start(bf16[2,1024,256]{2,1,0:T(8,128)(2,1)S(1)} %fusion.122), channel_id=1, source_target_pairs={{0,1},{1,0},{2,3},{3,2},{4,5},{5,4},{6,7},{7,6},{8,9},{9,8},{10,11... | collective-permute-start | bytes 3145736 | tf_op jit(solution)/shard_map/ppermute | solution.py:13
  77.9 4.3 %copy-start.3 = (bf16[2,2,1024,256]{3,2,1,0:T(8,128)(2,1)}, bf16[2,2,1024,256]{3,2,1,0:T(8,128)(2,1)S(1)}, u32[]{:S(2)}) copy-start(bf16[2,2,1024,256]{3,2,1,0:T(8,128)(2,1)S(1)} %fusion.16) | copy-start | bytes 6291460
  83.5 2.4 %copy-start.6 = (bf16[1024,1024]{1,0:T(8,128)(2,1)S(1)}, bf16[1024,1024]{1,0:T(8,128)(2,1)}, u32[]{:S(2)}) copy-start(bf16[1024,1024]{1,0:T(8,128)(2,1)} %param.20) | copy-start | bytes 6291460
  112.9 4.5 %collective-permute-start.8 = (f32[1024,2,256]{2,0,1:T(8,128)}, f32[1024,2,256]{2,0,1:T(8,128)}, u32[]{:S(2)}, u32[]{:S(2)}) collective-permute-start(f32[1024,2,256]{2,0,1:T(8,128)} %bitcast.115), channel_id=1, source_target_pairs={{0,1},{1,0},{2,3},{3,2},{4,5},{5,4},{6,7},{7,6},{8,9},{9,8},{10,11... | collective-permute-start | bytes 6291464 | tf_op jit(solution)/shard_map/ppermute | solution.py:13
  119.9 1.3 copy-start.1
  122.0 13.7 %collective-permute-start.9 = (bf16[1024,1,256]{2,0,1:T(8,128)(2,1)}, bf16[1024,1,256]{2,0,1:T(8,128)(2,1)}, u32[]{:S(2)}, u32[]{:S(2)}) collective-permute-start(bf16[1024,1,256]{2,0,1:T(8,128)(2,1)} %dynamic-slice_convert_fusion), channel_id=1, source_target_pairs={{0,2},{1,3},{2,0},{3,1},{4,6},{5,7},{6,4},{7,5},{8,10},{9,11},{10,... | collective-permute-start | bytes 1572872 | tf_op jit(solution)/shard_map/ppermute | solution.py:13
  137.8 4.9 %copy-start.2 = (bf16[2,512,256]{2,1,0:T(8,128)(2,1)S(1)}, bf16[2,512,256]{2,1,0:T(8,128)(2,1)}, u32[]{:S(2)}) copy-start(bf16[2,512,256]{2,1,0:T(8,128)(2,1)} %param.13) | copy-start | bytes 1572868
  139.8 21.3 %collective-permute-start.10 = (bf16[2,512,256]{2,1,0:T(8,128)(2,1)S(1)}, bf16[2,512,256]{2,1,0:T(8,128)(2,1)S(1)}, u32[]{:S(2)}, u32[]{:S(2)}) collective-permute-start(bf16[2,512,256]{2,1,0:T(8,128)(2,1)S(1)} %bitcast.145), channel_id=1, source_target_pairs={{0,31},{1,30},{2,29},{3,28},{4,27},{5,26},{6,25},{7,24},{8,23},{9,... | collective-permute-start | bytes 1572872 | tf_op jit(solution)/shard_map/ppermute | solution.py:8

commit v12 on v10

--- a/solution.py
+++ b/solution.py
@@ -133,10 +133,11 @@
         )
         return (jax.nn.silu(gate) * value).astype(jnp.bfloat16)
 
+    w_flip = jnp.dot(w_out, reversal(width, width), preferred_element_type=jnp.float32).astype(jnp.bfloat16)
+    rows_rev, w_flip = lax.optimization_barrier((rows_rev, w_flip))
     act_fwd = activation(rows_fwd)
     act_rev = activation(rows_rev)
     lane_flip = reversal(local_width, local_width)
-    w_flip = jnp.dot(w_out, reversal(width, width), preferred_element_type=jnp.float32).astype(jnp.bfloat16)
     part = jnp.dot(act_fwd, w_out, preferred_element_type=jnp.float32) + jnp.dot(
         act_rev, w_flip, preferred_element_type=jnp.float32
     )

time: 157 us -> 165 us (1.051)
  matrix products: 36.2 us -> 42.3 us
  starting transfers between devices: 21.7 us -> 18.6 us
  waiting for transfers between devices: 56 us -> 59 us
  local copies, waits for them, and re-layouts: 6.75 us -> 9.03 us
    ppermute x6, waiting for transfers between devices: 19.7 us -> 34.1 us  [partner(): lax.ppermute(value, axis, [(k, k ^ mask) for k in range(lax.axis_size(axi...]
    ppermute x3, waiting for transfers between devices: 33.4 us -> 21.9 us  [mirror(): return lax.ppermute(value, axes, [(k, count - 1 - k) for k in range(count)])]
    dot_general x1, matrix products: 4.4 us -> 11.8 us  [local(): jnp.dot(act_rev, w_flip, preferred_element_type=jnp.float32)]
    dot_general x1 -> x0, matrix products: 2.66 us -> none  [activation(): lax.dot_general(pieces, w_value.reshape(ch_count, local_width, -1), dims,...]
    dot_general x2, matrix products: 6.67 us -> 8.98 us  [activation(): lax.dot_general(pieces, w_gate.reshape(ch_count, local_width, -1), dims,...]
    ppermute x6, starting transfers between devices: 11.3 us -> 9.13 us  [partner(): lax.ppermute(value, axis, [(k, k ^ mask) for k in range(lax.axis_size(axi...]
    unnamed x34 -> x28, local copies, waits for them, and re-layouts: 0.86 us -> 2.98 us
  transfers between devices with their start and end apart: 11 -> 11, of which waited for: 6 -> 7; matrix products, arithmetic and copies ran while one was open for 16% -> 23% of each run, Pallas kernels for 0% -> 0%
where the time goes in v12:
time: 165 us
  waiting for transfers between devices  59 us (36%)
  matrix products  42.3 us (26%)
  other arithmetic  28.2 us (17%)
  starting transfers between devices  18.6 us (11%)
  local copies, waits for them, and re-layouts  9.03 us (5%)
  blocking collectives  6.53 us (4%)
    ppermute x6, waiting for transfers between devices, partner(): lax.ppermute(value, axis, [(k, k ^ mask) for k in range(lax.axis_size(axi...  34.1 us
    ppermute x3, waiting for transfers between devices, mirror(): return lax.ppermute(value, axes, [(k, count - 1 - k) for k in range(count)])  21.9 us
    dot_general x1, matrix products, local(): jnp.dot(act_rev, w_flip, preferred_element_type=jnp.float32)  11.8 us
    dot_general x1, matrix products, local(): jnp.dot(act_fwd, w_out, preferred_element_type=jnp.float32)  10.7 us
    ppermute x6, starting transfers between devices, partner(): lax.ppermute(value, axis, [(k, k ^ mask) for k in range(lax.axis_size(axi...  9.13 us
    dot_general x2, matrix products, activation(): lax.dot_general(pieces, w_gate.reshape(ch_count, local_width, -1), dims,...  8.98 us
    psum x1, blocking collectives, local(): lax.psum((jnp.sum(x_fwd * x_fwd, axis=-1), jnp.sum(x_rev * x_rev, axis=-1...  6.53 us
    another operation x6, other arithmetic, gather_blocks(): cur = jnp.stack([first, second], axis=1).reshape((-1,) + block.shape)  5.96 us
  transfers between devices with their start and end apart: 11, of which 7 were waited for; matrix products, arithmetic and copies ran while one was open for 23% of the time, Pallas kernels for 0%

profile of v12, /device:TPU:17, one launch (start us, length us, event | category | flops | bytes accessed | tf_op | source)
XLA Modules:
  0.0 164.7 jit_solution(8994675540482952546)
XLA Ops:
  5.6 3.6 %multiply_reduce_fusion.1 = (f32[2,512]{1,0:T(2,128)S(1)}, f32[2,512,256]{2,1,0:T(8,128)S(1)}) fusion(f32[256]{0:T(256)S(1)} %bitcast.173, pred[2,512]{1,0:T(4,128)(4,1)S(1)} %get-tuple-element.34, f32[256]{0:T(256)S(1)} %bitcast.170, pred[2,512]{1,0:T(4,128)(4,1)S(1)} %get-tuple-element.32, f32[256]{0:T(256)S(1)} %bitcast.167, ...), kind=kLoop, calls=%fused_computation.78 | loop fusion | flops 6290432 | bytes 2116608 | tf_op jit(solution)/shard_map/reduce_sum | solution.py:100
  9.4 6.5 %all-reduce = (f32[2,512]{1,0:T(2,128)S(1)}, f32[2,512]{1,0:T(2,128)S(1)}) all-reduce(f32[2,512]{1,0:T(2,128)S(1)} %multiply_reduce_fusion, f32[2,512]{1,0:T(2,128)S(1)} %get-tuple-element.29), channel_id=1, replica_groups=mesh['seq'=8,'ch'=4] {'ch'}, use_global_device_ids=true, to_apply=%region_3.4 | all-reduce | flops 2048 | bytes 16384 | tf_op jit(solution)/shard_map/psum | solution.py:99
  16.0 2.8 %fusion.40 = (bf16[1,2,512,256]{3,2,1,0:T(8,128)(2,1)S(1)}, bf16[1,2,512,256]{3,2,1,0:T(8,128)(2,1)S(1)}) fusion(f32[256]{0:T(256)S(1)} %copy-done.11, f32[2,512]{1,0:T(2,128)S(1)} %get-tuple-element.48, f32[256]{0:T(256)S(1)} %bitcast.174, pred[2,512]{1,0:T(4,128)(4,1)S(1)} %get-tuple-element.34, f32[256]{0:T(256)S(1)} %bitcast.171, ...), kind=kLoop, calls=%fused_computation.80 | loop fusion | flops 4456448 | bytes 2640896 | tf_op jit(solution)/shard_map/stack | solution.py:108
  18.8 3.0 %collective-permute-start.2 = (bf16[2,2,3,256]{3,2,1,0:T(4,128)(2,1)S(1)}, bf16[2,2,3,256]{3,2,1,0:T(4,128)(2,1)S(1)}, u32[]{:S(2)}, u32[]{:S(2)}) collective-permute-start(bf16[2,2,3,256]{3,2,1,0:T(4,128)(2,1)S(1)} %get-tuple-element.21), channel_id=1, source_target_pairs={{4,0},{8,4},{12,8},{16,12},{20,16},{24,20},{28,24},{5,1},{9,5},{13... | collective-permute-start | bytes 18440 | tf_op jit(solution)/shard_map/ppermute | solution.py:25
  21.9 2.3 %collective-permute-start.1 = (bf16[2,2,3,256]{3,2,1,0:T(4,128)(2,1)S(1)}, bf16[2,2,3,256]{3,2,1,0:T(4,128)(2,1)S(1)}, u32[]{:S(2)}, u32[]{:S(2)}) collective-permute-start(bf16[2,2,3,256]{3,2,1,0:T(4,128)(2,1)S(1)} %get-tuple-element.20), channel_id=1, source_target_pairs={{0,4},{4,8},{8,12},{12,16},{16,20},{20,24},{24,28},{1,5},{5,9},{9,... | collective-permute-start | bytes 18440 | tf_op jit(solution)/shard_map/ppermute | solution.py:23
  24.2 3.0 %collective-permute-done.1 = bf16[2,2,3,256]{3,2,1,0:T(4,128)(2,1)S(1)} collective-permute-done((bf16[2,2,3,256]{3,2,1,0:T(4,128)(2,1)S(1)}, bf16[2,2,3,256]{3,2,1,0:T(4,128)(2,1)S(1)}, u32[]{:S(2)}, u32[]{:S(2)}) %collective-permute-start.1) | collective-permute-done | bytes 6176 | tf_op jit(solution)/shard_map/ppermute | solution.py:23
  31.6 2.8 %convolution_convert_fusion.2 = bf16[1024,256]{1,0:T(8,128)(2,1)S(1)} fusion(bf16[1024,256]{1,0:T(8,128)(2,1)} %bitcast.160, s32[1024]{0:T(1024)S(1)} %get-tuple-element.50, s32[1024]{0:T(1024)S(1)} %get-tuple-element.51, s32[1024]{0:T(1024)S(1)} %get-tuple-element.49, s32[1024]{0:T(1024)S(1)} %get-tuple-element.52, ...), kind=kOutput, calls=%fused_computation.62 | convolution fusion | flops 545521664 | bytes 1067008 | tf_op jit(solution)/shard_map/dot_general | solution.py:118
  35.3 6.4 %collective-permute-done.3 = bf16[1,1024,256]{2,1,0:T(8,128)(2,1)} collective-permute-done((bf16[1,1024,256]{2,1,0:T(8,128)(2,1)}, bf16[1,1024,256]{2,1,0:T(8,128)(2,1)}, u32[]{:S(2)}, u32[]{:S(2)}) %collective-permute-start.3) | collective-permute-done | bytes 524320 | tf_op jit(solution)/shard_map/ppermute | solution.py:13
  44.8 3.3 %collective-permute-start.4 = (bf16[2,1024,256]{2,1,0:T(8,128)(2,1)}, bf16[2,1024,256]{2,1,0:T(8,128)(2,1)}, u32[]{:S(2)}, u32[]{:S(2)}) collective-permute-start(bf16[2,1024,256]{2,1,0:T(8,128)(2,1)} %maximum_bitcast_fusion), channel_id=1, source_target_pairs={{0,1},{1,0},{2,3},{3,2},{4,5},{5,4},{6,7},{7,6},{8,9},{9,8},{10,11... | collective-permute-start | bytes 3145736 | tf_op jit(solution)/shard_map/ppermute | solution.py:13
  48.1 4.6 %convert_bitcast_fusion = bf16[1024,1024]{0,1:T(8,128)(2,1)} fusion(bf16[1024,1024]{1,0:T(8,128)(2,1)S(1)} %copy-done.13, s32[1024]{0:T(1024)S(1)} %get-tuple-element.56, s32[1024]{0:T(1024)S(1)} %get-tuple-element.57, s32[1024]{0:T(1024)S(1)} %get-tuple-element.55, s32[1024]{0:T(1024)S(1)} %get-tuple-element.58, ...), kind=kOutput, calls=%fused_computation.44 | convolution fusion | flops 2157969408 | bytes 4212736 | tf_op jit(solution)/shard_map/dot_general | solution.py:136
  52.7 5.2 %collective-permute-done.5 = bf16[1024,256]{1,0:T(8,128)(2,1)} collective-permute-done((bf16[1024,256]{1,0:T(8,128)(2,1)S(1)}, bf16[1024,256]{1,0:T(8,128)(2,1)}, u32[]{:S(2)}, u32[]{:S(2)}) %collective-permute-start.5) | collective-permute-done | bytes 524320 | tf_op jit(solution)/shard_map/ppermute | solution.py:8
  58.1 10.5 %collective-permute-done.6 = bf16[1,1024,256]{2,1,0:T(8,128)(2,1)} collective-permute-done((bf16[1,1024,256]{2,1,0:T(8,128)(2,1)}, bf16[1,1024,256]{2,1,0:T(8,128)(2,1)}, u32[]{:S(2)}, u32[]{:S(2)}) %collective-permute-start.6) | collective-permute-done | bytes 524320 | tf_op jit(solution)/shard_map/ppermute | solution.py:13
  71.8 4.0 %collective-permute-start.7 = (bf16[2,1024,256]{2,1,0:T(8,128)(2,1)}, bf16[2,1024,256]{2,1,0:T(8,128)(2,1)}, u32[]{:S(2)}, u32[]{:S(2)}) collective-permute-start(bf16[2,1024,256]{2,1,0:T(8,128)(2,1)} %maximum_bitcast_fusion.1), channel_id=1, source_target_pairs={{0,1},{1,0},{2,3},{3,2},{4,5},{5,4},{6,7},{7,6},{8,9},{9,8},{10,11... | collective-permute-start | bytes 3145736 | tf_op jit(solution)/shard_map/ppermute | solution.py:13
  77.5 4.4 %fusion.99 = f32[1024,1024,1]{1,0,2:T(8,128)} fusion(bf16[4,1024,256]{2,1,0:T(8,128)(2,1)S(1)} %bitcast.158, bf16[4,256,1024]{2,1,0:T(8,128)(2,1)S(1)} %bitcast.151), kind=kOutput, calls=%fused_computation.155 | convolution fusion | flops 2147483648 | bytes 8388608 | tf_op jit(solution)/shard_map/dot_general | solution.py:128
  81.9 10.7 %fusion.39 = f32[1024,1024]{0,1:T(8,128)} fusion(bf16[1024,1024]{1,0:T(8,128)(2,1)} %param.21, f32[1024,1024,1]{1,0,2:T(8,128)} %fusion.99, bf16[4,1024,256]{2,1,0:T(8,128)(2,1)} %bitcast.159, bf16[4,256,1024]{2,1,0:T(8,128)(2,1)} %bitcast.183), kind=kOutput, calls=%fused_computation.59 | convolution fusion | flops 4301258752 | bytes 14680064 | tf_op jit(solution)/shard_map/dot_general | solution.py:141
  96.0 4.6 %fusion.100 = f32[1024,1024,1]{1,0,2:T(8,128)} fusion(bf16[4,1024,256]{2,1,0:T(8,128)(2,1)S(1)} %bitcast.156, bf16[4,256,1024]{2,1,0:T(8,128)(2,1)S(1)} %bitcast.152), kind=kOutput, calls=%fused_computation.156 | convolution fusion | flops 2147483648 | bytes 8388608 | tf_op jit(solution)/shard_map/dot_general | solution.py:128
  100.6 11.8 %convolution_add_fusion = f32[1024,1024]{0,1:T(8,128)} fusion(f32[1024,1024]{0,1:T(8,128)} %fusion.39, bf16[1024,1024]{0,1:T(8,128)(2,1)} %convert_bitcast_fusion, f32[1024,1024,1]{1,0,2:T(8,128)} %fusion.100, bf16[4,1024,256]{2,1,0:T(8,128)(2,1)} %bitcast.157, bf16[4,256,1024]{2,1,0:T(8,128)(2,1)} %bitcast.184), kind=kOutput, calls=%fused_computation.58 | convolution fusion | flops 4302307328 | bytes 18874368 | tf_op jit(solution)/shard_map/dot_general | solution.py:141
  112.3 2.8 %select_bitcast_fusion = f32[1024,2,256]{0,2,1:T(8,128)S(1)} fusion(f32[1024,2,2,256]{0,3,2,1:T(8,128)} %bitcast.153, pred[]{:T(512)S(6)} %eq.101), kind=kLoop, calls=%fused_computation.43 | loop fusion | flops 524288 | bytes 6291457 | tf_op jit(solution)/shard_map/jit(_where)/select_n | solution.py:56
  115.2 4.1 %collective-permute-done.8 = f32[1024,2,256]{0,2,1:T(8,128)S(1)} collective-permute-done((f32[1024,2,256]{0,2,1:T(8,128)S(1)}, f32[1024,2,256]{0,2,1:T(8,128)S(1)}, u32[]{:S(2)}, u32[]{:S(2)}) %collective-permute-start.8) | collective-permute-done | bytes 2097184 | tf_op jit(solution)/shard_map/ppermute | solution.py:13
  120.6 13.1 %collective-permute-done.9 = bf16[1024,1,256]{0,2,1:T(8,128)(2,1)S(1)} collective-permute-done((bf16[1024,1,256]{0,2,1:T(8,128)(2,1)S(1)}, bf16[1024,1,256]{0,2,1:T(8,128)(2,1)S(1)}, u32[]{:S(2)}, u32[]{:S(2)}) %collective-permute-start.9) | collective-permute-done | bytes 524320 | tf_op jit(solution)/shard_map/ppermute | solution.py:13
  134.6 2.8 %convolution_convert_fusion = bf16[1024,256]{1,0:T(8,128)(2,1)} fusion(s32[1024]{0:T(1024)S(1)} %get-tuple-element.50, s32[1024]{0:T(1024)S(1)} %get-tuple-element.51, s32[1024]{0:T(1024)S(1)} %get-tuple-element.49, s32[1024]{0:T(1024)S(1)} %get-tuple-element.52, pred[1024]{0:T(1024)(128)(4,1)S(1)} %get-tuple-element.53, ...), kind=kOutput, calls=%fused_computation.60 | convolution fusion | flops 545521664 | bytes 1067008 | tf_op jit(solution)/shard_map/dot_general | solution.py:148
  139.7 2.5 %copy.25 = f32[1024,1,256]{2,0,1:T(8,128)} copy(f32[1024,1,256]{0,2,1:T(8,128)} %copy-done.2) | data formatting | bytes 2097152 | tf_op jit(solution)/shard_map/add | solution.py:59
  142.2 3.8 %add_convert_fusion.1 = bf16[2,512,256]{2,1,0:T(8,128)(2,1)} fusion(f32[2,512,256]{2,1,0:T(8,128)} %bitcast.155, f32[256]{0:T(256)S(1)} %bitcast.175, pred[2,512]{1,0:T(4,128)(4,1)S(1)} %get-tuple-element.34, f32[256]{0:T(256)S(1)} %bitcast.172, pred[2,512]{1,0:T(4,128)(4,1)S(1)} %get-tuple-element.32, f32[256]{0:T(256)S(1)} %bitcast.169, ...), kind=kLoop, calls=%fused_computation.68 | loop fusion | flops 3407872 | bytes 2107392 | tf_op jit(solution)/shard_map/convert_element_type | solution.py:151
  146.0 16.7 %collective-permute-done.10 = bf16[2,512,256]{2,1,0:T(8,128)(2,1)} collective-permute-done((bf16[2,512,256]{2,1,0:T(8,128)(2,1)}, bf16[2,512,256]{2,1,0:T(8,128)(2,1)}, u32[]{:S(2)}, u32[]{:S(2)}) %collective-permute-start.10) | collective-permute-done | bytes 524320 | tf_op jit(solution)/shard_map/ppermute | solution.py:8
  (76 shorter events, 28.4 us)
Async XLA Ops:
  0.6 76.9 %copy-start = (bf16[1024,1024]{1,0:T(8,128)(2,1)S(1)}, bf16[1024,1024]{1,0:T(8,128)(2,1)}, u32[]{:S(2)}) copy-start(bf16[1024,1024]{1,0:T(8,128)(2,1)} %param.19) | copy-start | bytes 6291460
  0.6 15.3 %copy-start.11 = (f32[256]{0:T(256)S(1)}, f32[256]{0:T(256)}, u32[]{:S(2)}) copy-start(f32[256]{0:T(256)} %param.18) | copy-start | bytes 3076
  1.5 3.7 %collective-permute-start = (s32[2,512]{1,0:T(2,128)S(1)}, s32[2,512]{1,0:T(2,128)S(1)}, u32[]{:S(2)}, u32[]{:S(2)}) collective-permute-start(s32[2,512]{1,0:T(2,128)S(1)} %subtract_select_fusion), channel_id=1, source_target_pairs={{0,28},{4,24},{8,20},{12,16},{16,12},{20,8},{24,4},{28,0},{1,29},{... | collective-permute-start | bytes 12296 | tf_op jit(solution)/shard_map/ppermute | solution.py:8
  18.8 8.6 %copy-start.12 = (f32[256]{0:T(256)S(1)}, f32[256]{0:T(256)}, u32[]{:S(2)}) copy-start(f32[256]{0:T(256)} %param.17) | copy-start | bytes 3076
  18.8 5.3 %collective-permute-start.2 = (bf16[2,2,3,256]{3,2,1,0:T(4,128)(2,1)S(1)}, bf16[2,2,3,256]{3,2,1,0:T(4,128)(2,1)S(1)}, u32[]{:S(2)}, u32[]{:S(2)}) collective-permute-start(bf16[2,2,3,256]{3,2,1,0:T(4,128)(2,1)S(1)} %get-tuple-element.21), channel_id=1, source_target_pairs={{4,0},{8,4},{12,8},{16,12},{20,16},{24,20},{28,24},{5,1},{9,5},{13... | collective-permute-start | bytes 18440 | tf_op jit(solution)/shard_map/ppermute | solution.py:25
  21.9 5.3 %collective-permute-start.1 = (bf16[2,2,3,256]{3,2,1,0:T(4,128)(2,1)S(1)}, bf16[2,2,3,256]{3,2,1,0:T(4,128)(2,1)S(1)}, u32[]{:S(2)}, u32[]{:S(2)}) collective-permute-start(bf16[2,2,3,256]{3,2,1,0:T(4,128)(2,1)S(1)} %get-tuple-element.20), channel_id=1, source_target_pairs={{0,4},{4,8},{8,12},{12,16},{16,20},{20,24},{24,28},{1,5},{5,9},{9,... | collective-permute-start | bytes 18440 | tf_op jit(solution)/shard_map/ppermute | solution.py:23
  30.3 11.3 %collective-permute-start.3 = (bf16[1,1024,256]{2,1,0:T(8,128)(2,1)}, bf16[1,1024,256]{2,1,0:T(8,128)(2,1)}, u32[]{:S(2)}, u32[]{:S(2)}) collective-permute-start(bf16[1,1024,256]{2,1,0:T(8,128)(2,1)} %bitcast.14), channel_id=1, source_target_pairs={{0,2},{1,3},{2,0},{3,1},{4,6},{5,7},{6,4},{7,5},{8,10},{9,11},{10,... | collective-permute-start | bytes 1572872 | tf_op jit(solution)/shard_map/ppermute | solution.py:13
  34.4 13.7 %copy-start.13 = (bf16[1024,1024]{1,0:T(8,128)(2,1)S(1)}, bf16[1024,1024]{1,0:T(8,128)(2,1)}, u32[]{:S(2)}) copy-start(bf16[1024,1024]{1,0:T(8,128)(2,1)} %param.21) | copy-start | bytes 6291460
  34.4 23.5 %collective-permute-start.5 = (bf16[1024,256]{1,0:T(8,128)(2,1)S(1)}, bf16[1024,256]{1,0:T(8,128)(2,1)}, u32[]{:S(2)}, u32[]{:S(2)}) collective-permute-start(bf16[1024,256]{1,0:T(8,128)(2,1)S(1)} %convolution_convert_fusion.2), channel_id=1, source_target_pairs={{0,28},{4,24},{8,20},{12,16},{16,12},{20,8},{24,4},{28,0},{1,29},{... | collective-permute-start | bytes 1572872 | tf_op jit(solution)/shard_map/ppermute | solution.py:8
  42.9 0.8 copy-start.3
  42.9 1.9 %copy-start.5 = (bf16[1,1,1024,256]{3,2,1,0:T(8,128)(2,1)}, bf16[1,1,1024,256]{3,2,1,0:T(8,128)(2,1)S(1)}, u32[]{:S(2)}) copy-start(bf16[1,1,1024,256]{3,2,1,0:T(8,128)(2,1)S(1)} %get-tuple-element.19) | copy-start | bytes 1572868
  44.8 31.0 %collective-permute-start.4 = (bf16[2,1024,256]{2,1,0:T(8,128)(2,1)}, bf16[2,1024,256]{2,1,0:T(8,128)(2,1)}, u32[]{:S(2)}, u32[]{:S(2)}) collective-permute-start(bf16[2,1024,256]{2,1,0:T(8,128)(2,1)} %maximum_bitcast_fusion), channel_id=1, source_target_pairs={{0,1},{1,0},{2,3},{3,2},{4,5},{5,4},{6,7},{7,6},{8,9},{9,8},{10,11... | collective-permute-start | bytes 3145736 | tf_op jit(solution)/shard_map/ppermute | solution.py:13
  57.9 10.7 %collective-permute-start.6 = (bf16[1,1024,256]{2,1,0:T(8,128)(2,1)}, bf16[1,1024,256]{2,1,0:T(8,128)(2,1)}, u32[]{:S(2)}, u32[]{:S(2)}) collective-permute-start(bf16[1,1024,256]{2,1,0:T(8,128)(2,1)} %bitcast.27), channel_id=1, source_target_pairs={{0,2},{1,3},{2,0},{3,1},{4,6},{5,7},{6,4},{7,5},{8,10},{9,11},{10,... | collective-permute-start | bytes 1572872 | tf_op jit(solution)/shard_map/ppermute | solution.py:13
  58.1 17.6 %copy-start.4 = (bf16[1,1,1024,256]{3,2,1,0:T(8,128)(2,1)S(1)}, bf16[1,1,1024,256]{3,2,1,0:T(8,128)(2,1)}, u32[]{:S(2)}) copy-start(bf16[1,1,1024,256]{3,2,1,0:T(8,128)(2,1)} %copy-done.3) | copy-start | bytes 1572868
  58.1 17.6 %copy-start.6 = (bf16[1,1,1024,256]{3,2,1,0:T(8,128)(2,1)S(1)}, bf16[1,1,1024,256]{3,2,1,0:T(8,128)(2,1)}, u32[]{:S(2)}) copy-start(bf16[1,1,1024,256]{3,2,1,0:T(8,128)(2,1)} %copy-done.5) | copy-start | bytes 1572868
  69.9 1.9 %copy-start.8 = (bf16[1,1,1024,256]{3,2,1,0:T(8,128)(2,1)}, bf16[1,1,1024,256]{3,2,1,0:T(8,128)(2,1)S(1)}, u32[]{:S(2)}) copy-start(bf16[1,1,1024,256]{3,2,1,0:T(8,128)(2,1)S(1)} %get-tuple-element.15) | copy-start | bytes 1572868
  71.8 20.8 %collective-permute-start.7 = (bf16[2,1024,256]{2,1,0:T(8,128)(2,1)}, bf16[2,1024,256]{2,1,0:T(8,128)(2,1)}, u32[]{:S(2)}, u32[]{:S(2)}) collective-permute-start(bf16[2,1024,256]{2,1,0:T(8,128)(2,1)} %maximum_bitcast_fusion.1), channel_id=1, source_target_pairs={{0,1},{1,0},{2,3},{3,2},{4,5},{5,4},{6,7},{7,6},{8,9},{9,8},{10,11... | collective-permute-start | bytes 3145736 | tf_op jit(solution)/shard_map/ppermute | solution.py:13
  77.5 4.4 %copy-start.10 = (bf16[2,2,1024,256]{3,2,1,0:T(8,128)(2,1)}, bf16[2,2,1024,256]{3,2,1,0:T(8,128)(2,1)S(1)}, u32[]{:S(2)}) copy-start(bf16[2,2,1024,256]{3,2,1,0:T(8,128)(2,1)S(1)} %copy.19) | copy-start | bytes 6291460
  94.6 1.4 copy-start.9
  112.3 7.0 %copy-start.1 = (f32[1024,1024]{0,1:T(8,128)S(1)}, f32[1024,1024]{0,1:T(8,128)}, u32[]{:S(2)}) copy-start(f32[1024,1024]{0,1:T(8,128)} %convolution_add_fusion) | copy-start | bytes 12582916
  115.1 4.2 %collective-permute-start.8 = (f32[1024,2,256]{0,2,1:T(8,128)S(1)}, f32[1024,2,256]{0,2,1:T(8,128)S(1)}, u32[]{:S(2)}, u32[]{:S(2)}) collective-permute-start(f32[1024,2,256]{0,2,1:T(8,128)S(1)} %select_bitcast_fusion), channel_id=1, source_target_pairs={{0,1},{1,0},{2,3},{3,2},{4,5},{5,4},{6,7},{7,6},{8,9},{9,8},{10,11... | collective-permute-start | bytes 6291464 | tf_op jit(solution)/shard_map/ppermute | solution.py:13
  120.3 13.4 %collective-permute-start.9 = (bf16[1024,1,256]{0,2,1:T(8,128)(2,1)S(1)}, bf16[1024,1,256]{0,2,1:T(8,128)(2,1)S(1)}, u32[]{:S(2)}, u32[]{:S(2)}) collective-permute-start(bf16[1024,1,256]{0,2,1:T(8,128)(2,1)S(1)} %fusion.42), channel_id=1, source_target_pairs={{0,2},{1,3},{2,0},{3,1},{4,6},{5,7},{6,4},{7,5},{8,10},{9,11},{10,... | collective-permute-start | bytes 1572872 | tf_op jit(solution)/shard_map/ppermute | solution.py:13
  134.0 3.5 %copy-start.2 = (f32[1024,1,256]{0,2,1:T(8,128)}, f32[1024,1,256]{0,2,1:T(8,128)S(1)}, u32[]{:S(2)}) copy-start(f32[1024,1,256]{0,2,1:T(8,128)S(1)} %bitcast_add_fusion) | copy-start | bytes 3145732
  137.5 25.2 %collective-permute-start.10 = (bf16[2,512,256]{2,1,0:T(8,128)(2,1)}, bf16[2,512,256]{2,1,0:T(8,128)(2,1)}, u32[]{:S(2)}, u32[]{:S(2)}) collective-permute-start(bf16[2,512,256]{2,1,0:T(8,128)(2,1)} %bitcast.47), channel_id=1, source_target_pairs={{0,31},{1,30},{2,29},{3,28},{4,27},{5,26},{6,25},{7,24},{8,23},{9,... | collective-permute-start | bytes 1572872 | tf_op jit(solution)/shard_map/ppermute | solution.py:8
  (1 other events, 0.8 us)

commit v13 on v10

--- a/solution.py
+++ b/solution.py
@@ -54,9 +54,7 @@
         low = ((me >> bit) & 1) == 0
         keep = jnp.where(low, cur[:, :, 0], cur[:, :, 1])
         give = jnp.where(low, cur[:, :, 1], cur[:, :, 0])
-        if bit > 0:
-            give = give.astype(jnp.bfloat16)
-        cur = keep + partner(give, "ch", bit).astype(jnp.float32)
+        cur = keep + partner(give.astype(jnp.bfloat16), "ch", bit).astype(jnp.float32)
     return cur[:, 0]
 
 

time: 157 us -> 158 us (level)
    select_n x1 -> x0, other arithmetic: 2.93 us -> none  [scatter_blocks(): give = jnp.where(low, cur[:, :, 1], cur[:, :, 0])]
    convert_element_type x1 -> x2, other arithmetic: 0.09 us -> 2.5 us  [scatter_blocks(): give.astype(jnp.bfloat16)]
    reshape x1, other arithmetic: 0.87 us -> 2.84 us  [scatter_blocks(): cur = cur.reshape(rows, -1, 2, w)]
where the time goes in v13:
time: 158 us; the launch traced here: 157 us
  waiting for transfers between devices  54.7 us (35%)
  matrix products  36.8 us (23%)
  other arithmetic  29.7 us (19%)
  starting transfers between devices  21.7 us (14%)
  local copies, waits for them, and re-layouts  6.73 us (4%)
  blocking collectives  6.55 us (4%)
    ppermute x3, waiting for transfers between devices, mirror(): return lax.ppermute(value, axes, [(k, count - 1 - k) for k in range(count)])  33.5 us
    ppermute x6, waiting for transfers between devices, partner(): lax.ppermute(value, axis, [(k, k ^ mask) for k in range(lax.axis_size(axi...  18.2 us
    dot_general x1, matrix products, local(): jnp.dot(act_fwd, w_out, preferred_element_type=jnp.float32)  12.2 us
    ppermute x6, starting transfers between devices, partner(): lax.ppermute(value, axis, [(k, k ^ mask) for k in range(lax.axis_size(axi...  11.3 us
    dot_general x2, matrix products, activation(): lax.dot_general(pieces, w_gate.reshape(ch_count, local_width, -1), dims,...  6.67 us
    psum x1, blocking collectives, local(): lax.psum((jnp.sum(x_fwd * x_fwd, axis=-1), jnp.sum(x_rev * x_rev, axis=-1...  6.55 us
    another operation x6, other arithmetic, gather_blocks(): cur = jnp.stack([first, second], axis=1).reshape((-1,) + block.shape)  5.8 us
    convert_element_type x2, other arithmetic, local(): return (out_forward.astype(jnp.bfloat16), out_reverse.astype(jnp.bfloat16))  5.75 us
  transfers between devices with their start and end apart: 11, of which 6 were waited for; matrix products, arithmetic and copies ran while one was open for 16% of the time, Pallas kernels for 0%

profile of v13, /device:TPU:17, one launch (start us, length us, event | category | flops | bytes accessed | tf_op | source)
XLA Modules:
  0.0 157.2 jit_solution(2071075181529858359)
XLA Ops:
  5.6 3.6 %multiply_reduce_fusion.1 = (f32[2,512]{1,0:T(2,128)S(1)}, f32[2,512,256]{2,1,0:T(8,128)S(1)}) fusion(f32[256]{0:T(256)S(1)} %bitcast.174, pred[2,512]{1,0:T(4,128)(4,1)S(1)} %get-tuple-element.30, f32[256]{0:T(256)S(1)} %bitcast.171, pred[2,512]{1,0:T(4,128)(4,1)S(1)} %get-tuple-element.28, f32[256]{0:T(256)S(1)} %bitcast.168, ...), kind=kLoop, calls=%fused_computation.79 | loop fusion | flops 6290432 | bytes 2116608 | tf_op jit(solution)/shard_map/reduce_sum | solution.py:98
  9.4 6.6 %all-reduce = (f32[2,512]{1,0:T(2,128)S(1)}, f32[2,512]{1,0:T(2,128)S(1)}) all-reduce(f32[2,512]{1,0:T(2,128)S(1)} %multiply_reduce_fusion, f32[2,512]{1,0:T(2,128)S(1)} %get-tuple-element.25), channel_id=1, replica_groups=mesh['seq'=8,'ch'=4] {'ch'}, use_global_device_ids=true, to_apply=%region_3.4 | all-reduce | flops 2048 | bytes 16384 | tf_op jit(solution)/shard_map/psum | solution.py:97
  16.0 2.8 %fusion.44 = (bf16[1,2,512,256]{3,2,1,0:T(8,128)(2,1)S(1)}, bf16[1,2,512,256]{3,2,1,0:T(8,128)(2,1)S(1)}) fusion(f32[256]{0:T(256)S(1)} %copy-done.9, f32[2,512]{1,0:T(2,128)S(1)} %get-tuple-element.44, f32[256]{0:T(256)S(1)} %bitcast.175, pred[2,512]{1,0:T(4,128)(4,1)S(1)} %get-tuple-element.30, f32[256]{0:T(256)S(1)} %bitcast.172, ...), kind=kLoop, calls=%fused_computation.81 | loop fusion | flops 4456448 | bytes 2640896 | tf_op jit(solution)/shard_map/stack | solution.py:106
  18.8 3.0 %collective-permute-start.2 = (bf16[2,2,3,256]{3,2,1,0:T(4,128)(2,1)S(1)}, bf16[2,2,3,256]{3,2,1,0:T(4,128)(2,1)S(1)}, u32[]{:S(2)}, u32[]{:S(2)}) collective-permute-start(bf16[2,2,3,256]{3,2,1,0:T(4,128)(2,1)S(1)} %get-tuple-element.17), channel_id=1, source_target_pairs={{4,0},{8,4},{12,8},{16,12},{20,16},{24,20},{28,24},{5,1},{9,5},{13... | collective-permute-start | bytes 18440 | tf_op jit(solution)/shard_map/ppermute | solution.py:25
  24.2 3.0 %collective-permute-done.1 = bf16[2,2,3,256]{3,2,1,0:T(4,128)(2,1)S(1)} collective-permute-done((bf16[2,2,3,256]{3,2,1,0:T(4,128)(2,1)S(1)}, bf16[2,2,3,256]{3,2,1,0:T(4,128)(2,1)S(1)}, u32[]{:S(2)}, u32[]{:S(2)}) %collective-permute-start.1) | collective-permute-done | bytes 6176 | tf_op jit(solution)/shard_map/ppermute | solution.py:23
  30.1 2.8 %convolution_convert_fusion.2 = bf16[1024,256]{1,0:T(8,128)(2,1)} fusion(bf16[1024,256]{1,0:T(8,128)(2,1)S(1)} %bitcast.161, s32[1024]{0:T(1024)S(1)} %get-tuple-element.46, s32[1024]{0:T(1024)S(1)} %get-tuple-element.47, s32[1024]{0:T(1024)S(1)} %get-tuple-element.45, s32[1024]{0:T(1024)S(1)} %get-tuple-element.48, ...), kind=kOutput, calls=%fused_computation.62 | convolution fusion | flops 545521664 | bytes 1067008 | tf_op jit(solution)/shard_map/dot_general | solution.py:116
  35.0 21.6 %collective-permute-done.5 = bf16[1024,256]{1,0:T(8,128)(2,1)} collective-permute-done((bf16[1024,256]{1,0:T(8,128)(2,1)}, bf16[1024,256]{1,0:T(8,128)(2,1)}, u32[]{:S(2)}, u32[]{:S(2)}) %collective-permute-start.5) | collective-permute-done | bytes 524320 | tf_op jit(solution)/shard_map/ppermute | solution.py:8
  60.3 3.4 %collective-permute-start.4 = (bf16[2,1024,256]{2,1,0:T(8,128)(2,1)}, bf16[2,1024,256]{2,1,0:T(8,128)(2,1)}, u32[]{:S(2)}, u32[]{:S(2)}) collective-permute-start(bf16[2,1024,256]{2,1,0:T(8,128)(2,1)} %maximum_bitcast_fusion), channel_id=1, source_target_pairs={{0,1},{1,0},{2,3},{3,2},{4,5},{5,4},{6,7},{7,6},{8,9},{9,8},{10,11... | collective-permute-start | bytes 3145736 | tf_op jit(solution)/shard_map/ppermute | solution.py:13
  63.7 3.5 %collective-permute-done.6 = bf16[1,1024,256]{2,1,0:T(8,128)(2,1)S(1)} collective-permute-done((bf16[1,1024,256]{2,1,0:T(8,128)(2,1)}, bf16[1,1024,256]{2,1,0:T(8,128)(2,1)S(1)}, u32[]{:S(2)}, u32[]{:S(2)}) %collective-permute-start.6) | collective-permute-done | bytes 524320 | tf_op jit(solution)/shard_map/ppermute | solution.py:13
  70.2 4.0 %collective-permute-start.7 = (bf16[2,1024,256]{2,1,0:T(8,128)(2,1)}, bf16[2,1024,256]{2,1,0:T(8,128)(2,1)}, u32[]{:S(2)}, u32[]{:S(2)}) collective-permute-start(bf16[2,1024,256]{2,1,0:T(8,128)(2,1)} %maximum_bitcast_fusion.1), channel_id=1, source_target_pairs={{0,1},{1,0},{2,3},{3,2},{4,5},{5,4},{6,7},{7,6},{8,9},{9,8},{10,11... | collective-permute-start | bytes 3145736 | tf_op jit(solution)/shard_map/ppermute | solution.py:13
  74.2 4.6 %fusion.135 = bf16[1024,1024]{1,0:T(8,128)(2,1)} fusion(bf16[1024,1024]{1,0:T(8,128)(2,1)S(1)} %copy-done.12, s32[1024]{0:T(1024)S(1)} %get-tuple-element.52, s32[1024]{0:T(1024)S(1)} %get-tuple-element.53, s32[1024]{0:T(1024)S(1)} %get-tuple-element.51, s32[1024]{0:T(1024)S(1)} %get-tuple-element.54, pred[1024]{0:T(1024)(128)(4,1)S(1)} %get-tuple-element.55, ...), kind=kOutput, calls=%fused_computation.45.clone.1 | convolution fusion | flops 2157969408 | bytes 4212736 | tf_op jit(solution)/shard_map/dot_general | solution.py:137
  80.8 4.3 %fusion.103 = f32[1024,1024,1]{1,0,2:T(8,128)} fusion(bf16[4,1024,256]{2,1,0:T(8,128)(2,1)S(1)} %bitcast.157, bf16[4,256,1024]{2,1,0:T(8,128)(2,1)S(1)} %bitcast.152), kind=kOutput, calls=%fused_computation.155 | convolution fusion | flops 2147483648 | bytes 8388608 | tf_op jit(solution)/shard_map/dot_general | solution.py:126
  89.3 2.7 %fusion = bf16[1024,1024]{1,0:T(8,128)(2,1)S(1)} fusion(f32[1024,1024,1]{1,0,2:T(8,128)S(1)} %fusion.104, bf16[4,1024,256]{2,1,0:T(8,128)(2,1)S(1)} %bitcast.160, bf16[4,256,1024]{2,1,0:T(8,128)(2,1)S(1)} %bitcast.185), kind=kOutput, calls=%fused_computation.1 | convolution fusion | flops 2153775104 | bytes 10485760 | tf_op jit(solution)/shard_map/dot_general | solution.py:129
  91.9 4.4 %fusion.24 = f32[1024,1024]{0,1:T(8,128)} fusion(bf16[1024,1024]{1,0:T(8,128)(2,1)S(1)} %fusion, bf16[1024,1024]{1,0:T(8,128)(2,1)S(1)} %copy-done.13), kind=kOutput, calls=%fused_computation.44 | convolution fusion | flops 2147483648 | bytes 8388608 | tf_op jit(solution)/shard_map/dot_general | solution.py:138
  96.3 12.2 %convolution_add_fusion = f32[1024,1024]{0,1:T(8,128)} fusion(f32[1024,1024]{0,1:T(8,128)} %fusion.24, bf16[1024,1024]{1,0:T(8,128)(2,1)} %param.21, f32[1024,1024,1]{1,0,2:T(8,128)} %fusion.103, bf16[4,1024,256]{2,1,0:T(8,128)(2,1)} %bitcast.158, bf16[4,256,1024]{2,1,0:T(8,128)(2,1)} %bitcast.184), kind=kOutput, calls=%fused_computation.59 | convolution fusion | flops 4302307328 | bytes 18874368 | tf_op jit(solution)/shard_map/dot_general | solution.py:138
  108.5 2.4 %fusion.43 = bf16[1024,2,256]{0,2,1:T(8,128)(2,1)S(1)} fusion(f32[1024,2,2,256]{0,3,2,1:T(8,128)} %bitcast.154, pred[]{:T(512)S(6)} %eq.101), kind=kLoop, calls=%fused_computation.64 | loop fusion | flops 524288 | bytes 3145729 | tf_op jit(solution)/shard_map/convert_element_type | solution.py:57
  111.0 2.6 %collective-permute-done.8 = bf16[1024,2,256]{0,2,1:T(8,128)(2,1)S(1)} collective-permute-done((bf16[1024,2,256]{0,2,1:T(8,128)(2,1)S(1)}, bf16[1024,2,256]{0,2,1:T(8,128)(2,1)S(1)}, u32[]{:S(2)}, u32[]{:S(2)}) %collective-permute-start.8) | collective-permute-done | bytes 1048608 | tf_op jit(solution)/shard_map/ppermute | solution.py:13
  113.7 2.8 %fusion.23 = f32[1024,1,2,256]{0,3,2,1:T(8,128)S(1)} fusion(bf16[1024,2,256]{0,2,1:T(8,128)(2,1)S(1)} %collective-permute-done.8, f32[1024,2,2,256]{0,3,2,1:T(8,128)} %bitcast.155, pred[]{:T(512)S(6)} %eq.101), kind=kLoop, calls=%fused_computation.42 | loop fusion | flops 1572864 | bytes 7340033 | tf_op jit(solution)/shard_map/reshape | solution.py:53
  118.0 12.1 %collective-permute-done.9 = bf16[1024,1,256]{0,2,1:T(8,128)(2,1)S(1)} collective-permute-done((bf16[1024,1,256]{0,2,1:T(8,128)(2,1)S(1)}, bf16[1024,1,256]{0,2,1:T(8,128)(2,1)S(1)}, u32[]{:S(2)}, u32[]{:S(2)}) %collective-permute-start.9) | collective-permute-done | bytes 524320 | tf_op jit(solution)/shard_map/ppermute | solution.py:13
  130.9 2.8 %convolution_convert_fusion = bf16[1024,256]{1,0:T(8,128)(2,1)} fusion(s32[1024]{0:T(1024)S(1)} %get-tuple-element.46, s32[1024]{0:T(1024)S(1)} %get-tuple-element.47, s32[1024]{0:T(1024)S(1)} %get-tuple-element.45, s32[1024]{0:T(1024)S(1)} %get-tuple-element.48, pred[1024]{0:T(1024)(128)(4,1)S(1)} %get-tuple-element.49, ...), kind=kOutput, calls=%fused_computation.60 | convolution fusion | flops 545521664 | bytes 1067008 | tf_op jit(solution)/shard_map/dot_general | solution.py:145
  133.7 3.3 %collective-permute-start.10 = (bf16[2,512,256]{2,1,0:T(8,128)(2,1)}, bf16[2,512,256]{2,1,0:T(8,128)(2,1)}, u32[]{:S(2)}, u32[]{:S(2)}) collective-permute-start(bf16[2,512,256]{2,1,0:T(8,128)(2,1)} %bitcast.46), channel_id=1, source_target_pairs={{0,31},{1,30},{2,29},{3,28},{4,27},{5,26},{6,25},{7,24},{8,23},{9,... | collective-permute-start | bytes 1572872 | tf_op jit(solution)/shard_map/ppermute | solution.py:8
  137.0 2.5 %copy.25 = f32[1024,1,256]{2,0,1:T(8,128)} copy(f32[1024,1,256]{0,2,1:T(8,128)} %copy-done.1) | data formatting | bytes 2097152 | tf_op jit(solution)/shard_map/add | solution.py:57
  139.6 3.8 %add_convert_fusion.1 = bf16[2,512,256]{2,1,0:T(8,128)(2,1)} fusion(f32[2,512,256]{2,1,0:T(8,128)} %bitcast.156, f32[256]{0:T(256)S(1)} %bitcast.176, pred[2,512]{1,0:T(4,128)(4,1)S(1)} %get-tuple-element.30, f32[256]{0:T(256)S(1)} %bitcast.173, pred[2,512]{1,0:T(4,128)(4,1)S(1)} %get-tuple-element.28, f32[256]{0:T(256)S(1)} %bitcast.170, ...), kind=kLoop, calls=%fused_computation.69 | loop fusion | flops 3407872 | bytes 2107392 | tf_op jit(solution)/shard_map/convert_element_type | solution.py:148
  143.4 11.9 %collective-permute-done.10 = bf16[2,512,256]{2,1,0:T(8,128)(2,1)} collective-permute-done((bf16[2,512,256]{2,1,0:T(8,128)(2,1)}, bf16[2,512,256]{2,1,0:T(8,128)(2,1)}, u32[]{:S(2)}, u32[]{:S(2)}) %collective-permute-start.10) | collective-permute-done | bytes 524320 | tf_op jit(solution)/shard_map/ppermute | solution.py:8
  (77 shorter events, 29.5 us)
Async XLA Ops:
  0.6 80.1 %copy-start = (bf16[1024,1024]{1,0:T(8,128)(2,1)S(1)}, bf16[1024,1024]{1,0:T(8,128)(2,1)}, u32[]{:S(2)}) copy-start(bf16[1024,1024]{1,0:T(8,128)(2,1)} %param.19) | copy-start | bytes 6291460
  0.6 15.3 %copy-start.9 = (f32[256]{0:T(256)S(1)}, f32[256]{0:T(256)}, u32[]{:S(2)}) copy-start(f32[256]{0:T(256)} %param.18) | copy-start | bytes 3076
  1.5 3.7 %collective-permute-start = (s32[2,512]{1,0:T(2,128)S(1)}, s32[2,512]{1,0:T(2,128)S(1)}, u32[]{:S(2)}, u32[]{:S(2)}) collective-permute-start(s32[2,512]{1,0:T(2,128)S(1)} %subtract_select_fusion), channel_id=1, source_target_pairs={{0,28},{4,24},{8,20},{12,16},{16,12},{20,8},{24,4},{28,0},{1,29},{... | collective-permute-start | bytes 12296 | tf_op jit(solution)/shard_map/ppermute | solution.py:8
  18.8 8.6 %copy-start.10 = (f32[256]{0:T(256)S(1)}, f32[256]{0:T(256)}, u32[]{:S(2)}) copy-start(f32[256]{0:T(256)} %param.17) | copy-start | bytes 3076
  18.8 5.3 %collective-permute-start.2 = (bf16[2,2,3,256]{3,2,1,0:T(4,128)(2,1)S(1)}, bf16[2,2,3,256]{3,2,1,0:T(4,128)(2,1)S(1)}, u32[]{:S(2)}, u32[]{:S(2)}) collective-permute-start(bf16[2,2,3,256]{3,2,1,0:T(4,128)(2,1)S(1)} %get-tuple-element.17), channel_id=1, source_target_pairs={{4,0},{8,4},{12,8},{16,12},{20,16},{24,20},{28,24},{5,1},{9,5},{13... | collective-permute-start | bytes 18440 | tf_op jit(solution)/shard_map/ppermute | solution.py:25
  21.9 5.3 %collective-permute-start.1 = (bf16[2,2,3,256]{3,2,1,0:T(4,128)(2,1)S(1)}, bf16[2,2,3,256]{3,2,1,0:T(4,128)(2,1)S(1)}, u32[]{:S(2)}, u32[]{:S(2)}) collective-permute-start(bf16[2,2,3,256]{3,2,1,0:T(4,128)(2,1)S(1)} %get-tuple-element.16), channel_id=1, source_target_pairs={{0,4},{4,8},{8,12},{12,16},{16,20},{20,24},{24,28},{1,5},{5,9},{9,... | collective-permute-start | bytes 18440 | tf_op jit(solution)/shard_map/ppermute | solution.py:23
  33.0 23.7 %collective-permute-start.5 = (bf16[1024,256]{1,0:T(8,128)(2,1)}, bf16[1024,256]{1,0:T(8,128)(2,1)}, u32[]{:S(2)}, u32[]{:S(2)}) collective-permute-start(bf16[1024,256]{1,0:T(8,128)(2,1)} %convolution_convert_fusion.2), channel_id=1, source_target_pairs={{0,28},{4,24},{8,20},{12,16},{16,12},{20,8},{24,4},{28,0},{1,29},{... | collective-permute-start | bytes 1572872 | tf_op jit(solution)/shard_map/ppermute | solution.py:8
  33.8 24.1 %collective-permute-start.3 = (bf16[1,1024,256]{2,1,0:T(8,128)(2,1)}, bf16[1,1024,256]{2,1,0:T(8,128)(2,1)}, u32[]{:S(2)}, u32[]{:S(2)}) collective-permute-start(bf16[1,1024,256]{2,1,0:T(8,128)(2,1)} %bitcast.14), channel_id=1, source_target_pairs={{0,2},{1,3},{2,0},{3,1},{4,6},{5,7},{6,4},{7,5},{8,10},{9,11},{10,... | collective-permute-start | bytes 1572872 | tf_op jit(solution)/shard_map/ppermute | solution.py:13
  56.6 10.6 %collective-permute-start.6 = (bf16[1,1024,256]{2,1,0:T(8,128)(2,1)}, bf16[1,1024,256]{2,1,0:T(8,128)(2,1)S(1)}, u32[]{:S(2)}, u32[]{:S(2)}) collective-permute-start(bf16[1,1024,256]{2,1,0:T(8,128)(2,1)} %bitcast.26), channel_id=1, source_target_pairs={{0,2},{1,3},{2,0},{3,1},{4,6},{5,7},{6,4},{7,5},{8,10},{9,11},{10,... | collective-permute-start | bytes 1572872 | tf_op jit(solution)/shard_map/ppermute | solution.py:13
  59.2 4.6 %copy-start.6 = (bf16[1,1,1024,256]{3,2,1,0:T(8,128)(2,1)}, bf16[1,1,1024,256]{3,2,1,0:T(8,128)(2,1)S(1)}, u32[]{:S(2)}) copy-start(bf16[1,1,1024,256]{3,2,1,0:T(8,128)(2,1)S(1)} %get-tuple-element.10) | copy-start | bytes 1572868
  59.2 4.6 %copy-start.7 = (bf16[1,1,1024,256]{3,2,1,0:T(8,128)(2,1)}, bf16[1,1,1024,256]{3,2,1,0:T(8,128)(2,1)S(1)}, u32[]{:S(2)}) copy-start(bf16[1,1,1024,256]{3,2,1,0:T(8,128)(2,1)S(1)} %get-tuple-element.11) | copy-start | bytes 1572868
  60.3 13.8 %copy-start.12 = (bf16[1024,1024]{1,0:T(8,128)(2,1)S(1)}, bf16[1024,1024]{1,0:T(8,128)(2,1)}, u32[]{:S(2)}) copy-start(bf16[1024,1024]{1,0:T(8,128)(2,1)} %param.21) | copy-start | bytes 6291460
  60.3 18.4 %collective-permute-start.4 = (bf16[2,1024,256]{2,1,0:T(8,128)(2,1)}, bf16[2,1024,256]{2,1,0:T(8,128)(2,1)}, u32[]{:S(2)}, u32[]{:S(2)}) collective-permute-start(bf16[2,1024,256]{2,1,0:T(8,128)(2,1)} %maximum_bitcast_fusion), channel_id=1, source_target_pairs={{0,1},{1,0},{2,3},{3,2},{4,5},{5,4},{6,7},{7,6},{8,9},{9,8},{10,11... | collective-permute-start | bytes 3145736 | tf_op jit(solution)/shard_map/ppermute | solution.py:13
  68.3 1.9 %copy-start.4 = (bf16[1,1,1024,256]{3,2,1,0:T(8,128)(2,1)}, bf16[1,1,1024,256]{3,2,1,0:T(8,128)(2,1)S(1)}, u32[]{:S(2)}) copy-start(bf16[1,1,1024,256]{3,2,1,0:T(8,128)(2,1)S(1)} %get-tuple-element.15) | copy-start | bytes 1572868
  70.2 15.0 %collective-permute-start.7 = (bf16[2,1024,256]{2,1,0:T(8,128)(2,1)}, bf16[2,1024,256]{2,1,0:T(8,128)(2,1)}, u32[]{:S(2)}, u32[]{:S(2)}) collective-permute-start(bf16[2,1024,256]{2,1,0:T(8,128)(2,1)} %maximum_bitcast_fusion.1), channel_id=1, source_target_pairs={{0,1},{1,0},{2,3},{3,2},{4,5},{5,4},{6,7},{7,6},{8,9},{9,8},{10,11... | collective-permute-start | bytes 3145736 | tf_op jit(solution)/shard_map/ppermute | solution.py:13
  80.8 4.4 %copy-start.8 = (bf16[2,2,1024,256]{3,2,1,0:T(8,128)(2,1)}, bf16[2,2,1024,256]{3,2,1,0:T(8,128)(2,1)S(1)}, u32[]{:S(2)}) copy-start(bf16[2,2,1024,256]{3,2,1,0:T(8,128)(2,1)S(1)} %copy.19) | copy-start | bytes 6291460
  80.8 4.4 %copy-start.3 = (bf16[1,1,1024,256]{3,2,1,0:T(8,128)(2,1)S(1)}, bf16[1,1,1024,256]{3,2,1,0:T(8,128)(2,1)}, u32[]{:S(2)}) copy-start(bf16[1,1,1024,256]{3,2,1,0:T(8,128)(2,1)} %copy-done.2) | copy-start | bytes 1572868
  80.8 4.4 %copy-start.5 = (bf16[1,1,1024,256]{3,2,1,0:T(8,128)(2,1)S(1)}, bf16[1,1,1024,256]{3,2,1,0:T(8,128)(2,1)}, u32[]{:S(2)}) copy-start(bf16[1,1,1024,256]{3,2,1,0:T(8,128)(2,1)} %copy-done.4) | copy-start | bytes 1572868
  86.9 2.4 %copy-start.11 = (bf16[1024,1024]{1,0:T(8,128)(2,1)S(1)}, bf16[1024,1024]{1,0:T(8,128)(2,1)}, u32[]{:S(2)}) copy-start(bf16[1024,1024]{1,0:T(8,128)(2,1)} %param.20) | copy-start | bytes 6291460
  89.2 2.7 %copy-start.13 = (bf16[1024,1024]{1,0:T(8,128)(2,1)S(1)}, bf16[1024,1024]{1,0:T(8,128)(2,1)}, u32[]{:S(2)}) copy-start(bf16[1024,1024]{1,0:T(8,128)(2,1)} %fusion.135) | copy-start | bytes 6291460
  110.9 2.7 %collective-permute-start.8 = (bf16[1024,2,256]{0,2,1:T(8,128)(2,1)S(1)}, bf16[1024,2,256]{0,2,1:T(8,128)(2,1)S(1)}, u32[]{:S(2)}, u32[]{:S(2)}) collective-permute-start(bf16[1024,2,256]{0,2,1:T(8,128)(2,1)S(1)} %fusion.43), channel_id=1, source_target_pairs={{0,1},{1,0},{2,3},{3,2},{4,5},{5,4},{6,7},{7,6},{8,9},{9,8},{10,11... | collective-permute-start | bytes 3145736 | tf_op jit(solution)/shard_map/ppermute | solution.py:13
  116.6 13.4 %collective-permute-start.9 = (bf16[1024,1,256]{0,2,1:T(8,128)(2,1)S(1)}, bf16[1024,1,256]{0,2,1:T(8,128)(2,1)S(1)}, u32[]{:S(2)}, u32[]{:S(2)}) collective-permute-start(bf16[1024,1,256]{0,2,1:T(8,128)(2,1)S(1)} %fusion.46), channel_id=1, source_target_pairs={{0,2},{1,3},{2,0},{3,1},{4,6},{5,7},{6,4},{7,5},{8,10},{9,11},{10,... | collective-permute-start | bytes 1572872 | tf_op jit(solution)/shard_map/ppermute | solution.py:13
  130.3 3.5 %copy-start.1 = (f32[1024,1,256]{0,2,1:T(8,128)}, f32[1024,1,256]{0,2,1:T(8,128)S(1)}, u32[]{:S(2)}) copy-start(f32[1024,1,256]{0,2,1:T(8,128)S(1)} %bitcast_add_fusion) | copy-start | bytes 3145732
  133.7 21.6 %collective-permute-start.10 = (bf16[2,512,256]{2,1,0:T(8,128)(2,1)}, bf16[2,512,256]{2,1,0:T(8,128)(2,1)}, u32[]{:S(2)}, u32[]{:S(2)}) collective-permute-start(bf16[2,512,256]{2,1,0:T(8,128)(2,1)} %bitcast.46), channel_id=1, source_target_pairs={{0,31},{1,30},{2,29},{3,28},{4,27},{5,26},{6,25},{7,24},{8,23},{9,... | collective-permute-start | bytes 1572872 | tf_op jit(solution)/shard_map/ppermute | solution.py:8
  (1 other events, 0.8 us)

commit v14 on v10

--- a/solution.py
+++ b/solution.py
@@ -60,6 +60,14 @@
     return cur[:, 0]
 
 
+def flip_rows(values):
+    batch, rows, _ = values.shape
+    turn = jnp.broadcast_to(reversal(rows, rows), (batch, rows, rows))
+    return lax.dot_general(
+        turn, values, (((2,), (1,)), ((0,), (0,))), preferred_element_type=jnp.float32
+    ).astype(jnp.bfloat16)
+
+
 def reversal(n, block):
     rows = lax.broadcasted_iota(jnp.int32, (n, n), 0)
     cols = lax.broadcasted_iota(jnp.int32, (n, n), 1)
@@ -115,9 +123,7 @@
     rows_fwd = conv[0].reshape(-1, local_width)
     rows_all = rows_fwd.shape[0]
     rows_rev = mirror(
-        jnp.dot(
-            reversal(rows_all, length), conv[1].reshape(rows_all, -1), preferred_element_type=jnp.float32
-        ).astype(jnp.bfloat16),
+        flip_rows(conv[1]).reshape(rows_all, -1),
         "seq",
         seq_count,
     )
@@ -142,10 +148,9 @@
     )
     share = scatter_blocks(part.reshape(part.shape[0], ch_count, local_width), ch_bits, me)
     out_forward = x_fwd + share.reshape(x_fwd.shape)
-    row_flip = reversal(share.shape[0], x_fwd.shape[1])
     turned = jnp.dot(share.astype(jnp.bfloat16), lane_flip, preferred_element_type=jnp.float32)
-    turned = jnp.dot(row_flip, turned.astype(jnp.bfloat16), preferred_element_type=jnp.float32)
-    sent = mirror(turned.astype(jnp.bfloat16).reshape(x_fwd.shape), ("seq", "ch"), seq_count * ch_count)
+    turned = flip_rows(turned.astype(jnp.bfloat16).reshape(x_fwd.shape))
+    sent = mirror(turned, ("seq", "ch"), seq_count * ch_count)
     out_reverse = x_rev + sent.astype(jnp.float32)
     return (out_forward.astype(jnp.bfloat16), out_reverse.astype(jnp.bfloat16))
 

time: 157 us -> 155 us (0.987)
  matrix products: 36.2 us -> 33.6 us
    dot_general x2, matrix products: 5.66 us -> 2.47 us  [flip_rows(): lax.dot_general(turn, values, (((2,), (1,)), ((0,), (0,))), preferred_ele...]
  transfers between devices with their start and end apart: 11 -> 11, of which waited for: 6 -> 6; matrix products, arithmetic and copies ran while one was open for 16% -> 17% of each run, Pallas kernels for 0% -> 0%
where the time goes in v14:
time: 155 us; the launch traced here: 154 us
  waiting for transfers between devices  55.1 us (36%)
  matrix products  33.6 us (22%)
  other arithmetic  29.7 us (19%)
  starting transfers between devices  21.9 us (14%)
  local copies, waits for them, and re-layouts  6.57 us (4%)
  blocking collectives  6.16 us (4%)
    ppermute x3, waiting for transfers between devices, mirror(): return lax.ppermute(value, axes, [(k, count - 1 - k) for k in range(count)])  32.4 us
    ppermute x6, waiting for transfers between devices, partner(): lax.ppermute(value, axis, [(k, k ^ mask) for k in range(lax.axis_size(axi...  19.8 us
    dot_general x1, matrix products, local(): jnp.dot(act_fwd, w_out, preferred_element_type=jnp.float32)  12 us
    ppermute x6, starting transfers between devices, partner(): lax.ppermute(value, axis, [(k, k ^ mask) for k in range(lax.axis_size(axi...  11.2 us
    dot_general x2, matrix products, activation(): lax.dot_general(pieces, w_gate.reshape(ch_count, local_width, -1), dims,...  6.67 us
    psum x1, blocking collectives, local(): lax.psum((jnp.sum(x_fwd * x_fwd, axis=-1), jnp.sum(x_rev * x_rev, axis=-1...  6.16 us
    another operation x6, other arithmetic, gather_blocks(): cur = jnp.stack([first, second], axis=1).reshape((-1,) + block.shape)  5.8 us
    convert_element_type x2, other arithmetic, local(): return (out_forward.astype(jnp.bfloat16), out_reverse.astype(jnp.bfloat16))  5.75 us
  transfers between devices with their start and end apart: 11, of which 6 were waited for; matrix products, arithmetic and copies ran while one was open for 17% of the time, Pallas kernels for 0%

profile of v14, /device:TPU:17, one launch (start us, length us, event | category | flops | bytes accessed | tf_op | source)
XLA Modules:
  0.0 154.2 jit_solution(2093343575033443749)
XLA Ops:
  6.0 3.6 %multiply_reduce_fusion.1 = (f32[2,512]{1,0:T(2,128)S(1)}, f32[2,512,256]{2,1,0:T(8,128)S(1)}) fusion(f32[256]{0:T(256)S(1)} %bitcast.171, pred[2,512]{1,0:T(4,128)(4,1)S(1)} %get-tuple-element.28, f32[256]{0:T(256)S(1)} %bitcast.168, pred[2,512]{1,0:T(4,128)(4,1)S(1)} %get-tuple-element.26, f32[256]{0:T(256)S(1)} %bitcast.165, ...), kind=kLoop, calls=%fused_computation.77 | loop fusion | flops 6290432 | bytes 2116608 | tf_op jit(solution)/shard_map/reduce_sum | solution.py:108
  9.8 6.2 %all-reduce = (f32[2,512]{1,0:T(2,128)S(1)}, f32[2,512]{1,0:T(2,128)S(1)}) all-reduce(f32[2,512]{1,0:T(2,128)S(1)} %multiply_reduce_fusion, f32[2,512]{1,0:T(2,128)S(1)} %get-tuple-element.23), channel_id=1, replica_groups=mesh['seq'=8,'ch'=4] {'ch'}, use_global_device_ids=true, to_apply=%region_3.4 | all-reduce | flops 2048 | bytes 16384 | tf_op jit(solution)/shard_map/psum | solution.py:107
  16.0 2.8 %fusion.44 = (bf16[1,2,512,256]{3,2,1,0:T(8,128)(2,1)S(1)}, bf16[1,2,512,256]{3,2,1,0:T(8,128)(2,1)S(1)}) fusion(f32[256]{0:T(256)S(1)} %copy-done.13, f32[2,512]{1,0:T(2,128)S(1)} %get-tuple-element.42, f32[256]{0:T(256)S(1)} %bitcast.172, pred[2,512]{1,0:T(4,128)(4,1)S(1)} %get-tuple-element.28, f32[256]{0:T(256)S(1)} %bitcast.169, ...), kind=kLoop, calls=%fused_computation.81 | loop fusion | flops 4456448 | bytes 2640896 | tf_op jit(solution)/shard_map/stack | solution.py:116
  18.9 3.1 %collective-permute-start.2 = (bf16[2,2,3,256]{3,2,1,0:T(4,128)(2,1)S(1)}, bf16[2,2,3,256]{3,2,1,0:T(4,128)(2,1)S(1)}, u32[]{:S(2)}, u32[]{:S(2)}) collective-permute-start(bf16[2,2,3,256]{3,2,1,0:T(4,128)(2,1)S(1)} %get-tuple-element.15), channel_id=1, source_target_pairs={{4,0},{8,4},{12,8},{16,12},{20,16},{24,20},{28,24},{5,1},{9,5},{13... | collective-permute-start | bytes 18440 | tf_op jit(solution)/shard_map/ppermute | solution.py:25
  21.9 2.2 %collective-permute-start.1 = (bf16[2,2,3,256]{3,2,1,0:T(4,128)(2,1)S(1)}, bf16[2,2,3,256]{3,2,1,0:T(4,128)(2,1)S(1)}, u32[]{:S(2)}, u32[]{:S(2)}) collective-permute-start(bf16[2,2,3,256]{3,2,1,0:T(4,128)(2,1)S(1)} %get-tuple-element.14), channel_id=1, source_target_pairs={{0,4},{4,8},{8,12},{12,16},{16,20},{20,24},{24,28},{1,5},{5,9},{9,... | collective-permute-start | bytes 18440 | tf_op jit(solution)/shard_map/ppermute | solution.py:23
  24.2 3.0 %collective-permute-done.1 = bf16[2,2,3,256]{3,2,1,0:T(4,128)(2,1)S(1)} collective-permute-done((bf16[2,2,3,256]{3,2,1,0:T(4,128)(2,1)S(1)}, bf16[2,2,3,256]{3,2,1,0:T(4,128)(2,1)S(1)}, u32[]{:S(2)}, u32[]{:S(2)}) %collective-permute-start.1) | collective-permute-done | bytes 6176 | tf_op jit(solution)/shard_map/ppermute | solution.py:23
  27.5 2.1 %fusion.13 = bf16[2,2,512,256]{3,2,1,0:T(8,128)(2,1)S(1)} fusion(f32[2,2,518,256]{3,2,1,0:T(8,128)S(1)} %maximum_convert_fusion, f32[256]{0:T(256)S(1)} %bitcast.179, f32[256]{0:T(256)S(1)} %bitcast.180, f32[256]{0:T(256)S(1)} %bitcast.175, f32[256]{0:T(256)S(1)} %bitcast.176, f32[256]{0:T(256)S(1)} %bitcast.177, f32[256]{0:T(256)S(1)} %bitcast.178, ...), kind=kLoop, calls=%fused_computation.21 | loop fusion | flops 7864320 | bytes 15736832 | tf_op jit(solution)/shard_map/convert_element_type | solution.py:122
  33.9 20.6 %collective-permute-done.5 = bf16[1024,256]{1,0:T(8,128)(2,1)} collective-permute-done((bf16[1024,256]{1,0:T(8,128)(2,1)}, bf16[1024,256]{1,0:T(8,128)(2,1)}, u32[]{:S(2)}, u32[]{:S(2)}) %collective-permute-start.5) | collective-permute-done | bytes 524320 | tf_op jit(solution)/shard_map/ppermute | solution.py:8
  58.2 3.4 %collective-permute-start.4 = (bf16[2,1024,256]{2,1,0:T(8,128)(2,1)}, bf16[2,1024,256]{2,1,0:T(8,128)(2,1)}, u32[]{:S(2)}, u32[]{:S(2)}) collective-permute-start(bf16[2,1024,256]{2,1,0:T(8,128)(2,1)} %maximum_bitcast_fusion), channel_id=1, source_target_pairs={{0,1},{1,0},{2,3},{3,2},{4,5},{5,4},{6,7},{7,6},{8,9},{9,8},{10,11... | collective-permute-start | bytes 3145736 | tf_op jit(solution)/shard_map/ppermute | solution.py:13
  61.6 3.5 %collective-permute-done.6 = bf16[1,1024,256]{2,1,0:T(8,128)(2,1)S(1)} collective-permute-done((bf16[1,1024,256]{2,1,0:T(8,128)(2,1)}, bf16[1,1024,256]{2,1,0:T(8,128)(2,1)S(1)}, u32[]{:S(2)}, u32[]{:S(2)}) %collective-permute-start.6) | collective-permute-done | bytes 524320 | tf_op jit(solution)/shard_map/ppermute | solution.py:13
  68.2 3.9 %collective-permute-start.7 = (bf16[2,1024,256]{2,1,0:T(8,128)(2,1)}, bf16[2,1024,256]{2,1,0:T(8,128)(2,1)}, u32[]{:S(2)}, u32[]{:S(2)}) collective-permute-start(bf16[2,1024,256]{2,1,0:T(8,128)(2,1)} %maximum_bitcast_fusion.1), channel_id=1, source_target_pairs={{0,1},{1,0},{2,3},{3,2},{4,5},{5,4},{6,7},{7,6},{8,9},{9,8},{10,11... | collective-permute-start | bytes 3145736 | tf_op jit(solution)/shard_map/ppermute | solution.py:13
  72.1 4.6 %fusion.109 = bf16[1024,1024]{1,0:T(8,128)(2,1)} fusion(bf16[1024,1024]{1,0:T(8,128)(2,1)S(1)} %copy-done.16, s32[1024]{0:T(1024)S(1)} %get-tuple-element.50, s32[1024]{0:T(1024)S(1)} %get-tuple-element.51, s32[1024]{0:T(1024)S(1)} %get-tuple-element.49, s32[1024]{0:T(1024)S(1)} %get-tuple-element.52, pred[1024]{0:T(1024)(128)(4,1)S(1)} %get-tuple-element.53, ...), kind=kOutput, calls=%fused_computation.42.clone.1 | convolution fusion | flops 2157969408 | bytes 4212736 | tf_op jit(solution)/shard_map/dot_general | solution.py:145
  78.6 4.3 %fusion.86 = f32[1024,1024,1]{1,0,2:T(8,128)} fusion(bf16[4,1024,256]{2,1,0:T(8,128)(2,1)S(1)} %bitcast.154, bf16[4,256,1024]{2,1,0:T(8,128)(2,1)S(1)} %bitcast.149), kind=kOutput, calls=%fused_computation.159 | convolution fusion | flops 2147483648 | bytes 8388608 | tf_op jit(solution)/shard_map/dot_general | solution.py:134
  84.7 2.3 %fusion.87 = f32[1024,1024,1]{1,0,2:T(8,128)S(1)} fusion(bf16[4,1024,256]{2,1,0:T(8,128)(2,1)S(1)} %bitcast.156, bf16[4,256,1024]{2,1,0:T(8,128)(2,1)S(1)} %bitcast.150), kind=kOutput, calls=%fused_computation.160 | convolution fusion | flops 2147483648 | bytes 8388608 | tf_op jit(solution)/shard_map/dot_general | solution.py:134
  87.1 2.7 %fusion = bf16[1024,1024]{1,0:T(8,128)(2,1)S(1)} fusion(f32[1024,1024,1]{1,0,2:T(8,128)S(1)} %fusion.87, bf16[4,1024,256]{2,1,0:T(8,128)(2,1)S(1)} %bitcast.157, bf16[4,256,1024]{2,1,0:T(8,128)(2,1)S(1)} %bitcast.182), kind=kOutput, calls=%fused_computation.1 | convolution fusion | flops 2153775104 | bytes 10485760 | tf_op jit(solution)/shard_map/dot_general | solution.py:137
  89.8 4.6 %fusion.23 = f32[1024,1024]{0,1:T(8,128)} fusion(bf16[1024,1024]{1,0:T(8,128)(2,1)S(1)} %fusion, bf16[1024,1024]{1,0:T(8,128)(2,1)S(1)} %copy-done.17), kind=kOutput, calls=%fused_computation.41 | convolution fusion | flops 2147483648 | bytes 8388608 | tf_op jit(solution)/shard_map/dot_general | solution.py:146
  94.4 12.0 %convolution_add_fusion = f32[1024,1024]{0,1:T(8,128)} fusion(f32[1024,1024]{0,1:T(8,128)} %fusion.23, bf16[1024,1024]{1,0:T(8,128)(2,1)} %param.21, f32[1024,1024,1]{1,0,2:T(8,128)} %fusion.86, bf16[4,1024,256]{2,1,0:T(8,128)(2,1)} %bitcast.155, bf16[4,256,1024]{2,1,0:T(8,128)(2,1)} %bitcast.181), kind=kOutput, calls=%fused_computation.56 | convolution fusion | flops 4302307328 | bytes 18874368 | tf_op jit(solution)/shard_map/dot_general | solution.py:146
  106.4 2.8 %select_bitcast_fusion = f32[1024,2,256]{0,2,1:T(8,128)S(1)} fusion(f32[1024,2,2,256]{0,3,2,1:T(8,128)} %bitcast.151, pred[]{:T(512)S(6)} %eq.102), kind=kLoop, calls=%fused_computation.40 | loop fusion | flops 524288 | bytes 6291457 | tf_op jit(solution)/shard_map/jit(_where)/select_n | solution.py:56
  109.2 4.1 %collective-permute-done.8 = f32[1024,2,256]{0,2,1:T(8,128)S(1)} collective-permute-done((f32[1024,2,256]{0,2,1:T(8,128)S(1)}, f32[1024,2,256]{0,2,1:T(8,128)S(1)}, u32[]{:S(2)}, u32[]{:S(2)}) %collective-permute-start.8) | collective-permute-done | bytes 2097184 | tf_op jit(solution)/shard_map/ppermute | solution.py:13
  115.7 12.1 %collective-permute-done.9 = bf16[1024,1,256]{0,2,1:T(8,128)(2,1)S(1)} collective-permute-done((bf16[1024,1,256]{0,2,1:T(8,128)(2,1)S(1)}, bf16[1024,1,256]{0,2,1:T(8,128)(2,1)S(1)}, u32[]{:S(2)}, u32[]{:S(2)}) %collective-permute-start.9) | collective-permute-done | bytes 524320 | tf_op jit(solution)/shard_map/ppermute | solution.py:13
  130.8 3.4 %collective-permute-start.10 = (bf16[2,512,256]{2,1,0:T(8,128)(2,1)}, bf16[2,512,256]{2,1,0:T(8,128)(2,1)}, u32[]{:S(2)}, u32[]{:S(2)}) collective-permute-start(bf16[2,512,256]{2,1,0:T(8,128)(2,1)} %convolution_convert_fusion), channel_id=1, source_target_pairs={{0,31},{1,30},{2,29},{3,28},{4,27},{5,26},{6,25},{7,24},{8,23},{9,... | collective-permute-start | bytes 1572872 | tf_op jit(solution)/shard_map/ppermute | solution.py:8
  134.2 2.5 %copy.19 = f32[1024,1,256]{2,0,1:T(8,128)} copy(f32[1024,1,256]{0,2,1:T(8,128)} %copy-done.2) | data formatting | bytes 2097152 | tf_op jit(solution)/shard_map/add | solution.py:59
  136.7 3.8 %add_convert_fusion.1 = bf16[2,512,256]{2,1,0:T(8,128)(2,1)} fusion(f32[2,512,256]{2,1,0:T(8,128)} %bitcast.153, f32[256]{0:T(256)S(1)} %bitcast.173, pred[2,512]{1,0:T(4,128)(4,1)S(1)} %get-tuple-element.28, f32[256]{0:T(256)S(1)} %bitcast.170, pred[2,512]{1,0:T(4,128)(4,1)S(1)} %get-tuple-element.26, f32[256]{0:T(256)S(1)} %bitcast.167, ...), kind=kLoop, calls=%fused_computation.65 | loop fusion | flops 3407872 | bytes 2107392 | tf_op jit(solution)/shard_map/convert_element_type | solution.py:155
  140.5 11.8 %collective-permute-done.10 = bf16[2,512,256]{2,1,0:T(8,128)(2,1)} collective-permute-done((bf16[2,512,256]{2,1,0:T(8,128)(2,1)}, bf16[2,512,256]{2,1,0:T(8,128)(2,1)}, u32[]{:S(2)}, u32[]{:S(2)}) %collective-permute-start.10) | collective-permute-done | bytes 524320 | tf_op jit(solution)/shard_map/ppermute | solution.py:8
  (85 shorter events, 27.9 us)
Async XLA Ops:
  0.6 78.0 %copy-start = (bf16[1024,1024]{1,0:T(8,128)(2,1)S(1)}, bf16[1024,1024]{1,0:T(8,128)(2,1)}, u32[]{:S(2)}) copy-start(bf16[1024,1024]{1,0:T(8,128)(2,1)} %param.19) | copy-start | bytes 6291460
  0.6 15.3 %copy-start.13 = (f32[256]{0:T(256)S(1)}, f32[256]{0:T(256)}, u32[]{:S(2)}) copy-start(f32[256]{0:T(256)} %param.18) | copy-start | bytes 3076
  1.5 4.1 %collective-permute-start = (s32[2,512]{1,0:T(2,128)S(1)}, s32[2,512]{1,0:T(2,128)S(1)}, u32[]{:S(2)}, u32[]{:S(2)}) collective-permute-start(s32[2,512]{1,0:T(2,128)S(1)} %subtract_select_fusion), channel_id=1, source_target_pairs={{0,28},{4,24},{8,20},{12,16},{16,12},{20,8},{24,4},{28,0},{1,29},{... | collective-permute-start | bytes 12296 | tf_op jit(solution)/shard_map/ppermute | solution.py:8
  9.8 14.4 %copy-start.12 = (f32[7,256]{1,0:T(8,128)S(1)}, f32[7,256]{1,0:T(8,128)}, u32[]{:S(2)}) copy-start(f32[7,256]{1,0:T(8,128)} %param.16) | copy-start | bytes 21508
  18.8 8.6 %copy-start.14 = (f32[256]{0:T(256)S(1)}, f32[256]{0:T(256)}, u32[]{:S(2)}) copy-start(f32[256]{0:T(256)} %param.17) | copy-start | bytes 3076
  18.9 5.3 %collective-permute-start.2 = (bf16[2,2,3,256]{3,2,1,0:T(4,128)(2,1)S(1)}, bf16[2,2,3,256]{3,2,1,0:T(4,128)(2,1)S(1)}, u32[]{:S(2)}, u32[]{:S(2)}) collective-permute-start(bf16[2,2,3,256]{3,2,1,0:T(4,128)(2,1)S(1)} %get-tuple-element.15), channel_id=1, source_target_pairs={{4,0},{8,4},{12,8},{16,12},{20,16},{24,20},{28,24},{5,1},{9,5},{13... | collective-permute-start | bytes 18440 | tf_op jit(solution)/shard_map/ppermute | solution.py:25
  21.9 5.3 %collective-permute-start.1 = (bf16[2,2,3,256]{3,2,1,0:T(4,128)(2,1)S(1)}, bf16[2,2,3,256]{3,2,1,0:T(4,128)(2,1)S(1)}, u32[]{:S(2)}, u32[]{:S(2)}) collective-permute-start(bf16[2,2,3,256]{3,2,1,0:T(4,128)(2,1)S(1)} %get-tuple-element.14), channel_id=1, source_target_pairs={{0,4},{4,8},{8,12},{12,16},{16,20},{20,24},{24,28},{1,5},{5,9},{9,... | collective-permute-start | bytes 18440 | tf_op jit(solution)/shard_map/ppermute | solution.py:23
  30.8 23.7 %collective-permute-start.5 = (bf16[1024,256]{1,0:T(8,128)(2,1)}, bf16[1024,256]{1,0:T(8,128)(2,1)}, u32[]{:S(2)}, u32[]{:S(2)}) collective-permute-start(bf16[1024,256]{1,0:T(8,128)(2,1)} %bitcast.27), channel_id=1, source_target_pairs={{0,28},{4,24},{8,20},{12,16},{16,12},{20,8},{24,4},{28,0},{1,29},{... | collective-permute-start | bytes 1572872 | tf_op jit(solution)/shard_map/ppermute | solution.py:8
  32.6 23.1 %collective-permute-start.3 = (bf16[1,1024,256]{2,1,0:T(8,128)(2,1)}, bf16[1,1024,256]{2,1,0:T(8,128)(2,1)}, u32[]{:S(2)}, u32[]{:S(2)}) collective-permute-start(bf16[1,1024,256]{2,1,0:T(8,128)(2,1)} %bitcast.14), channel_id=1, source_target_pairs={{0,2},{1,3},{2,0},{3,1},{4,6},{5,7},{6,4},{7,5},{8,10},{9,11},{10,... | collective-permute-start | bytes 1572872 | tf_op jit(solution)/shard_map/ppermute | solution.py:13
  54.5 10.6 %collective-permute-start.6 = (bf16[1,1024,256]{2,1,0:T(8,128)(2,1)}, bf16[1,1024,256]{2,1,0:T(8,128)(2,1)S(1)}, u32[]{:S(2)}, u32[]{:S(2)}) collective-permute-start(bf16[1,1024,256]{2,1,0:T(8,128)(2,1)} %bitcast.28), channel_id=1, source_target_pairs={{0,2},{1,3},{2,0},{3,1},{4,6},{5,7},{6,4},{7,5},{8,10},{9,11},{10,... | collective-permute-start | bytes 1572872 | tf_op jit(solution)/shard_map/ppermute | solution.py:13
  57.0 4.5 %copy-start.7 = (bf16[1,1,1024,256]{3,2,1,0:T(8,128)(2,1)}, bf16[1,1,1024,256]{3,2,1,0:T(8,128)(2,1)S(1)}, u32[]{:S(2)}) copy-start(bf16[1,1,1024,256]{3,2,1,0:T(8,128)(2,1)S(1)} %get-tuple-element.10) | copy-start | bytes 1572868
  57.0 4.5 %copy-start.8 = (bf16[1,1,1024,256]{3,2,1,0:T(8,128)(2,1)}, bf16[1,1,1024,256]{3,2,1,0:T(8,128)(2,1)S(1)}, u32[]{:S(2)}) copy-start(bf16[1,1,1024,256]{3,2,1,0:T(8,128)(2,1)S(1)} %get-tuple-element.11) | copy-start | bytes 1572868
  58.2 13.9 %copy-start.16 = (bf16[1024,1024]{1,0:T(8,128)(2,1)S(1)}, bf16[1024,1024]{1,0:T(8,128)(2,1)}, u32[]{:S(2)}) copy-start(bf16[1024,1024]{1,0:T(8,128)(2,1)} %param.21) | copy-start | bytes 6291460
  58.2 18.5 %collective-permute-start.4 = (bf16[2,1024,256]{2,1,0:T(8,128)(2,1)}, bf16[2,1024,256]{2,1,0:T(8,128)(2,1)}, u32[]{:S(2)}, u32[]{:S(2)}) collective-permute-start(bf16[2,1024,256]{2,1,0:T(8,128)(2,1)} %maximum_bitcast_fusion), channel_id=1, source_target_pairs={{0,1},{1,0},{2,3},{3,2},{4,5},{5,4},{6,7},{7,6},{8,9},{9,8},{10,11... | collective-permute-start | bytes 3145736 | tf_op jit(solution)/shard_map/ppermute | solution.py:13
  68.2 14.8 %collective-permute-start.7 = (bf16[2,1024,256]{2,1,0:T(8,128)(2,1)}, bf16[2,1024,256]{2,1,0:T(8,128)(2,1)}, u32[]{:S(2)}, u32[]{:S(2)}) collective-permute-start(bf16[2,1024,256]{2,1,0:T(8,128)(2,1)} %maximum_bitcast_fusion.1), channel_id=1, source_target_pairs={{0,1},{1,0},{2,3},{3,2},{4,5},{5,4},{6,7},{7,6},{8,9},{9,8},{10,11... | collective-permute-start | bytes 3145736 | tf_op jit(solution)/shard_map/ppermute | solution.py:13
  78.6 4.4 %copy-start.9 = (bf16[2,2,1024,256]{3,2,1,0:T(8,128)(2,1)}, bf16[2,2,1024,256]{3,2,1,0:T(8,128)(2,1)S(1)}, u32[]{:S(2)}) copy-start(bf16[2,2,1024,256]{3,2,1,0:T(8,128)(2,1)S(1)} %pad_maximum_fusion) | copy-start | bytes 6291460
  78.6 4.4 %copy-start.4 = (bf16[1,1,1024,256]{3,2,1,0:T(8,128)(2,1)S(1)}, bf16[1,1,1024,256]{3,2,1,0:T(8,128)(2,1)}, u32[]{:S(2)}) copy-start(bf16[1,1,1024,256]{3,2,1,0:T(8,128)(2,1)} %copy-done.3) | copy-start | bytes 1572868
  78.6 4.4 %copy-start.6 = (bf16[1,1,1024,256]{3,2,1,0:T(8,128)(2,1)S(1)}, bf16[1,1,1024,256]{3,2,1,0:T(8,128)(2,1)}, u32[]{:S(2)}) copy-start(bf16[1,1,1024,256]{3,2,1,0:T(8,128)(2,1)} %copy-done.5) | copy-start | bytes 1572868
  87.1 2.7 %copy-start.17 = (bf16[1024,1024]{1,0:T(8,128)(2,1)S(1)}, bf16[1024,1024]{1,0:T(8,128)(2,1)}, u32[]{:S(2)}) copy-start(bf16[1024,1024]{1,0:T(8,128)(2,1)} %fusion.109) | copy-start | bytes 6291460
  106.4 7.0 %copy-start.1 = (f32[1024,1024]{0,1:T(8,128)S(1)}, f32[1024,1024]{0,1:T(8,128)}, u32[]{:S(2)}) copy-start(f32[1024,1024]{0,1:T(8,128)} %convolution_add_fusion) | copy-start | bytes 12582916
  109.1 4.2 %collective-permute-start.8 = (f32[1024,2,256]{0,2,1:T(8,128)S(1)}, f32[1024,2,256]{0,2,1:T(8,128)S(1)}, u32[]{:S(2)}, u32[]{:S(2)}) collective-permute-start(f32[1024,2,256]{0,2,1:T(8,128)S(1)} %select_bitcast_fusion), channel_id=1, source_target_pairs={{0,1},{1,0},{2,3},{3,2},{4,5},{5,4},{6,7},{7,6},{8,9},{9,8},{10,11... | collective-permute-start | bytes 6291464 | tf_op jit(solution)/shard_map/ppermute | solution.py:13
  114.3 13.4 %collective-permute-start.9 = (bf16[1024,1,256]{0,2,1:T(8,128)(2,1)S(1)}, bf16[1024,1,256]{0,2,1:T(8,128)(2,1)S(1)}, u32[]{:S(2)}, u32[]{:S(2)}) collective-permute-start(bf16[1024,1,256]{0,2,1:T(8,128)(2,1)S(1)} %fusion.46), channel_id=1, source_target_pairs={{0,2},{1,3},{2,0},{3,1},{4,6},{5,7},{6,4},{7,5},{8,10},{9,11},{10,... | collective-permute-start | bytes 1572872 | tf_op jit(solution)/shard_map/ppermute | solution.py:13
  115.7 13.9 %copy-start.11 = (bf16[512,512]{1,0:T(8,128)(2,1)S(1)}, bf16[512,512]{1,0:T(8,128)(2,1)}, u32[]{:S(2)}) copy-start(bf16[512,512]{1,0:T(8,128)(2,1)} %fusion.43) | copy-start | bytes 1572868
  130.8 21.4 %collective-permute-start.10 = (bf16[2,512,256]{2,1,0:T(8,128)(2,1)}, bf16[2,512,256]{2,1,0:T(8,128)(2,1)}, u32[]{:S(2)}, u32[]{:S(2)}) collective-permute-start(bf16[2,512,256]{2,1,0:T(8,128)(2,1)} %convolution_convert_fusion), channel_id=1, source_target_pairs={{0,31},{1,30},{2,29},{3,28},{4,27},{5,26},{6,25},{7,24},{8,23},{9,... | collective-permute-start | bytes 1572872 | tf_op jit(solution)/shard_map/ppermute | solution.py:8
  (5 other events, 8.1 us)

commit v15 on v14

--- a/solution.py
+++ b/solution.py
@@ -142,7 +142,15 @@
     act_fwd = activation(rows_fwd)
     act_rev = activation(rows_rev)
     lane_flip = reversal(local_width, local_width)
-    w_flip = jnp.dot(w_out, reversal(width, width), preferred_element_type=jnp.float32).astype(jnp.bfloat16)
+    w_flip = jnp.concatenate(
+        [
+            jnp.dot(
+                w_out[:, k * local_width : (k + 1) * local_width], lane_flip, preferred_element_type=jnp.float32
+            ).astype(jnp.bfloat16)
+            for k in reversed(range(ch_count))
+        ],
+        axis=1,
+    )
     part = jnp.dot(act_fwd, w_out, preferred_element_type=jnp.float32) + jnp.dot(
         act_rev, w_flip, preferred_element_type=jnp.float32
     )

time: 155 us -> 161 us (1.039)
  matrix products: 33.6 us -> 44.3 us
  starting transfers between devices: 21.9 us -> 17.2 us
  waiting for transfers between devices: 55.1 us -> 51.4 us
  local copies, waits for them, and re-layouts: 6.57 us -> 9.65 us
    ppermute x3, waiting for transfers between devices: 32.4 us -> 21.8 us  [mirror(): return lax.ppermute(value, axes, [(k, count - 1 - k) for k in range(count)])]
    dot_general x1, matrix products: 4.62 us -> 12 us  [local(): jnp.dot(act_rev, w_flip, preferred_element_type=jnp.float32)]
    ppermute x6, waiting for transfers between devices: 19.8 us -> 26.5 us  [partner(): lax.ppermute(value, axis, [(k, k ^ mask) for k in range(lax.axis_size(axi...]
    ppermute x6, starting transfers between devices: 11.2 us -> 8.44 us  [partner(): lax.ppermute(value, axis, [(k, k ^ mask) for k in range(lax.axis_size(axi...]
    dot_general x2 -> x4, matrix products: 7.29 us -> 9.77 us  [local(): jnp.dot(w_out[:, k * local_width:(k + 1) * local_width], lane_flip, prefe...]
    unnamed x36 -> x30, local copies, waits for them, and re-layouts: 1.83 us -> 3.95 us
    dot_general x2, matrix products: 6.67 us -> 8.75 us  [activation(): lax.dot_general(pieces, w_gate.reshape(ch_count, local_width, -1), dims,...]
    ppermute x3, starting transfers between devices: 5.47 us -> 3.46 us  [mirror(): return lax.ppermute(value, axes, [(k, count - 1 - k) for k in range(count)])]
  transfers between devices with their start and end apart: 11 -> 11, of which waited for: 6 -> 7; matrix products, arithmetic and copies ran while one was open for 17% -> 27% of each run, Pallas kernels for 0% -> 0%
where the time goes in v15:
time: 161 us; the launch traced here: 159 us
  waiting for transfers between devices  51.4 us (32%)
  matrix products  44.3 us (28%)
  other arithmetic  29.7 us (18%)
  starting transfers between devices  17.2 us (11%)
  local copies, waits for them, and re-layouts  9.65 us (6%)
  blocking collectives  6.04 us (4%)
    ppermute x6, waiting for transfers between devices, partner(): lax.ppermute(value, axis, [(k, k ^ mask) for k in range(lax.axis_size(axi...  26.5 us
    ppermute x3, waiting for transfers between devices, mirror(): return lax.ppermute(value, axes, [(k, count - 1 - k) for k in range(count)])  21.8 us
    dot_general x1, matrix products, local(): jnp.dot(act_rev, w_flip, preferred_element_type=jnp.float32)  12 us
    dot_general x1, matrix products, local(): jnp.dot(act_fwd, w_out, preferred_element_type=jnp.float32)  10.7 us
    dot_general x4, matrix products, local(): jnp.dot(w_out[:, k * local_width:(k + 1) * local_width], lane_flip, prefe...  9.77 us
    dot_general x2, matrix products, activation(): lax.dot_general(pieces, w_gate.reshape(ch_count, local_width, -1), dims,...  8.75 us
    ppermute x6, starting transfers between devices, partner(): lax.ppermute(value, axis, [(k, k ^ mask) for k in range(lax.axis_size(axi...  8.44 us
    psum x1, blocking collectives, local(): lax.psum((jnp.sum(x_fwd * x_fwd, axis=-1), jnp.sum(x_rev * x_rev, axis=-1...  6.04 us
  transfers between devices with their start and end apart: 11, of which 7 were waited for; matrix products, arithmetic and copies ran while one was open for 27% of the time, Pallas kernels for 0%

profile of v15, /device:TPU:17, one launch (start us, length us, event | category | flops | bytes accessed | tf_op | source)
XLA Modules:
  0.0 159.3 jit_solution(17913210810170704705)
XLA Ops:
  7.0 3.6 %multiply_reduce_fusion.1 = (f32[2,512]{1,0:T(2,128)S(1)}, f32[2,512,256]{2,1,0:T(8,128)S(1)}) fusion(f32[256]{0:T(256)S(1)} %bitcast.176, pred[2,512]{1,0:T(4,128)(4,1)S(1)} %get-tuple-element.28, f32[256]{0:T(256)S(1)} %bitcast.173, pred[2,512]{1,0:T(4,128)(4,1)S(1)} %get-tuple-element.26, f32[256]{0:T(256)S(1)} %bitcast.170, ...), kind=kLoop, calls=%fused_computation.74 | loop fusion | flops 6290432 | bytes 2116608 | tf_op jit(solution)/shard_map/reduce_sum | solution.py:108
  10.7 6.0 %all-reduce = (f32[2,512]{1,0:T(2,128)S(1)}, f32[2,512]{1,0:T(2,128)S(1)}) all-reduce(f32[2,512]{1,0:T(2,128)S(1)} %multiply_reduce_fusion, f32[2,512]{1,0:T(2,128)S(1)} %get-tuple-element.23), channel_id=1, replica_groups=mesh['seq'=8,'ch'=4] {'ch'}, use_global_device_ids=true, to_apply=%region_3.4 | all-reduce | flops 2048 | bytes 16384 | tf_op jit(solution)/shard_map/psum | solution.py:107
  16.8 2.8 %fusion.37 = (bf16[1,2,512,256]{3,2,1,0:T(8,128)(2,1)S(1)}, bf16[1,2,512,256]{3,2,1,0:T(8,128)(2,1)S(1)}) fusion(f32[256]{0:T(256)S(1)} %copy-done.13, f32[2,512]{1,0:T(2,128)S(1)} %get-tuple-element.42, f32[256]{0:T(256)S(1)} %bitcast.177, pred[2,512]{1,0:T(4,128)(4,1)S(1)} %get-tuple-element.28, f32[256]{0:T(256)S(1)} %bitcast.174, ...), kind=kLoop, calls=%fused_computation.78 | loop fusion | flops 4456448 | bytes 2640896 | tf_op jit(solution)/shard_map/stack | solution.py:116
  19.7 3.2 %collective-permute-start.2 = (bf16[2,2,3,256]{3,2,1,0:T(4,128)(2,1)S(1)}, bf16[2,2,3,256]{3,2,1,0:T(4,128)(2,1)S(1)}, u32[]{:S(2)}, u32[]{:S(2)}) collective-permute-start(bf16[2,2,3,256]{3,2,1,0:T(4,128)(2,1)S(1)} %get-tuple-element.15), channel_id=1, source_target_pairs={{4,0},{8,4},{12,8},{16,12},{20,16},{24,20},{28,24},{5,1},{9,5},{13... | collective-permute-start | bytes 18440 | tf_op jit(solution)/shard_map/ppermute | solution.py:25
  25.0 3.2 %collective-permute-done.1 = bf16[2,2,3,256]{3,2,1,0:T(4,128)(2,1)S(1)} collective-permute-done((bf16[2,2,3,256]{3,2,1,0:T(4,128)(2,1)S(1)}, bf16[2,2,3,256]{3,2,1,0:T(4,128)(2,1)S(1)}, u32[]{:S(2)}, u32[]{:S(2)}) %collective-permute-start.1) | collective-permute-done | bytes 6176 | tf_op jit(solution)/shard_map/ppermute | solution.py:23
  34.8 2.4 %fusion.34 = bf16[1024,256]{0,1:T(8,128)(2,1)} fusion(bf16[1024,1024]{1,0:T(8,128)(2,1)} %param.21, s32[256]{0:T(256)S(1)} %get-tuple-element.44, s32[256]{0:T(256)S(1)} %get-tuple-element.47, s32[256]{0:T(256)S(1)} %get-tuple-element.43, s32[256]{0:T(256)S(1)} %get-tuple-element.48, pred[256]{0:T(512)(128)(4,1)S(1)} %get-tuple-element.45, ...), kind=kOutput, calls=%fused_computation.56 | convolution fusion | flops 135069696 | bytes 1058816 | tf_op jit(solution)/shard_map/dot_general | solution.py:147
  37.3 5.1 %collective-permute-done.3 = bf16[1,1024,256]{2,1,0:T(8,128)(2,1)} collective-permute-done((bf16[1,1024,256]{2,1,0:T(8,128)(2,1)}, bf16[1,1024,256]{2,1,0:T(8,128)(2,1)}, u32[]{:S(2)}, u32[]{:S(2)}) %collective-permute-start.3) | collective-permute-done | bytes 524320 | tf_op jit(solution)/shard_map/ppermute | solution.py:13
  45.5 3.6 %collective-permute-start.4 = (bf16[2,1024,256]{2,1,0:T(8,128)(2,1)}, bf16[2,1024,256]{2,1,0:T(8,128)(2,1)}, u32[]{:S(2)}, u32[]{:S(2)}) collective-permute-start(bf16[2,1024,256]{2,1,0:T(8,128)(2,1)} %maximum_bitcast_fusion), channel_id=1, source_target_pairs={{0,1},{1,0},{2,3},{3,2},{4,5},{5,4},{6,7},{7,6},{8,9},{9,8},{10,11... | collective-permute-start | bytes 3145736 | tf_op jit(solution)/shard_map/ppermute | solution.py:13
  49.1 9.4 %collective-permute-done.5 = bf16[1024,256]{1,0:T(8,128)(2,1)} collective-permute-done((bf16[1024,256]{1,0:T(8,128)(2,1)}, bf16[1024,256]{1,0:T(8,128)(2,1)}, u32[]{:S(2)}, u32[]{:S(2)}) %collective-permute-start.5) | collective-permute-done | bytes 524320 | tf_op jit(solution)/shard_map/ppermute | solution.py:8
  58.7 2.4 %fusion.33 = bf16[1024,256]{0,1:T(8,128)(2,1)} fusion(bf16[1024,1024]{1,0:T(8,128)(2,1)} %param.21, s32[256]{0:T(256)S(1)} %get-tuple-element.44, s32[256]{0:T(256)S(1)} %get-tuple-element.47, s32[256]{0:T(256)S(1)} %get-tuple-element.43, s32[256]{0:T(256)S(1)} %get-tuple-element.48, pred[256]{0:T(512)(128)(4,1)S(1)} %get-tuple-element.45, ...), kind=kOutput, calls=%fused_computation.55 | convolution fusion | flops 135069696 | bytes 1058816 | tf_op jit(solution)/shard_map/dot_general | solution.py:147
  61.1 2.5 %fusion.32 = bf16[1024,256]{0,1:T(8,128)(2,1)} fusion(bf16[1024,1024]{1,0:T(8,128)(2,1)} %param.21, s32[256]{0:T(256)S(1)} %get-tuple-element.44, s32[256]{0:T(256)S(1)} %get-tuple-element.47, s32[256]{0:T(256)S(1)} %get-tuple-element.43, s32[256]{0:T(256)S(1)} %get-tuple-element.48, pred[256]{0:T(512)(128)(4,1)S(1)} %get-tuple-element.45, ...), kind=kOutput, calls=%fused_computation.54 | convolution fusion | flops 135069696 | bytes 1058816 | tf_op jit(solution)/shard_map/dot_general | solution.py:147
  63.6 2.5 %fusion.31 = bf16[1024,256]{0,1:T(8,128)(2,1)} fusion(bf16[1024,1024]{1,0:T(8,128)(2,1)} %param.21, s32[256]{0:T(256)S(1)} %get-tuple-element.44, s32[256]{0:T(256)S(1)} %get-tuple-element.47, s32[256]{0:T(256)S(1)} %get-tuple-element.43, s32[256]{0:T(256)S(1)} %get-tuple-element.48, pred[256]{0:T(512)(128)(4,1)S(1)} %get-tuple-element.45, ...), kind=kOutput, calls=%fused_computation.53 | convolution fusion | flops 135069696 | bytes 1058816 | tf_op jit(solution)/shard_map/dot_general | solution.py:147
  66.1 4.1 %collective-permute-done.6 = bf16[1,1024,256]{2,1,0:T(8,128)(2,1)} collective-permute-done((bf16[1,1024,256]{2,1,0:T(8,128)(2,1)}, bf16[1,1024,256]{2,1,0:T(8,128)(2,1)}, u32[]{:S(2)}, u32[]{:S(2)}) %collective-permute-start.6) | collective-permute-done | bytes 524320 | tf_op jit(solution)/shard_map/ppermute | solution.py:13
  73.4 3.0 %collective-permute-start.7 = (bf16[2,1024,256]{2,1,0:T(8,128)(2,1)}, bf16[2,1024,256]{2,1,0:T(8,128)(2,1)}, u32[]{:S(2)}, u32[]{:S(2)}) collective-permute-start(bf16[2,1024,256]{2,1,0:T(8,128)(2,1)} %maximum_bitcast_fusion.1), channel_id=1, source_target_pairs={{0,1},{1,0},{2,3},{3,2},{4,5},{5,4},{6,7},{7,6},{8,9},{9,8},{10,11... | collective-permute-start | bytes 3145736 | tf_op jit(solution)/shard_map/ppermute | solution.py:13
  77.9 4.4 %fusion.71 = f32[1024,1024,1]{1,0,2:T(8,128)} fusion(bf16[4,1024,256]{2,1,0:T(8,128)(2,1)S(1)} %bitcast.161, bf16[4,256,1024]{2,1,0:T(8,128)(2,1)S(1)} %bitcast.154), kind=kOutput, calls=%fused_computation.141 | convolution fusion | flops 2147483648 | bytes 8388608 | tf_op jit(solution)/shard_map/dot_general | solution.py:134
  82.3 10.7 %fusion.30 = f32[1024,1024]{0,1:T(8,128)} fusion(bf16[1024,1024]{1,0:T(8,128)(2,1)} %param.21, f32[1024,1024,1]{1,0,2:T(8,128)} %fusion.71, bf16[4,1024,256]{2,1,0:T(8,128)(2,1)} %bitcast.162, bf16[4,256,1024]{2,1,0:T(8,128)(2,1)} %bitcast.186), kind=kOutput, calls=%fused_computation.45 | convolution fusion | flops 4301258752 | bytes 14680064 | tf_op jit(solution)/shard_map/dot_general | solution.py:154
  96.4 4.4 %fusion.72 = f32[1024,1024,1]{1,0,2:T(8,128)} fusion(bf16[4,1024,256]{2,1,0:T(8,128)(2,1)S(1)} %bitcast.159, bf16[4,256,1024]{2,1,0:T(8,128)(2,1)S(1)} %bitcast.155), kind=kOutput, calls=%fused_computation.142 | convolution fusion | flops 2147483648 | bytes 8388608 | tf_op jit(solution)/shard_map/dot_general | solution.py:134
  100.8 12.0 %fusion.27 = f32[1024,1024]{0,1:T(8,128)} fusion(f32[1024,1024]{0,1:T(8,128)} %fusion.30, bf16[1024,256]{0,1:T(8,128)(2,1)} %fusion.34, bf16[1024,256]{0,1:T(8,128)(2,1)} %fusion.33, bf16[1024,256]{0,1:T(8,128)(2,1)} %fusion.32, bf16[1024,256]{0,1:T(8,128)(2,1)} %fusion.31, f32[1024,1024,1]{1,0,2:T(8,128)} %fusion.72, bf16[4,1024,256]{2,1,0:T(8,128)(2,1)} %bitcast.160, ...), kind=kOutput, calls=%fused_computation.44 | convolution fusion | flops 4310695936 | bytes 18874368 | tf_op jit(solution)/shard_map/dot_general | solution.py:154
  112.8 2.8 %select_bitcast_fusion = f32[1024,2,256]{0,2,1:T(8,128)S(1)} fusion(f32[1024,2,2,256]{0,3,2,1:T(8,128)} %bitcast.156, pred[]{:T(512)S(6)} %eq.106), kind=kLoop, calls=%fused_computation.43 | loop fusion | flops 524288 | bytes 6291457 | tf_op jit(solution)/shard_map/jit(_where)/select_n | solution.py:56
  115.6 4.1 %collective-permute-done.8 = f32[1024,2,256]{0,2,1:T(8,128)S(1)} collective-permute-done((f32[1024,2,256]{0,2,1:T(8,128)S(1)}, f32[1024,2,256]{0,2,1:T(8,128)S(1)}, u32[]{:S(2)}, u32[]{:S(2)}) %collective-permute-start.8) | collective-permute-done | bytes 2097184 | tf_op jit(solution)/shard_map/ppermute | solution.py:13
  121.1 13.1 %collective-permute-done.9 = bf16[1024,1,256]{0,2,1:T(8,128)(2,1)S(1)} collective-permute-done((bf16[1024,1,256]{0,2,1:T(8,128)(2,1)S(1)}, bf16[1024,1,256]{0,2,1:T(8,128)(2,1)S(1)}, u32[]{:S(2)}, u32[]{:S(2)}) %collective-permute-start.9) | collective-permute-done | bytes 524320 | tf_op jit(solution)/shard_map/ppermute | solution.py:13
  138.6 2.5 %copy.19 = f32[1024,1,256]{2,0,1:T(8,128)} copy(f32[1024,1,256]{0,2,1:T(8,128)} %copy-done.2) | data formatting | bytes 2097152 | tf_op jit(solution)/shard_map/add | solution.py:59
  141.1 3.8 %add_convert_fusion.1 = bf16[2,512,256]{2,1,0:T(8,128)(2,1)} fusion(f32[2,512,256]{2,1,0:T(8,128)} %bitcast.158, f32[256]{0:T(256)S(1)} %bitcast.178, pred[2,512]{1,0:T(4,128)(4,1)S(1)} %get-tuple-element.28, f32[256]{0:T(256)S(1)} %bitcast.175, pred[2,512]{1,0:T(4,128)(4,1)S(1)} %get-tuple-element.26, f32[256]{0:T(256)S(1)} %bitcast.172, ...), kind=kLoop, calls=%fused_computation.62 | loop fusion | flops 3407872 | bytes 2107392 | tf_op jit(solution)/shard_map/convert_element_type | solution.py:163
  144.9 12.4 %collective-permute-done.10 = bf16[2,512,256]{2,1,0:T(8,128)(2,1)} collective-permute-done((bf16[2,512,256]{2,1,0:T(8,128)(2,1)}, bf16[2,512,256]{2,1,0:T(8,128)(2,1)}, u32[]{:S(2)}, u32[]{:S(2)}) %collective-permute-start.10) | collective-permute-done | bytes 524320 | tf_op jit(solution)/shard_map/ppermute | solution.py:8
  (78 shorter events, 34.4 us)
Async XLA Ops:
  0.6 77.3 %copy-start = (bf16[1024,1024]{1,0:T(8,128)(2,1)S(1)}, bf16[1024,1024]{1,0:T(8,128)(2,1)}, u32[]{:S(2)}) copy-start(bf16[1024,1024]{1,0:T(8,128)(2,1)} %param.19) | copy-start | bytes 6291460
  0.6 16.2 %copy-start.13 = (f32[256]{0:T(256)S(1)}, f32[256]{0:T(256)}, u32[]{:S(2)}) copy-start(f32[256]{0:T(256)} %param.18) | copy-start | bytes 3076
  1.5 5.1 %collective-permute-start = (s32[2,512]{1,0:T(2,128)S(1)}, s32[2,512]{1,0:T(2,128)S(1)}, u32[]{:S(2)}, u32[]{:S(2)}) collective-permute-start(s32[2,512]{1,0:T(2,128)S(1)} %subtract_select_fusion), channel_id=1, source_target_pairs={{0,28},{4,24},{8,20},{12,16},{16,12},{20,8},{24,4},{28,0},{1,29},{... | collective-permute-start | bytes 12296 | tf_op jit(solution)/shard_map/ppermute | solution.py:8
  19.7 8.7 %copy-start.14 = (f32[256]{0:T(256)S(1)}, f32[256]{0:T(256)}, u32[]{:S(2)}) copy-start(f32[256]{0:T(256)} %param.17) | copy-start | bytes 3076
  19.7 5.3 %collective-permute-start.2 = (bf16[2,2,3,256]{3,2,1,0:T(4,128)(2,1)S(1)}, bf16[2,2,3,256]{3,2,1,0:T(4,128)(2,1)S(1)}, u32[]{:S(2)}, u32[]{:S(2)}) collective-permute-start(bf16[2,2,3,256]{3,2,1,0:T(4,128)(2,1)S(1)} %get-tuple-element.15), channel_id=1, source_target_pairs={{4,0},{8,4},{12,8},{16,12},{20,16},{24,20},{28,24},{5,1},{9,5},{13... | collective-permute-start | bytes 18440 | tf_op jit(solution)/shard_map/ppermute | solution.py:25
  22.9 5.3 %collective-permute-start.1 = (bf16[2,2,3,256]{3,2,1,0:T(4,128)(2,1)S(1)}, bf16[2,2,3,256]{3,2,1,0:T(4,128)(2,1)S(1)}, u32[]{:S(2)}, u32[]{:S(2)}) collective-permute-start(bf16[2,2,3,256]{3,2,1,0:T(4,128)(2,1)S(1)} %get-tuple-element.14), channel_id=1, source_target_pairs={{0,4},{4,8},{8,12},{12,16},{16,20},{20,24},{24,28},{1,5},{5,9},{9,... | collective-permute-start | bytes 18440 | tf_op jit(solution)/shard_map/ppermute | solution.py:23
  28.4 4.2 %copy-start.11 = (bf16[512,512]{1,0:T(8,128)(2,1)S(1)}, bf16[512,512]{1,0:T(8,128)(2,1)}, u32[]{:S(2)}) copy-start(bf16[512,512]{1,0:T(8,128)(2,1)} %fusion.36) | copy-start | bytes 1572868
  31.3 11.0 %collective-permute-start.3 = (bf16[1,1024,256]{2,1,0:T(8,128)(2,1)}, bf16[1,1024,256]{2,1,0:T(8,128)(2,1)}, u32[]{:S(2)}, u32[]{:S(2)}) collective-permute-start(bf16[1,1024,256]{2,1,0:T(8,128)(2,1)} %bitcast.14), channel_id=1, source_target_pairs={{0,2},{1,3},{2,0},{3,1},{4,6},{5,7},{6,4},{7,5},{8,10},{9,11},{10,... | collective-permute-start | bytes 1572872 | tf_op jit(solution)/shard_map/ppermute | solution.py:13
  33.8 24.7 %collective-permute-start.5 = (bf16[1024,256]{1,0:T(8,128)(2,1)}, bf16[1024,256]{1,0:T(8,128)(2,1)}, u32[]{:S(2)}, u32[]{:S(2)}) collective-permute-start(bf16[1024,256]{1,0:T(8,128)(2,1)} %bitcast.27), channel_id=1, source_target_pairs={{0,28},{4,24},{8,20},{12,16},{16,12},{20,8},{24,4},{28,0},{1,29},{... | collective-permute-start | bytes 1572872 | tf_op jit(solution)/shard_map/ppermute | solution.py:8
  43.6 1.9 %copy-start.5 = (bf16[1,1,1024,256]{3,2,1,0:T(8,128)(2,1)}, bf16[1,1,1024,256]{3,2,1,0:T(8,128)(2,1)S(1)}, u32[]{:S(2)}) copy-start(bf16[1,1,1024,256]{3,2,1,0:T(8,128)(2,1)S(1)} %get-tuple-element.13) | copy-start | bytes 1572868
  45.5 30.9 %collective-permute-start.4 = (bf16[2,1024,256]{2,1,0:T(8,128)(2,1)}, bf16[2,1024,256]{2,1,0:T(8,128)(2,1)}, u32[]{:S(2)}, u32[]{:S(2)}) collective-permute-start(bf16[2,1024,256]{2,1,0:T(8,128)(2,1)} %maximum_bitcast_fusion), channel_id=1, source_target_pairs={{0,1},{1,0},{2,3},{3,2},{4,5},{5,4},{6,7},{7,6},{8,9},{9,8},{10,11... | collective-permute-start | bytes 3145736 | tf_op jit(solution)/shard_map/ppermute | solution.py:13
  58.5 11.7 %collective-permute-start.6 = (bf16[1,1024,256]{2,1,0:T(8,128)(2,1)}, bf16[1,1024,256]{2,1,0:T(8,128)(2,1)}, u32[]{:S(2)}, u32[]{:S(2)}) collective-permute-start(bf16[1,1024,256]{2,1,0:T(8,128)(2,1)} %bitcast.28), channel_id=1, source_target_pairs={{0,2},{1,3},{2,0},{3,1},{4,6},{5,7},{6,4},{7,5},{8,10},{9,11},{10,... | collective-permute-start | bytes 1572872 | tf_op jit(solution)/shard_map/ppermute | solution.py:13
  66.1 10.3 %copy-start.4 = (bf16[1,1,1024,256]{3,2,1,0:T(8,128)(2,1)S(1)}, bf16[1,1,1024,256]{3,2,1,0:T(8,128)(2,1)}, u32[]{:S(2)}) copy-start(bf16[1,1,1024,256]{3,2,1,0:T(8,128)(2,1)} %copy-done.3) | copy-start | bytes 1572868
  66.1 10.3 %copy-start.6 = (bf16[1,1,1024,256]{3,2,1,0:T(8,128)(2,1)S(1)}, bf16[1,1,1024,256]{3,2,1,0:T(8,128)(2,1)}, u32[]{:S(2)}) copy-start(bf16[1,1,1024,256]{3,2,1,0:T(8,128)(2,1)} %copy-done.5) | copy-start | bytes 1572868
  71.5 1.9 %copy-start.8 = (bf16[1,1,1024,256]{3,2,1,0:T(8,128)(2,1)}, bf16[1,1,1024,256]{3,2,1,0:T(8,128)(2,1)S(1)}, u32[]{:S(2)}) copy-start(bf16[1,1,1024,256]{3,2,1,0:T(8,128)(2,1)S(1)} %get-tuple-element.11) | copy-start | bytes 1572868
  73.4 19.7 %collective-permute-start.7 = (bf16[2,1024,256]{2,1,0:T(8,128)(2,1)}, bf16[2,1024,256]{2,1,0:T(8,128)(2,1)}, u32[]{:S(2)}, u32[]{:S(2)}) collective-permute-start(bf16[2,1024,256]{2,1,0:T(8,128)(2,1)} %maximum_bitcast_fusion.1), channel_id=1, source_target_pairs={{0,1},{1,0},{2,3},{3,2},{4,5},{5,4},{6,7},{7,6},{8,9},{9,8},{10,11... | collective-permute-start | bytes 3145736 | tf_op jit(solution)/shard_map/ppermute | solution.py:13
  77.9 4.4 %copy-start.10 = (bf16[2,2,1024,256]{3,2,1,0:T(8,128)(2,1)}, bf16[2,2,1024,256]{3,2,1,0:T(8,128)(2,1)S(1)}, u32[]{:S(2)}) copy-start(bf16[2,2,1024,256]{3,2,1,0:T(8,128)(2,1)S(1)} %pad_maximum_fusion) | copy-start | bytes 6291460
  95.0 1.4 copy-start.9
  112.8 7.0 %copy-start.1 = (f32[1024,1024]{0,1:T(8,128)S(1)}, f32[1024,1024]{0,1:T(8,128)}, u32[]{:S(2)}) copy-start(f32[1024,1024]{0,1:T(8,128)} %fusion.27) | copy-start | bytes 12582916
  115.6 4.2 %collective-permute-start.8 = (f32[1024,2,256]{0,2,1:T(8,128)S(1)}, f32[1024,2,256]{0,2,1:T(8,128)S(1)}, u32[]{:S(2)}, u32[]{:S(2)}) collective-permute-start(f32[1024,2,256]{0,2,1:T(8,128)S(1)} %select_bitcast_fusion), channel_id=1, source_target_pairs={{0,1},{1,0},{2,3},{3,2},{4,5},{5,4},{6,7},{7,6},{8,9},{9,8},{10,11... | collective-permute-start | bytes 6291464 | tf_op jit(solution)/shard_map/ppermute | solution.py:13
  120.8 15.3 %copy-start.12 = (bf16[512,512]{1,0:T(8,128)(2,1)S(1)}, bf16[512,512]{1,0:T(8,128)(2,1)}, u32[]{:S(2)}) copy-start(bf16[512,512]{1,0:T(8,128)(2,1)} %fusion.36) | copy-start | bytes 1572868
  120.8 13.4 %collective-permute-start.9 = (bf16[1024,1,256]{0,2,1:T(8,128)(2,1)S(1)}, bf16[1024,1,256]{0,2,1:T(8,128)(2,1)S(1)}, u32[]{:S(2)}, u32[]{:S(2)}) collective-permute-start(bf16[1024,1,256]{0,2,1:T(8,128)(2,1)S(1)} %fusion.39), channel_id=1, source_target_pairs={{0,2},{1,3},{2,0},{3,1},{4,6},{5,7},{6,4},{7,5},{8,10},{9,11},{10,... | collective-permute-start | bytes 1572872 | tf_op jit(solution)/shard_map/ppermute | solution.py:13
  134.4 1.0 copy-start.2
  137.3 20.1 %collective-permute-start.10 = (bf16[2,512,256]{2,1,0:T(8,128)(2,1)}, bf16[2,512,256]{2,1,0:T(8,128)(2,1)}, u32[]{:S(2)}, u32[]{:S(2)}) collective-permute-start(bf16[2,512,256]{2,1,0:T(8,128)(2,1)} %convolution_convert_fusion.4), channel_id=1, source_target_pairs={{0,31},{1,30},{2,29},{3,28},{4,27},{5,26},{6,25},{7,24},{8,23},{9,... | collective-permute-start | bytes 1572872 | tf_op jit(solution)/shard_map/ppermute | solution.py:8
  (2 other events, 1.6 us)

commit v16 on v14

--- a/solution.py
+++ b/solution.py
@@ -102,7 +102,7 @@
     taps = conv_kernel.shape[0]
     half_width = taps // 2
 
-    x_fwd = hidden_forward.astype(jnp.float32) + embedded(base_in, table)
+    x_fwd = lax.optimization_barrier(hidden_forward.astype(jnp.float32) + embedded(base_in, table))
     x_rev = lax.optimization_barrier(hidden_reverse.astype(jnp.float32) + embedded(comp_back, table))
     square_fwd, square_rev = lax.psum(
         (jnp.sum(x_fwd * x_fwd, axis=-1), jnp.sum(x_rev * x_rev, axis=-1)), "ch"

time: 155 us -> 154 us (level)
  other arithmetic: 29.7 us -> 27.1 us
    reduce_sum x1, other arithmetic: 3.56 us -> 0.21 us  [local(): jnp.sum(x_fwd * x_fwd, axis=-1)]
    add x0 -> x1, other arithmetic: none -> 3.28 us  [local(): hidden_reverse.astype(jnp.float32) + embedded(comp_back, table)]
  transfers between devices with their start and end apart: 11 -> 11, of which waited for: 6 -> 6; matrix products, arithmetic and copies ran while one was open for 17% -> 16% of each run, Pallas kernels for 0% -> 0%
where the time goes in v16:
time: 154 us
  waiting for transfers between devices  56.5 us (37%)
  matrix products  33.6 us (22%)
  other arithmetic  27.1 us (18%)
  starting transfers between devices  21.9 us (14%)
  local copies, waits for them, and re-layouts  7.37 us (5%)
  blocking collectives  6.16 us (4%)
    ppermute x3, waiting for transfers between devices, mirror(): return lax.ppermute(value, axes, [(k, count - 1 - k) for k in range(count)])  33.7 us
    ppermute x6, waiting for transfers between devices, partner(): lax.ppermute(value, axis, [(k, k ^ mask) for k in range(lax.axis_size(axi...  19.7 us
    dot_general x1, matrix products, local(): jnp.dot(act_fwd, w_out, preferred_element_type=jnp.float32)  12 us
    ppermute x6, starting transfers between devices, partner(): lax.ppermute(value, axis, [(k, k ^ mask) for k in range(lax.axis_size(axi...  11.2 us
    dot_general x2, matrix products, activation(): lax.dot_general(pieces, w_gate.reshape(ch_count, local_width, -1), dims,...  6.66 us
    psum x1, blocking collectives, local(): lax.psum((jnp.sum(x_fwd * x_fwd, axis=-1), jnp.sum(x_rev * x_rev, axis=-1...  6.16 us
    another operation x6, other arithmetic, gather_blocks(): cur = jnp.stack([first, second], axis=1).reshape((-1,) + block.shape)  5.8 us
    ppermute x3, starting transfers between devices, mirror(): return lax.ppermute(value, axes, [(k, count - 1 - k) for k in range(count)])  5.47 us
  transfers between devices with their start and end apart: 11, of which 6 were waited for; matrix products, arithmetic and copies ran while one was open for 16% of the time, Pallas kernels for 0%

profile of v16, /device:TPU:17, one launch (start us, length us, event | category | flops | bytes accessed | tf_op | source)
XLA Modules:
  0.0 153.7 jit_solution(11569577933858577655)
XLA Ops:
  6.0 3.3 %add_add_fusion = (f32[2,512,256]{2,1,0:T(8,128)S(1)}, f32[2,512,256]{2,1,0:T(8,128)S(1)}) fusion(bf16[2,512,256]{2,1,0:T(8,128)(2,1)} %param.14, f32[256]{0:T(256)S(1)} %bitcast.170, f32[256]{0:T(256)S(1)} %bitcast.169, f32[256]{0:T(256)S(1)} %bitcast.168, f32[256]{0:T(256)S(1)} %bitcast.167, f32[256]{0:T(256)S(1)} %bitcast.166, ...), kind=kLoop, calls=%fused_computation.75 | loop fusion | flops 5767168 | bytes 3161088 | tf_op jit(solution)/shard_map/add | solution.py:106
  10.5 6.2 %all-reduce = (f32[2,512]{1,0:T(2,128)S(1)}, f32[2,512]{1,0:T(2,128)S(1)}) all-reduce(f32[2,512]{1,0:T(2,128)S(1)} %multiply_reduce_fusion, f32[2,512]{1,0:T(2,128)S(1)} %multiply_reduce_fusion.1), channel_id=1, replica_groups=mesh['seq'=8,'ch'=4] {'ch'}, use_global_device_ids=true, to_apply=%region_3.4 | all-reduce | flops 2048 | bytes 16384 | tf_op jit(solution)/shard_map/psum | solution.py:107
  18.3 3.1 %collective-permute-start.2 = (bf16[2,2,3,256]{3,2,1,0:T(4,128)(2,1)S(1)}, bf16[2,2,3,256]{3,2,1,0:T(4,128)(2,1)S(1)}, u32[]{:S(2)}, u32[]{:S(2)}) collective-permute-start(bf16[2,2,3,256]{3,2,1,0:T(4,128)(2,1)S(1)} %get-tuple-element.15), channel_id=1, source_target_pairs={{4,0},{8,4},{12,8},{16,12},{20,16},{24,20},{28,24},{5,1},{9,5},{13... | collective-permute-start | bytes 18440 | tf_op jit(solution)/shard_map/ppermute | solution.py:25
  21.4 2.2 %collective-permute-start.1 = (bf16[2,2,3,256]{3,2,1,0:T(4,128)(2,1)S(1)}, bf16[2,2,3,256]{3,2,1,0:T(4,128)(2,1)S(1)}, u32[]{:S(2)}, u32[]{:S(2)}) collective-permute-start(bf16[2,2,3,256]{3,2,1,0:T(4,128)(2,1)S(1)} %get-tuple-element.14), channel_id=1, source_target_pairs={{0,4},{4,8},{8,12},{12,16},{16,20},{20,24},{24,28},{1,5},{5,9},{9,... | collective-permute-start | bytes 18440 | tf_op jit(solution)/shard_map/ppermute | solution.py:23
  23.6 3.0 %collective-permute-done.1 = bf16[2,2,3,256]{3,2,1,0:T(4,128)(2,1)S(1)} collective-permute-done((bf16[2,2,3,256]{3,2,1,0:T(4,128)(2,1)S(1)}, bf16[2,2,3,256]{3,2,1,0:T(4,128)(2,1)S(1)}, u32[]{:S(2)}, u32[]{:S(2)}) %collective-permute-start.1) | collective-permute-done | bytes 6176 | tf_op jit(solution)/shard_map/ppermute | solution.py:23
  26.9 2.1 %fusion.13 = bf16[2,2,512,256]{3,2,1,0:T(8,128)(2,1)S(1)} fusion(f32[2,2,518,256]{3,2,1,0:T(8,128)S(1)} %maximum_convert_fusion, f32[256]{0:T(256)S(1)} %bitcast.164, f32[256]{0:T(256)S(1)} %bitcast.165, f32[256]{0:T(256)S(1)} %bitcast.160, f32[256]{0:T(256)S(1)} %bitcast.161, f32[256]{0:T(256)S(1)} %bitcast.162, f32[256]{0:T(256)S(1)} %bitcast.163, ...), kind=kLoop, calls=%fused_computation.21 | loop fusion | flops 7864320 | bytes 15736832 | tf_op jit(solution)/shard_map/convert_element_type | solution.py:122
  33.3 20.6 %collective-permute-done.5 = bf16[1024,256]{1,0:T(8,128)(2,1)} collective-permute-done((bf16[1024,256]{1,0:T(8,128)(2,1)}, bf16[1024,256]{1,0:T(8,128)(2,1)}, u32[]{:S(2)}, u32[]{:S(2)}) %collective-permute-start.5) | collective-permute-done | bytes 524320 | tf_op jit(solution)/shard_map/ppermute | solution.py:8
  57.7 3.4 %collective-permute-start.4 = (bf16[2,1024,256]{2,1,0:T(8,128)(2,1)}, bf16[2,1024,256]{2,1,0:T(8,128)(2,1)}, u32[]{:S(2)}, u32[]{:S(2)}) collective-permute-start(bf16[2,1024,256]{2,1,0:T(8,128)(2,1)} %maximum_bitcast_fusion), channel_id=1, source_target_pairs={{0,1},{1,0},{2,3},{3,2},{4,5},{5,4},{6,7},{7,6},{8,9},{9,8},{10,11... | collective-permute-start | bytes 3145736 | tf_op jit(solution)/shard_map/ppermute | solution.py:13
  61.0 3.5 %collective-permute-done.6 = bf16[1,1024,256]{2,1,0:T(8,128)(2,1)S(1)} collective-permute-done((bf16[1,1024,256]{2,1,0:T(8,128)(2,1)}, bf16[1,1024,256]{2,1,0:T(8,128)(2,1)S(1)}, u32[]{:S(2)}, u32[]{:S(2)}) %collective-permute-start.6) | collective-permute-done | bytes 524320 | tf_op jit(solution)/shard_map/ppermute | solution.py:13
  67.6 3.9 %collective-permute-start.7 = (bf16[2,1024,256]{2,1,0:T(8,128)(2,1)}, bf16[2,1024,256]{2,1,0:T(8,128)(2,1)}, u32[]{:S(2)}, u32[]{:S(2)}) collective-permute-start(bf16[2,1024,256]{2,1,0:T(8,128)(2,1)} %maximum_bitcast_fusion.1), channel_id=1, source_target_pairs={{0,1},{1,0},{2,3},{3,2},{4,5},{5,4},{6,7},{7,6},{8,9},{9,8},{10,11... | collective-permute-start | bytes 3145736 | tf_op jit(solution)/shard_map/ppermute | solution.py:13
  71.6 4.6 %fusion.109 = bf16[1024,1024]{1,0:T(8,128)(2,1)} fusion(bf16[1024,1024]{1,0:T(8,128)(2,1)S(1)} %copy-done.17, s32[1024]{0:T(1024)S(1)} %get-tuple-element.50, s32[1024]{0:T(1024)S(1)} %get-tuple-element.51, s32[1024]{0:T(1024)S(1)} %get-tuple-element.49, s32[1024]{0:T(1024)S(1)} %get-tuple-element.52, pred[1024]{0:T(1024)(128)(4,1)S(1)} %get-tuple-element.53, ...), kind=kOutput, calls=%fused_computation.42.clone.1 | convolution fusion | flops 2157969408 | bytes 4212736 | tf_op jit(solution)/shard_map/dot_general | solution.py:145
  78.1 4.3 %fusion.86 = f32[1024,1024,1]{1,0,2:T(8,128)} fusion(bf16[4,1024,256]{2,1,0:T(8,128)(2,1)S(1)} %bitcast.154, bf16[4,256,1024]{2,1,0:T(8,128)(2,1)S(1)} %bitcast.149), kind=kOutput, calls=%fused_computation.159 | convolution fusion | flops 2147483648 | bytes 8388608 | tf_op jit(solution)/shard_map/dot_general | solution.py:134
  84.2 2.3 %fusion.87 = f32[1024,1024,1]{1,0,2:T(8,128)S(1)} fusion(bf16[4,1024,256]{2,1,0:T(8,128)(2,1)S(1)} %bitcast.156, bf16[4,256,1024]{2,1,0:T(8,128)(2,1)S(1)} %bitcast.150), kind=kOutput, calls=%fused_computation.160 | convolution fusion | flops 2147483648 | bytes 8388608 | tf_op jit(solution)/shard_map/dot_general | solution.py:134
  86.5 2.7 %fusion = bf16[1024,1024]{1,0:T(8,128)(2,1)S(1)} fusion(f32[1024,1024,1]{1,0,2:T(8,128)S(1)} %fusion.87, bf16[4,1024,256]{2,1,0:T(8,128)(2,1)S(1)} %bitcast.157, bf16[4,256,1024]{2,1,0:T(8,128)(2,1)S(1)} %bitcast.172), kind=kOutput, calls=%fused_computation.1 | convolution fusion | flops 2153775104 | bytes 10485760 | tf_op jit(solution)/shard_map/dot_general | solution.py:137
  89.2 4.6 %fusion.23 = f32[1024,1024]{0,1:T(8,128)} fusion(bf16[1024,1024]{1,0:T(8,128)(2,1)S(1)} %fusion, bf16[1024,1024]{1,0:T(8,128)(2,1)S(1)} %copy-done.18), kind=kOutput, calls=%fused_computation.41 | convolution fusion | flops 2147483648 | bytes 8388608 | tf_op jit(solution)/shard_map/dot_general | solution.py:146
  93.8 12.0 %convolution_add_fusion = f32[1024,1024]{0,1:T(8,128)} fusion(f32[1024,1024]{0,1:T(8,128)} %fusion.23, bf16[1024,1024]{1,0:T(8,128)(2,1)} %param.21, f32[1024,1024,1]{1,0,2:T(8,128)} %fusion.86, bf16[4,1024,256]{2,1,0:T(8,128)(2,1)} %bitcast.155, bf16[4,256,1024]{2,1,0:T(8,128)(2,1)} %bitcast.171), kind=kOutput, calls=%fused_computation.56 | convolution fusion | flops 4302307328 | bytes 18874368 | tf_op jit(solution)/shard_map/dot_general | solution.py:146
  105.8 2.8 %select_bitcast_fusion = f32[1024,2,256]{0,2,1:T(8,128)S(1)} fusion(f32[1024,2,2,256]{0,3,2,1:T(8,128)} %bitcast.151, pred[]{:T(512)S(6)} %eq.102), kind=kLoop, calls=%fused_computation.40 | loop fusion | flops 524288 | bytes 6291457 | tf_op jit(solution)/shard_map/jit(_where)/select_n | solution.py:56
  108.7 4.1 %collective-permute-done.8 = f32[1024,2,256]{0,2,1:T(8,128)S(1)} collective-permute-done((f32[1024,2,256]{0,2,1:T(8,128)S(1)}, f32[1024,2,256]{0,2,1:T(8,128)S(1)}, u32[]{:S(2)}, u32[]{:S(2)}) %collective-permute-start.8) | collective-permute-done | bytes 2097184 | tf_op jit(solution)/shard_map/ppermute | solution.py:13
  115.1 12.1 %collective-permute-done.9 = bf16[1024,1,256]{0,2,1:T(8,128)(2,1)S(1)} collective-permute-done((bf16[1024,1,256]{0,2,1:T(8,128)(2,1)S(1)}, bf16[1024,1,256]{0,2,1:T(8,128)(2,1)S(1)}, u32[]{:S(2)}, u32[]{:S(2)}) %collective-permute-start.9) | collective-permute-done | bytes 524320 | tf_op jit(solution)/shard_map/ppermute | solution.py:13
  130.3 3.3 %collective-permute-start.10 = (bf16[2,512,256]{2,1,0:T(8,128)(2,1)}, bf16[2,512,256]{2,1,0:T(8,128)(2,1)}, u32[]{:S(2)}, u32[]{:S(2)}) collective-permute-start(bf16[2,512,256]{2,1,0:T(8,128)(2,1)} %convolution_convert_fusion), channel_id=1, source_target_pairs={{0,31},{1,30},{2,29},{3,28},{4,27},{5,26},{6,25},{7,24},{8,23},{9,... | collective-permute-start | bytes 1572872 | tf_op jit(solution)/shard_map/ppermute | solution.py:8
  133.6 2.5 %copy.19 = f32[1024,1,256]{2,0,1:T(8,128)} copy(f32[1024,1,256]{0,2,1:T(8,128)} %copy-done.3) | data formatting | bytes 2097152 | tf_op jit(solution)/shard_map/add | solution.py:59
  136.2 2.4 %add_convert_fusion.1 = bf16[2,512,256]{2,1,0:T(8,128)(2,1)} fusion(f32[2,512,256]{2,1,0:T(8,128)} %copy-done.2, f32[2,512,256]{2,1,0:T(8,128)} %bitcast.153), kind=kLoop, calls=%fused_computation.65 | loop fusion | flops 524288 | bytes 2621440 | tf_op jit(solution)/shard_map/convert_element_type | solution.py:155
  138.6 13.1 %collective-permute-done.10 = bf16[2,512,256]{2,1,0:T(8,128)(2,1)} collective-permute-done((bf16[2,512,256]{2,1,0:T(8,128)(2,1)}, bf16[2,512,256]{2,1,0:T(8,128)(2,1)}, u32[]{:S(2)}, u32[]{:S(2)}) %collective-permute-start.10) | collective-permute-done | bytes 524320 | tf_op jit(solution)/shard_map/ppermute | solution.py:8
  151.7 1.9 %add_convert_fusion = bf16[2,512,256]{2,1,0:T(8,128)(2,1)} fusion(f32[2,512,256]{2,1,0:T(8,128)S(1)} %get-tuple-element.23, bf16[2,512,256]{2,1,0:T(8,128)(2,1)} %collective-permute-done.10), kind=kLoop, calls=%fused_computation.64 | loop fusion | flops 786432 | bytes 2097152 | tf_op jit(solution)/shard_map/convert_element_type | solution.py:155
  (88 shorter events, 28.5 us)
Async XLA Ops:
  0.6 77.4 %copy-start = (bf16[1024,1024]{1,0:T(8,128)(2,1)S(1)}, bf16[1024,1024]{1,0:T(8,128)(2,1)}, u32[]{:S(2)}) copy-start(bf16[1024,1024]{1,0:T(8,128)(2,1)} %param.19) | copy-start | bytes 6291460
  1.5 4.1 %collective-permute-start = (s32[2,512]{1,0:T(2,128)S(1)}, s32[2,512]{1,0:T(2,128)S(1)}, u32[]{:S(2)}, u32[]{:S(2)}) collective-permute-start(s32[2,512]{1,0:T(2,128)S(1)} %subtract_select_fusion), channel_id=1, source_target_pairs={{0,28},{4,24},{8,20},{12,16},{16,12},{20,8},{24,4},{28,0},{1,29},{... | collective-permute-start | bytes 12296 | tf_op jit(solution)/shard_map/ppermute | solution.py:8
  6.0 10.7 %copy-start.14 = (f32[256]{0:T(256)S(1)}, f32[256]{0:T(256)}, u32[]{:S(2)}) copy-start(f32[256]{0:T(256)} %param.18) | copy-start | bytes 3076
  16.7 6.9 %copy-start.13 = (f32[7,256]{1,0:T(8,128)S(1)}, f32[7,256]{1,0:T(8,128)}, u32[]{:S(2)}) copy-start(f32[7,256]{1,0:T(8,128)} %param.16) | copy-start | bytes 21508
  18.3 8.6 %copy-start.15 = (f32[256]{0:T(256)S(1)}, f32[256]{0:T(256)}, u32[]{:S(2)}) copy-start(f32[256]{0:T(256)} %param.17) | copy-start | bytes 3076
  18.3 5.3 %collective-permute-start.2 = (bf16[2,2,3,256]{3,2,1,0:T(4,128)(2,1)S(1)}, bf16[2,2,3,256]{3,2,1,0:T(4,128)(2,1)S(1)}, u32[]{:S(2)}, u32[]{:S(2)}) collective-permute-start(bf16[2,2,3,256]{3,2,1,0:T(4,128)(2,1)S(1)} %get-tuple-element.15), channel_id=1, source_target_pairs={{4,0},{8,4},{12,8},{16,12},{20,16},{24,20},{28,24},{5,1},{9,5},{13... | collective-permute-start | bytes 18440 | tf_op jit(solution)/shard_map/ppermute | solution.py:25
  21.4 5.3 %collective-permute-start.1 = (bf16[2,2,3,256]{3,2,1,0:T(4,128)(2,1)S(1)}, bf16[2,2,3,256]{3,2,1,0:T(4,128)(2,1)S(1)}, u32[]{:S(2)}, u32[]{:S(2)}) collective-permute-start(bf16[2,2,3,256]{3,2,1,0:T(4,128)(2,1)S(1)} %get-tuple-element.14), channel_id=1, source_target_pairs={{0,4},{4,8},{8,12},{12,16},{16,20},{20,24},{24,28},{1,5},{5,9},{9,... | collective-permute-start | bytes 18440 | tf_op jit(solution)/shard_map/ppermute | solution.py:23
  30.2 23.7 %collective-permute-start.5 = (bf16[1024,256]{1,0:T(8,128)(2,1)}, bf16[1024,256]{1,0:T(8,128)(2,1)}, u32[]{:S(2)}, u32[]{:S(2)}) collective-permute-start(bf16[1024,256]{1,0:T(8,128)(2,1)} %bitcast.27), channel_id=1, source_target_pairs={{0,28},{4,24},{8,20},{12,16},{16,12},{20,8},{24,4},{28,0},{1,29},{... | collective-permute-start | bytes 1572872 | tf_op jit(solution)/shard_map/ppermute | solution.py:8
  32.1 23.1 %collective-permute-start.3 = (bf16[1,1024,256]{2,1,0:T(8,128)(2,1)}, bf16[1,1024,256]{2,1,0:T(8,128)(2,1)}, u32[]{:S(2)}, u32[]{:S(2)}) collective-permute-start(bf16[1,1024,256]{2,1,0:T(8,128)(2,1)} %bitcast.14), channel_id=1, source_target_pairs={{0,2},{1,3},{2,0},{3,1},{4,6},{5,7},{6,4},{7,5},{8,10},{9,11},{10,... | collective-permute-start | bytes 1572872 | tf_op jit(solution)/shard_map/ppermute | solution.py:13
  53.9 10.6 %collective-permute-start.6 = (bf16[1,1024,256]{2,1,0:T(8,128)(2,1)}, bf16[1,1024,256]{2,1,0:T(8,128)(2,1)S(1)}, u32[]{:S(2)}, u32[]{:S(2)}) collective-permute-start(bf16[1,1024,256]{2,1,0:T(8,128)(2,1)} %bitcast.28), channel_id=1, source_target_pairs={{0,2},{1,3},{2,0},{3,1},{4,6},{5,7},{6,4},{7,5},{8,10},{9,11},{10,... | collective-permute-start | bytes 1572872 | tf_op jit(solution)/shard_map/ppermute | solution.py:13
  56.5 4.5 %copy-start.8 = (bf16[1,1,1024,256]{3,2,1,0:T(8,128)(2,1)}, bf16[1,1,1024,256]{3,2,1,0:T(8,128)(2,1)S(1)}, u32[]{:S(2)}) copy-start(bf16[1,1,1024,256]{3,2,1,0:T(8,128)(2,1)S(1)} %get-tuple-element.10) | copy-start | bytes 1572868
  56.5 4.5 %copy-start.9 = (bf16[1,1,1024,256]{3,2,1,0:T(8,128)(2,1)}, bf16[1,1,1024,256]{3,2,1,0:T(8,128)(2,1)S(1)}, u32[]{:S(2)}) copy-start(bf16[1,1,1024,256]{3,2,1,0:T(8,128)(2,1)S(1)} %get-tuple-element.11) | copy-start | bytes 1572868
  57.7 13.9 %copy-start.17 = (bf16[1024,1024]{1,0:T(8,128)(2,1)S(1)}, bf16[1024,1024]{1,0:T(8,128)(2,1)}, u32[]{:S(2)}) copy-start(bf16[1024,1024]{1,0:T(8,128)(2,1)} %param.21) | copy-start | bytes 6291460
  57.7 18.5 %collective-permute-start.4 = (bf16[2,1024,256]{2,1,0:T(8,128)(2,1)}, bf16[2,1024,256]{2,1,0:T(8,128)(2,1)}, u32[]{:S(2)}, u32[]{:S(2)}) collective-permute-start(bf16[2,1024,256]{2,1,0:T(8,128)(2,1)} %maximum_bitcast_fusion), channel_id=1, source_target_pairs={{0,1},{1,0},{2,3},{3,2},{4,5},{5,4},{6,7},{7,6},{8,9},{9,8},{10,11... | collective-permute-start | bytes 3145736 | tf_op jit(solution)/shard_map/ppermute | solution.py:13
  67.6 14.8 %collective-permute-start.7 = (bf16[2,1024,256]{2,1,0:T(8,128)(2,1)}, bf16[2,1024,256]{2,1,0:T(8,128)(2,1)}, u32[]{:S(2)}, u32[]{:S(2)}) collective-permute-start(bf16[2,1024,256]{2,1,0:T(8,128)(2,1)} %maximum_bitcast_fusion.1), channel_id=1, source_target_pairs={{0,1},{1,0},{2,3},{3,2},{4,5},{5,4},{6,7},{7,6},{8,9},{9,8},{10,11... | collective-permute-start | bytes 3145736 | tf_op jit(solution)/shard_map/ppermute | solution.py:13
  78.1 4.4 %copy-start.10 = (bf16[2,2,1024,256]{3,2,1,0:T(8,128)(2,1)}, bf16[2,2,1024,256]{3,2,1,0:T(8,128)(2,1)S(1)}, u32[]{:S(2)}) copy-start(bf16[2,2,1024,256]{3,2,1,0:T(8,128)(2,1)S(1)} %pad_maximum_fusion) | copy-start | bytes 6291460
  78.1 4.4 %copy-start.5 = (bf16[1,1,1024,256]{3,2,1,0:T(8,128)(2,1)S(1)}, bf16[1,1,1024,256]{3,2,1,0:T(8,128)(2,1)}, u32[]{:S(2)}) copy-start(bf16[1,1,1024,256]{3,2,1,0:T(8,128)(2,1)} %copy-done.4) | copy-start | bytes 1572868
  78.1 4.3 %copy-start.7 = (bf16[1,1,1024,256]{3,2,1,0:T(8,128)(2,1)S(1)}, bf16[1,1,1024,256]{3,2,1,0:T(8,128)(2,1)}, u32[]{:S(2)}) copy-start(bf16[1,1,1024,256]{3,2,1,0:T(8,128)(2,1)} %copy-done.6) | copy-start | bytes 1572868
  86.5 2.7 %copy-start.18 = (bf16[1024,1024]{1,0:T(8,128)(2,1)S(1)}, bf16[1024,1024]{1,0:T(8,128)(2,1)}, u32[]{:S(2)}) copy-start(bf16[1024,1024]{1,0:T(8,128)(2,1)} %fusion.109) | copy-start | bytes 6291460
  105.8 7.0 %copy-start.1 = (f32[1024,1024]{0,1:T(8,128)S(1)}, f32[1024,1024]{0,1:T(8,128)}, u32[]{:S(2)}) copy-start(f32[1024,1024]{0,1:T(8,128)} %convolution_add_fusion) | copy-start | bytes 12582916
  108.6 4.2 %collective-permute-start.8 = (f32[1024,2,256]{0,2,1:T(8,128)S(1)}, f32[1024,2,256]{0,2,1:T(8,128)S(1)}, u32[]{:S(2)}, u32[]{:S(2)}) collective-permute-start(f32[1024,2,256]{0,2,1:T(8,128)S(1)} %select_bitcast_fusion), channel_id=1, source_target_pairs={{0,1},{1,0},{2,3},{3,2},{4,5},{5,4},{6,7},{7,6},{8,9},{9,8},{10,11... | collective-permute-start | bytes 6291464 | tf_op jit(solution)/shard_map/ppermute | solution.py:13
  113.8 13.4 %collective-permute-start.9 = (bf16[1024,1,256]{0,2,1:T(8,128)(2,1)S(1)}, bf16[1024,1,256]{0,2,1:T(8,128)(2,1)S(1)}, u32[]{:S(2)}, u32[]{:S(2)}) collective-permute-start(bf16[1024,1,256]{0,2,1:T(8,128)(2,1)S(1)} %fusion.46), channel_id=1, source_target_pairs={{0,2},{1,3},{2,0},{3,1},{4,6},{5,7},{6,4},{7,5},{8,10},{9,11},{10,... | collective-permute-start | bytes 1572872 | tf_op jit(solution)/shard_map/ppermute | solution.py:13
  115.1 13.9 %copy-start.12 = (bf16[512,512]{1,0:T(8,128)(2,1)S(1)}, bf16[512,512]{1,0:T(8,128)(2,1)}, u32[]{:S(2)}) copy-start(bf16[512,512]{1,0:T(8,128)(2,1)} %fusion.43) | copy-start | bytes 1572868
  130.3 21.5 %collective-permute-start.10 = (bf16[2,512,256]{2,1,0:T(8,128)(2,1)}, bf16[2,512,256]{2,1,0:T(8,128)(2,1)}, u32[]{:S(2)}, u32[]{:S(2)}) collective-permute-start(bf16[2,512,256]{2,1,0:T(8,128)(2,1)} %convolution_convert_fusion), channel_id=1, source_target_pairs={{0,31},{1,30},{2,29},{3,28},{4,27},{5,26},{6,25},{7,24},{8,23},{9,... | collective-permute-start | bytes 1572872 | tf_op jit(solution)/shard_map/ppermute | solution.py:8
  (6 other events, 9.2 us)

commit v17 on v14

--- a/solution.py
+++ b/solution.py
@@ -54,9 +54,7 @@
         low = ((me >> bit) & 1) == 0
         keep = jnp.where(low, cur[:, :, 0], cur[:, :, 1])
         give = jnp.where(low, cur[:, :, 1], cur[:, :, 0])
-        if bit > 0:
-            give = give.astype(jnp.bfloat16)
-        cur = keep + partner(give, "ch", bit).astype(jnp.float32)
+        cur = keep + partner(give.astype(jnp.bfloat16), "ch", bit).astype(jnp.float32)
     return cur[:, 0]
 
 

time: 155 us -> 155 us (level)
  other arithmetic: 29.7 us -> 31.4 us
    select_n x1 -> x0, other arithmetic: 2.77 us -> none  [scatter_blocks(): give = jnp.where(low, cur[:, :, 1], cur[:, :, 0])]
    convert_element_type x1 -> x2, other arithmetic: 0.09 us -> 2.5 us  [scatter_blocks(): give.astype(jnp.bfloat16)]
    reshape x1, other arithmetic: 0.87 us -> 2.84 us  [scatter_blocks(): cur = cur.reshape(rows, -1, 2, w)]
where the time goes in v17:
time: 155 us; the launch traced here: 154 us
  waiting for transfers between devices  53.7 us (35%)
  matrix products  33.6 us (22%)
  other arithmetic  31.4 us (20%)
  starting transfers between devices  21.9 us (14%)
  local copies, waits for them, and re-layouts  6.6 us (4%)
  blocking collectives  6.16 us (4%)
    ppermute x3, waiting for transfers between devices, mirror(): return lax.ppermute(value, axes, [(k, count - 1 - k) for k in range(count)])  32.4 us
    ppermute x6, waiting for transfers between devices, partner(): lax.ppermute(value, axis, [(k, k ^ mask) for k in range(lax.axis_size(axi...  18.3 us
    dot_general x1, matrix products, local(): jnp.dot(act_fwd, w_out, preferred_element_type=jnp.float32)  12 us
    ppermute x6, starting transfers between devices, partner(): lax.ppermute(value, axis, [(k, k ^ mask) for k in range(lax.axis_size(axi...  11.2 us
    dot_general x2, matrix products, activation(): lax.dot_general(pieces, w_gate.reshape(ch_count, local_width, -1), dims,...  6.68 us
    psum x1, blocking collectives, local(): lax.psum((jnp.sum(x_fwd * x_fwd, axis=-1), jnp.sum(x_rev * x_rev, axis=-1...  6.16 us
    another operation x6, other arithmetic, gather_blocks(): cur = jnp.stack([first, second], axis=1).reshape((-1,) + block.shape)  5.8 us
    convert_element_type x2, other arithmetic, local(): return (out_forward.astype(jnp.bfloat16), out_reverse.astype(jnp.bfloat16))  5.75 us
  transfers between devices with their start and end apart: 11, of which 6 were waited for; matrix products, arithmetic and copies ran while one was open for 17% of the time, Pallas kernels for 0%

profile of v17, /device:TPU:17, one launch (start us, length us, event | category | flops | bytes accessed | tf_op | source)
XLA Modules:
  0.0 154.4 jit_solution(2934020772457990057)
XLA Ops:
  6.0 3.6 %multiply_reduce_fusion.1 = (f32[2,512]{1,0:T(2,128)S(1)}, f32[2,512,256]{2,1,0:T(8,128)S(1)}) fusion(f32[256]{0:T(256)S(1)} %bitcast.173, pred[2,512]{1,0:T(4,128)(4,1)S(1)} %get-tuple-element.28, f32[256]{0:T(256)S(1)} %bitcast.170, pred[2,512]{1,0:T(4,128)(4,1)S(1)} %get-tuple-element.26, f32[256]{0:T(256)S(1)} %bitcast.167, ...), kind=kLoop, calls=%fused_computation.78 | loop fusion | flops 6290432 | bytes 2116608 | tf_op jit(solution)/shard_map/reduce_sum | solution.py:106
  9.8 6.2 %all-reduce = (f32[2,512]{1,0:T(2,128)S(1)}, f32[2,512]{1,0:T(2,128)S(1)}) all-reduce(f32[2,512]{1,0:T(2,128)S(1)} %multiply_reduce_fusion, f32[2,512]{1,0:T(2,128)S(1)} %get-tuple-element.23), channel_id=1, replica_groups=mesh['seq'=8,'ch'=4] {'ch'}, use_global_device_ids=true, to_apply=%region_3.4 | all-reduce | flops 2048 | bytes 16384 | tf_op jit(solution)/shard_map/psum | solution.py:105
  16.0 2.8 %fusion.45 = (bf16[1,2,512,256]{3,2,1,0:T(8,128)(2,1)S(1)}, bf16[1,2,512,256]{3,2,1,0:T(8,128)(2,1)S(1)}) fusion(f32[256]{0:T(256)S(1)} %copy-done.12, f32[2,512]{1,0:T(2,128)S(1)} %get-tuple-element.42, f32[256]{0:T(256)S(1)} %bitcast.174, pred[2,512]{1,0:T(4,128)(4,1)S(1)} %get-tuple-element.28, f32[256]{0:T(256)S(1)} %bitcast.171, ...), kind=kLoop, calls=%fused_computation.82 | loop fusion | flops 4456448 | bytes 2640896 | tf_op jit(solution)/shard_map/stack | solution.py:114
  18.9 3.1 %collective-permute-start.2 = (bf16[2,2,3,256]{3,2,1,0:T(4,128)(2,1)S(1)}, bf16[2,2,3,256]{3,2,1,0:T(4,128)(2,1)S(1)}, u32[]{:S(2)}, u32[]{:S(2)}) collective-permute-start(bf16[2,2,3,256]{3,2,1,0:T(4,128)(2,1)S(1)} %get-tuple-element.15), channel_id=1, source_target_pairs={{4,0},{8,4},{12,8},{16,12},{20,16},{24,20},{28,24},{5,1},{9,5},{13... | collective-permute-start | bytes 18440 | tf_op jit(solution)/shard_map/ppermute | solution.py:25
  21.9 2.2 %collective-permute-start.1 = (bf16[2,2,3,256]{3,2,1,0:T(4,128)(2,1)S(1)}, bf16[2,2,3,256]{3,2,1,0:T(4,128)(2,1)S(1)}, u32[]{:S(2)}, u32[]{:S(2)}) collective-permute-start(bf16[2,2,3,256]{3,2,1,0:T(4,128)(2,1)S(1)} %get-tuple-element.14), channel_id=1, source_target_pairs={{0,4},{4,8},{8,12},{12,16},{16,20},{20,24},{24,28},{1,5},{5,9},{9,... | collective-permute-start | bytes 18440 | tf_op jit(solution)/shard_map/ppermute | solution.py:23
  24.2 3.0 %collective-permute-done.1 = bf16[2,2,3,256]{3,2,1,0:T(4,128)(2,1)S(1)} collective-permute-done((bf16[2,2,3,256]{3,2,1,0:T(4,128)(2,1)S(1)}, bf16[2,2,3,256]{3,2,1,0:T(4,128)(2,1)S(1)}, u32[]{:S(2)}, u32[]{:S(2)}) %collective-permute-start.1) | collective-permute-done | bytes 6176 | tf_op jit(solution)/shard_map/ppermute | solution.py:23
  33.9 20.6 %collective-permute-done.5 = bf16[1024,256]{1,0:T(8,128)(2,1)} collective-permute-done((bf16[1024,256]{1,0:T(8,128)(2,1)}, bf16[1024,256]{1,0:T(8,128)(2,1)}, u32[]{:S(2)}, u32[]{:S(2)}) %collective-permute-start.5) | collective-permute-done | bytes 524320 | tf_op jit(solution)/shard_map/ppermute | solution.py:8
  58.2 3.4 %collective-permute-start.4 = (bf16[2,1024,256]{2,1,0:T(8,128)(2,1)}, bf16[2,1024,256]{2,1,0:T(8,128)(2,1)}, u32[]{:S(2)}, u32[]{:S(2)}) collective-permute-start(bf16[2,1024,256]{2,1,0:T(8,128)(2,1)} %maximum_bitcast_fusion), channel_id=1, source_target_pairs={{0,1},{1,0},{2,3},{3,2},{4,5},{5,4},{6,7},{7,6},{8,9},{9,8},{10,11... | collective-permute-start | bytes 3145736 | tf_op jit(solution)/shard_map/ppermute | solution.py:13
  61.6 3.5 %collective-permute-done.6 = bf16[1,1024,256]{2,1,0:T(8,128)(2,1)S(1)} collective-permute-done((bf16[1,1024,256]{2,1,0:T(8,128)(2,1)}, bf16[1,1024,256]{2,1,0:T(8,128)(2,1)S(1)}, u32[]{:S(2)}, u32[]{:S(2)}) %collective-permute-start.6) | collective-permute-done | bytes 524320 | tf_op jit(solution)/shard_map/ppermute | solution.py:13
  68.2 3.9 %collective-permute-start.7 = (bf16[2,1024,256]{2,1,0:T(8,128)(2,1)}, bf16[2,1024,256]{2,1,0:T(8,128)(2,1)}, u32[]{:S(2)}, u32[]{:S(2)}) collective-permute-start(bf16[2,1024,256]{2,1,0:T(8,128)(2,1)} %maximum_bitcast_fusion.1), channel_id=1, source_target_pairs={{0,1},{1,0},{2,3},{3,2},{4,5},{5,4},{6,7},{7,6},{8,9},{9,8},{10,11... | collective-permute-start | bytes 3145736 | tf_op jit(solution)/shard_map/ppermute | solution.py:13
  72.1 4.6 %fusion.110 = bf16[1024,1024]{1,0:T(8,128)(2,1)} fusion(bf16[1024,1024]{1,0:T(8,128)(2,1)S(1)} %copy-done.15, s32[1024]{0:T(1024)S(1)} %get-tuple-element.50, s32[1024]{0:T(1024)S(1)} %get-tuple-element.51, s32[1024]{0:T(1024)S(1)} %get-tuple-element.49, s32[1024]{0:T(1024)S(1)} %get-tuple-element.52, pred[1024]{0:T(1024)(128)(4,1)S(1)} %get-tuple-element.53, ...), kind=kOutput, calls=%fused_computation.42.clone.1 | convolution fusion | flops 2157969408 | bytes 4212736 | tf_op jit(solution)/shard_map/dot_general | solution.py:143
  78.7 4.3 %fusion.87 = f32[1024,1024,1]{1,0,2:T(8,128)} fusion(bf16[4,1024,256]{2,1,0:T(8,128)(2,1)S(1)} %bitcast.156, bf16[4,256,1024]{2,1,0:T(8,128)(2,1)S(1)} %bitcast.151), kind=kOutput, calls=%fused_computation.160 | convolution fusion | flops 2147483648 | bytes 8388608 | tf_op jit(solution)/shard_map/dot_general | solution.py:132
  84.8 2.3 %fusion.88 = f32[1024,1024,1]{1,0,2:T(8,128)S(1)} fusion(bf16[4,1024,256]{2,1,0:T(8,128)(2,1)S(1)} %bitcast.158, bf16[4,256,1024]{2,1,0:T(8,128)(2,1)S(1)} %bitcast.152), kind=kOutput, calls=%fused_computation.161 | convolution fusion | flops 2147483648 | bytes 8388608 | tf_op jit(solution)/shard_map/dot_general | solution.py:132
  87.1 2.7 %fusion = bf16[1024,1024]{1,0:T(8,128)(2,1)S(1)} fusion(f32[1024,1024,1]{1,0,2:T(8,128)S(1)} %fusion.88, bf16[4,1024,256]{2,1,0:T(8,128)(2,1)S(1)} %bitcast.159, bf16[4,256,1024]{2,1,0:T(8,128)(2,1)S(1)} %bitcast.184), kind=kOutput, calls=%fused_computation.1 | convolution fusion | flops 2153775104 | bytes 10485760 | tf_op jit(solution)/shard_map/dot_general | solution.py:135
  89.8 4.6 %fusion.23 = f32[1024,1024]{0,1:T(8,128)} fusion(bf16[1024,1024]{1,0:T(8,128)(2,1)S(1)} %fusion, bf16[1024,1024]{1,0:T(8,128)(2,1)S(1)} %copy-done.16), kind=kOutput, calls=%fused_computation.41 | convolution fusion | flops 2147483648 | bytes 8388608 | tf_op jit(solution)/shard_map/dot_general | solution.py:144
  94.4 12.0 %convolution_add_fusion = f32[1024,1024]{0,1:T(8,128)} fusion(f32[1024,1024]{0,1:T(8,128)} %fusion.23, bf16[1024,1024]{1,0:T(8,128)(2,1)} %param.21, f32[1024,1024,1]{1,0,2:T(8,128)} %fusion.87, bf16[4,1024,256]{2,1,0:T(8,128)(2,1)} %bitcast.157, bf16[4,256,1024]{2,1,0:T(8,128)(2,1)} %bitcast.183), kind=kOutput, calls=%fused_computation.56 | convolution fusion | flops 4302307328 | bytes 18874368 | tf_op jit(solution)/shard_map/dot_general | solution.py:144
  106.4 2.4 %fusion.42 = bf16[1024,2,256]{0,2,1:T(8,128)(2,1)S(1)} fusion(f32[1024,2,2,256]{0,3,2,1:T(8,128)} %bitcast.153, pred[]{:T(512)S(6)} %eq.102), kind=kLoop, calls=%fused_computation.61 | loop fusion | flops 524288 | bytes 3145729 | tf_op jit(solution)/shard_map/convert_element_type | solution.py:57
  108.9 2.6 %collective-permute-done.8 = bf16[1024,2,256]{0,2,1:T(8,128)(2,1)S(1)} collective-permute-done((bf16[1024,2,256]{0,2,1:T(8,128)(2,1)S(1)}, bf16[1024,2,256]{0,2,1:T(8,128)(2,1)S(1)}, u32[]{:S(2)}, u32[]{:S(2)}) %collective-permute-start.8) | collective-permute-done | bytes 1048608 | tf_op jit(solution)/shard_map/ppermute | solution.py:13
  111.5 2.8 %fusion.22 = f32[1024,1,2,256]{0,3,2,1:T(8,128)S(1)} fusion(bf16[1024,2,256]{0,2,1:T(8,128)(2,1)S(1)} %collective-permute-done.8, f32[1024,2,2,256]{0,3,2,1:T(8,128)} %bitcast.154, pred[]{:T(512)S(6)} %eq.102), kind=kLoop, calls=%fused_computation.39 | loop fusion | flops 1572864 | bytes 7340033 | tf_op jit(solution)/shard_map/reshape | solution.py:53
  115.8 12.1 %collective-permute-done.9 = bf16[1024,1,256]{0,2,1:T(8,128)(2,1)S(1)} collective-permute-done((bf16[1024,1,256]{0,2,1:T(8,128)(2,1)S(1)}, bf16[1024,1,256]{0,2,1:T(8,128)(2,1)S(1)}, u32[]{:S(2)}, u32[]{:S(2)}) %collective-permute-start.9) | collective-permute-done | bytes 524320 | tf_op jit(solution)/shard_map/ppermute | solution.py:13
  131.0 3.3 %collective-permute-start.10 = (bf16[2,512,256]{2,1,0:T(8,128)(2,1)}, bf16[2,512,256]{2,1,0:T(8,128)(2,1)}, u32[]{:S(2)}, u32[]{:S(2)}) collective-permute-start(bf16[2,512,256]{2,1,0:T(8,128)(2,1)} %convolution_convert_fusion), channel_id=1, source_target_pairs={{0,31},{1,30},{2,29},{3,28},{4,27},{5,26},{6,25},{7,24},{8,23},{9,... | collective-permute-start | bytes 1572872 | tf_op jit(solution)/shard_map/ppermute | solution.py:8
  134.4 2.5 %copy.19 = f32[1024,1,256]{2,0,1:T(8,128)} copy(f32[1024,1,256]{0,2,1:T(8,128)} %copy-done.1) | data formatting | bytes 2097152 | tf_op jit(solution)/shard_map/add | solution.py:57
  136.9 3.8 %add_convert_fusion.1 = bf16[2,512,256]{2,1,0:T(8,128)(2,1)} fusion(f32[2,512,256]{2,1,0:T(8,128)} %bitcast.155, f32[256]{0:T(256)S(1)} %bitcast.175, pred[2,512]{1,0:T(4,128)(4,1)S(1)} %get-tuple-element.28, f32[256]{0:T(256)S(1)} %bitcast.172, pred[2,512]{1,0:T(4,128)(4,1)S(1)} %get-tuple-element.26, f32[256]{0:T(256)S(1)} %bitcast.169, ...), kind=kLoop, calls=%fused_computation.66 | loop fusion | flops 3407872 | bytes 2107392 | tf_op jit(solution)/shard_map/convert_element_type | solution.py:153
  140.7 11.7 %collective-permute-done.10 = bf16[2,512,256]{2,1,0:T(8,128)(2,1)} collective-permute-done((bf16[2,512,256]{2,1,0:T(8,128)(2,1)}, bf16[2,512,256]{2,1,0:T(8,128)(2,1)}, u32[]{:S(2)}, u32[]{:S(2)}) %collective-permute-start.10) | collective-permute-done | bytes 524320 | tf_op jit(solution)/shard_map/ppermute | solution.py:8
  (83 shorter events, 29.1 us)
Async XLA Ops:
  0.6 78.0 %copy-start = (bf16[1024,1024]{1,0:T(8,128)(2,1)S(1)}, bf16[1024,1024]{1,0:T(8,128)(2,1)}, u32[]{:S(2)}) copy-start(bf16[1024,1024]{1,0:T(8,128)(2,1)} %param.19) | copy-start | bytes 6291460
  0.6 15.3 %copy-start.12 = (f32[256]{0:T(256)S(1)}, f32[256]{0:T(256)}, u32[]{:S(2)}) copy-start(f32[256]{0:T(256)} %param.18) | copy-start | bytes 3076
  1.5 4.1 %collective-permute-start = (s32[2,512]{1,0:T(2,128)S(1)}, s32[2,512]{1,0:T(2,128)S(1)}, u32[]{:S(2)}, u32[]{:S(2)}) collective-permute-start(s32[2,512]{1,0:T(2,128)S(1)} %subtract_select_fusion), channel_id=1, source_target_pairs={{0,28},{4,24},{8,20},{12,16},{16,12},{20,8},{24,4},{28,0},{1,29},{... | collective-permute-start | bytes 12296 | tf_op jit(solution)/shard_map/ppermute | solution.py:8
  9.8 14.4 %copy-start.11 = (f32[7,256]{1,0:T(8,128)S(1)}, f32[7,256]{1,0:T(8,128)}, u32[]{:S(2)}) copy-start(f32[7,256]{1,0:T(8,128)} %param.16) | copy-start | bytes 21508
  18.8 8.6 %copy-start.13 = (f32[256]{0:T(256)S(1)}, f32[256]{0:T(256)}, u32[]{:S(2)}) copy-start(f32[256]{0:T(256)} %param.17) | copy-start | bytes 3076
  18.9 5.3 %collective-permute-start.2 = (bf16[2,2,3,256]{3,2,1,0:T(4,128)(2,1)S(1)}, bf16[2,2,3,256]{3,2,1,0:T(4,128)(2,1)S(1)}, u32[]{:S(2)}, u32[]{:S(2)}) collective-permute-start(bf16[2,2,3,256]{3,2,1,0:T(4,128)(2,1)S(1)} %get-tuple-element.15), channel_id=1, source_target_pairs={{4,0},{8,4},{12,8},{16,12},{20,16},{24,20},{28,24},{5,1},{9,5},{13... | collective-permute-start | bytes 18440 | tf_op jit(solution)/shard_map/ppermute | solution.py:25
  21.9 5.3 %collective-permute-start.1 = (bf16[2,2,3,256]{3,2,1,0:T(4,128)(2,1)S(1)}, bf16[2,2,3,256]{3,2,1,0:T(4,128)(2,1)S(1)}, u32[]{:S(2)}, u32[]{:S(2)}) collective-permute-start(bf16[2,2,3,256]{3,2,1,0:T(4,128)(2,1)S(1)} %get-tuple-element.14), channel_id=1, source_target_pairs={{0,4},{4,8},{8,12},{12,16},{16,20},{20,24},{24,28},{1,5},{5,9},{9,... | collective-permute-start | bytes 18440 | tf_op jit(solution)/shard_map/ppermute | solution.py:23
  30.8 23.7 %collective-permute-start.5 = (bf16[1024,256]{1,0:T(8,128)(2,1)}, bf16[1024,256]{1,0:T(8,128)(2,1)}, u32[]{:S(2)}, u32[]{:S(2)}) collective-permute-start(bf16[1024,256]{1,0:T(8,128)(2,1)} %bitcast.27), channel_id=1, source_target_pairs={{0,28},{4,24},{8,20},{12,16},{16,12},{20,8},{24,4},{28,0},{1,29},{... | collective-permute-start | bytes 1572872 | tf_op jit(solution)/shard_map/ppermute | solution.py:8
  32.6 23.1 %collective-permute-start.3 = (bf16[1,1024,256]{2,1,0:T(8,128)(2,1)}, bf16[1,1024,256]{2,1,0:T(8,128)(2,1)}, u32[]{:S(2)}, u32[]{:S(2)}) collective-permute-start(bf16[1,1024,256]{2,1,0:T(8,128)(2,1)} %bitcast.14), channel_id=1, source_target_pairs={{0,2},{1,3},{2,0},{3,1},{4,6},{5,7},{6,4},{7,5},{8,10},{9,11},{10,... | collective-permute-start | bytes 1572872 | tf_op jit(solution)/shard_map/ppermute | solution.py:13
  54.5 10.6 %collective-permute-start.6 = (bf16[1,1024,256]{2,1,0:T(8,128)(2,1)}, bf16[1,1024,256]{2,1,0:T(8,128)(2,1)S(1)}, u32[]{:S(2)}, u32[]{:S(2)}) collective-permute-start(bf16[1,1024,256]{2,1,0:T(8,128)(2,1)} %bitcast.28), channel_id=1, source_target_pairs={{0,2},{1,3},{2,0},{3,1},{4,6},{5,7},{6,4},{7,5},{8,10},{9,11},{10,... | collective-permute-start | bytes 1572872 | tf_op jit(solution)/shard_map/ppermute | solution.py:13
  57.0 4.5 %copy-start.6 = (bf16[1,1,1024,256]{3,2,1,0:T(8,128)(2,1)}, bf16[1,1,1024,256]{3,2,1,0:T(8,128)(2,1)S(1)}, u32[]{:S(2)}) copy-start(bf16[1,1,1024,256]{3,2,1,0:T(8,128)(2,1)S(1)} %get-tuple-element.10) | copy-start | bytes 1572868
  57.0 4.5 %copy-start.7 = (bf16[1,1,1024,256]{3,2,1,0:T(8,128)(2,1)}, bf16[1,1,1024,256]{3,2,1,0:T(8,128)(2,1)S(1)}, u32[]{:S(2)}) copy-start(bf16[1,1,1024,256]{3,2,1,0:T(8,128)(2,1)S(1)} %get-tuple-element.11) | copy-start | bytes 1572868
  58.2 13.9 %copy-start.15 = (bf16[1024,1024]{1,0:T(8,128)(2,1)S(1)}, bf16[1024,1024]{1,0:T(8,128)(2,1)}, u32[]{:S(2)}) copy-start(bf16[1024,1024]{1,0:T(8,128)(2,1)} %param.21) | copy-start | bytes 6291460
  58.2 18.6 %collective-permute-start.4 = (bf16[2,1024,256]{2,1,0:T(8,128)(2,1)}, bf16[2,1024,256]{2,1,0:T(8,128)(2,1)}, u32[]{:S(2)}, u32[]{:S(2)}) collective-permute-start(bf16[2,1024,256]{2,1,0:T(8,128)(2,1)} %maximum_bitcast_fusion), channel_id=1, source_target_pairs={{0,1},{1,0},{2,3},{3,2},{4,5},{5,4},{6,7},{7,6},{8,9},{9,8},{10,11... | collective-permute-start | bytes 3145736 | tf_op jit(solution)/shard_map/ppermute | solution.py:13
  68.2 14.8 %collective-permute-start.7 = (bf16[2,1024,256]{2,1,0:T(8,128)(2,1)}, bf16[2,1024,256]{2,1,0:T(8,128)(2,1)}, u32[]{:S(2)}, u32[]{:S(2)}) collective-permute-start(bf16[2,1024,256]{2,1,0:T(8,128)(2,1)} %maximum_bitcast_fusion.1), channel_id=1, source_target_pairs={{0,1},{1,0},{2,3},{3,2},{4,5},{5,4},{6,7},{7,6},{8,9},{9,8},{10,11... | collective-permute-start | bytes 3145736 | tf_op jit(solution)/shard_map/ppermute | solution.py:13
  78.6 4.4 %copy-start.8 = (bf16[2,2,1024,256]{3,2,1,0:T(8,128)(2,1)}, bf16[2,2,1024,256]{3,2,1,0:T(8,128)(2,1)S(1)}, u32[]{:S(2)}) copy-start(bf16[2,2,1024,256]{3,2,1,0:T(8,128)(2,1)S(1)} %pad_maximum_fusion) | copy-start | bytes 6291460
  78.6 4.4 %copy-start.3 = (bf16[1,1,1024,256]{3,2,1,0:T(8,128)(2,1)S(1)}, bf16[1,1,1024,256]{3,2,1,0:T(8,128)(2,1)}, u32[]{:S(2)}) copy-start(bf16[1,1,1024,256]{3,2,1,0:T(8,128)(2,1)} %copy-done.2) | copy-start | bytes 1572868
  78.7 4.4 %copy-start.5 = (bf16[1,1,1024,256]{3,2,1,0:T(8,128)(2,1)S(1)}, bf16[1,1,1024,256]{3,2,1,0:T(8,128)(2,1)}, u32[]{:S(2)}) copy-start(bf16[1,1,1024,256]{3,2,1,0:T(8,128)(2,1)} %copy-done.4) | copy-start | bytes 1572868
  84.7 2.4 %copy-start.14 = (bf16[1024,1024]{1,0:T(8,128)(2,1)S(1)}, bf16[1024,1024]{1,0:T(8,128)(2,1)}, u32[]{:S(2)}) copy-start(bf16[1024,1024]{1,0:T(8,128)(2,1)} %param.20) | copy-start | bytes 6291460
  87.1 2.7 %copy-start.16 = (bf16[1024,1024]{1,0:T(8,128)(2,1)S(1)}, bf16[1024,1024]{1,0:T(8,128)(2,1)}, u32[]{:S(2)}) copy-start(bf16[1024,1024]{1,0:T(8,128)(2,1)} %fusion.110) | copy-start | bytes 6291460
  108.8 2.7 %collective-permute-start.8 = (bf16[1024,2,256]{0,2,1:T(8,128)(2,1)S(1)}, bf16[1024,2,256]{0,2,1:T(8,128)(2,1)S(1)}, u32[]{:S(2)}, u32[]{:S(2)}) collective-permute-start(bf16[1024,2,256]{0,2,1:T(8,128)(2,1)S(1)} %fusion.42), channel_id=1, source_target_pairs={{0,1},{1,0},{2,3},{3,2},{4,5},{5,4},{6,7},{7,6},{8,9},{9,8},{10,11... | collective-permute-start | bytes 3145736 | tf_op jit(solution)/shard_map/ppermute | solution.py:13
  114.5 13.4 %collective-permute-start.9 = (bf16[1024,1,256]{0,2,1:T(8,128)(2,1)S(1)}, bf16[1024,1,256]{0,2,1:T(8,128)(2,1)S(1)}, u32[]{:S(2)}, u32[]{:S(2)}) collective-permute-start(bf16[1024,1,256]{0,2,1:T(8,128)(2,1)S(1)} %fusion.47), channel_id=1, source_target_pairs={{0,2},{1,3},{2,0},{3,1},{4,6},{5,7},{6,4},{7,5},{8,10},{9,11},{10,... | collective-permute-start | bytes 1572872 | tf_op jit(solution)/shard_map/ppermute | solution.py:13
  115.8 13.9 %copy-start.10 = (bf16[512,512]{1,0:T(8,128)(2,1)S(1)}, bf16[512,512]{1,0:T(8,128)(2,1)}, u32[]{:S(2)}) copy-start(bf16[512,512]{1,0:T(8,128)(2,1)} %fusion.44) | copy-start | bytes 1572868
  131.0 21.4 %collective-permute-start.10 = (bf16[2,512,256]{2,1,0:T(8,128)(2,1)}, bf16[2,512,256]{2,1,0:T(8,128)(2,1)}, u32[]{:S(2)}, u32[]{:S(2)}) collective-permute-start(bf16[2,512,256]{2,1,0:T(8,128)(2,1)} %convolution_convert_fusion), channel_id=1, source_target_pairs={{0,31},{1,30},{2,29},{3,28},{4,27},{5,26},{6,25},{7,24},{8,23},{9,... | collective-permute-start | bytes 1572872 | tf_op jit(solution)/shard_map/ppermute | solution.py:8
  (4 other events, 5.8 us)
